TPU v7x, 32 devices: a whole 2x2x4 slice. The times are simulated.
32 devices in a mesh: rows: 4 (over y, x), cols: 8 (over z, core).
Axes of the slice: x: 2, y: 2, z: 4, core: 2. Of those that a mesh axis runs over, the one named last changes fastest.
Arguments:
- features: bfloat16 [32, 128, 1024], P('rows', 'cols'), may hold values from -24 to 24
- w_query: bfloat16 [1024, 1024], replicated, may hold values from -0.1875 to 0.1875
- w_key: bfloat16 [1024, 1024], replicated, may hold values from -0.1875 to 0.1875
- w_value: bfloat16 [1024, 1024], replicated, may hold values from -0.1875 to 0.1875
- w_out: bfloat16 [1024, 1024], replicated, may hold values from -0.1875 to 0.1875
- reg_pos: int32 [32], replicated, may hold values from 0 to 4095, as said below
- grad_out: bfloat16 [32, 128, 1024], P('rows', 'cols'), may hold values from -6 to 6
Outputs:
- layer_out: bfloat16 [32, 128, 1024], P('rows', 'cols')
- grad_in: bfloat16 [32, 128, 1024], P('rows', 'cols')
Inputs may be any that keep to these rules, and one draw needn't show every extreme that they name: The 32 global tokens are distinct, one in each tile of 128 tokens: reg_pos[r] lies in tile row r // 8 and tile column r % 8, tiles counted row by row.
All inputs are finite; a program needn't handle non-finite values.
Results may differ from a plain program's by a relative error of at most 0.03.
The roundings to bfloat16 on the way count: a program that leaves them out, or rounds other values in their place, can miss the bound.
Values may be sent and summed in bfloat16 or wider, within the bound.
No kernel may reach another device: no remote copies, remote signals or barrier semaphores. Data moves between devices by JAX's collectives and lax.ppermute only.
A program may use at most 128 MiB of HBM per device.

v0:
```python
import math

import jax
import jax.numpy as jnp
from jax import lax
from jax.sharding import PartitionSpec as P

HEADS = 16
KW = 13
RAD = 6
BLK = 8


def with_halo(block, sides, width):
    for axis, dim in sides:
        count = lax.axis_size(axis)
        forward = [(i, i + 1) for i in range(count - 1)]
        backward = [(target, source) for source, target in forward]
        low = lax.ppermute(
            lax.slice_in_dim(block, block.shape[dim] - width, None, axis=dim), axis, forward
        )
        high = lax.ppermute(lax.slice_in_dim(block, 0, width, axis=dim), axis, backward)
        block = jnp.concatenate([low, block, high], axis=dim)
    return block


def from_behind(x, axis, by):
    size = lax.axis_size(axis)
    pairs = [(i, i + by) for i in range(size) if 0 <= i + by < size]
    return lax.ppermute(x, axis, pairs)


def axis_mask(first_cell, extent, block_count):
    block_ids = jnp.arange(block_count, dtype=jnp.int32)[:, None, None]
    within = jnp.arange(BLK, dtype=jnp.int32)[None, :, None]
    offsets = jnp.arange(BLK + 2 * RAD, dtype=jnp.int32)[None, None, :]
    query_cell = first_cell + BLK * block_ids + within
    window_start = jnp.clip(query_cell - RAD, 0, extent - KW)
    key_cell = first_cell + BLK * block_ids - RAD + offsets
    return (key_cell >= window_start) & (key_cell <= window_start + KW - 1)


def block_mask(row_mask, col_mask):
    row_blocks = row_mask.shape[0]
    col_blocks = col_mask.shape[0]
    span_cells = BLK + 2 * RAD
    joined = row_mask[:, None, :, None, :, None] & col_mask[None, :, None, :, None, :]
    return joined.reshape(row_blocks * col_blocks, BLK * BLK, span_cells * span_cells)


def to_blocks(cell_grid, row_blocks, col_blocks):
    channels = cell_grid.shape[-1]
    shaped = cell_grid.reshape(row_blocks, BLK, col_blocks, BLK, channels).transpose(0, 2, 1, 3, 4)
    return shaped.reshape(row_blocks * col_blocks, BLK * BLK, channels)


def from_blocks(blocks, row_blocks, col_blocks):
    channels = blocks.shape[-1]
    shaped = blocks.reshape(row_blocks, col_blocks, BLK, BLK, channels).transpose(0, 2, 1, 3, 4)
    return shaped.reshape(row_blocks * BLK, col_blocks * BLK, channels)


def windows(framed, row_blocks, col_blocks):
    channels = framed.shape[-1]
    span_cells = BLK + 2 * RAD
    block_ids = jnp.arange(row_blocks * col_blocks, dtype=jnp.int32)

    def cut_box(block_id):
        top_cell = block_id // col_blocks * BLK
        left_cell = block_id % col_blocks * BLK
        box = lax.dynamic_slice(
            framed, (top_cell, left_cell, jnp.int32(0)), (span_cells, span_cells, channels)
        )
        return box.reshape(span_cells * span_cells, channels)

    return jax.vmap(cut_box)(block_ids)


def windows_adjoint(block_grads, row_blocks, col_blocks):
    channels = block_grads.shape[-1]
    span_cells = BLK + 2 * RAD
    total = jnp.zeros(
        (row_blocks * BLK + 2 * RAD, col_blocks * BLK + 2 * RAD, channels), jnp.float32
    )

    def add_box(block_id, accum):
        top_cell = block_id // col_blocks * BLK
        left_cell = block_id % col_blocks * BLK
        start = (top_cell, left_cell, jnp.int32(0))
        piece = lax.dynamic_index_in_dim(block_grads, block_id, 0, keepdims=False).reshape(
            span_cells, span_cells, channels
        )
        current = lax.dynamic_slice(accum, start, (span_cells, span_cells, channels))
        return lax.dynamic_update_slice(accum, current + piece, start)

    return lax.fori_loop(0, row_blocks * col_blocks, add_box, total)


def split_heads(query_blocks, window_kv, global_kv):
    block_count, query_count, model_width = query_blocks.shape
    head_size = model_width // HEADS
    query_heads = query_blocks.reshape(block_count, query_count, HEADS, head_size)
    window_keys = window_kv[:, :, :model_width].reshape(block_count, -1, HEADS, head_size)
    window_values = window_kv[:, :, model_width:].reshape(block_count, -1, HEADS, head_size)
    global_keys = global_kv[:, :model_width].reshape(-1, HEADS, head_size)
    global_values = global_kv[:, model_width:].reshape(-1, HEADS, head_size)
    return (query_heads, window_keys, window_values, global_keys, global_values)


def einsum_wide(form, left, right):
    return jnp.einsum(form, left, right, preferred_element_type=jnp.float32)


def forward_block(query_blocks, window_kv, global_kv, window_mask):
    block_count, query_count, model_width = query_blocks.shape
    score_scale = 1.0 / math.sqrt(model_width // HEADS)
    query_heads, window_keys, window_values, global_keys, global_values = split_heads(
        query_blocks, window_kv, global_kv
    )
    window_scores = einsum_wide("bqhd,bkhd->bhqk", query_heads, window_keys) * score_scale
    window_scores = jnp.where(window_mask[:, None], window_scores, -1e30)
    global_scores = einsum_wide("bqhd,rhd->bhqr", query_heads, global_keys) * score_scale
    row_max = jnp.maximum(
        jnp.max(window_scores, axis=-1, keepdims=True),
        jnp.max(global_scores, axis=-1, keepdims=True),
    )
    window_exp = jnp.exp(window_scores - row_max)
    global_exp = jnp.exp(global_scores - row_max)
    denominator = jnp.sum(window_exp, axis=-1, keepdims=True) + jnp.sum(
        global_exp, axis=-1, keepdims=True
    )
    window_probs = window_exp / denominator
    global_probs = global_exp / denominator
    window_rounded = window_probs.astype(jnp.bfloat16)
    global_rounded = global_probs.astype(jnp.bfloat16)
    attended = einsum_wide("bhqk,bkhd->bqhd", window_rounded, window_values) + einsum_wide(
        "bhqr,rhd->bqhd", global_rounded, global_values
    )
    attended = attended.astype(jnp.bfloat16).reshape(block_count, query_count, model_width)
    return ((window_probs, global_probs, window_rounded, global_rounded), attended)


def backward_block(query_blocks, window_kv, global_kv, probs, attended, grad_blocks):
    block_count, query_count, model_width = query_blocks.shape
    head_size = model_width // HEADS
    score_scale = 1.0 / math.sqrt(head_size)
    window_probs, global_probs, window_rounded, global_rounded = probs
    query_heads, window_keys, window_values, global_keys, global_values = split_heads(
        query_blocks, window_kv, global_kv
    )
    grad_heads = grad_blocks.reshape(block_count, query_count, HEADS, head_size)
    attended_heads = attended.reshape(block_count, query_count, HEADS, head_size)
    delta_terms = einsum_wide("bqhd,bqhd->bhq", grad_heads, attended_heads)[..., None]
    window_dots = einsum_wide("bqhd,bkhd->bhqk", grad_heads, window_values)
    global_dots = einsum_wide("bqhd,rhd->bhqr", grad_heads, global_values)
    window_slopes = (window_probs * (window_dots - delta_terms) * score_scale).astype(jnp.bfloat16)
    global_slopes = (global_probs * (global_dots - delta_terms) * score_scale).astype(jnp.bfloat16)
    query_grads = einsum_wide("bhqk,bkhd->bqhd", window_slopes, window_keys) + einsum_wide(
        "bhqr,rhd->bqhd", global_slopes, global_keys
    )
    query_grads = query_grads.astype(jnp.bfloat16).reshape(block_count, query_count, model_width)
    window_key_grads = einsum_wide("bhqk,bqhd->bkhd", window_slopes, query_heads).reshape(
        block_count, -1, model_width
    )
    window_value_grads = einsum_wide("bhqk,bqhd->bkhd", window_rounded, grad_heads).reshape(
        block_count, -1, model_width
    )
    global_key_grads = einsum_wide("bhqr,bqhd->rhd", global_slopes, query_heads).reshape(
        -1, model_width
    )
    global_value_grads = einsum_wide("bhqr,bqhd->rhd", global_rounded, grad_heads).reshape(
        -1, model_width
    )
    return (
        query_grads,
        jnp.concatenate([window_key_grads, window_value_grads], axis=-1),
        jnp.concatenate([global_key_grads, global_value_grads], axis=-1),
    )


def shards(features, w_query, w_key, w_value, w_out, reg_pos, grad_out):
    tile_rows, tile_cols, model_width = features.shape
    row_count = lax.axis_size("rows")
    col_count = lax.axis_size("cols")
    row_index = lax.axis_index("rows")
    col_index = lax.axis_index("cols")
    first_row = row_index * tile_rows
    first_col = col_index * tile_cols
    row_blocks = tile_rows // BLK
    col_blocks = tile_cols // BLK
    flat_tokens = features.reshape(-1, model_width)
    queries = jnp.dot(flat_tokens, w_query, preferred_element_type=jnp.float32).astype(jnp.bfloat16)
    keys_local = jnp.dot(flat_tokens, w_key, preferred_element_type=jnp.float32).astype(
        jnp.bfloat16
    )
    values_local = jnp.dot(flat_tokens, w_value, preferred_element_type=jnp.float32).astype(
        jnp.bfloat16
    )
    key_value = jnp.concatenate([keys_local, values_local], axis=1)
    framed = with_halo(
        key_value.reshape(tile_rows, tile_cols, 2 * model_width), (("rows", 0), ("cols", 1)), RAD
    )
    row_cells = first_row + jnp.arange(tile_rows, dtype=jnp.int32)
    col_cells = first_col + jnp.arange(tile_cols, dtype=jnp.int32)
    places = (row_cells[:, None] * (tile_cols * col_count) + col_cells[None, :]).reshape(-1)
    own_index = row_index * col_count + col_index
    own_place = lax.dynamic_slice_in_dim(reg_pos, own_index, 1)
    selector = (reg_pos[:, None] == places[None, :]).astype(jnp.bfloat16)
    picked = jnp.dot(selector, key_value, preferred_element_type=jnp.float32)
    global_kv = lax.psum(picked, ("rows", "cols")).astype(jnp.bfloat16)
    window_kv = windows(framed, row_blocks, col_blocks)
    window_mask = block_mask(
        axis_mask(first_row, tile_rows * row_count, row_blocks),
        axis_mask(first_col, tile_cols * col_count, col_blocks),
    )
    query_blocks = to_blocks(
        queries.reshape(tile_rows, tile_cols, model_width), row_blocks, col_blocks
    )
    probs, attended = forward_block(query_blocks, window_kv, global_kv, window_mask)
    attended_flat = from_blocks(attended, row_blocks, col_blocks).reshape(-1, model_width)
    layer_out = (
        jnp.dot(attended_flat, w_out, preferred_element_type=jnp.float32)
        .astype(jnp.bfloat16)
        .reshape(features.shape)
    )
    grad_attended = jnp.dot(
        grad_out.reshape(-1, model_width), w_out.T, preferred_element_type=jnp.float32
    ).astype(jnp.bfloat16)
    grad_blocks = to_blocks(
        grad_attended.reshape(tile_rows, tile_cols, model_width), row_blocks, col_blocks
    )
    query_grads, window_grads, global_grads = backward_block(
        query_blocks, window_kv, global_kv, probs, attended, grad_blocks
    )
    frame_grads = windows_adjoint(window_grads, row_blocks, col_blocks)
    left_rim = frame_grads[:, :RAD]
    right_rim = frame_grads[:, tile_cols + RAD :]
    centre = frame_grads[:, RAD : tile_cols + RAD]
    from_right = from_behind(left_rim.astype(jnp.bfloat16), "cols", -1).astype(left_rim.dtype)
    from_left = from_behind(right_rim.astype(jnp.bfloat16), "cols", 1).astype(right_rim.dtype)
    centre = centre.at[:, tile_cols - RAD :].add(from_right).at[:, :RAD].add(from_left)
    upper_rim = centre[:RAD]
    lower_rim = centre[tile_rows + RAD :]
    middle = centre[RAD : tile_rows + RAD]
    from_below = from_behind(upper_rim.astype(jnp.bfloat16), "rows", -1).astype(upper_rim.dtype)
    from_above = from_behind(lower_rim.astype(jnp.bfloat16), "rows", 1).astype(lower_rim.dtype)
    middle = middle.at[tile_rows - RAD :].add(from_below).at[:RAD].add(from_above)
    summed = lax.psum(global_grads, ("rows", "cols"))
    own_grads = lax.dynamic_slice_in_dim(summed, own_index, 1, 0)
    own_mask = (places == own_place[0])[:, None]
    kv_grads = (middle.reshape(-1, 2 * model_width) + jnp.where(own_mask, own_grads, 0.0)).astype(
        jnp.bfloat16
    )
    query_flat = from_blocks(query_grads, row_blocks, col_blocks).reshape(-1, model_width)
    grad_in = (
        jnp.dot(query_flat, w_query.T, preferred_element_type=jnp.float32)
        + jnp.dot(kv_grads[:, :model_width], w_key.T, preferred_element_type=jnp.float32)
        + jnp.dot(kv_grads[:, model_width:], w_value.T, preferred_element_type=jnp.float32)
    )
    grad_in = grad_in.astype(jnp.bfloat16).reshape(features.shape)
    return (layer_out, grad_in)


def solution(mesh):
    placed = (P("rows", "cols", None), P(), P(), P(), P(), P(), P("rows", "cols", None))
    return jax.shard_map(
        shards,
        mesh=mesh,
        in_specs=placed,
        out_specs=(P("rows", "cols", None), P("rows", "cols", None)),
        check_vma=False,
    )
```

profile of v0, /device:TPU:0, one launch (start us, length us, event | category | flops | bytes accessed | tf_op | source)
XLA Modules:
  0.0 398.9 jit_solution(14206506281566383169)
XLA Ops:
  7.2 2.3 convolution_convert_fusion.3
  9.5 2.1 convolution_convert_fusion.4
  12.8 5.6 %collective-permute-start = (bf16[6,16,2048]{2,0,1:T(8,128)(2,1)}, bf16[6,16,2048]{2,0,1:T(8,128)(2,1)}, u32[]{:S(2)}, u32[]{:S(2)}) collective-permute-start(bf16[6,16,2048]{2,0,1:T(8,128)(2,1)} %copy.132), channel_id=1, source_target_pairs={{0,8},{8,16},{16,24},{1,9},{9,17},{17,25},{2,10},{10,18},{18,26},{... | collective-permute-start | bytes 1179656 | tf_op jit(solution)/shard_map/ppermute | solution.py:19
  22.8 56.1 %all-reduce.4 = bf16[32,2048]{1,0:T(8,128)(2,1)S(1)} all-reduce(f32[32,2048]{1,0:T(8,128)S(1)} %fusion.38), channel_id=1, replica_groups=mesh['rows'=4,'cols'=8] {'rows','cols'}, use_global_device_ids=true, to_apply=%region_1.2 | all-reduce | flops 65536 | bytes 393216 | tf_op jit(solution)/shard_map/psum | solution.py:210
  78.9 2.5 convolution_convert_fusion
  85.8 2.7 pad_maximum_fusion.5
  88.5 2.1 collective-permute-start.2
  98.8 2.6 copy.176
  103.7 3.6 pad_maximum_fusion.1
  107.3 4.4 %gather_fusion = bf16[2,20,20,2048]{3,1,2,0:T(8,128)(2,1)} fusion(bf16[20,28,2048]{2,0,1:T(8,128)(2,1)} %pad_maximum_fusion.1, s32[2]{0:T(128)S(1)} %fusion.46), kind=kCustom, calls=%fused_computation | custom fusion | bytes 6553624 | tf_op jit(solution)/shard_map/vmap()/gather | solution.py:71
  111.7 5.5 %copy.135 = bf16[2,20,20,2048]{3,0,2,1:T(2,128)(2,1)S(1)} copy(bf16[2,20,20,2048]{3,1,2,0:T(8,128)(2,1)} %gather_fusion) | data formatting | bytes 6553600 | tf_op jit(solution)/shard_map/vmap()/gather | solution.py:71
  117.2 3.5 fusion.53
  120.7 6.0 %copy.136 = bf16[2,400,1024]{1,2,0:T(8,128)(2,1)} copy(bf16[2,400,1024]{2,0,1:T(2,128)(2,1)} %get-tuple-element.146) | data formatting | bytes 3276800 | tf_op jit(solution)/shard_map/slice | solution.py:104
  126.8 6.0 %copy.138 = bf16[2,400,1024]{1,2,0:T(8,128)(2,1)} copy(bf16[2,400,1024]{2,0,1:T(2,128)(2,1)} %get-tuple-element.147) | data formatting | bytes 3276800 | tf_op jit(solution)/shard_map/slice | solution.py:103
  132.8 2.7 fusion
  138.3 3.1 fusion.14
  141.4 2.5 multiply_reduce_fusion
  143.9 2.9 multiply_convert_fusion
  149.7 5.4 %copy.162 = f32[2,400,1024]{2,1,0:T(8,128)} copy(f32[2,400,1024]{1,2,0:T(8,128)} %bitcast.124) | data formatting | bytes 6553600 | tf_op jit(solution)/shard_map/reshape | solution.py:165
  155.1 4.2 %fusion.59 = f32[2,16,64,400]{3,2,1,0:T(8,128)} fusion(bf16[2,64,16,64]{1,3,2,0:T(8,128)(2,1)S(1)} %copy-done.7, bf16[2,16,64,400]{3,2,1,0:T(8,128)(2,1)} %multiply_convert_fusion), kind=kOutput, calls=%fused_computation.125 | convolution fusion | flops 104857600 | bytes 5177344 | tf_op jit(solution)/shard_map/bhqk,bqhd->bkhd/dot_general | solution.py:111
  159.3 5.2 %copy.161 = f32[2,400,1024]{2,1,0:T(8,128)} copy(f32[2,400,1024]{1,2,0:T(8,128)} %bitcast.122) | data formatting | bytes 6553600 | tf_op jit(solution)/shard_map/reshape | solution.py:162
  164.6 6.5 %pad_maximum_fusion = f32[2,400,2048]{2,1,0:T(8,128)} fusion(f32[2,400,1024]{2,1,0:T(8,128)} %copy.162, f32[2,400,1024]{2,1,0:T(8,128)} %copy.161), kind=kLoop, calls=%fused_computation.3 | loop fusion | flops 1638400 | bytes 13107200 | tf_op jit(solution)/shard_map/concatenate | solution.py:176
  171.0 3.0 broadcast_in_dim.31
  174.0 59.6 %while.19 = (s32[]{:T(128)}, f32[20,28,2048]{2,1,0:T(8,128)}, f32[2,400,2048]{2,1,0:T(8,128)}, s32[]{:T(128)}, s32[]{:T(128)}, /*index=5*/s32[]{:T(128)}, s32[]{:T(128)}, s32[]{:T(128)}) while((s32[]{:T(128)}, f32[20,28,2048]{2,1,0:T(8,128)}, f32[2,400,2048]{2,1,0:T(8,128)}, s32[]{:T(128)}, s32[]{:T(128)}, /*index=5*/s32[]{:T(128)}, ...), condition=%wide.region_6.7_spmd, body=%wide.region_5.6_spmd.sunk | while | flops 819212 | bytes 29491408 | solution.py:96
  174.0 4.0 %constant_dynamic-slice_fusion.3 = f32[1,400,2048]{2,1,0:T(8,128)} fusion(f32[2,400,2048]{2,1,0:T(8,128)} %get-tuple-element.207, s32[]{:T(128)S(6)} %copy.226), kind=kLoop, calls=%fused_computation.2.clone.1 | loop fusion | bytes 6553604 | tf_op jit(solution)/shard_map/while/body/eval_jaxpr/jit(dynamic_index_in_dim)/dynamic_slice | solution.py:90
  178.0 4.6 %reshape.534 = f32[20,20,2048]{2,1,0:T(8,128)} reshape(f32[1,400,2048]{2,1,0:T(8,128)} %constant_dynamic-slice_fusion.3) | data formatting | bytes 6553600 | tf_op jit(solution)/shard_map/while/body/eval_jaxpr/reshape | solution.py:90
  182.6 6.9 %dynamic-slice_add_fusion.2 = f32[20,20,2048]{2,1,0:T(8,128)} fusion(f32[20,20,2048]{2,1,0:T(8,128)} %reshape.534, f32[20,28,2048]{2,1,0:T(8,128)} %get-tuple-element.198, s32[]{:T(128)S(6)} %select_n.177), kind=kLoop, calls=%fused_computation.1.clone.1 | loop fusion | flops 819200 | bytes 9830404 | tf_op jit(solution)/shard_map/while/body/eval_jaxpr/add | solution.py:94
  189.5 14.7 %dynamic_update_slice.12 = f32[20,28,2048]{2,1,0:T(8,128)} dynamic-update-slice(f32[20,28,2048]{2,1,0:T(8,128)} %get-tuple-element.198, f32[20,20,2048]{2,1,0:T(8,128)} %dynamic-slice_add_fusion.2, s32[]{:T(128)} %constant.262.clone.1..sunk, s32[]{:T(128)S(6)} %select_n.177, s32[]{:T(128)} %constant.262.clone.1..sunk) | dynamic-update-slice | bytes 6553604 | tf_op jit(solution)/shard_map/while/body/eval_jaxpr/dynamic_update_slice | solution.py:94
  204.3 4.0 %constant_dynamic-slice_fusion.3 = f32[1,400,2048]{2,1,0:T(8,128)} fusion(f32[2,400,2048]{2,1,0:T(8,128)} %get-tuple-element.207, s32[]{:T(128)S(6)} %copy.226), kind=kLoop, calls=%fused_computation.2.clone.1 | loop fusion | bytes 6553604 | tf_op jit(solution)/shard_map/while/body/eval_jaxpr/jit(dynamic_index_in_dim)/dynamic_slice | solution.py:90
  208.3 4.6 %reshape.534 = f32[20,20,2048]{2,1,0:T(8,128)} reshape(f32[1,400,2048]{2,1,0:T(8,128)} %constant_dynamic-slice_fusion.3) | data formatting | bytes 6553600 | tf_op jit(solution)/shard_map/while/body/eval_jaxpr/reshape | solution.py:90
  212.8 6.6 %dynamic-slice_add_fusion.2 = f32[20,20,2048]{2,1,0:T(8,128)} fusion(f32[20,20,2048]{2,1,0:T(8,128)} %reshape.534, f32[20,28,2048]{2,1,0:T(8,128)} %get-tuple-element.198, s32[]{:T(128)S(6)} %select_n.177), kind=kLoop, calls=%fused_computation.1.clone.1 | loop fusion | flops 819200 | bytes 9830404 | tf_op jit(solution)/shard_map/while/body/eval_jaxpr/add | solution.py:94
  219.4 14.2 %dynamic_update_slice.12 = f32[20,28,2048]{2,1,0:T(8,128)} dynamic-update-slice(f32[20,28,2048]{2,1,0:T(8,128)} %get-tuple-element.198, f32[20,20,2048]{2,1,0:T(8,128)} %dynamic-slice_add_fusion.2, s32[]{:T(128)} %constant.262.clone.1..sunk, s32[]{:T(128)S(6)} %select_n.177, s32[]{:T(128)} %constant.262.clone.1..sunk) | dynamic-update-slice | bytes 6553604 | tf_op jit(solution)/shard_map/while/body/eval_jaxpr/dynamic_update_slice | solution.py:94
  233.6 4.3 %slice.170 = f32[20,16,2048]{2,1,0:T(8,128)} slice(f32[20,28,2048]{2,1,0:T(8,128)} %get-tuple-element.139), slice={[0:20], [6:22], [0:2048]} | slice | bytes 5242880 | tf_op jit(solution)/shard_map/slice | solution.py:238
  237.9 4.0 %copy.215 = bf16[20,28,2048]{2,0,1:T(8,128)(2,1)} copy(f32[20,28,2048]{2,1,0:T(8,128)S(1)} %copy-done.1) | data formatting | bytes 6881280 | tf_op jit(solution)/shard_map/while | solution.py:96
  244.2 2.2 copy.148
  248.6 1.6 pad_maximum_fusion.6
  250.2 2.6 fusion.54
  254.1 3.1 fusion.6
  259.1 4.5 %collective-permute-start.5 = (bf16[20,6,2048]{2,0,1:T(8,128)(2,1)}, bf16[20,6,2048]{2,0,1:T(8,128)(2,1)}, u32[]{:S(2)}, u32[]{:S(2)}) collective-permute-start(bf16[20,6,2048]{2,0,1:T(8,128)(2,1)} %get-tuple-element.148), channel_id=1, source_target_pairs={{0,1},{1,2},{2,3},{3,4},{4,5},{5,6},{6,7},{8,9},{9,10},{10,11},{11... | collective-permute-start | bytes 1474568 | tf_op jit(solution)/shard_map/ppermute | solution.py:30
  263.6 1.6 fusion.58
  265.2 1.8 convert_add_fusion
  267.0 6.2 %scatter-add.14 = f32[20,16,2048]{2,1,0:T(8,128)} dynamic-update-slice(f32[20,16,2048]{2,1,0:T(8,128)} %slice.170, f32[20,6,2048]{2,1,0:T(8,128)S(1)} %convert_add_fusion, s32[]{:T(128)} %constant.262.clone.1, s32[]{:T(128)} %constant.280.clone.1, s32[]{:T(128)} %constant.262.clone.1) | dynamic-update-slice | bytes 1966084 | tf_op jit(solution)/shard_map/scatter-add | solution.py:241
  273.3 1.8 slice_add_fusion
  275.1 7.0 %scatter-add.15 = f32[20,16,2048]{2,1,0:T(8,128)} dynamic-update-slice(f32[20,16,2048]{2,1,0:T(8,128)} %scatter-add.14, f32[20,6,2048]{2,1,0:T(8,128)S(1)} %slice_add_fusion, s32[]{:T(128)} %constant.262.clone.1, s32[]{:T(128)} %constant.262.clone.1, s32[]{:T(128)} %constant.262.clone.1) | dynamic-update-slice | bytes 1966084 | tf_op jit(solution)/shard_map/scatter-add | solution.py:241
  282.1 2.1 convert.9
  286.8 89.3 %all-reduce.3.cloned.1.call-done = f32[32,2048]{1,0:T(8,128)} async-done(((f32[32,2048]{1,0:T(8,128)}), f32[32,2048]{1,0:T(8,128)}) %all-reduce.3.cloned.1.call-update) | async-done | bytes 262160 | tf_op jit(solution)/shard_map/psum | solution.py:248
  378.3 3.5 collective-permute-start.7
  383.0 6.3 %collective-permute-done.7 = bf16[6,16,2048]{2,1,0:T(8,128)(2,1)S(1)} collective-permute-done((bf16[6,16,2048]{2,1,0:T(8,128)(2,1)S(1)}, bf16[6,16,2048]{2,1,0:T(8,128)(2,1)S(1)}, u32[]{:S(2)}, u32[]{:S(2)}) %collective-permute-start.7) | collective-permute-done | bytes 393248 | tf_op jit(solution)/shard_map/ppermute | solution.py:30
  (122 shorter events, 42.1 us)
Async XLA Ops:
  7.2 77.8 %copy-start = (bf16[1024,1024]{1,0:T(8,128)(2,1)S(1)}, bf16[1024,1024]{1,0:T(8,128)(2,1)}, u32[]{:S(2)}) copy-start(bf16[1024,1024]{1,0:T(8,128)(2,1)} %param.18) | copy-start | bytes 6291460
  7.2 368.9 %all-reduce.3.cloned.1.call-start = ((), (), s32[]{:S(2)}) async-start(), calls=%async_computation | async-start | bytes 524288 | tf_op jit(solution)/shard_map/psum | solution.py:248
  9.5 12.4 %copy-start.20 = (s32[32]{0:T(128)S(1)}, s32[32]{0:T(128)}, u32[]{:S(2)}) copy-start(s32[32]{0:T(128)} %param.22) | copy-start | bytes 388
  11.6 67.2 %copy-start.17 = (bf16[8,16,1024]{2,1,0:T(8,128)(2,1)S(1)}, bf16[8,16,1024]{2,1,0:T(8,128)(2,1)}, u32[]{:S(2)}) copy-start(bf16[8,16,1024]{2,1,0:T(8,128)(2,1)} %param.23) | copy-start | bytes 786436
  12.8 72.7 %collective-permute-start = (bf16[6,16,2048]{2,0,1:T(8,128)(2,1)}, bf16[6,16,2048]{2,0,1:T(8,128)(2,1)}, u32[]{:S(2)}, u32[]{:S(2)}) collective-permute-start(bf16[6,16,2048]{2,0,1:T(8,128)(2,1)} %copy.132), channel_id=1, source_target_pairs={{0,8},{8,16},{16,24},{1,9},{9,17},{17,25},{2,10},{10,18},{18,26},{... | collective-permute-start | bytes 1179656 | tf_op jit(solution)/shard_map/ppermute | solution.py:19
  19.4 66.0 %collective-permute-start.1 = (bf16[6,16,2048]{2,0,1:T(8,128)(2,1)}, bf16[6,16,2048]{2,0,1:T(8,128)(2,1)}, u32[]{:S(2)}, u32[]{:S(2)}) collective-permute-start(bf16[6,16,2048]{2,0,1:T(8,128)(2,1)} %copy.133), channel_id=1, source_target_pairs={{8,0},{16,8},{24,16},{9,1},{17,9},{25,17},{10,2},{18,10},{26,18},{... | collective-permute-start | bytes 1179656 | tf_op jit(solution)/shard_map/ppermute | solution.py:22
  78.9 6.1 %copy-start.9 = (bf16[8,16,1024]{2,1,0:T(8,128)(2,1)S(1)}, bf16[8,16,1024]{2,1,0:T(8,128)(2,1)}, u32[]{:S(2)}) copy-start(bf16[8,16,1024]{2,1,0:T(8,128)(2,1)} %param.17) | copy-start | bytes 786436
  85.0 0.8 copy-start.6
  88.5 15.2 %collective-permute-start.2 = (bf16[20,6,2048]{2,0,1:T(8,128)(2,1)}, bf16[20,6,2048]{2,0,1:T(8,128)(2,1)}, u32[]{:S(2)}, u32[]{:S(2)}) collective-permute-start(bf16[20,6,2048]{2,0,1:T(8,128)(2,1)} %get-tuple-element.150), channel_id=1, source_target_pairs={{0,1},{1,2},{2,3},{3,4},{4,5},{5,6},{6,7},{8,9},{9,10},{10,11},{11... | collective-permute-start | bytes 1474568 | tf_op jit(solution)/shard_map/ppermute | solution.py:19
  90.6 13.1 %collective-permute-start.3 = (bf16[20,6,2048]{2,0,1:T(8,128)(2,1)}, bf16[20,6,2048]{2,0,1:T(8,128)(2,1)}, u32[]{:S(2)}, u32[]{:S(2)}) collective-permute-start(bf16[20,6,2048]{2,0,1:T(8,128)(2,1)} %get-tuple-element.151), channel_id=1, source_target_pairs={{1,0},{2,1},{3,2},{4,3},{5,4},{6,5},{7,6},{9,8},{10,9},{11,10},{12... | collective-permute-start | bytes 1474568 | tf_op jit(solution)/shard_map/ppermute | solution.py:22
  97.5 4.8 %copy-start.13 = (bf16[32,16,64]{2,1,0:T(8,128)(2,1)S(1)}, bf16[32,16,64]{2,1,0:T(8,128)(2,1)}, u32[]{:S(2)}) copy-start(bf16[32,16,64]{2,1,0:T(8,128)(2,1)} %reshape.508) | copy-start | bytes 196612
  135.5 1.2 copy-start.11
  135.6 2.4 copy-start.19
  136.7 1.6 copy-start.16
  138.3 3.1 copy-start.10
  138.3 3.1 copy-start.15
  149.7 5.4 %copy-start.7 = (bf16[2,64,16,64]{1,3,2,0:T(8,128)(2,1)S(1)}, bf16[2,64,16,64]{1,3,2,0:T(8,128)(2,1)}, u32[]{:S(2)}) copy-start(bf16[2,64,16,64]{1,3,2,0:T(8,128)(2,1)} %copy.159) | copy-start | bytes 786436
  233.6 4.3 %copy-start.1 = (f32[20,28,2048]{2,1,0:T(8,128)S(1)}, f32[20,28,2048]{2,1,0:T(8,128)}, u32[]{:S(2)}) copy-start(f32[20,28,2048]{2,1,0:T(8,128)} %get-tuple-element.139) | copy-start | bytes 13762564
  237.9 4.0 %copy-start.18 = (f32[32,16,64]{2,0,1:T(8,128)S(1)}, f32[32,16,64]{2,0,1:T(8,128)}, u32[]{:S(2)}) copy-start(f32[32,16,64]{2,0,1:T(8,128)} %convolution_bitcast_fusion.5) | copy-start | bytes 393220
  242.2 11.9 %copy-start.8 = (f32[2,64,16,64]{1,3,2,0:T(8,128)S(1)}, f32[2,64,16,64]{1,3,2,0:T(8,128)}, u32[]{:S(2)}) copy-start(f32[2,64,16,64]{1,3,2,0:T(8,128)} %convolution_bitcast_fusion) | copy-start | bytes 1572868
  250.2 3.9 copy-start.2
  252.8 12.4 %collective-permute-start.4 = (bf16[20,6,2048]{2,0,1:T(8,128)(2,1)}, bf16[20,6,2048]{2,0,1:T(8,128)(2,1)}, u32[]{:S(2)}, u32[]{:S(2)}) collective-permute-start(bf16[20,6,2048]{2,0,1:T(8,128)(2,1)} %get-tuple-element.149), channel_id=1, source_target_pairs={{1,0},{2,1},{3,2},{4,3},{5,4},{6,5},{7,6},{9,8},{10,9},{11,10},{12... | collective-permute-start | bytes 1474568 | tf_op jit(solution)/shard_map/ppermute | solution.py:30
  259.1 14.2 %collective-permute-start.5 = (bf16[20,6,2048]{2,0,1:T(8,128)(2,1)}, bf16[20,6,2048]{2,0,1:T(8,128)(2,1)}, u32[]{:S(2)}, u32[]{:S(2)}) collective-permute-start(bf16[20,6,2048]{2,0,1:T(8,128)(2,1)} %get-tuple-element.148), channel_id=1, source_target_pairs={{0,1},{1,2},{2,3},{3,4},{4,5},{5,6},{6,7},{8,9},{9,10},{10,11},{11... | collective-permute-start | bytes 1474568 | tf_op jit(solution)/shard_map/ppermute | solution.py:30
  282.1 3.5 copy-start.3
  282.1 3.5 copy-start.14
  284.3 97.5 %collective-permute-start.6 = (bf16[6,16,2048]{2,1,0:T(8,128)(2,1)S(1)}, bf16[6,16,2048]{2,1,0:T(8,128)(2,1)S(1)}, u32[]{:S(2)}, u32[]{:S(2)}) collective-permute-start(bf16[6,16,2048]{2,1,0:T(8,128)(2,1)S(1)} %get-tuple-element.153), channel_id=1, source_target_pairs={{8,0},{16,8},{24,16},{9,1},{17,9},{25,17},{10,2},{18,10},{26,18},{... | collective-permute-start | bytes 1179656 | tf_op jit(solution)/shard_map/ppermute | solution.py:30
  378.2 11.5 %copy-start.5 = (bf16[1024,1024]{1,0:T(8,128)(2,1)S(1)}, bf16[1024,1024]{1,0:T(8,128)(2,1)}, u32[]{:S(2)}) copy-start(bf16[1024,1024]{1,0:T(8,128)(2,1)} %param.19) | copy-start | bytes 6291460
  378.2 11.5 %copy-start.12 = (f32[128,1024]{1,0:T(8,128)S(1)}, f32[128,1024]{1,0:T(8,128)}, u32[]{:S(2)}) copy-start(f32[128,1024]{1,0:T(8,128)} %fusion.58) | copy-start | bytes 1572868
  378.3 11.1 %collective-permute-start.7 = (bf16[6,16,2048]{2,1,0:T(8,128)(2,1)S(1)}, bf16[6,16,2048]{2,1,0:T(8,128)(2,1)S(1)}, u32[]{:S(2)}, u32[]{:S(2)}) collective-permute-start(bf16[6,16,2048]{2,1,0:T(8,128)(2,1)S(1)} %get-tuple-element.152), channel_id=1, source_target_pairs={{0,8},{8,16},{16,24},{1,9},{9,17},{17,25},{2,10},{10,18},{18,26},{... | collective-permute-start | bytes 1179656 | tf_op jit(solution)/shard_map/ppermute | solution.py:30
  383.0 7.5 %copy-start.4 = (bf16[1024,1024]{1,0:T(8,128)(2,1)S(1)}, bf16[1024,1024]{1,0:T(8,128)(2,1)}, u32[]{:S(2)}) copy-start(bf16[1024,1024]{1,0:T(8,128)(2,1)} %param.20) | copy-start | bytes 6291460
Sparse Core Ops, SparseCore 0:
  250.3 125.6 all-reduce.2
where the time goes:
time: 402 us; the launch traced here: 399 us
  local copies, waits for them, and re-layouts  134 us (33%)
  waiting for transfers between devices  95.7 us (24%)
  blocking collectives  56.1 us (14%)
  other arithmetic  40.4 us (10%)
  matrix products  36.9 us (9%)
  starting transfers between devices  21 us (5%)
  between operations  14.7 us (4%)
    psum x1, waiting for transfers between devices, shards(): summed = lax.psum(global_grads, ('rows', 'cols'))  89.3 us
    psum x1, blocking collectives, shards(): global_kv = lax.psum(picked, ('rows', 'cols')).astype(jnp.bfloat16)  56.1 us
    dynamic_update_slice x2, local copies, waits for them, and re-layouts, add_box(): return lax.dynamic_update_slice(accum, current + piece, start)  28.9 us
    dot_general x12, matrix products, einsum_wide(): return jnp.einsum(form, left, right, preferred_element_type=jnp.float32)  24.2 us
    add x2, other arithmetic, add_box(): return lax.dynamic_update_slice(accum, current + piece, start)  13.5 us
    scatter-add x2, local copies, waits for them, and re-layouts, shards(): centre.at[:, tile_cols - RAD:].add(from_right).at[:, :RAD].add(from_left)  13.2 us
    ppermute x4, starting transfers between devices, from_behind(): return lax.ppermute(x, axis, pairs)  10.6 us
    gather x2, local copies, waits for them, and re-layouts, cut_box(): lax.dynamic_slice(framed, (top_cell, left_cell, jnp.int32(0)), (span_cell...  9.92 us
  transfers between devices with their start and end apart: 9, of which 2 were waited for; matrix products, arithmetic and copies ran while one was open for 14% of the time, Pallas kernels for 0%

commit v1 on v0

v1 whole, which is shorter than its diff:
```python
import math

import jax
import jax.numpy as jnp
from jax import lax
from jax.sharding import PartitionSpec as P

HEADS = 16
KW = 13
RAD = 6


def with_halo(block, sides, width):
    for axis, dim in sides:
        count = lax.axis_size(axis)
        forward = [(i, i + 1) for i in range(count - 1)]
        backward = [(target, source) for source, target in forward]
        low = lax.ppermute(
            lax.slice_in_dim(block, block.shape[dim] - width, None, axis=dim), axis, forward
        )
        high = lax.ppermute(lax.slice_in_dim(block, 0, width, axis=dim), axis, backward)
        block = jnp.concatenate([low, block, high], axis=dim)
    return block


def from_behind(x, axis, by):
    size = lax.axis_size(axis)
    pairs = [(i, i + by) for i in range(size) if 0 <= i + by < size]
    return lax.ppermute(x, axis, pairs)


def axis_valid(first_cell, tile, extent):
    query_cell = first_cell + jnp.arange(tile, dtype=jnp.int32)[:, None]
    key_cell = first_cell - RAD + jnp.arange(tile + 2 * RAD, dtype=jnp.int32)[None, :]
    window_start = jnp.clip(query_cell - RAD, 0, extent - KW)
    return (key_cell >= window_start) & (key_cell <= window_start + KW - 1)


def einsum_wide(form, left, right):
    return jnp.einsum(form, left, right, preferred_element_type=jnp.float32)


def to_heads(x):
    count, width = x.shape
    return x.reshape(count, HEADS, width // HEADS).transpose(1, 0, 2)


def from_heads(x):
    heads, count, size = x.shape
    return x.transpose(1, 0, 2).reshape(count, heads * size)


def shards(features, w_query, w_key, w_value, w_out, reg_pos, grad_out):
    tile_rows, tile_cols, model_width = features.shape
    head_size = model_width // HEADS
    score_scale = 1.0 / math.sqrt(head_size)
    row_count = lax.axis_size("rows")
    col_count = lax.axis_size("cols")
    row_index = lax.axis_index("rows")
    col_index = lax.axis_index("cols")
    band_cols = tile_cols * col_count
    first_row = row_index * tile_rows
    first_col = col_index * tile_cols
    tokens = tile_rows * tile_cols
    frame_rows = tile_rows + 2 * RAD
    frame_cols = tile_cols + 2 * RAD

    flat_tokens = features.reshape(-1, model_width)
    queries = jnp.dot(flat_tokens, w_query, preferred_element_type=jnp.float32).astype(jnp.bfloat16)
    keys_local = jnp.dot(flat_tokens, w_key, preferred_element_type=jnp.float32).astype(
        jnp.bfloat16
    )
    values_local = jnp.dot(flat_tokens, w_value, preferred_element_type=jnp.float32).astype(
        jnp.bfloat16
    )
    key_value = jnp.concatenate([keys_local, values_local], axis=1)

    own_index = row_index * col_count + col_index
    own_place = lax.dynamic_index_in_dim(reg_pos, own_index, 0, keepdims=False)
    own_local = (own_place // band_cols - first_row) * tile_cols + (own_place % band_cols - first_col)
    own_kv = lax.dynamic_slice_in_dim(key_value, own_local, 1, 0)
    global_kv = lax.all_gather(own_kv, ("rows", "cols"), axis=0, tiled=True)

    framed = with_halo(
        key_value.reshape(tile_rows, tile_cols, 2 * model_width), (("rows", 0), ("cols", 1)), RAD
    ).reshape(frame_rows * frame_cols, 2 * model_width)
    all_kv = jnp.concatenate([framed, global_kv], axis=0)
    key_count = all_kv.shape[0]

    row_valid = axis_valid(first_row, tile_rows, tile_rows * row_count)
    col_valid = axis_valid(first_col, tile_cols, band_cols)
    window_mask = (row_valid[:, None, :, None] & col_valid[None, :, None, :]).reshape(
        tokens, frame_rows * frame_cols
    )
    full_mask = jnp.concatenate(
        [window_mask, jnp.ones((tokens, key_count - frame_rows * frame_cols), jnp.bool_)], axis=1
    )

    query_heads = to_heads(queries)
    key_heads = to_heads(all_kv[:, :model_width])
    value_heads = to_heads(all_kv[:, model_width:])

    scores = einsum_wide("hqd,hkd->hqk", query_heads, key_heads) * score_scale
    scores = jnp.where(full_mask[None], scores, -1e30)
    row_max = jnp.max(scores, axis=-1, keepdims=True)
    exps = jnp.exp(scores - row_max)
    denominator = jnp.sum(exps, axis=-1, keepdims=True)
    probs = exps / denominator
    rounded = probs.astype(jnp.bfloat16)
    attended_heads = einsum_wide("hqk,hkd->hqd", rounded, value_heads).astype(jnp.bfloat16)
    attended = from_heads(attended_heads)

    layer_out = (
        jnp.dot(attended, w_out, preferred_element_type=jnp.float32)
        .astype(jnp.bfloat16)
        .reshape(features.shape)
    )
    grad_attended = jnp.dot(
        grad_out.reshape(-1, model_width), w_out.T, preferred_element_type=jnp.float32
    ).astype(jnp.bfloat16)
    grad_heads = to_heads(grad_attended)

    delta = einsum_wide("hqd,hqd->hq", grad_heads, attended_heads)[..., None]
    dots = einsum_wide("hqd,hkd->hqk", grad_heads, value_heads)
    slopes = (probs * (dots - delta) * score_scale).astype(jnp.bfloat16)
    query_grads = from_heads(
        einsum_wide("hqk,hkd->hqd", slopes, key_heads).astype(jnp.bfloat16)
    )
    key_grads = from_heads(einsum_wide("hqk,hqd->hkd", slopes, query_heads))
    value_grads = from_heads(einsum_wide("hqk,hqd->hkd", rounded, grad_heads))
    kv_grads_all = jnp.concatenate([key_grads, value_grads], axis=1)

    global_grads = kv_grads_all[frame_rows * frame_cols :]
    own_grads = lax.psum_scatter(global_grads, ("rows", "cols"), scatter_dimension=0, tiled=True)

    frame_grads = kv_grads_all[: frame_rows * frame_cols].reshape(
        frame_rows, frame_cols, 2 * model_width
    )
    left_rim = frame_grads[:, :RAD]
    right_rim = frame_grads[:, tile_cols + RAD :]
    centre = frame_grads[:, RAD : tile_cols + RAD]
    from_right = from_behind(left_rim.astype(jnp.bfloat16), "cols", -1).astype(left_rim.dtype)
    from_left = from_behind(right_rim.astype(jnp.bfloat16), "cols", 1).astype(right_rim.dtype)
    centre = centre.at[:, tile_cols - RAD :].add(from_right).at[:, :RAD].add(from_left)
    upper_rim = centre[:RAD]
    lower_rim = centre[tile_rows + RAD :]
    middle = centre[RAD : tile_rows + RAD]
    from_below = from_behind(upper_rim.astype(jnp.bfloat16), "rows", -1).astype(upper_rim.dtype)
    from_above = from_behind(lower_rim.astype(jnp.bfloat16), "rows", 1).astype(lower_rim.dtype)
    middle = middle.at[tile_rows - RAD :].add(from_below).at[:RAD].add(from_above)
    middle = middle.reshape(tokens, 2 * model_width)
    own_row = lax.dynamic_slice_in_dim(middle, own_local, 1, 0) + own_grads
    kv_grads = lax.dynamic_update_slice_in_dim(middle, own_row, own_local, 0).astype(jnp.bfloat16)

    grad_in = (
        jnp.dot(query_grads, w_query.T, preferred_element_type=jnp.float32)
        + jnp.dot(kv_grads[:, :model_width], w_key.T, preferred_element_type=jnp.float32)
        + jnp.dot(kv_grads[:, model_width:], w_value.T, preferred_element_type=jnp.float32)
    )
    grad_in = grad_in.astype(jnp.bfloat16).reshape(features.shape)
    return (layer_out, grad_in)


def solution(mesh):
    placed = (P("rows", "cols", None), P(), P(), P(), P(), P(), P("rows", "cols", None))
    return jax.shard_map(
        shards,
        mesh=mesh,
        in_specs=placed,
        out_specs=(P("rows", "cols", None), P("rows", "cols", None)),
        check_vma=False,
    )
```

time: 402 us -> 323 us (0.80)
  local copies, waits for them, and re-layouts: 134 us -> 47.4 us
  waiting for transfers between devices: 95.7 us -> 137 us
  other arithmetic: 40.4 us -> 27 us
  blocking collectives: 56.1 us -> 43.1 us
  matrix products: 36.9 us -> 28.9 us
    unnamed x1 -> x2, waiting for transfers between devices: 0.02 us -> 117 us
    psum x1 -> x0, waiting for transfers between devices: 89.3 us -> none  [shards(): summed = lax.psum(global_grads, ('rows', 'cols'))]
    psum x1 -> x0, blocking collectives: 56.1 us -> none  [shards(): global_kv = lax.psum(picked, ('rows', 'cols')).astype(jnp.bfloat16)]
    all_gather x0 -> x1, blocking collectives: none -> 43.1 us  [shards(): global_kv = lax.all_gather(own_kv, ('rows', 'cols'), axis=0, tiled=True)]
    dynamic_update_slice x2 -> x1, local copies, waits for them, and re-layouts: 28.9 us -> 0.2 us  [shards(): lax.dynamic_update_slice_in_dim(middle, own_row, own_local, 0)]
    dot_general x12 -> x5, matrix products: 24.2 us -> 8.87 us  [einsum_wide(): return jnp.einsum(form, left, right, preferred_element_type=jnp.float32)]
    ppermute x2, waiting for transfers between devices: 0.01 us -> 13.2 us  [with_halo(): lax.ppermute(lax.slice_in_dim(block, 0, width, axis=dim), axis, backward)]
    add x8 -> x3, other arithmetic: 13.7 us -> 0.86 us  [the longest x1 0.85 us: shards(): own_row = lax.dynamic_slice_in_dim(middle, own_local, 1, 0) + own_grads]
  transfers between devices with their start and end apart: 9 -> 9, of which waited for: 2 -> 5; matrix products, arithmetic and copies ran while one was open for 14% -> 7% of each run, Pallas kernels for 0% -> 0%
where the time goes in v1:
time: 323 us; the launch traced here: 322 us
  waiting for transfers between devices  137 us (42%)
  local copies, waits for them, and re-layouts  47.4 us (15%)
  blocking collectives  43.1 us (13%)
  matrix products  28.9 us (9%)
  other arithmetic  27 us (8%)
  starting transfers between devices  21.5 us (7%)
  between operations  17.1 us (5%)
    unnamed x2, waiting for transfers between devices  117 us
    all_gather x1, blocking collectives, shards(): global_kv = lax.all_gather(own_kv, ('rows', 'cols'), axis=0, tiled=True)  43.1 us
    scatter-add x2, local copies, waits for them, and re-layouts, shards(): centre.at[:, tile_cols - RAD:].add(from_right).at[:, :RAD].add(from_left)  13.2 us
    ppermute x2, waiting for transfers between devices, with_halo(): lax.ppermute(lax.slice_in_dim(block, 0, width, axis=dim), axis, backward)  13.2 us
    ppermute x4, starting transfers between devices, from_behind(): return lax.ppermute(x, axis, pairs)  11.1 us
    dot_general x5, matrix products, einsum_wide(): return jnp.einsum(form, left, right, preferred_element_type=jnp.float32)  8.87 us
    ppermute x2, starting transfers between devices, with_halo(): lax.ppermute(lax.slice_in_dim(block, block.shape[dim] - width, None, axis...  7.75 us
  transfers between devices with their start and end apart: 9, of which 5 were waited for; matrix products, arithmetic and copies ran while one was open for 7% of the time, Pallas kernels for 0%

profile of v1, /device:TPU:0, one launch (start us, length us, event | category | flops | bytes accessed | tf_op | source)
XLA Modules:
  0.0 321.7 jit_solution(17571939604907091626)
XLA Ops:
  7.2 2.3 convolution_convert_fusion.4
  10.2 1.1 copy.41
  11.3 5.6 %collective-permute-start = (bf16[6,16,2048]{2,0,1:T(8,128)(2,1)}, bf16[6,16,2048]{2,0,1:T(8,128)(2,1)}, u32[]{:S(2)}, u32[]{:S(2)}) collective-permute-start(bf16[6,16,2048]{2,0,1:T(8,128)(2,1)} %copy.41), channel_id=1, source_target_pairs={{0,8},{8,16},{16,24},{1,9},{9,17},{17,25},{2,10},{10,18},{18,26},{... | collective-permute-start | bytes 1179656 | tf_op jit(solution)/shard_map/ppermute | solution.py:18
  16.9 1.0 copy.42
  18.0 1.3 collective-permute-start.1
  22.6 2.8 convolution_convert_fusion.6
  27.6 13.2 %collective-permute-done.1 = bf16[6,16,2048]{2,0,1:T(8,128)(2,1)} collective-permute-done((bf16[6,16,2048]{2,0,1:T(8,128)(2,1)}, bf16[6,16,2048]{2,0,1:T(8,128)(2,1)}, u32[]{:S(2)}, u32[]{:S(2)}) %collective-permute-start.1) | collective-permute-done | bytes 393248 | tf_op jit(solution)/shard_map/ppermute | solution.py:21
  40.8 2.7 pad_maximum_fusion.5
  43.5 2.1 collective-permute-start.2
  45.6 1.3 collective-permute-start.3
  46.9 43.1 %all-gather = bf16[32,1,2048]{2,1,0:T(2,128)(2,1)S(1)} all-gather(bf16[1,1,2048]{2,1,0:T(2,128)(2,1)S(1)} %fusion.19), channel_id=1, replica_groups=mesh['rows'=4,'cols'=8] {'rows','cols'}, dimensions={0}, use_global_device_ids=true | all-gather | bytes 135168 | tf_op jit(solution)/shard_map/all_gather | solution.py:82
  92.8 2.4 pad_maximum_fusion
  95.2 2.8 copy.44
  98.0 4.0 %reshape.324 = bf16[560,2048]{1,0:T(8,128)(2,1)} reshape(bf16[20,28,2048]{2,1,0:T(8,128)(2,1)} %copy.44) | data formatting | bytes 4587520 | tf_op jit(solution)/shard_map/reshape | solution.py:86
  102.0 3.3 %pad_maximum_fusion.1 = (bf16[592,1024]{1,0:T(8,128)(2,1)}, bf16[592,1024]{1,0:T(8,128)(2,1)}) fusion(bf16[32,2048]{1,0:T(8,128)(2,1)S(1)} %bitcast.90, bf16[560,2048]{1,0:T(8,128)(2,1)} %reshape.324), kind=kLoop, calls=%fused_computation.21 | loop fusion | flops 4849664 | bytes 4849664 | tf_op jit(solution)/shard_map/concatenate | solution.py:87
  105.2 1.7 copy.45
  106.9 2.4 copy.46
  109.4 5.0 %fusion.24 = (f32[16,128]{1,0:T(8,128)S(1)}, f32[16,128,592]{1,2,0:T(8,128)}) fusion(pred[128,592]{0,1:T(8,128)(4,1)S(1)} %concatenate.26.clone, bf16[16,128,64]{1,2,0:T(8,128)(2,1)} %bitcast.87, bf16[16,592,64]{1,2,0:T(8,128)(2,1)S(1)} %bitcast.72), kind=kOutput, calls=%fused_computation.69 | convolution fusion | flops 160039504 | bytes 6408192 | tf_op jit(solution)/shard_map/sub | solution.py:106
  114.4 2.9 fusion.6
  117.3 1.3 fusion.11
  118.6 2.4 fusion.27
  121.0 1.3 multiply_convert_fusion
  122.4 2.4 fusion.26
  124.9 3.2 copy.49
  128.1 3.2 copy.48
  131.3 5.0 %fusion.1 = f32[560,2048]{1,0:T(8,128)} fusion(f32[592,1024]{1,0:T(8,128)} %copy.48, f32[592,1024]{1,0:T(8,128)} %copy.49), kind=kLoop, calls=%fused_computation.6 | loop fusion | flops 1146880 | bytes 9437184 | tf_op jit(solution)/shard_map/concatenate | solution.py:131
  136.3 5.4 %reshape.334 = f32[20,28,2048]{2,1,0:T(8,128)} reshape(f32[560,2048]{1,0:T(8,128)} %fusion.1) | data formatting | bytes 9175040 | tf_op jit(solution)/shard_map/reshape | solution.py:136
  141.7 3.0 convert.8
  144.7 1.0 copy-done.1
  145.8 2.0 slice.186
  148.0 1.1 copy.52
  149.4 1.3 collective-permute-start.4
  150.7 3.9 %collective-permute-start.5 = (bf16[20,6,2048]{2,0,1:T(8,128)(2,1)}, bf16[20,6,2048]{2,0,1:T(8,128)(2,1)}, u32[]{:S(2)}, u32[]{:S(2)}) collective-permute-start(bf16[20,6,2048]{2,0,1:T(8,128)(2,1)} %copy.52), channel_id=1, source_target_pairs={{0,1},{1,2},{2,3},{3,4},{4,5},{5,6},{6,7},{8,9},{9,10},{10,11},{11... | collective-permute-start | bytes 1474568 | tf_op jit(solution)/shard_map/ppermute | solution.py:29
  154.6 1.2 convolution_convert_fusion.3
  155.7 1.4 convolution_convert_fusion
  157.5 6.2 %scatter-add.14 = f32[20,16,2048]{2,1,0:T(8,128)} dynamic-update-slice(f32[20,16,2048]{2,1,0:T(8,128)} %slice.186, f32[20,6,2048]{2,1,0:T(8,128)S(1)} %slice_add_fusion.1, s32[]{:T(128)} %constant.163.clone.1, s32[]{:T(128)} %constant.180.clone.1, s32[]{:T(128)} %constant.163.clone.1) | dynamic-update-slice | bytes 1966084 | tf_op jit(solution)/shard_map/scatter-add | solution.py:144
  163.7 1.8 slice_add_fusion
  165.5 7.0 %scatter-add.15 = f32[20,16,2048]{2,1,0:T(8,128)} dynamic-update-slice(f32[20,16,2048]{2,1,0:T(8,128)} %scatter-add.14, f32[20,6,2048]{2,1,0:T(8,128)S(1)} %slice_add_fusion, s32[]{:T(128)} %constant.163.clone.1, s32[]{:T(128)} %constant.163.clone.1, s32[]{:T(128)} %constant.163.clone.1) | dynamic-update-slice | bytes 1966084 | tf_op jit(solution)/shard_map/scatter-add | solution.py:144
  172.5 2.1 convert.9
  175.4 1.4 collective-permute-start.6
  177.6 3.4 %fusion.25 = f32[128,1024]{1,0:T(8,128)} fusion(bf16[128,1024]{0,1:T(8,128)(2,1)S(1)} %bitcast.89, bf16[1024,1024]{1,0:T(8,128)(2,1)} %param.16), kind=kOutput, calls=%fused_computation.70 | convolution fusion | flops 268435456 | bytes 2883584 | tf_op jit(solution)/shard_map/dot_general | solution.py:156
  181.1 4.6 %collective-permute-start.7 = (bf16[6,16,2048]{2,1,0:T(8,128)(2,1)S(1)}, bf16[6,16,2048]{2,1,0:T(8,128)(2,1)S(1)}, u32[]{:S(2)}, u32[]{:S(2)}) collective-permute-start(bf16[6,16,2048]{2,1,0:T(8,128)(2,1)S(1)} %get-tuple-element.56), channel_id=1, source_target_pairs={{0,8},{8,16},{16,24},{1,9},{9,17},{17,25},{2,10},{10,18},{18,26},{... | collective-permute-start | bytes 1179656 | tf_op jit(solution)/shard_map/ppermute | solution.py:29
  185.7 1.1 collective-permute-done.6
  186.8 1.1 fusion.10
  187.9 4.8 %collective-permute-done.7 = bf16[6,16,2048]{2,1,0:T(8,128)(2,1)S(1)} collective-permute-done((bf16[6,16,2048]{2,1,0:T(8,128)(2,1)S(1)}, bf16[6,16,2048]{2,1,0:T(8,128)(2,1)S(1)}, u32[]{:S(2)}, u32[]{:S(2)}) %collective-permute-start.7) | collective-permute-done | bytes 393248 | tf_op jit(solution)/shard_map/ppermute | solution.py:29
  192.9 116.6 %all-reduce.4.cloned.1.call-done = f32[32,2048]{1,0:T(8,128)} async-done(((f32[32,2048]{1,0:T(8,128)}), f32[32,2048]{1,0:T(8,128)}) %all-reduce.4.cloned.1.call-update) | async-done | bytes 262160
  310.7 2.6 convolution_add_fusion.1
  313.3 1.5 fusion.8
  (77 shorter events, 10.3 us)
Async XLA Ops:
  7.2 18.6 %copy-start = (bf16[1024,1024]{1,0:T(8,128)(2,1)S(1)}, bf16[1024,1024]{1,0:T(8,128)(2,1)}, u32[]{:S(2)}) copy-start(bf16[1024,1024]{1,0:T(8,128)(2,1)} %param.19) | copy-start | bytes 6291460
  7.2 2.3 copy-start.10
  7.2 302.3 %all-reduce.4.cloned.1.call-start = ((), (), s32[]{:S(2)}) async-start(), calls=%async_computation | async-start | bytes 524288
  7.2 2.5 copy-start.8
  9.7 9.6 %copy-start.17 = (s32[32]{0:T(128)S(1)}, s32[32]{0:T(128)}, u32[]{:S(2)}) copy-start(s32[32]{0:T(128)} %param.20) | copy-start | bytes 388
  11.3 16.3 %collective-permute-start = (bf16[6,16,2048]{2,0,1:T(8,128)(2,1)}, bf16[6,16,2048]{2,0,1:T(8,128)(2,1)}, u32[]{:S(2)}, u32[]{:S(2)}) collective-permute-start(bf16[6,16,2048]{2,0,1:T(8,128)(2,1)} %copy.41), channel_id=1, source_target_pairs={{0,8},{8,16},{16,24},{1,9},{9,17},{17,25},{2,10},{10,18},{18,26},{... | collective-permute-start | bytes 1179656 | tf_op jit(solution)/shard_map/ppermute | solution.py:18
  18.0 22.8 %collective-permute-start.1 = (bf16[6,16,2048]{2,0,1:T(8,128)(2,1)}, bf16[6,16,2048]{2,0,1:T(8,128)(2,1)}, u32[]{:S(2)}, u32[]{:S(2)}) collective-permute-start(bf16[6,16,2048]{2,0,1:T(8,128)(2,1)} %copy.42), channel_id=1, source_target_pairs={{8,0},{16,8},{24,16},{9,1},{17,9},{25,17},{10,2},{18,10},{26,18},{... | collective-permute-start | bytes 1179656 | tf_op jit(solution)/shard_map/ppermute | solution.py:21
  22.6 3.2 copy-start.16
  25.8 64.2 %copy-start.13 = (bf16[128,1024]{1,0:T(8,128)(2,1)S(1)}, bf16[128,1024]{1,0:T(8,128)(2,1)}, u32[]{:S(2)}) copy-start(bf16[128,1024]{1,0:T(8,128)(2,1)} %convolution_convert_fusion.6) | copy-start | bytes 786436
  43.5 49.3 %collective-permute-start.2 = (bf16[20,6,2048]{2,0,1:T(8,128)(2,1)}, bf16[20,6,2048]{2,0,1:T(8,128)(2,1)}, u32[]{:S(2)}, u32[]{:S(2)}) collective-permute-start(bf16[20,6,2048]{2,0,1:T(8,128)(2,1)} %get-tuple-element.54), channel_id=1, source_target_pairs={{0,1},{1,2},{2,3},{3,4},{4,5},{5,6},{6,7},{8,9},{9,10},{10,11},{11... | collective-permute-start | bytes 1474568 | tf_op jit(solution)/shard_map/ppermute | solution.py:18
  45.6 47.2 %collective-permute-start.3 = (bf16[20,6,2048]{2,0,1:T(8,128)(2,1)}, bf16[20,6,2048]{2,0,1:T(8,128)(2,1)}, u32[]{:S(2)}, u32[]{:S(2)}) collective-permute-start(bf16[20,6,2048]{2,0,1:T(8,128)(2,1)} %get-tuple-element.55), channel_id=1, source_target_pairs={{1,0},{2,1},{3,2},{4,3},{5,4},{6,5},{7,6},{9,8},{10,9},{11,10},{12... | collective-permute-start | bytes 1474568 | tf_op jit(solution)/shard_map/ppermute | solution.py:21
  114.4 2.9 copy-start.9
  114.4 2.9 copy-start.11
  114.4 6.7 %slice-start = ((s8[4849664]{0:T(1024)(128)(4,1)}), s8[4194304]{0:T(1024)(128)(4,1)S(1)}, s32[]{:S(2)}) async-start(s8[4849664]{0:T(1024)(128)(4,1)} %bitcast.76), calls=%async_computation.1 | async-start | bytes 8388608
  117.3 3.8 %slice-start.1 = ((s8[4849664]{0:T(1024)(128)(4,1)}), s8[655360]{0:T(1024)(128)(4,1)S(1)}, s32[]{:S(2)}) async-start(s8[4849664]{0:T(1024)(128)(4,1)} %bitcast.76), calls=%async_computation.2 | async-start | bytes 1310720
  121.0 1.4 copy-start.14
  122.4 2.4 copy-start.5
  141.7 4.0 %copy-start.1 = (f32[20,28,2048]{2,1,0:T(8,128)S(1)}, f32[20,28,2048]{2,1,0:T(8,128)}, u32[]{:S(2)}) copy-start(f32[20,28,2048]{2,1,0:T(8,128)} %reshape.334) | copy-start | bytes 13762564
  147.7 6.8 %copy-start.12 = (bf16[16,128,64]{1,2,0:T(8,128)(2,1)S(1)}, bf16[16,128,64]{1,2,0:T(8,128)(2,1)}, u32[]{:S(2)}) copy-start(bf16[16,128,64]{1,2,0:T(8,128)(2,1)} %get-tuple-element.63) | copy-start | bytes 786436
  148.0 7.7 %copy-start.6 = (bf16[16,128,592]{1,2,0:T(8,128)(2,1)S(1)}, bf16[16,128,592]{1,2,0:T(8,128)(2,1)}, u32[]{:S(2)}) copy-start(bf16[16,128,592]{1,2,0:T(8,128)(2,1)} %copy-done.5) | copy-start | bytes 7274500
  149.4 7.7 %collective-permute-start.4 = (bf16[20,6,2048]{2,0,1:T(8,128)(2,1)S(1)}, bf16[20,6,2048]{2,0,1:T(8,128)(2,1)S(1)}, u32[]{:S(2)}, u32[]{:S(2)}) collective-permute-start(bf16[20,6,2048]{2,0,1:T(8,128)(2,1)S(1)} %copy.50), channel_id=1, source_target_pairs={{1,0},{2,1},{3,2},{4,3},{5,4},{6,5},{7,6},{9,8},{10,9},{11,10},{12... | collective-permute-start | bytes 1474568 | tf_op jit(solution)/shard_map/ppermute | solution.py:29
  150.7 13.0 %collective-permute-start.5 = (bf16[20,6,2048]{2,0,1:T(8,128)(2,1)}, bf16[20,6,2048]{2,0,1:T(8,128)(2,1)}, u32[]{:S(2)}, u32[]{:S(2)}) collective-permute-start(bf16[20,6,2048]{2,0,1:T(8,128)(2,1)} %copy.52), channel_id=1, source_target_pairs={{0,1},{1,2},{2,3},{3,4},{4,5},{5,6},{6,7},{8,9},{9,10},{10,11},{11... | collective-permute-start | bytes 1474568 | tf_op jit(solution)/shard_map/ppermute | solution.py:29
  172.5 4.3 %copy-start.3 = (f32[592,1024]{1,0:T(8,128)S(1)}, f32[592,1024]{1,0:T(8,128)}, u32[]{:S(2)}) copy-start(f32[592,1024]{1,0:T(8,128)} %copy.49) | copy-start | bytes 7274500
  172.5 4.3 %copy-start.4 = (f32[592,1024]{1,0:T(8,128)S(1)}, f32[592,1024]{1,0:T(8,128)}, u32[]{:S(2)}) copy-start(f32[592,1024]{1,0:T(8,128)} %copy.48) | copy-start | bytes 7274500
  175.4 2.2 copy-start.15
  175.4 11.4 %collective-permute-start.6 = (bf16[6,16,2048]{2,1,0:T(8,128)(2,1)}, bf16[6,16,2048]{2,1,0:T(8,128)(2,1)}, u32[]{:S(2)}, u32[]{:S(2)}) collective-permute-start(bf16[6,16,2048]{2,1,0:T(8,128)(2,1)} %get-tuple-element.57), channel_id=1, source_target_pairs={{8,0},{16,8},{24,16},{9,1},{17,9},{25,17},{10,2},{18,10},{26,18},{... | collective-permute-start | bytes 1179656 | tf_op jit(solution)/shard_map/ppermute | solution.py:29
  177.6 3.4 %copy-start.2 = (f32[20,16,2048]{2,1,0:T(8,128)S(1)}, f32[20,16,2048]{2,1,0:T(8,128)}, u32[]{:S(2)}) copy-start(f32[20,16,2048]{2,1,0:T(8,128)} %scatter-add.15) | copy-start | bytes 7864324
  181.1 11.6 %collective-permute-start.7 = (bf16[6,16,2048]{2,1,0:T(8,128)(2,1)S(1)}, bf16[6,16,2048]{2,1,0:T(8,128)(2,1)S(1)}, u32[]{:S(2)}, u32[]{:S(2)}) collective-permute-start(bf16[6,16,2048]{2,1,0:T(8,128)(2,1)S(1)} %get-tuple-element.56), channel_id=1, source_target_pairs={{0,8},{8,16},{16,24},{1,9},{9,17},{17,25},{2,10},{10,18},{18,26},{... | collective-permute-start | bytes 1179656 | tf_op jit(solution)/shard_map/ppermute | solution.py:29
  310.6 2.7 copy-start.7
Sparse Core Ops, SparseCore 0:
  177.7 131.7 all-reduce.3

commit v2 on v1

--- a/solution.py
+++ b/solution.py
@@ -10,23 +10,113 @@
 RAD = 6
 
 
-def with_halo(block, sides, width):
-    for axis, dim in sides:
-        count = lax.axis_size(axis)
-        forward = [(i, i + 1) for i in range(count - 1)]
-        backward = [(target, source) for source, target in forward]
-        low = lax.ppermute(
-            lax.slice_in_dim(block, block.shape[dim] - width, None, axis=dim), axis, forward
+def shifted(x, axes, steps):
+    sizes = [lax.axis_size(a) for a in axes]
+    pairs = []
+    for source in range(math.prod(sizes)):
+        coords, rest = [], source
+        for size in reversed(sizes):
+            coords.append(rest % size)
+            rest //= size
+        coords = coords[::-1]
+        target = [c + s for c, s in zip(coords, steps)]
+        if all(0 <= t < size for t, size in zip(target, sizes)):
+            linear = 0
+            for t, size in zip(target, sizes):
+                linear = linear * size + t
+            pairs.append((source, linear))
+    return lax.ppermute(x, tuple(axes), pairs)
+
+
+def with_halo(tile, width):
+    rows, cols = tile.shape[0], tile.shape[1]
+    top, bottom = tile[rows - width :], tile[:width]
+    both = ("rows", "cols")
+    mid = jnp.concatenate(
+        [
+            shifted(tile[:, cols - width :], ("cols",), (1,)),
+            tile,
+            shifted(tile[:, :width], ("cols",), (-1,)),
+        ],
+        axis=1,
+    )
+    upper = jnp.concatenate(
+        [
+            shifted(top[:, cols - width :], both, (1, 1)),
+            shifted(top, ("rows",), (1,)),
+            shifted(top[:, :width], both, (1, -1)),
+        ],
+        axis=1,
+    )
+    lower = jnp.concatenate(
+        [
+            shifted(bottom[:, cols - width :], both, (-1, 1)),
+            shifted(bottom, ("rows",), (-1,)),
+            shifted(bottom[:, :width], both, (-1, -1)),
+        ],
+        axis=1,
+    )
+    return jnp.concatenate([upper, mid, lower], axis=0)
+
+
+def fold_halo(frame, width):
+    rows, cols = frame.shape[0] - 2 * width, frame.shape[1] - 2 * width
+    both = ("rows", "cols")
+    w = width
+
+    def sent(piece, axes, steps):
+        return shifted(piece.astype(jnp.bfloat16), axes, steps).astype(frame.dtype)
+
+    def placed(piece, row_at, col_at):
+        return jnp.pad(
+            piece,
+            ((row_at, rows - row_at - piece.shape[0]), (col_at, cols - col_at - piece.shape[1]), (0, 0)),
         )
-        high = lax.ppermute(lax.slice_in_dim(block, 0, width, axis=dim), axis, backward)
-        block = jnp.concatenate([low, block, high], axis=dim)
-    return block
-
-
-def from_behind(x, axis, by):
-    size = lax.axis_size(axis)
-    pairs = [(i, i + by) for i in range(size) if 0 <= i + by < size]
-    return lax.ppermute(x, axis, pairs)
+
+    total = frame[w : w + rows, w : w + cols]
+    total = total + placed(sent(frame[:w, w : w + cols], ("rows",), (-1,)), rows - w, 0)
+    total = total + placed(sent(frame[w + rows :, w : w + cols], ("rows",), (1,)), 0, 0)
+    total = total + placed(sent(frame[w : w + rows, :w], ("cols",), (-1,)), 0, cols - w)
+    total = total + placed(sent(frame[w : w + rows, w + cols :], ("cols",), (1,)), 0, 0)
+    total = total + placed(sent(frame[:w, :w], both, (-1, -1)), rows - w, cols - w)
+    total = total + placed(sent(frame[:w, w + cols :], both, (-1, 1)), rows - w, 0)
+    total = total + placed(sent(frame[w + rows :, :w], both, (1, -1)), 0, cols - w)
+    total = total + placed(sent(frame[w + rows :, w + cols :], both, (1, 1)), 0, 0)
+    return total
+
+
+def tree_gather(x, axes):
+    for axis in reversed(axes):
+        size = lax.axis_size(axis)
+        index = lax.axis_index(axis)
+        step = 1
+        while step < size:
+            other = lax.ppermute(x, axis, [(i, i ^ step) for i in range(size)])
+            low = (index // step) % 2 == 0
+            x = jnp.where(low, jnp.concatenate([x, other]), jnp.concatenate([other, x]))
+            step *= 2
+    return x
+
+
+def tree_reduce_scatter(x, axes):
+    for axis in axes:
+        size = lax.axis_size(axis)
+        index = lax.axis_index(axis)
+        x = x.reshape((size, -1) + x.shape[1:])
+        step = size // 2
+        while step >= 1:
+            high = (index // step) % 2 == 1
+            lower, upper = x[:step], x[step : 2 * step]
+            keep = jnp.where(high, upper, lower)
+            send = jnp.where(high, lower, upper)
+            x = keep + lax.ppermute(send, axis, [(i, i ^ step) for i in range(size)])
+            step //= 2
+        x = x.reshape(x.shape[1:])
+    return x
+
+
+def power_of_two(n):
+    return n & (n - 1) == 0
 
 
 def axis_valid(first_cell, tile, extent):
@@ -79,11 +169,14 @@
     own_place = lax.dynamic_index_in_dim(reg_pos, own_index, 0, keepdims=False)
     own_local = (own_place // band_cols - first_row) * tile_cols + (own_place % band_cols - first_col)
     own_kv = lax.dynamic_slice_in_dim(key_value, own_local, 1, 0)
-    global_kv = lax.all_gather(own_kv, ("rows", "cols"), axis=0, tiled=True)
-
-    framed = with_halo(
-        key_value.reshape(tile_rows, tile_cols, 2 * model_width), (("rows", 0), ("cols", 1)), RAD
-    ).reshape(frame_rows * frame_cols, 2 * model_width)
+    if power_of_two(row_count) and power_of_two(col_count):
+        global_kv = tree_gather(own_kv, ("rows", "cols"))
+    else:
+        global_kv = lax.all_gather(own_kv, ("rows", "cols"), axis=0, tiled=True)
+
+    framed = with_halo(key_value.reshape(tile_rows, tile_cols, 2 * model_width), RAD).reshape(
+        frame_rows * frame_cols, 2 * model_width
+    )
     all_kv = jnp.concatenate([framed, global_kv], axis=0)
     key_count = all_kv.shape[0]
 
@@ -131,23 +224,17 @@
     kv_grads_all = jnp.concatenate([key_grads, value_grads], axis=1)
 
     global_grads = kv_grads_all[frame_rows * frame_cols :]
-    own_grads = lax.psum_scatter(global_grads, ("rows", "cols"), scatter_dimension=0, tiled=True)
+    if power_of_two(row_count) and power_of_two(col_count):
+        own_grads = tree_reduce_scatter(global_grads, ("rows", "cols"))
+    else:
+        own_grads = lax.psum_scatter(
+            global_grads, ("rows", "cols"), scatter_dimension=0, tiled=True
+        )
 
     frame_grads = kv_grads_all[: frame_rows * frame_cols].reshape(
         frame_rows, frame_cols, 2 * model_width
     )
-    left_rim = frame_grads[:, :RAD]
-    right_rim = frame_grads[:, tile_cols + RAD :]
-    centre = frame_grads[:, RAD : tile_cols + RAD]
-    from_right = from_behind(left_rim.astype(jnp.bfloat16), "cols", -1).astype(left_rim.dtype)
-    from_left = from_behind(right_rim.astype(jnp.bfloat16), "cols", 1).astype(right_rim.dtype)
-    centre = centre.at[:, tile_cols - RAD :].add(from_right).at[:, :RAD].add(from_left)
-    upper_rim = centre[:RAD]
-    lower_rim = centre[tile_rows + RAD :]
-    middle = centre[RAD : tile_rows + RAD]
-    from_below = from_behind(upper_rim.astype(jnp.bfloat16), "rows", -1).astype(upper_rim.dtype)
-    from_above = from_behind(lower_rim.astype(jnp.bfloat16), "rows", 1).astype(lower_rim.dtype)
-    middle = middle.at[tile_rows - RAD :].add(from_below).at[:RAD].add(from_above)
+    middle = fold_halo(frame_grads, RAD)
     middle = middle.reshape(tokens, 2 * model_width)
     own_row = lax.dynamic_slice_in_dim(middle, own_local, 1, 0) + own_grads
     kv_grads = lax.dynamic_update_slice_in_dim(middle, own_row, own_local, 0).astype(jnp.bfloat16)

time: 323 us -> 187 us (0.58)
  the two profiles are of different devices: /device:TPU:0 before, /device:TPU:15 now
where the time goes in v2:
time: 187 us; the launch traced here: 185 us
  starting transfers between devices  56.3 us (30%)
  waiting for transfers between devices  44.9 us (24%)
  local copies, waits for them, and re-layouts  32.7 us (17%)
  matrix products  25.1 us (13%)
  other arithmetic  22.6 us (12%)
  between operations  3.87 us (2%)
    ppermute x16, starting transfers between devices, shifted(): return lax.ppermute(x, tuple(axes), pairs)  44.6 us
    ppermute x16, waiting for transfers between devices, shifted(): return lax.ppermute(x, tuple(axes), pairs)  30.1 us
    ppermute x5, waiting for transfers between devices, tree_gather(): other = lax.ppermute(x, axis, [(i, i ^ step) for i in range(size)])  8.58 us
    reshape x2, local copies, waits for them, and re-layouts, shards(): with_halo(key_value.reshape(tile_rows, tile_cols, 2 * model_width), RAD)  8.39 us
    dot_general x5, matrix products, einsum_wide(): return jnp.einsum(form, left, right, preferred_element_type=jnp.float32)  8.14 us
    reshape x2, local copies, waits for them, and re-layouts, from_heads(): return x.transpose(1, 0, 2).reshape(count, heads * size)  6.34 us
    ppermute x5, waiting for transfers between devices, tree_reduce_scatter(): x = keep + lax.ppermute(send, axis, [(i, i ^ step) for i in range(size)])  6.2 us
    ppermute x5, starting transfers between devices, tree_gather(): other = lax.ppermute(x, axis, [(i, i ^ step) for i in range(size)])  6.06 us
  transfers between devices with their start and end apart: 26, of which 12 were waited for; matrix products, arithmetic and copies ran while one was open for 10% of the time, Pallas kernels for 0%

profile of v2, /device:TPU:15, one launch (start us, length us, event | category | flops | bytes accessed | tf_op | source)
XLA Modules:
  0.0 185.5 jit_solution(15022276329814614666)
XLA Ops:
  0.7 1.4 dynamic_slice.10
  4.7 2.3 %convolution_convert_fusion.4 = bf16[128,1024]{1,0:T(8,128)(2,1)S(1)} fusion(bf16[128,1024]{1,0:T(8,128)(2,1)} %bitcast.87, bf16[1024,1024]{1,0:T(8,128)(2,1)} %param.10), kind=kOutput, calls=%fused_computation.26 | convolution fusion | flops 268566528 | bytes 2621440 | tf_op jit(solution)/shard_map/dot_general | solution.py:163
  9.2 2.9 %collective-permute-start.6 = (bf16[6,16,2048]{2,1,0:T(8,128)(2,1)}, bf16[6,16,2048]{2,1,0:T(8,128)(2,1)}, u32[]{:S(2)}, u32[]{:S(2)}) collective-permute-start(bf16[6,16,2048]{2,1,0:T(8,128)(2,1)} %bitcast.5), channel_id=1, source_target_pairs={{8,0},{16,8},{24,16},{9,1},{17,9},{25,17},{10,2},{18,10},{26,18},{... | collective-permute-start | bytes 1179656 | tf_op jit(solution)/shard_map/ppermute | solution.py:28
  12.1 1.8 fusion.36
  14.0 4.2 %collective-permute-start.5 = (bf16[6,6,2048]{2,1,0:T(8,128)(2,1)}, bf16[6,6,2048]{2,1,0:T(8,128)(2,1)}, u32[]{:S(2)}, u32[]{:S(2)}) collective-permute-start(bf16[6,6,2048]{2,1,0:T(8,128)(2,1)} %get-tuple-element.21), channel_id=1, source_target_pairs={{8,1},{9,2},{10,3},{11,4},{12,5},{13,6},{14,7},{16,9},{17,10},{18,... | collective-permute-start | bytes 442376 | tf_op jit(solution)/shard_map/ppermute | solution.py:28
  18.1 2.0 %collective-permute-start.7 = (bf16[6,6,2048]{2,1,0:T(8,128)(2,1)}, bf16[6,6,2048]{2,1,0:T(8,128)(2,1)}, u32[]{:S(2)}, u32[]{:S(2)}) collective-permute-start(bf16[6,6,2048]{2,1,0:T(8,128)(2,1)} %get-tuple-element.22), channel_id=1, source_target_pairs={{9,0},{10,1},{11,2},{12,3},{13,4},{14,5},{15,6},{17,8},{18,9},{19,... | collective-permute-start | bytes 442376 | tf_op jit(solution)/shard_map/ppermute | solution.py:28
  21.4 1.8 fusion.35
  25.1 1.8 convolution_convert_fusion.2
  27.3 2.3 %collective-permute-done.9 = bf16[2,2048]{1,0:T(2,128)(2,1)S(1)} collective-permute-done((bf16[2,2048]{1,0:T(2,128)(2,1)S(1)}, bf16[2,2048]{1,0:T(2,128)(2,1)S(1)}, u32[]{:S(2)}, u32[]{:S(2)}) %collective-permute-start.9) | collective-permute-done | bytes 8224 | tf_op jit(solution)/shard_map/ppermute | solution.py:94
  29.6 2.1 %collective-permute-start.10 = (bf16[4,2048]{1,0:T(4,128)(2,1)S(1)}, bf16[4,2048]{1,0:T(4,128)(2,1)S(1)}, u32[]{:S(2)}, u32[]{:S(2)}) collective-permute-start(bf16[4,2048]{1,0:T(4,128)(2,1)S(1)} %maximum_select_fusion.3), channel_id=1, source_target_pairs={{0,4},{1,5},{2,6},{3,7},{4,0},{5,1},{6,2},{7,3},{8,12},{9,13},{10,... | collective-permute-start | bytes 49160 | tf_op jit(solution)/shard_map/ppermute | solution.py:94
  31.6 1.5 collective-permute-done.10
  33.2 2.9 %collective-permute-start.11 = (bf16[8,2048]{1,0:T(8,128)(2,1)S(1)}, bf16[8,2048]{1,0:T(8,128)(2,1)S(1)}, u32[]{:S(2)}, u32[]{:S(2)}) collective-permute-start(bf16[8,2048]{1,0:T(8,128)(2,1)S(1)} %maximum_select_fusion.2), channel_id=1, source_target_pairs={{0,8},{8,0},{16,24},{24,16},{1,9},{9,1},{17,25},{25,17},{2,10},{10... | collective-permute-start | bytes 98312 | tf_op jit(solution)/shard_map/ppermute | solution.py:94
  36.1 3.5 %collective-permute-done.11 = bf16[8,2048]{1,0:T(8,128)(2,1)S(1)} collective-permute-done((bf16[8,2048]{1,0:T(8,128)(2,1)S(1)}, bf16[8,2048]{1,0:T(8,128)(2,1)S(1)}, u32[]{:S(2)}, u32[]{:S(2)}) %collective-permute-start.11) | collective-permute-done | bytes 32800 | tf_op jit(solution)/shard_map/ppermute | solution.py:94
  47.0 5.1 %collective-permute-start.3 = (bf16[8,6,2048]{2,1,0:T(8,128)(2,1)}, bf16[8,6,2048]{2,1,0:T(8,128)(2,1)S(1)}, u32[]{:S(2)}, u32[]{:S(2)}) collective-permute-start(bf16[8,6,2048]{2,1,0:T(8,128)(2,1)} %get-tuple-element.17), channel_id=1, source_target_pairs={{0,1},{1,2},{2,3},{3,4},{4,5},{5,6},{6,7},{8,9},{9,10},{10,11},{11... | collective-permute-start | bytes 589832 | tf_op jit(solution)/shard_map/ppermute | solution.py:28
  52.2 2.5 %collective-permute-done = bf16[6,6,2048]{2,1,0:T(8,128)(2,1)S(1)} collective-permute-done((bf16[6,6,2048]{2,1,0:T(8,128)(2,1)}, bf16[6,6,2048]{2,1,0:T(8,128)(2,1)S(1)}, u32[]{:S(2)}, u32[]{:S(2)}) %collective-permute-start) | collective-permute-done | bytes 147488 | tf_op jit(solution)/shard_map/ppermute | solution.py:28
  54.7 2.1 %collective-permute-start.4 = (bf16[8,6,2048]{2,1,0:T(8,128)(2,1)}, bf16[8,6,2048]{2,1,0:T(8,128)(2,1)S(1)}, u32[]{:S(2)}, u32[]{:S(2)}) collective-permute-start(bf16[8,6,2048]{2,1,0:T(8,128)(2,1)} %get-tuple-element.18), channel_id=1, source_target_pairs={{1,0},{2,1},{3,2},{4,3},{5,4},{6,5},{7,6},{9,8},{10,9},{11,10},{12... | collective-permute-start | bytes 589832 | tf_op jit(solution)/shard_map/ppermute | solution.py:28
  58.7 3.8 %collective-permute-done.4 = bf16[8,6,2048]{2,1,0:T(8,128)(2,1)S(1)} collective-permute-done((bf16[8,6,2048]{2,1,0:T(8,128)(2,1)}, bf16[8,6,2048]{2,1,0:T(8,128)(2,1)S(1)}, u32[]{:S(2)}, u32[]{:S(2)}) %collective-permute-start.4) | collective-permute-done | bytes 196640 | tf_op jit(solution)/shard_map/ppermute | solution.py:28
  62.6 3.6 %maximum_maximum_fusion = bf16[20,28,2048]{2,1,0:T(8,128)(2,1)} fusion(bf16[6,6,2048]{2,1,0:T(8,128)(2,1)} %collective-permute-done.7, bf16[6,16,2048]{2,1,0:T(8,128)(2,1)} %collective-permute-done.6, bf16[6,6,2048]{2,1,0:T(8,128)(2,1)} %collective-permute-done.5, bf16[8,6,2048]{2,1,0:T(8,128)(2,1)S(1)} %collective-permute-done.4, ...), kind=kLoop, calls=%fused_computation.10 | loop fusion | flops 20643840 | bytes 4587520 | tf_op jit(solution)/shard_map/concatenate | solution.py:59
  66.2 4.0 %reshape.263 = bf16[560,2048]{1,0:T(8,128)(2,1)} reshape(bf16[20,28,2048]{2,1,0:T(8,128)(2,1)} %maximum_maximum_fusion) | data formatting | bytes 4587520 | tf_op jit(solution)/shard_map/reshape | solution.py:177
  70.2 4.3 %copy.19 = bf16[560,2048]{0,1:T(8,128)(2,1)} copy(bf16[560,2048]{1,0:T(8,128)(2,1)} %reshape.263) | data formatting | bytes 4587520 | tf_op jit(solution)/shard_map/reshape | solution.py:177
  74.6 3.4 %pad_maximum_fusion = (bf16[592,1024]{0,1:T(8,128)(2,1)S(1)}, bf16[592,1024]{0,1:T(8,128)(2,1)}) fusion(bf16[32,2048]{0,1:T(8,128)(2,1)} %copy.20, bf16[560,2048]{0,1:T(8,128)(2,1)} %copy.19), kind=kLoop, calls=%fused_computation.19 | loop fusion | flops 4849664 | bytes 4849664 | tf_op jit(solution)/shard_map/concatenate | solution.py:180
  77.9 5.0 %fusion.37 = (f32[16,128]{1,0:T(8,128)S(1)}, f32[16,128,592]{1,2,0:T(8,128)}) fusion(pred[128,592]{0,1:T(8,128)(4,1)S(1)} %copy-done.14, bf16[16,128,64]{1,2,0:T(8,128)(2,1)} %bitcast.93, bf16[16,592,64]{1,2,0:T(8,128)(2,1)S(1)} %bitcast.77), kind=kOutput, calls=%fused_computation.90 | convolution fusion | flops 160039504 | bytes 6408192 | tf_op jit(solution)/shard_map/sub | solution.py:199
  83.0 2.9 %fusion.6 = bf16[16,128,592]{1,2,0:T(8,128)(2,1)S(1)} fusion(f32[16,128,592]{1,2,0:T(8,128)} %get-tuple-element.24, f32[16,128]{1,0:T(8,128)S(1)} %get-tuple-element.23), kind=kLoop, calls=%fused_computation.17 | loop fusion | flops 2424832 | bytes 7282688 | tf_op jit(solution)/shard_map/convert_element_type | solution.py:202
  87.2 2.4 %fusion.40 = f32[16,592,64]{1,2,0:T(8,128)} fusion(bf16[16,128,592]{1,2,0:T(8,128)(2,1)S(1)} %fusion.6, bf16[16,128,64]{1,2,0:T(8,128)(2,1)S(1)} %bitcast.90), kind=kOutput, calls=%fused_computation.93 | convolution fusion | flops 155189248 | bytes 5111808 | tf_op jit(solution)/shard_map/hqk,hqd->hkd/dot_general | solution.py:130
  89.7 1.3 multiply_convert_fusion
  91.0 2.4 %fusion.39 = f32[16,592,64]{1,2,0:T(8,128)} fusion(bf16[16,128,592]{1,2,0:T(8,128)(2,1)S(1)} %multiply_convert_fusion, bf16[16,128,64]{1,2,0:T(8,128)(2,1)S(1)} %bitcast.94), kind=kOutput, calls=%fused_computation.92 | convolution fusion | flops 155189248 | bytes 5111808 | tf_op jit(solution)/shard_map/hqk,hqd->hkd/dot_general | solution.py:130
  93.4 3.2 %copy.23 = f32[592,1024]{1,0:T(8,128)} copy(f32[592,1024]{0,1:T(8,128)} %bitcast.75) | data formatting | bytes 4849664 | tf_op jit(solution)/shard_map/reshape | solution.py:140
  96.6 3.2 %copy.22 = f32[592,1024]{1,0:T(8,128)} copy(f32[592,1024]{0,1:T(8,128)} %bitcast.76) | data formatting | bytes 4849664 | tf_op jit(solution)/shard_map/reshape | solution.py:140
  99.8 5.0 %fusion.1 = f32[560,2048]{1,0:T(8,128)} fusion(f32[592,1024]{1,0:T(8,128)} %copy.22, f32[592,1024]{1,0:T(8,128)} %copy.23), kind=kLoop, calls=%fused_computation.8 | loop fusion | flops 1146880 | bytes 9437184 | tf_op jit(solution)/shard_map/concatenate | solution.py:224
  104.8 5.4 %reshape.273 = f32[20,28,2048]{2,1,0:T(8,128)} reshape(f32[560,2048]{1,0:T(8,128)} %fusion.1) | data formatting | bytes 9175040 | tf_op jit(solution)/shard_map/reshape | solution.py:234
  110.2 3.0 %convert.26 = bf16[20,28,2048]{2,1,0:T(8,128)(2,1)S(1)} convert(f32[20,28,2048]{2,1,0:T(8,128)} %reshape.273) | non-fusion elementwise | flops 1146880 | bytes 6881280 | tf_op jit(solution)/shard_map/convert.23
  115.0 2.6 %collective-permute-start.21 = (f32[2,8,2048]{2,1,0:T(8,128)S(1)}, f32[2,8,2048]{2,1,0:T(8,128)S(1)}, u32[]{:S(2)}, u32[]{:S(2)}) collective-permute-start(f32[2,8,2048]{2,1,0:T(8,128)S(1)} %get-tuple-element.2), channel_id=1, source_target_pairs={{0,16},{8,24},{16,0},{24,8},{1,17},{9,25},{17,1},{25,9},{2,18},{10... | collective-permute-start | bytes 393224 | tf_op jit(solution)/shard_map/ppermute | solution.py:112
  117.8 2.6 %collective-permute-done.21 = f32[2,8,2048]{2,1,0:T(8,128)S(1)} collective-permute-done((f32[2,8,2048]{2,1,0:T(8,128)S(1)}, f32[2,8,2048]{2,1,0:T(8,128)S(1)}, u32[]{:S(2)}, u32[]{:S(2)}) %collective-permute-start.21) | collective-permute-done | bytes 131104 | tf_op jit(solution)/shard_map/ppermute | solution.py:112
  120.4 2.4 %collective-permute-start.22 = (f32[1,8,2048]{2,1,0:T(8,128)S(1)}, f32[1,8,2048]{2,1,0:T(8,128)S(1)}, u32[]{:S(2)}, u32[]{:S(2)}) collective-permute-start(f32[1,8,2048]{2,1,0:T(8,128)S(1)} %slice_select_fusion), channel_id=1, source_target_pairs={{0,8},{8,0},{16,24},{24,16},{1,9},{9,1},{17,25},{25,17},{2,10},{10... | collective-permute-start | bytes 196616 | tf_op jit(solution)/shard_map/ppermute | solution.py:112
  123.5 1.6 collective-permute-done.22
  125.2 1.7 fusion.38
  126.9 2.0 %collective-permute-done.23 = f32[4,1,2048]{2,0,1:T(4,128)S(1)} collective-permute-done((f32[4,1,2048]{2,0,1:T(4,128)S(1)}, f32[4,1,2048]{2,0,1:T(4,128)S(1)}, u32[]{:S(2)}, u32[]{:S(2)}) %collective-permute-start.23) | collective-permute-done | bytes 32800 | tf_op jit(solution)/shard_map/ppermute | solution.py:112
  130.5 3.1 %collective-permute-start.15 = (bf16[8,6,2048]{2,1,0:T(8,128)(2,1)S(1)}, bf16[8,6,2048]{2,1,0:T(8,128)(2,1)S(1)}, u32[]{:S(2)}, u32[]{:S(2)}) collective-permute-start(bf16[8,6,2048]{2,1,0:T(8,128)(2,1)S(1)} %get-tuple-element.9), channel_id=1, source_target_pairs={{1,0},{2,1},{3,2},{4,3},{5,4},{6,5},{7,6},{9,8},{10,9},{11,10},{12... | collective-permute-start | bytes 589832 | tf_op jit(solution)/shard_map/ppermute | solution.py:28
  133.6 3.9 %collective-permute-start.16 = (bf16[8,6,2048]{2,1,0:T(8,128)(2,1)S(1)}, bf16[8,6,2048]{2,1,0:T(8,128)(2,1)S(1)}, u32[]{:S(2)}, u32[]{:S(2)}) collective-permute-start(bf16[8,6,2048]{2,1,0:T(8,128)(2,1)S(1)} %get-tuple-element.10), channel_id=1, source_target_pairs={{0,1},{1,2},{2,3},{3,4},{4,5},{5,6},{6,7},{8,9},{9,10},{10,11},{11... | collective-permute-start | bytes 589832 | tf_op jit(solution)/shard_map/ppermute | solution.py:28
  137.6 2.3 %collective-permute-start.17 = (bf16[6,6,2048]{2,1,0:T(8,128)(2,1)S(1)}, bf16[6,6,2048]{2,1,0:T(8,128)(2,1)S(1)}, u32[]{:S(2)}, u32[]{:S(2)}) collective-permute-start(bf16[6,6,2048]{2,1,0:T(8,128)(2,1)S(1)} %get-tuple-element.11), channel_id=1, source_target_pairs={{9,0},{10,1},{11,2},{12,3},{13,4},{14,5},{15,6},{17,8},{18,9},{19,... | collective-permute-start | bytes 442376 | tf_op jit(solution)/shard_map/ppermute | solution.py:28
  142.5 8.3 %collective-permute-start.18 = (bf16[6,6,2048]{2,1,0:T(8,128)(2,1)S(1)}, bf16[6,6,2048]{2,1,0:T(8,128)(2,1)S(1)}, u32[]{:S(2)}, u32[]{:S(2)}) collective-permute-start(bf16[6,6,2048]{2,1,0:T(8,128)(2,1)S(1)} %get-tuple-element.14), channel_id=1, source_target_pairs={{8,1},{9,2},{10,3},{11,4},{12,5},{13,6},{14,7},{16,9},{17,10},{18,... | collective-permute-start | bytes 442376 | tf_op jit(solution)/shard_map/ppermute | solution.py:28
  150.7 7.2 %collective-permute-done.20 = bf16[6,6,2048]{2,1,0:T(8,128)(2,1)S(1)} collective-permute-done((bf16[6,6,2048]{2,1,0:T(8,128)(2,1)S(1)}, bf16[6,6,2048]{2,1,0:T(8,128)(2,1)S(1)}, u32[]{:S(2)}, u32[]{:S(2)}) %collective-permute-start.20) | collective-permute-done | bytes 147488 | tf_op jit(solution)/shard_map/ppermute | solution.py:28
  157.9 3.1 %collective-permute-start.13 = (bf16[6,16,2048]{2,1,0:T(8,128)(2,1)S(1)}, bf16[6,16,2048]{2,1,0:T(8,128)(2,1)S(1)}, u32[]{:S(2)}, u32[]{:S(2)}) collective-permute-start(bf16[6,16,2048]{2,1,0:T(8,128)(2,1)S(1)} %get-tuple-element.7), channel_id=1, source_target_pairs={{8,0},{16,8},{24,16},{9,1},{17,9},{25,17},{10,2},{18,10},{26,18},{... | collective-permute-start | bytes 1179656 | tf_op jit(solution)/shard_map/ppermute | solution.py:28
  162.5 6.4 %collective-permute-done.13 = bf16[6,16,2048]{2,1,0:T(8,128)(2,1)S(1)} collective-permute-done((bf16[6,16,2048]{2,1,0:T(8,128)(2,1)S(1)}, bf16[6,16,2048]{2,1,0:T(8,128)(2,1)S(1)}, u32[]{:S(2)}, u32[]{:S(2)}) %collective-permute-start.13) | collective-permute-done | bytes 393248 | tf_op jit(solution)/shard_map/ppermute | solution.py:28
  168.9 10.1 %collective-permute-done.14 = bf16[6,16,2048]{2,1,0:T(8,128)(2,1)S(1)} collective-permute-done((bf16[6,16,2048]{2,1,0:T(8,128)(2,1)S(1)}, bf16[6,16,2048]{2,1,0:T(8,128)(2,1)S(1)}, u32[]{:S(2)}, u32[]{:S(2)}) %collective-permute-start.14) | collective-permute-done | bytes 393248 | tf_op jit(solution)/shard_map/ppermute | solution.py:28
  179.0 2.0 %fusion.15 = f32[8,16,2048]{2,1,0:T(8,128)S(1)} fusion(f32[20,28,2048]{2,1,0:T(8,128)} %reshape.273, bf16[6,6,2048]{2,1,0:T(8,128)(2,1)S(1)} %collective-permute-done.20, bf16[6,6,2048]{2,1,0:T(8,128)(2,1)S(1)} %collective-permute-done.19, bf16[6,6,2048]{2,1,0:T(8,128)(2,1)S(1)} %collective-permute-done.18, ...), kind=kLoop, calls=%fused_computation.37 | loop fusion | flops 4194304 | bytes 3866624 | tf_op jit(solution)/shard_map/add | solution.py:84
  181.3 2.6 %convolution_add_fusion.1 = f32[128,1024]{1,0:T(8,128)S(1)} fusion(f32[128,1024]{1,0:T(8,128)} %fusion.38, bf16[1024,1024]{1,0:T(8,128)(2,1)} %param.9, bf16[128,2048]{1,0:T(8,128)(2,1)S(1)} %convert_element_type.84), kind=kOutput, calls=%fused_computation.21 | convolution fusion | flops 268566528 | bytes 3407872 | tf_op jit(solution)/shard_map/dot_general | solution.py:244
  183.9 1.5 fusion.8
  (106 shorter events, 24.9 us)
Async XLA Ops:
  0.6 22.7 %copy-start = (bf16[1024,1024]{1,0:T(8,128)(2,1)S(1)}, bf16[1024,1024]{1,0:T(8,128)(2,1)}, u32[]{:S(2)}) copy-start(bf16[1024,1024]{1,0:T(8,128)(2,1)} %param.8) | copy-start | bytes 6291460
  0.6 6.3 %copy-start.10 = (bf16[8,16,1024]{2,1,0:T(8,128)(2,1)S(1)}, bf16[8,16,1024]{2,1,0:T(8,128)(2,1)}, u32[]{:S(2)}) copy-start(bf16[8,16,1024]{2,1,0:T(8,128)(2,1)} %param.7) | copy-start | bytes 786436
  4.7 2.3 %copy-start.8 = (bf16[1024,1024]{1,0:T(8,128)(2,1)S(1)}, bf16[1024,1024]{1,0:T(8,128)(2,1)}, u32[]{:S(2)}) copy-start(bf16[1024,1024]{1,0:T(8,128)(2,1)} %param.9) | copy-start | bytes 6291460
  7.5 19.4 %collective-permute-start.8 = (bf16[1,2048]{1,0:T(2,128)(2,1)S(1)}, bf16[1,2048]{1,0:T(2,128)(2,1)S(1)}, u32[]{:S(2)}, u32[]{:S(2)}) collective-permute-start(bf16[1,2048]{1,0:T(2,128)(2,1)S(1)} %fusion.24), channel_id=1, source_target_pairs={{0,1},{1,0},{2,3},{3,2},{4,5},{5,4},{6,7},{7,6},{8,9},{9,8},{10,11... | collective-permute-start | bytes 12296 | tf_op jit(solution)/shard_map/ppermute | solution.py:94
  9.2 53.4 %collective-permute-start.6 = (bf16[6,16,2048]{2,1,0:T(8,128)(2,1)}, bf16[6,16,2048]{2,1,0:T(8,128)(2,1)}, u32[]{:S(2)}, u32[]{:S(2)}) collective-permute-start(bf16[6,16,2048]{2,1,0:T(8,128)(2,1)} %bitcast.5), channel_id=1, source_target_pairs={{8,0},{16,8},{24,16},{9,1},{17,9},{25,17},{10,2},{18,10},{26,18},{... | collective-permute-start | bytes 1179656 | tf_op jit(solution)/shard_map/ppermute | solution.py:28
  14.0 31.8 %collective-permute-start.5 = (bf16[6,6,2048]{2,1,0:T(8,128)(2,1)}, bf16[6,6,2048]{2,1,0:T(8,128)(2,1)}, u32[]{:S(2)}, u32[]{:S(2)}) collective-permute-start(bf16[6,6,2048]{2,1,0:T(8,128)(2,1)} %get-tuple-element.21), channel_id=1, source_target_pairs={{8,1},{9,2},{10,3},{11,4},{12,5},{13,6},{14,7},{16,9},{17,10},{18,... | collective-permute-start | bytes 442376 | tf_op jit(solution)/shard_map/ppermute | solution.py:28
  18.1 28.9 %collective-permute-start.7 = (bf16[6,6,2048]{2,1,0:T(8,128)(2,1)}, bf16[6,6,2048]{2,1,0:T(8,128)(2,1)}, u32[]{:S(2)}, u32[]{:S(2)}) collective-permute-start(bf16[6,6,2048]{2,1,0:T(8,128)(2,1)} %get-tuple-element.22), channel_id=1, source_target_pairs={{9,0},{10,1},{11,2},{12,3},{13,4},{14,5},{15,6},{17,8},{18,9},{19,... | collective-permute-start | bytes 442376 | tf_op jit(solution)/shard_map/ppermute | solution.py:28
  20.1 42.5 %collective-permute-start.1 = (bf16[6,16,2048]{2,1,0:T(8,128)(2,1)}, bf16[6,16,2048]{2,1,0:T(8,128)(2,1)}, u32[]{:S(2)}, u32[]{:S(2)}) collective-permute-start(bf16[6,16,2048]{2,1,0:T(8,128)(2,1)} %bitcast.3), channel_id=1, source_target_pairs={{0,8},{8,16},{16,24},{1,9},{9,17},{17,25},{2,10},{10,18},{18,26},{... | collective-permute-start | bytes 1179656 | tf_op jit(solution)/shard_map/ppermute | solution.py:28
  23.3 1.8 copy-start.5
  27.0 2.6 %collective-permute-start.9 = (bf16[2,2048]{1,0:T(2,128)(2,1)S(1)}, bf16[2,2048]{1,0:T(2,128)(2,1)S(1)}, u32[]{:S(2)}, u32[]{:S(2)}) collective-permute-start(bf16[2,2048]{1,0:T(2,128)(2,1)S(1)} %broadcast_select_fusion.3), channel_id=1, source_target_pairs={{0,2},{1,3},{2,0},{3,1},{4,6},{5,7},{6,4},{7,5},{8,10},{9,11},{10,... | collective-permute-start | bytes 24584 | tf_op jit(solution)/shard_map/ppermute | solution.py:94
  29.6 3.6 %collective-permute-start.10 = (bf16[4,2048]{1,0:T(4,128)(2,1)S(1)}, bf16[4,2048]{1,0:T(4,128)(2,1)S(1)}, u32[]{:S(2)}, u32[]{:S(2)}) collective-permute-start(bf16[4,2048]{1,0:T(4,128)(2,1)S(1)} %maximum_select_fusion.3), channel_id=1, source_target_pairs={{0,4},{1,5},{2,6},{3,7},{4,0},{5,1},{6,2},{7,3},{8,12},{9,13},{10,... | collective-permute-start | bytes 49160 | tf_op jit(solution)/shard_map/ppermute | solution.py:94
  33.2 6.5 %collective-permute-start.11 = (bf16[8,2048]{1,0:T(8,128)(2,1)S(1)}, bf16[8,2048]{1,0:T(8,128)(2,1)S(1)}, u32[]{:S(2)}, u32[]{:S(2)}) collective-permute-start(bf16[8,2048]{1,0:T(8,128)(2,1)S(1)} %maximum_select_fusion.2), channel_id=1, source_target_pairs={{0,8},{8,0},{16,24},{24,16},{1,9},{9,1},{17,25},{25,17},{2,10},{10... | collective-permute-start | bytes 98312 | tf_op jit(solution)/shard_map/ppermute | solution.py:94
  39.7 3.2 %collective-permute-start.12 = (bf16[16,2048]{1,0:T(8,128)(2,1)S(1)}, bf16[16,2048]{1,0:T(8,128)(2,1)S(1)}, u32[]{:S(2)}, u32[]{:S(2)}) collective-permute-start(bf16[16,2048]{1,0:T(8,128)(2,1)S(1)} %maximum_select_fusion.1), channel_id=1, source_target_pairs={{0,16},{8,24},{16,0},{24,8},{1,17},{9,25},{17,1},{25,9},{2,18},{10... | collective-permute-start | bytes 196616 | tf_op jit(solution)/shard_map/ppermute | solution.py:94
  42.8 11.8 %copy-start.15 = (bf16[16,2048]{1,0:T(8,128)(2,1)}, bf16[16,2048]{1,0:T(8,128)(2,1)S(1)}, u32[]{:S(2)}) copy-start(bf16[16,2048]{1,0:T(8,128)(2,1)S(1)} %collective-permute-done.12) | copy-start | bytes 196612
  42.8 11.8 %collective-permute-start = (bf16[6,6,2048]{2,1,0:T(8,128)(2,1)}, bf16[6,6,2048]{2,1,0:T(8,128)(2,1)S(1)}, u32[]{:S(2)}, u32[]{:S(2)}) collective-permute-start(bf16[6,6,2048]{2,1,0:T(8,128)(2,1)} %get-tuple-element.19), channel_id=1, source_target_pairs={{0,9},{1,10},{2,11},{3,12},{4,13},{5,14},{6,15},{8,17},{9,18},{10,... | collective-permute-start | bytes 442376 | tf_op jit(solution)/shard_map/ppermute | solution.py:28
  45.7 13.0 %collective-permute-start.2 = (bf16[6,6,2048]{2,1,0:T(8,128)(2,1)}, bf16[6,6,2048]{2,1,0:T(8,128)(2,1)}, u32[]{:S(2)}, u32[]{:S(2)}) collective-permute-start(bf16[6,6,2048]{2,1,0:T(8,128)(2,1)} %get-tuple-element.20), channel_id=1, source_target_pairs={{1,8},{2,9},{3,10},{4,11},{5,12},{6,13},{7,14},{9,16},{10,17},{11,... | collective-permute-start | bytes 442376 | tf_op jit(solution)/shard_map/ppermute | solution.py:28
  47.0 11.7 %collective-permute-start.3 = (bf16[8,6,2048]{2,1,0:T(8,128)(2,1)}, bf16[8,6,2048]{2,1,0:T(8,128)(2,1)S(1)}, u32[]{:S(2)}, u32[]{:S(2)}) collective-permute-start(bf16[8,6,2048]{2,1,0:T(8,128)(2,1)} %get-tuple-element.17), channel_id=1, source_target_pairs={{0,1},{1,2},{2,3},{3,4},{4,5},{5,6},{6,7},{8,9},{9,10},{10,11},{11... | collective-permute-start | bytes 589832 | tf_op jit(solution)/shard_map/ppermute | solution.py:28
  54.7 7.9 %collective-permute-start.4 = (bf16[8,6,2048]{2,1,0:T(8,128)(2,1)}, bf16[8,6,2048]{2,1,0:T(8,128)(2,1)S(1)}, u32[]{:S(2)}, u32[]{:S(2)}) collective-permute-start(bf16[8,6,2048]{2,1,0:T(8,128)(2,1)} %get-tuple-element.18), channel_id=1, source_target_pairs={{1,0},{2,1},{3,2},{4,3},{5,4},{6,5},{7,6},{9,8},{10,9},{11,10},{12... | collective-permute-start | bytes 589832 | tf_op jit(solution)/shard_map/ppermute | solution.py:28
  74.6 3.4 %copy-start.14 = (pred[128,592]{0,1:T(8,128)(4,1)S(1)}, pred[128,592]{0,1:T(8,128)(4,1)}, u32[]{:S(2)}) copy-start(pred[128,592]{0,1:T(8,128)(4,1)} %concatenate.54.clone) | copy-start | bytes 227332
  83.0 2.9 %copy-start.9 = (bf16[592,1024]{0,1:T(8,128)(2,1)S(1)}, bf16[592,1024]{0,1:T(8,128)(2,1)}, u32[]{:S(2)}) copy-start(bf16[592,1024]{0,1:T(8,128)(2,1)} %get-tuple-element.6) | copy-start | bytes 3637252
  83.0 2.9 %copy-start.11 = (bf16[128,1024]{0,1:T(8,128)(2,1)S(1)}, bf16[128,1024]{0,1:T(8,128)(2,1)}, u32[]{:S(2)}) copy-start(bf16[128,1024]{0,1:T(8,128)(2,1)} %copy.21) | copy-start | bytes 786436
  83.0 6.7 %slice-start = ((s8[4849664]{0:T(1024)(128)(4,1)}), s8[4194304]{0:T(1024)(128)(4,1)S(1)}, s32[]{:S(2)}) async-start(s8[4849664]{0:T(1024)(128)(4,1)} %bitcast.81), calls=%async_computation | async-start | bytes 8388608
  85.9 3.8 %slice-start.1 = ((s8[4849664]{0:T(1024)(128)(4,1)}), s8[655360]{0:T(1024)(128)(4,1)S(1)}, s32[]{:S(2)}) async-start(s8[4849664]{0:T(1024)(128)(4,1)} %bitcast.81), calls=%async_computation.1 | async-start | bytes 1310720
  89.6 1.4 copy-start.13
  91.0 2.4 %copy-start.3 = (bf16[16,128,592]{1,2,0:T(8,128)(2,1)}, bf16[16,128,592]{1,2,0:T(8,128)(2,1)S(1)}, u32[]{:S(2)}) copy-start(bf16[16,128,592]{1,2,0:T(8,128)(2,1)S(1)} %multiply_convert_fusion) | copy-start | bytes 7274500
  110.2 3.4 %copy-start.2 = (f32[592,1024]{1,0:T(8,128)S(1)}, f32[592,1024]{1,0:T(8,128)}, u32[]{:S(2)}) copy-start(f32[592,1024]{1,0:T(8,128)} %copy.22) | copy-start | bytes 7274500
  113.3 1.7 copy-start.1
  115.0 7.9 %copy-start.4 = (bf16[16,128,592]{1,2,0:T(8,128)(2,1)S(1)}, bf16[16,128,592]{1,2,0:T(8,128)(2,1)}, u32[]{:S(2)}) copy-start(bf16[16,128,592]{1,2,0:T(8,128)(2,1)} %copy-done.3) | copy-start | bytes 7274500
  115.0 5.3 %collective-permute-start.21 = (f32[2,8,2048]{2,1,0:T(8,128)S(1)}, f32[2,8,2048]{2,1,0:T(8,128)S(1)}, u32[]{:S(2)}, u32[]{:S(2)}) collective-permute-start(f32[2,8,2048]{2,1,0:T(8,128)S(1)} %get-tuple-element.2), channel_id=1, source_target_pairs={{0,16},{8,24},{16,0},{24,8},{1,17},{9,25},{17,1},{25,9},{2,18},{10... | collective-permute-start | bytes 393224 | tf_op jit(solution)/shard_map/ppermute | solution.py:112
  120.4 4.7 %collective-permute-start.22 = (f32[1,8,2048]{2,1,0:T(8,128)S(1)}, f32[1,8,2048]{2,1,0:T(8,128)S(1)}, u32[]{:S(2)}, u32[]{:S(2)}) collective-permute-start(f32[1,8,2048]{2,1,0:T(8,128)S(1)} %slice_select_fusion), channel_id=1, source_target_pairs={{0,8},{8,0},{16,24},{24,16},{1,9},{9,1},{17,25},{25,17},{2,10},{10... | collective-permute-start | bytes 196616 | tf_op jit(solution)/shard_map/ppermute | solution.py:112
  123.5 5.8 %copy-start.6 = (bf16[1024,1024]{1,0:T(8,128)(2,1)S(1)}, bf16[1024,1024]{1,0:T(8,128)(2,1)}, u32[]{:S(2)}) copy-start(bf16[1024,1024]{1,0:T(8,128)(2,1)} %param.11) | copy-start | bytes 6291460
  123.5 5.8 %copy-start.12 = (bf16[16,128,64]{1,2,0:T(8,128)(2,1)S(1)}, bf16[16,128,64]{1,2,0:T(8,128)(2,1)}, u32[]{:S(2)}) copy-start(bf16[16,128,64]{1,2,0:T(8,128)(2,1)} %get-tuple-element.26) | copy-start | bytes 786436
  125.2 3.7 %collective-permute-start.23 = (f32[4,1,2048]{2,0,1:T(4,128)S(1)}, f32[4,1,2048]{2,0,1:T(4,128)S(1)}, u32[]{:S(2)}, u32[]{:S(2)}) collective-permute-start(f32[4,1,2048]{2,0,1:T(4,128)S(1)} %select_bitcast_fusion.1), channel_id=1, source_target_pairs={{0,4},{1,5},{2,6},{3,7},{4,0},{5,1},{6,2},{7,3},{8,12},{9,13},{10,... | collective-permute-start | bytes 98312 | tf_op jit(solution)/shard_map/ppermute | solution.py:112
  128.9 12.2 %collective-permute-start.24 = (f32[2,1,2048]{2,0,1:T(2,128)S(1)}, f32[2,1,2048]{2,0,1:T(2,128)S(1)}, u32[]{:S(2)}, u32[]{:S(2)}) collective-permute-start(f32[2,1,2048]{2,0,1:T(2,128)S(1)} %broadcast_select_fusion), channel_id=1, source_target_pairs={{0,2},{1,3},{2,0},{3,1},{4,6},{5,7},{6,4},{7,5},{8,10},{9,11},{10,... | collective-permute-start | bytes 49160 | tf_op jit(solution)/shard_map/ppermute | solution.py:112
  130.5 31.9 %collective-permute-start.15 = (bf16[8,6,2048]{2,1,0:T(8,128)(2,1)S(1)}, bf16[8,6,2048]{2,1,0:T(8,128)(2,1)S(1)}, u32[]{:S(2)}, u32[]{:S(2)}) collective-permute-start(bf16[8,6,2048]{2,1,0:T(8,128)(2,1)S(1)} %get-tuple-element.9), channel_id=1, source_target_pairs={{1,0},{2,1},{3,2},{4,3},{5,4},{6,5},{7,6},{9,8},{10,9},{11,10},{12... | collective-permute-start | bytes 589832 | tf_op jit(solution)/shard_map/ppermute | solution.py:28
  133.6 28.8 %collective-permute-start.16 = (bf16[8,6,2048]{2,1,0:T(8,128)(2,1)S(1)}, bf16[8,6,2048]{2,1,0:T(8,128)(2,1)S(1)}, u32[]{:S(2)}, u32[]{:S(2)}) collective-permute-start(bf16[8,6,2048]{2,1,0:T(8,128)(2,1)S(1)} %get-tuple-element.10), channel_id=1, source_target_pairs={{0,1},{1,2},{2,3},{3,4},{4,5},{5,6},{6,7},{8,9},{9,10},{10,11},{11... | collective-permute-start | bytes 589832 | tf_op jit(solution)/shard_map/ppermute | solution.py:28
  137.6 4.9 %collective-permute-start.17 = (bf16[6,6,2048]{2,1,0:T(8,128)(2,1)S(1)}, bf16[6,6,2048]{2,1,0:T(8,128)(2,1)S(1)}, u32[]{:S(2)}, u32[]{:S(2)}) collective-permute-start(bf16[6,6,2048]{2,1,0:T(8,128)(2,1)S(1)} %get-tuple-element.11), channel_id=1, source_target_pairs={{9,0},{10,1},{11,2},{12,3},{13,4},{14,5},{15,6},{17,8},{18,9},{19,... | collective-permute-start | bytes 442376 | tf_op jit(solution)/shard_map/ppermute | solution.py:28
  139.8 18.1 %collective-permute-start.20 = (bf16[6,6,2048]{2,1,0:T(8,128)(2,1)S(1)}, bf16[6,6,2048]{2,1,0:T(8,128)(2,1)S(1)}, u32[]{:S(2)}, u32[]{:S(2)}) collective-permute-start(bf16[6,6,2048]{2,1,0:T(8,128)(2,1)S(1)} %get-tuple-element.12), channel_id=1, source_target_pairs={{0,9},{1,10},{2,11},{3,12},{4,13},{5,14},{6,15},{8,17},{9,18},{10,... | collective-permute-start | bytes 442376 | tf_op jit(solution)/shard_map/ppermute | solution.py:28
  141.1 19.9 %collective-permute-start.19 = (bf16[6,6,2048]{2,1,0:T(8,128)(2,1)S(1)}, bf16[6,6,2048]{2,1,0:T(8,128)(2,1)S(1)}, u32[]{:S(2)}, u32[]{:S(2)}) collective-permute-start(bf16[6,6,2048]{2,1,0:T(8,128)(2,1)S(1)} %get-tuple-element.13), channel_id=1, source_target_pairs={{1,8},{2,9},{3,10},{4,11},{5,12},{6,13},{7,14},{9,16},{10,17},{11,... | collective-permute-start | bytes 442376 | tf_op jit(solution)/shard_map/ppermute | solution.py:28
  142.5 19.9 %collective-permute-start.18 = (bf16[6,6,2048]{2,1,0:T(8,128)(2,1)S(1)}, bf16[6,6,2048]{2,1,0:T(8,128)(2,1)S(1)}, u32[]{:S(2)}, u32[]{:S(2)}) collective-permute-start(bf16[6,6,2048]{2,1,0:T(8,128)(2,1)S(1)} %get-tuple-element.14), channel_id=1, source_target_pairs={{8,1},{9,2},{10,3},{11,4},{12,5},{13,6},{14,7},{16,9},{17,10},{18,... | collective-permute-start | bytes 442376 | tf_op jit(solution)/shard_map/ppermute | solution.py:28
  157.9 10.9 %collective-permute-start.13 = (bf16[6,16,2048]{2,1,0:T(8,128)(2,1)S(1)}, bf16[6,16,2048]{2,1,0:T(8,128)(2,1)S(1)}, u32[]{:S(2)}, u32[]{:S(2)}) collective-permute-start(bf16[6,16,2048]{2,1,0:T(8,128)(2,1)S(1)} %get-tuple-element.7), channel_id=1, source_target_pairs={{8,0},{16,8},{24,16},{9,1},{17,9},{25,17},{10,2},{18,10},{26,18},{... | collective-permute-start | bytes 1179656 | tf_op jit(solution)/shard_map/ppermute | solution.py:28
  161.0 17.9 %collective-permute-start.14 = (bf16[6,16,2048]{2,1,0:T(8,128)(2,1)S(1)}, bf16[6,16,2048]{2,1,0:T(8,128)(2,1)S(1)}, u32[]{:S(2)}, u32[]{:S(2)}) collective-permute-start(bf16[6,16,2048]{2,1,0:T(8,128)(2,1)S(1)} %get-tuple-element.8), channel_id=1, source_target_pairs={{0,8},{8,16},{16,24},{1,9},{9,17},{17,25},{2,10},{10,18},{18,26},{... | collective-permute-start | bytes 1179656 | tf_op jit(solution)/shard_map/ppermute | solution.py:28
  162.4 18.6 %collective-permute-start.25 = (f32[1,1,2048]{2,0,1:T(1,128)S(1)}, f32[1,1,2048]{2,0,1:T(1,128)S(1)}, u32[]{:S(2)}, u32[]{:S(2)}) collective-permute-start(f32[1,1,2048]{2,0,1:T(1,128)S(1)} %broadcast_select_fusion.1), channel_id=1, source_target_pairs={{0,1},{1,0},{2,3},{3,2},{4,5},{5,4},{6,7},{7,6},{8,9},{9,8},{10,11... | collective-permute-start | bytes 24584 | tf_op jit(solution)/shard_map/ppermute | solution.py:112
  181.2 2.7 %copy-start.7 = (bf16[1024,1024]{1,0:T(8,128)(2,1)S(1)}, bf16[1024,1024]{1,0:T(8,128)(2,1)}, u32[]{:S(2)}) copy-start(bf16[1024,1024]{1,0:T(8,128)(2,1)} %param.10) | copy-start | bytes 6291460

commit v3 on v2

--- a/solution.py
+++ b/solution.py
@@ -3,6 +3,7 @@
 import jax
 import jax.numpy as jnp
 from jax import lax
+from jax.experimental import pallas as pl
 from jax.sharding import PartitionSpec as P
 
 HEADS = 16
@@ -126,18 +127,82 @@
     return (key_cell >= window_start) & (key_cell <= window_start + KW - 1)
 
 
-def einsum_wide(form, left, right):
-    return jnp.einsum(form, left, right, preferred_element_type=jnp.float32)
-
-
-def to_heads(x):
-    count, width = x.shape
-    return x.reshape(count, HEADS, width // HEADS).transpose(1, 0, 2)
-
-
-def from_heads(x):
-    heads, count, size = x.shape
-    return x.transpose(1, 0, 2).reshape(count, heads * size)
+def attention_kernel(q_ref, k_ref, v_ref, g_ref, mask_ref, o_ref, dq_ref, dk_ref, dv_ref):
+    head_size = q_ref.shape[1] // 2
+    score_scale = 1.0 / math.sqrt(head_size)
+    q = q_ref[...]
+    k = k_ref[...]
+    v = v_ref[...]
+    g = g_ref[...]
+    keep = mask_ref[...] > 0
+    lane_head = lax.broadcasted_iota(jnp.int32, q.shape, 1) // head_size
+    lane_head_keys = lax.broadcasted_iota(jnp.int32, k.shape, 1) // head_size
+    rows = (((1,), (1,)), ((), ()))
+    cols = (((0,), (0,)), ((), ()))
+    out = jnp.zeros(q.shape, jnp.float32)
+    dq = jnp.zeros(q.shape, jnp.float32)
+    dk = jnp.zeros(k.shape, jnp.float32)
+    dv = jnp.zeros(k.shape, jnp.float32)
+    for head in range(2):
+        mine = lane_head == head
+        mine_keys = lane_head_keys == head
+        q_head = jnp.where(mine, q, jnp.zeros_like(q))
+        g_head = jnp.where(mine, g, jnp.zeros_like(g))
+        scores = lax.dot_general(q_head, k, rows, preferred_element_type=jnp.float32) * score_scale
+        scores = jnp.where(keep, scores, -1e30)
+        row_max = jnp.max(scores, axis=1, keepdims=True)
+        exps = jnp.exp(scores - row_max)
+        probs = exps / jnp.sum(exps, axis=1, keepdims=True)
+        rounded = probs.astype(jnp.bfloat16)
+        attended = jnp.dot(rounded, v, preferred_element_type=jnp.float32)
+        attended = attended.astype(jnp.bfloat16).astype(jnp.float32)
+        out = jnp.where(mine, attended, out)
+        delta = jnp.sum(
+            jnp.where(mine, g.astype(jnp.float32) * attended, 0.0), axis=1, keepdims=True
+        )
+        dots = lax.dot_general(g_head, v, rows, preferred_element_type=jnp.float32)
+        slopes = (probs * (dots - delta) * score_scale).astype(jnp.bfloat16)
+        dq = jnp.where(mine, jnp.dot(slopes, k, preferred_element_type=jnp.float32), dq)
+        dk = jnp.where(
+            mine_keys, lax.dot_general(slopes, q, cols, preferred_element_type=jnp.float32), dk
+        )
+        dv = jnp.where(
+            mine_keys, lax.dot_general(rounded, g, cols, preferred_element_type=jnp.float32), dv
+        )
+    o_ref[...] = out.astype(o_ref.dtype)
+    dq_ref[...] = dq.astype(dq_ref.dtype)
+    dk_ref[...] = dk
+    dv_ref[...] = dv
+
+
+def attention(queries, all_kv, grad_attended, keep):
+    tokens, model_width = queries.shape
+    key_count = all_kv.shape[0]
+    lanes = 2 * (model_width // HEADS)
+    steps = model_width // lanes
+    token_block = pl.BlockSpec((tokens, lanes), lambda i: (0, i))
+    key_block = pl.BlockSpec((key_count, lanes), lambda i: (0, i))
+    value_block = pl.BlockSpec((key_count, lanes), lambda i: (0, i + steps))
+    mask_block = pl.BlockSpec((tokens, key_count), lambda i: (0, 0))
+    flops = 2 * 2 * 6 * tokens * key_count * model_width
+    moved = 2 * (3 * tokens * model_width + 2 * key_count * model_width) + 4 * (
+        tokens * key_count + 2 * key_count * model_width
+    )
+    return pl.pallas_call(
+        attention_kernel,
+        grid=(steps,),
+        in_specs=[token_block, key_block, value_block, token_block, mask_block],
+        out_specs=[token_block, token_block, key_block, key_block],
+        out_shape=[
+            jax.ShapeDtypeStruct((tokens, model_width), jnp.bfloat16),
+            jax.ShapeDtypeStruct((tokens, model_width), jnp.bfloat16),
+            jax.ShapeDtypeStruct((key_count, model_width), jnp.float32),
+            jax.ShapeDtypeStruct((key_count, model_width), jnp.float32),
+        ],
+        cost_estimate=pl.CostEstimate(
+            flops=flops, transcendentals=HEADS * tokens * key_count, bytes_accessed=moved
+        ),
+    )(queries, all_kv, all_kv, grad_attended, keep)
 
 
 def shards(features, w_query, w_key, w_value, w_out, reg_pos, grad_out):
@@ -177,53 +242,42 @@
     framed = with_halo(key_value.reshape(tile_rows, tile_cols, 2 * model_width), RAD).reshape(
         frame_rows * frame_cols, 2 * model_width
     )
-    all_kv = jnp.concatenate([framed, global_kv], axis=0)
-    key_count = all_kv.shape[0]
+    frame_cells = frame_rows * frame_cols
+    used = frame_cells + global_kv.shape[0]
+    key_count = -(-used // 128) * 128
+    all_kv = jnp.concatenate(
+        [framed, global_kv, jnp.zeros((key_count - used, 2 * model_width), framed.dtype)], axis=0
+    )
 
     row_valid = axis_valid(first_row, tile_rows, tile_rows * row_count)
     col_valid = axis_valid(first_col, tile_cols, band_cols)
     window_mask = (row_valid[:, None, :, None] & col_valid[None, :, None, :]).reshape(
-        tokens, frame_rows * frame_cols
-    )
-    full_mask = jnp.concatenate(
-        [window_mask, jnp.ones((tokens, key_count - frame_rows * frame_cols), jnp.bool_)], axis=1
-    )
-
-    query_heads = to_heads(queries)
-    key_heads = to_heads(all_kv[:, :model_width])
-    value_heads = to_heads(all_kv[:, model_width:])
-
-    scores = einsum_wide("hqd,hkd->hqk", query_heads, key_heads) * score_scale
-    scores = jnp.where(full_mask[None], scores, -1e30)
-    row_max = jnp.max(scores, axis=-1, keepdims=True)
-    exps = jnp.exp(scores - row_max)
-    denominator = jnp.sum(exps, axis=-1, keepdims=True)
-    probs = exps / denominator
-    rounded = probs.astype(jnp.bfloat16)
-    attended_heads = einsum_wide("hqk,hkd->hqd", rounded, value_heads).astype(jnp.bfloat16)
-    attended = from_heads(attended_heads)
-
+        tokens, frame_cells
+    )
+    keep = jnp.concatenate(
+        [
+            window_mask.astype(jnp.float32),
+            jnp.ones((tokens, used - frame_cells), jnp.float32),
+            jnp.zeros((tokens, key_count - used), jnp.float32),
+        ],
+        axis=1,
+    )
+
+    grad_attended = jnp.dot(
+        grad_out.reshape(-1, model_width), w_out.T, preferred_element_type=jnp.float32
+    ).astype(jnp.bfloat16)
+    attended, query_grads, key_grads, value_grads = attention(
+        queries, all_kv, grad_attended, keep
+    )
     layer_out = (
         jnp.dot(attended, w_out, preferred_element_type=jnp.float32)
         .astype(jnp.bfloat16)
         .reshape(features.shape)
     )
-    grad_attended = jnp.dot(
-        grad_out.reshape(-1, model_width), w_out.T, preferred_element_type=jnp.float32
-    ).astype(jnp.bfloat16)
-    grad_heads = to_heads(grad_attended)
-
-    delta = einsum_wide("hqd,hqd->hq", grad_heads, attended_heads)[..., None]
-    dots = einsum_wide("hqd,hkd->hqk", grad_heads, value_heads)
-    slopes = (probs * (dots - delta) * score_scale).astype(jnp.bfloat16)
-    query_grads = from_heads(
-        einsum_wide("hqk,hkd->hqd", slopes, key_heads).astype(jnp.bfloat16)
-    )
-    key_grads = from_heads(einsum_wide("hqk,hqd->hkd", slopes, query_heads))
-    value_grads = from_heads(einsum_wide("hqk,hqd->hkd", rounded, grad_heads))
-    kv_grads_all = jnp.concatenate([key_grads, value_grads], axis=1)
-
-    global_grads = kv_grads_all[frame_rows * frame_cols :]
+
+    global_grads = jnp.concatenate(
+        [key_grads[frame_cells:used], value_grads[frame_cells:used]], axis=1
+    )
     if power_of_two(row_count) and power_of_two(col_count):
         own_grads = tree_reduce_scatter(global_grads, ("rows", "cols"))
     else:
@@ -231,11 +285,13 @@
             global_grads, ("rows", "cols"), scatter_dimension=0, tiled=True
         )
 
-    frame_grads = kv_grads_all[: frame_rows * frame_cols].reshape(
-        frame_rows, frame_cols, 2 * model_width
-    )
-    middle = fold_halo(frame_grads, RAD)
-    middle = middle.reshape(tokens, 2 * model_width)
+    middle = jnp.concatenate(
+        [
+            fold_halo(key_grads[:frame_cells].reshape(frame_rows, frame_cols, model_width), RAD),
+            fold_halo(value_grads[:frame_cells].reshape(frame_rows, frame_cols, model_width), RAD),
+        ],
+        axis=2,
+    ).reshape(tokens, 2 * model_width)
     own_row = lax.dynamic_slice_in_dim(middle, own_local, 1, 0) + own_grads
     kv_grads = lax.dynamic_update_slice_in_dim(middle, own_row, own_local, 0).astype(jnp.bfloat16)
 

time: 187 us -> 189 us (1.011)
  the two profiles are of different devices: /device:TPU:15 before, /device:TPU:29 now
where the time goes in v3:
time: 189 us; the launch traced here: 187 us
  starting transfers between devices  90 us (48%)
  local copies, waits for them, and re-layouts  25.9 us (14%)
  other arithmetic  19.2 us (10%)
  waiting for transfers between devices  17.6 us (9%)
  Pallas kernels  16.6 us (9%)
  matrix products  14 us (7%)
  between operations  4.02 us (2%)
    ppermute x24, starting transfers between devices, shifted(): return lax.ppermute(x, tuple(axes), pairs)  77.8 us
    pallas_call x1, Pallas kernels, attention(): pl.pallas_call(attention_kernel, grid=(steps,), in_specs=[token_block, ke...  16.6 us
    ppermute x5, starting transfers between devices, tree_reduce_scatter(): x = keep + lax.ppermute(send, axis, [(i, i ^ step) for i in range(size)])  9.5 us
    ppermute x5, waiting for transfers between devices, tree_gather(): other = lax.ppermute(x, axis, [(i, i ^ step) for i in range(size)])  7.76 us
    ppermute x24, waiting for transfers between devices, shifted(): return lax.ppermute(x, tuple(axes), pairs)  7.3 us
    reshape x1, local copies, waits for them, and re-layouts, shards(): with_halo(key_value.reshape(tile_rows, tile_cols, 2 * model_width), RAD)  4.04 us
    another operation x2, other arithmetic  3.9 us
  transfers between devices with their start and end apart: 34, of which 11 were waited for; matrix products, arithmetic and copies ran while one was open for 11% of the time, Pallas kernels for 0%

profile of v3, /device:TPU:29, one launch (start us, length us, event | category | flops | bytes accessed | tf_op | source)
XLA Modules:
  0.0 187.2 jit_solution(3929016452171894281)
XLA Ops:
  0.7 1.4 dynamic_slice.10
  4.7 2.3 %convolution_convert_fusion.2 = bf16[128,1024]{1,0:T(8,128)(2,1)S(1)} fusion(bf16[128,1024]{1,0:T(8,128)(2,1)} %bitcast.39, bf16[1024,1024]{1,0:T(8,128)(2,1)} %param.10), kind=kOutput, calls=%fused_computation.7 | convolution fusion | flops 268566528 | bytes 2621440 | tf_op jit(solution)/shard_map/dot_general | solution.py:228
  9.2 3.1 %collective-permute-start.6 = (bf16[6,16,2048]{2,1,0:T(8,128)(2,1)}, bf16[6,16,2048]{2,1,0:T(8,128)(2,1)}, u32[]{:S(2)}, u32[]{:S(2)}) collective-permute-start(bf16[6,16,2048]{2,1,0:T(8,128)(2,1)} %bitcast.3), channel_id=1, source_target_pairs={{8,0},{16,8},{24,16},{9,1},{17,9},{25,17},{10,2},{18,10},{26,18},{... | collective-permute-start | bytes 1179656 | tf_op jit(solution)/shard_map/ppermute | solution.py:29
  12.3 1.8 fusion.32
  15.4 3.6 %collective-permute-start.7 = (bf16[6,6,2048]{2,1,0:T(8,128)(2,1)}, bf16[6,6,2048]{2,1,0:T(8,128)(2,1)}, u32[]{:S(2)}, u32[]{:S(2)}) collective-permute-start(bf16[6,6,2048]{2,1,0:T(8,128)(2,1)} %get-tuple-element.33), channel_id=1, source_target_pairs={{9,0},{10,1},{11,2},{12,3},{13,4},{14,5},{15,6},{17,8},{18,9},{19,... | collective-permute-start | bytes 442376 | tf_op jit(solution)/shard_map/ppermute | solution.py:29
  19.0 3.5 %collective-permute-start.1 = (bf16[6,16,2048]{2,1,0:T(8,128)(2,1)}, bf16[6,16,2048]{2,1,0:T(8,128)(2,1)}, u32[]{:S(2)}, u32[]{:S(2)}) collective-permute-start(bf16[6,16,2048]{2,1,0:T(8,128)(2,1)} %bitcast.1), channel_id=1, source_target_pairs={{0,8},{8,16},{16,24},{1,9},{9,17},{17,25},{2,10},{10,18},{18,26},{... | collective-permute-start | bytes 1179656 | tf_op jit(solution)/shard_map/ppermute | solution.py:29
  23.1 1.9 fusion.31
  25.0 2.7 %convolution_convert_fusion.4.q_ref = bf16[128,1024]{1,0:T(8,128)(2,1)} fusion(bf16[128,1024]{1,0:T(8,128)(2,1)S(1)} %bitcast.41, bf16[1024,1024]{1,0:T(8,128)(2,1)} %param.8), kind=kOutput, calls=%fused_computation.9 | convolution fusion | flops 268566528 | bytes 2621440 | tf_op jit(solution)/shard_map/dot_general | solution.py:224
  27.8 1.5 convolution_convert_fusion.1.g_ref
  30.5 2.0 %collective-permute-done.9 = bf16[2,2048]{1,0:T(2,128)(2,1)S(1)} collective-permute-done((bf16[2,2048]{1,0:T(2,128)(2,1)S(1)}, bf16[2,2048]{1,0:T(2,128)(2,1)S(1)}, u32[]{:S(2)}, u32[]{:S(2)}) %collective-permute-start.9) | collective-permute-done | bytes 8224 | tf_op jit(solution)/shard_map/ppermute | solution.py:95
  33.4 3.1 %collective-permute-done.10 = bf16[4,2048]{1,0:T(4,128)(2,1)S(1)} collective-permute-done((bf16[4,2048]{1,0:T(4,128)(2,1)S(1)}, bf16[4,2048]{1,0:T(4,128)(2,1)S(1)}, u32[]{:S(2)}, u32[]{:S(2)}) %collective-permute-start.10) | collective-permute-done | bytes 16416 | tf_op jit(solution)/shard_map/ppermute | solution.py:95
  36.7 2.7 %collective-permute-done.11 = bf16[8,2048]{1,0:T(8,128)(2,1)S(1)} collective-permute-done((bf16[8,2048]{1,0:T(8,128)(2,1)S(1)}, bf16[8,2048]{1,0:T(8,128)(2,1)S(1)}, u32[]{:S(2)}, u32[]{:S(2)}) %collective-permute-start.11) | collective-permute-done | bytes 32800 | tf_op jit(solution)/shard_map/ppermute | solution.py:95
  39.4 1.4 and_convert_fusion
  41.0 1.8 reshape.247
  45.0 6.6 %collective-permute-start.2 = (bf16[6,6,2048]{2,1,0:T(8,128)(2,1)}, bf16[6,6,2048]{2,1,0:T(8,128)(2,1)S(1)}, u32[]{:S(2)}, u32[]{:S(2)}) collective-permute-start(bf16[6,6,2048]{2,1,0:T(8,128)(2,1)} %get-tuple-element.31), channel_id=1, source_target_pairs={{1,8},{2,9},{3,10},{4,11},{5,12},{6,13},{7,14},{9,16},{10,17},{11,... | collective-permute-start | bytes 442376 | tf_op jit(solution)/shard_map/ppermute | solution.py:29
  51.6 1.3 collective-permute-start.3
  53.6 5.5 %collective-permute-start.4 = (bf16[8,6,2048]{2,1,0:T(8,128)(2,1)S(1)}, bf16[8,6,2048]{2,1,0:T(8,128)(2,1)S(1)}, u32[]{:S(2)}, u32[]{:S(2)}) collective-permute-start(bf16[8,6,2048]{2,1,0:T(8,128)(2,1)S(1)} %get-tuple-element.29), channel_id=1, source_target_pairs={{1,0},{2,1},{3,2},{4,3},{5,4},{6,5},{7,6},{9,8},{10,9},{11,10},{12... | collective-permute-start | bytes 589832 | tf_op jit(solution)/shard_map/ppermute | solution.py:29
  60.2 3.5 %maximum_maximum_fusion = bf16[20,28,2048]{2,1,0:T(8,128)(2,1)} fusion(bf16[6,6,2048]{2,1,0:T(8,128)(2,1)} %collective-permute-done.7, bf16[6,16,2048]{2,1,0:T(8,128)(2,1)} %collective-permute-done.6, bf16[6,6,2048]{2,1,0:T(8,128)(2,1)} %collective-permute-done.5, bf16[8,6,2048]{2,1,0:T(8,128)(2,1)S(1)} %collective-permute-done.4, ...), kind=kLoop, calls=%fused_computation | loop fusion | flops 20643840 | bytes 4587520 | tf_op jit(solution)/shard_map/concatenate | solution.py:60
  63.7 4.0 %reshape.239 = bf16[560,2048]{1,0:T(8,128)(2,1)} reshape(bf16[20,28,2048]{2,1,0:T(8,128)(2,1)} %maximum_maximum_fusion) | data formatting | bytes 4587520 | tf_op jit(solution)/shard_map/reshape | solution.py:242
  67.7 3.6 %maximum_maximum_fusion.1.k_ref.v_ref = bf16[640,2048]{1,0:T(8,128)(2,1)} fusion(bf16[32,2048]{1,0:T(8,128)(2,1)S(1)} %maximum_select_fusion, bf16[560,2048]{1,0:T(8,128)(2,1)} %reshape.239, bf16[640]{0:T(1024)(128)(2,1)S(1)} %pad.145.clone), kind=kLoop, calls=%fused_computation.1 | loop fusion | flops 7864320 | bytes 5047552 | tf_op jit(solution)/shard_map/concatenate | solution.py:248
  71.3 16.6 %shard_map.86 = (bf16[128,1024]{1,0:T(8,128)(2,1)}, bf16[128,1024]{1,0:T(8,128)(2,1)}, f32[640,1024]{1,0:T(8,128)}, f32[640,1024]{1,0:T(8,128)}) custom-call(bf16[128,1024]{1,0:T(8,128)(2,1)} %convolution_convert_fusion.4.q_ref, bf16[640,2048]{1,0:T(8,128)(2,1)} %maximum_maximum_fusion.1.k_ref.v_ref, bf16[640,2048]{1,0:T(8,128)(2,1)} %maximum_maximum_fusion.1.k_ref.v_ref, ...), custom_call_target="tpu_custom_call" | custom-call | flops 2013265920 | bytes 8978432 | tf_op jit(solution)/shard_map/pallas_call | solution.py:191
  89.0 3.4 %slice.162 = f32[560,1024]{1,0:T(8,128)} slice(f32[640,1024]{1,0:T(8,128)} %get-tuple-element.8), slice={[0:560], [0:1024]} | slice | bytes 4587520 | tf_op jit(solution)/shard_map/slice | solution.py:290
  93.1 1.5 slice.172
  94.6 2.9 %reshape.242 = f32[20,28,1024]{2,1,0:T(8,128)} reshape(f32[560,1024]{1,0:T(8,128)} %slice.162) | data formatting | bytes 4587520 | tf_op jit(solution)/shard_map/reshape | solution.py:290
  97.5 1.9 %convert.53 = bf16[20,28,1024]{2,1,0:T(8,128)(2,1)S(1)} convert(f32[20,28,1024]{2,1,0:T(8,128)} %reshape.242) | non-fusion elementwise | flops 573440 | bytes 3440640 | tf_op jit(solution)/shard_map/convert.48
  101.1 2.9 %reshape.243 = f32[20,28,1024]{2,1,0:T(8,128)} reshape(f32[560,1024]{1,0:T(8,128)} %slice.172) | data formatting | bytes 4587520 | tf_op jit(solution)/shard_map/reshape | solution.py:291
  104.0 2.0 %convert.54 = bf16[20,28,1024]{2,1,0:T(8,128)(2,1)S(1)} convert(f32[20,28,1024]{2,1,0:T(8,128)} %reshape.243) | non-fusion elementwise | flops 573440 | bytes 3440640 | tf_op jit(solution)/shard_map/convert.40
  107.4 1.4 collective-permute-start.29
  108.8 1.6 fusion.33
  112.6 8.6 %collective-permute-start.15 = (bf16[8,6,1024]{2,1,0:T(8,128)(2,1)S(1)}, bf16[8,6,1024]{2,1,0:T(8,128)(2,1)S(1)}, u32[]{:S(2)}, u32[]{:S(2)}) collective-permute-start(bf16[8,6,1024]{2,1,0:T(8,128)(2,1)S(1)} %get-tuple-element.12), channel_id=1, source_target_pairs={{1,0},{2,1},{3,2},{4,3},{5,4},{6,5},{7,6},{9,8},{10,9},{11,10},{12... | collective-permute-start | bytes 294920 | tf_op jit(solution)/shard_map/ppermute | solution.py:29
  121.2 1.3 collective-permute-start.16
  122.5 3.9 %collective-permute-start.17 = (bf16[6,6,1024]{2,1,0:T(8,128)(2,1)S(1)}, bf16[6,6,1024]{2,1,0:T(8,128)(2,1)S(1)}, u32[]{:S(2)}, u32[]{:S(2)}) collective-permute-start(bf16[6,6,1024]{2,1,0:T(8,128)(2,1)S(1)} %copy-done.15), channel_id=1, source_target_pairs={{9,0},{10,1},{11,2},{12,3},{13,4},{14,5},{15,6},{17,8},{18,9},{19,... | collective-permute-start | bytes 221192 | tf_op jit(solution)/shard_map/ppermute | solution.py:29
  127.8 4.3 %collective-permute-start.19 = (bf16[6,6,1024]{2,1,0:T(8,128)(2,1)S(1)}, bf16[6,6,1024]{2,1,0:T(8,128)(2,1)S(1)}, u32[]{:S(2)}, u32[]{:S(2)}) collective-permute-start(bf16[6,6,1024]{2,1,0:T(8,128)(2,1)S(1)} %copy-done.13), channel_id=1, source_target_pairs={{1,8},{2,9},{3,10},{4,11},{5,12},{6,13},{7,14},{9,16},{10,17},{11,... | collective-permute-start | bytes 221192 | tf_op jit(solution)/shard_map/ppermute | solution.py:29
  133.5 3.9 %collective-permute-start.13 = (bf16[6,16,1024]{2,1,0:T(8,128)(2,1)S(1)}, bf16[6,16,1024]{2,1,0:T(8,128)(2,1)S(1)}, u32[]{:S(2)}, u32[]{:S(2)}) collective-permute-start(bf16[6,16,1024]{2,1,0:T(8,128)(2,1)S(1)} %copy-done.11), channel_id=1, source_target_pairs={{8,0},{16,8},{24,16},{9,1},{17,9},{25,17},{10,2},{18,10},{26,18},{... | collective-permute-start | bytes 589832 | tf_op jit(solution)/shard_map/ppermute | solution.py:29
  137.4 1.9 %collective-permute-start.14 = (bf16[6,16,1024]{2,1,0:T(8,128)(2,1)S(1)}, bf16[6,16,1024]{2,1,0:T(8,128)(2,1)S(1)}, u32[]{:S(2)}, u32[]{:S(2)}) collective-permute-start(bf16[6,16,1024]{2,1,0:T(8,128)(2,1)S(1)} %copy-done.10), channel_id=1, source_target_pairs={{0,8},{8,16},{16,24},{1,9},{9,17},{17,25},{2,10},{10,18},{18,26},{... | collective-permute-start | bytes 589832 | tf_op jit(solution)/shard_map/ppermute | solution.py:29
  140.1 4.3 %collective-permute-start.23 = (bf16[8,6,1024]{2,1,0:T(8,128)(2,1)S(1)}, bf16[8,6,1024]{2,1,0:T(8,128)(2,1)S(1)}, u32[]{:S(2)}, u32[]{:S(2)}) collective-permute-start(bf16[8,6,1024]{2,1,0:T(8,128)(2,1)S(1)} %get-tuple-element.20), channel_id=1, source_target_pairs={{1,0},{2,1},{3,2},{4,3},{5,4},{6,5},{7,6},{9,8},{10,9},{11,10},{12... | collective-permute-start | bytes 294920 | tf_op jit(solution)/shard_map/ppermute | solution.py:29
  145.8 6.4 %collective-permute-start.25 = (bf16[6,6,1024]{2,1,0:T(8,128)(2,1)S(1)}, bf16[6,6,1024]{2,1,0:T(8,128)(2,1)S(1)}, u32[]{:S(2)}, u32[]{:S(2)}) collective-permute-start(bf16[6,6,1024]{2,1,0:T(8,128)(2,1)S(1)} %get-tuple-element.22), channel_id=1, source_target_pairs={{9,0},{10,1},{11,2},{12,3},{13,4},{14,5},{15,6},{17,8},{18,9},{19,... | collective-permute-start | bytes 221192 | tf_op jit(solution)/shard_map/ppermute | solution.py:29
  153.6 2.9 %collective-permute-start.31 = (f32[4,1,2048]{2,0,1:T(4,128)S(1)}, f32[4,1,2048]{2,0,1:T(4,128)S(1)}, u32[]{:S(2)}, u32[]{:S(2)}) collective-permute-start(f32[4,1,2048]{2,0,1:T(4,128)S(1)} %select_bitcast_fusion.1), channel_id=1, source_target_pairs={{0,4},{1,5},{2,6},{3,7},{4,0},{5,1},{6,2},{7,3},{8,12},{9,13},{10,... | collective-permute-start | bytes 98312 | tf_op jit(solution)/shard_map/ppermute | solution.py:113
  156.4 1.4 fusion.14
  158.8 3.1 %collective-permute-start.27 = (bf16[6,6,1024]{2,1,0:T(8,128)(2,1)S(1)}, bf16[6,6,1024]{2,1,0:T(8,128)(2,1)S(1)}, u32[]{:S(2)}, u32[]{:S(2)}) collective-permute-start(bf16[6,6,1024]{2,1,0:T(8,128)(2,1)S(1)} %get-tuple-element.24), channel_id=1, source_target_pairs={{1,8},{2,9},{3,10},{4,11},{5,12},{6,13},{7,14},{9,16},{10,17},{11,... | collective-permute-start | bytes 221192 | tf_op jit(solution)/shard_map/ppermute | solution.py:29
  161.9 1.3 collective-permute-start.26
  163.2 5.4 %collective-permute-start.21 = (bf16[6,16,1024]{2,1,0:T(8,128)(2,1)S(1)}, bf16[6,16,1024]{2,1,0:T(8,128)(2,1)S(1)}, u32[]{:S(2)}, u32[]{:S(2)}) collective-permute-start(bf16[6,16,1024]{2,1,0:T(8,128)(2,1)S(1)} %get-tuple-element.18), channel_id=1, source_target_pairs={{8,0},{16,8},{24,16},{9,1},{17,9},{25,17},{10,2},{18,10},{26,18},{... | collective-permute-start | bytes 589832 | tf_op jit(solution)/shard_map/ppermute | solution.py:29
  168.6 1.9 %collective-permute-start.22 = (bf16[6,16,1024]{2,1,0:T(8,128)(2,1)S(1)}, bf16[6,16,1024]{2,1,0:T(8,128)(2,1)S(1)}, u32[]{:S(2)}, u32[]{:S(2)}) collective-permute-start(bf16[6,16,1024]{2,1,0:T(8,128)(2,1)S(1)} %get-tuple-element.19), channel_id=1, source_target_pairs={{0,8},{8,16},{16,24},{1,9},{9,17},{17,25},{2,10},{10,18},{18,26},{... | collective-permute-start | bytes 589832 | tf_op jit(solution)/shard_map/ppermute | solution.py:29
  170.6 3.1 %collective-permute-start.32 = (f32[2,1,2048]{2,0,1:T(2,128)S(1)}, f32[2,1,2048]{2,0,1:T(2,128)S(1)}, u32[]{:S(2)}, u32[]{:S(2)}) collective-permute-start(f32[2,1,2048]{2,0,1:T(2,128)S(1)} %broadcast_select_fusion), channel_id=1, source_target_pairs={{0,2},{1,3},{2,0},{3,1},{4,6},{5,7},{6,4},{7,5},{8,10},{9,11},{10,... | collective-permute-start | bytes 49160 | tf_op jit(solution)/shard_map/ppermute | solution.py:113
  173.9 5.6 %collective-permute-done.22 = bf16[6,16,1024]{2,1,0:T(8,128)(2,1)S(1)} collective-permute-done((bf16[6,16,1024]{2,1,0:T(8,128)(2,1)S(1)}, bf16[6,16,1024]{2,1,0:T(8,128)(2,1)S(1)}, u32[]{:S(2)}, u32[]{:S(2)}) %collective-permute-start.22) | collective-permute-done | bytes 196640 | tf_op jit(solution)/shard_map/ppermute | solution.py:29
  179.4 1.4 fusion.7
  183.1 2.6 %convolution_add_fusion.1 = f32[128,1024]{1,0:T(8,128)S(1)} fusion(f32[128,1024]{1,0:T(8,128)} %fusion.33, bf16[1024,1024]{1,0:T(8,128)(2,1)} %param.9, bf16[128,2048]{1,0:T(8,128)(2,1)S(1)} %convert_element_type.50), kind=kOutput, calls=%fused_computation.4 | convolution fusion | flops 268566528 | bytes 3407872 | tf_op jit(solution)/shard_map/dot_general | solution.py:300
  185.7 1.5 fusion
  (124 shorter events, 26.7 us)
Async XLA Ops:
  0.6 27.2 %copy-start = (bf16[1024,1024]{1,0:T(8,128)(2,1)S(1)}, bf16[1024,1024]{1,0:T(8,128)(2,1)}, u32[]{:S(2)}) copy-start(bf16[1024,1024]{1,0:T(8,128)(2,1)} %param.11) | copy-start | bytes 6291460
  0.6 6.3 %copy-start.4 = (bf16[8,16,1024]{2,1,0:T(8,128)(2,1)S(1)}, bf16[8,16,1024]{2,1,0:T(8,128)(2,1)}, u32[]{:S(2)}) copy-start(bf16[8,16,1024]{2,1,0:T(8,128)(2,1)} %param.7) | copy-start | bytes 786436
  7.5 22.0 %collective-permute-start.8 = (bf16[1,2048]{1,0:T(2,128)(2,1)S(1)}, bf16[1,2048]{1,0:T(2,128)(2,1)S(1)}, u32[]{:S(2)}, u32[]{:S(2)}) collective-permute-start(bf16[1,2048]{1,0:T(2,128)(2,1)S(1)} %fusion.20), channel_id=1, source_target_pairs={{0,1},{1,0},{2,3},{3,2},{4,5},{5,4},{6,7},{7,6},{8,9},{9,8},{10,11... | collective-permute-start | bytes 12296 | tf_op jit(solution)/shard_map/ppermute | solution.py:95
  9.2 50.9 %collective-permute-start.6 = (bf16[6,16,2048]{2,1,0:T(8,128)(2,1)}, bf16[6,16,2048]{2,1,0:T(8,128)(2,1)}, u32[]{:S(2)}, u32[]{:S(2)}) collective-permute-start(bf16[6,16,2048]{2,1,0:T(8,128)(2,1)} %bitcast.3), channel_id=1, source_target_pairs={{8,0},{16,8},{24,16},{9,1},{17,9},{25,17},{10,2},{18,10},{26,18},{... | collective-permute-start | bytes 1179656 | tf_op jit(solution)/shard_map/ppermute | solution.py:29
  14.1 30.8 %collective-permute-start.5 = (bf16[6,6,2048]{2,1,0:T(8,128)(2,1)}, bf16[6,6,2048]{2,1,0:T(8,128)(2,1)}, u32[]{:S(2)}, u32[]{:S(2)}) collective-permute-start(bf16[6,6,2048]{2,1,0:T(8,128)(2,1)} %get-tuple-element.32), channel_id=1, source_target_pairs={{8,1},{9,2},{10,3},{11,4},{12,5},{13,6},{14,7},{16,9},{17,10},{18,... | collective-permute-start | bytes 442376 | tf_op jit(solution)/shard_map/ppermute | solution.py:29
  15.4 36.2 %collective-permute-start.7 = (bf16[6,6,2048]{2,1,0:T(8,128)(2,1)}, bf16[6,6,2048]{2,1,0:T(8,128)(2,1)}, u32[]{:S(2)}, u32[]{:S(2)}) collective-permute-start(bf16[6,6,2048]{2,1,0:T(8,128)(2,1)} %get-tuple-element.33), channel_id=1, source_target_pairs={{9,0},{10,1},{11,2},{12,3},{13,4},{14,5},{15,6},{17,8},{18,9},{19,... | collective-permute-start | bytes 442376 | tf_op jit(solution)/shard_map/ppermute | solution.py:29
  19.0 41.1 %collective-permute-start.1 = (bf16[6,16,2048]{2,1,0:T(8,128)(2,1)}, bf16[6,16,2048]{2,1,0:T(8,128)(2,1)}, u32[]{:S(2)}, u32[]{:S(2)}) collective-permute-start(bf16[6,16,2048]{2,1,0:T(8,128)(2,1)} %bitcast.1), channel_id=1, source_target_pairs={{0,8},{8,16},{16,24},{1,9},{9,17},{17,25},{2,10},{10,18},{18,26},{... | collective-permute-start | bytes 1179656 | tf_op jit(solution)/shard_map/ppermute | solution.py:29
  23.1 4.7 %copy-start.7 = (bf16[8,16,1024]{2,1,0:T(8,128)(2,1)S(1)}, bf16[8,16,1024]{2,1,0:T(8,128)(2,1)}, u32[]{:S(2)}) copy-start(bf16[8,16,1024]{2,1,0:T(8,128)(2,1)} %param.13) | copy-start | bytes 786436
  25.0 4.4 %copy-start.16 = (s32[16]{0:T(128)S(1)}, s32[16]{0:T(128)}, u32[]{:S(2)}) copy-start(s32[16]{0:T(128)} %get-tuple-element.34) | copy-start | bytes 196
  25.0 4.4 %copy-start.17 = (s32[16]{0:T(128)S(1)}, s32[16]{0:T(128)}, u32[]{:S(2)}) copy-start(s32[16]{0:T(128)} %get-tuple-element.35) | copy-start | bytes 196
  29.5 3.0 %collective-permute-start.9 = (bf16[2,2048]{1,0:T(2,128)(2,1)S(1)}, bf16[2,2048]{1,0:T(2,128)(2,1)S(1)}, u32[]{:S(2)}, u32[]{:S(2)}) collective-permute-start(bf16[2,2048]{1,0:T(2,128)(2,1)S(1)} %broadcast_select_fusion.3), channel_id=1, source_target_pairs={{0,2},{1,3},{2,0},{3,1},{4,6},{5,7},{6,4},{7,5},{8,10},{9,11},{10,... | collective-permute-start | bytes 24584 | tf_op jit(solution)/shard_map/ppermute | solution.py:95
  32.5 4.0 %collective-permute-start.10 = (bf16[4,2048]{1,0:T(4,128)(2,1)S(1)}, bf16[4,2048]{1,0:T(4,128)(2,1)S(1)}, u32[]{:S(2)}, u32[]{:S(2)}) collective-permute-start(bf16[4,2048]{1,0:T(4,128)(2,1)S(1)} %maximum_select_fusion.3), channel_id=1, source_target_pairs={{0,4},{1,5},{2,6},{3,7},{4,0},{5,1},{6,2},{7,3},{8,12},{9,13},{10,... | collective-permute-start | bytes 49160 | tf_op jit(solution)/shard_map/ppermute | solution.py:95
  36.5 2.8 %collective-permute-start.11 = (bf16[8,2048]{1,0:T(8,128)(2,1)S(1)}, bf16[8,2048]{1,0:T(8,128)(2,1)S(1)}, u32[]{:S(2)}, u32[]{:S(2)}) collective-permute-start(bf16[8,2048]{1,0:T(8,128)(2,1)S(1)} %maximum_select_fusion.2), channel_id=1, source_target_pairs={{0,8},{8,0},{16,24},{24,16},{1,9},{9,1},{17,25},{25,17},{2,10},{10... | collective-permute-start | bytes 98312 | tf_op jit(solution)/shard_map/ppermute | solution.py:95
  39.4 3.5 %collective-permute-start.12 = (bf16[16,2048]{1,0:T(8,128)(2,1)S(1)}, bf16[16,2048]{1,0:T(8,128)(2,1)}, u32[]{:S(2)}, u32[]{:S(2)}) collective-permute-start(bf16[16,2048]{1,0:T(8,128)(2,1)S(1)} %maximum_select_fusion.1), channel_id=1, source_target_pairs={{0,16},{8,24},{16,0},{24,8},{1,17},{9,25},{17,1},{25,9},{2,18},{10... | collective-permute-start | bytes 196616 | tf_op jit(solution)/shard_map/ppermute | solution.py:95
  42.9 10.7 %collective-permute-start = (bf16[6,6,2048]{2,1,0:T(8,128)(2,1)}, bf16[6,6,2048]{2,1,0:T(8,128)(2,1)S(1)}, u32[]{:S(2)}, u32[]{:S(2)}) collective-permute-start(bf16[6,6,2048]{2,1,0:T(8,128)(2,1)} %get-tuple-element.30), channel_id=1, source_target_pairs={{0,9},{1,10},{2,11},{3,12},{4,13},{5,14},{6,15},{8,17},{9,18},{10,... | collective-permute-start | bytes 442376 | tf_op jit(solution)/shard_map/ppermute | solution.py:29
  45.0 15.0 %collective-permute-start.2 = (bf16[6,6,2048]{2,1,0:T(8,128)(2,1)}, bf16[6,6,2048]{2,1,0:T(8,128)(2,1)S(1)}, u32[]{:S(2)}, u32[]{:S(2)}) collective-permute-start(bf16[6,6,2048]{2,1,0:T(8,128)(2,1)} %get-tuple-element.31), channel_id=1, source_target_pairs={{1,8},{2,9},{3,10},{4,11},{5,12},{6,13},{7,14},{9,16},{10,17},{11,... | collective-permute-start | bytes 442376 | tf_op jit(solution)/shard_map/ppermute | solution.py:29
  51.6 8.4 %collective-permute-start.3 = (bf16[8,6,2048]{2,1,0:T(8,128)(2,1)S(1)}, bf16[8,6,2048]{2,1,0:T(8,128)(2,1)S(1)}, u32[]{:S(2)}, u32[]{:S(2)}) collective-permute-start(bf16[8,6,2048]{2,1,0:T(8,128)(2,1)S(1)} %get-tuple-element.28), channel_id=1, source_target_pairs={{0,1},{1,2},{2,3},{3,4},{4,5},{5,6},{6,7},{8,9},{9,10},{10,11},{11... | collective-permute-start | bytes 589832 | tf_op jit(solution)/shard_map/ppermute | solution.py:29
  53.6 6.6 %collective-permute-start.4 = (bf16[8,6,2048]{2,1,0:T(8,128)(2,1)S(1)}, bf16[8,6,2048]{2,1,0:T(8,128)(2,1)S(1)}, u32[]{:S(2)}, u32[]{:S(2)}) collective-permute-start(bf16[8,6,2048]{2,1,0:T(8,128)(2,1)S(1)} %get-tuple-element.29), channel_id=1, source_target_pairs={{1,0},{2,1},{3,2},{4,3},{5,4},{6,5},{7,6},{9,8},{10,9},{11,10},{12... | collective-permute-start | bytes 589832 | tf_op jit(solution)/shard_map/ppermute | solution.py:29
  87.9 4.4 %copy-start.5 = (f32[640,1024]{1,0:T(8,128)S(1)}, f32[640,1024]{1,0:T(8,128)}, u32[]{:S(2)}) copy-start(f32[640,1024]{1,0:T(8,128)} %get-tuple-element.9) | copy-start | bytes 7864324
  106.0 2.8 %copy-start.2 = (bf16[1024,1024]{1,0:T(8,128)(2,1)S(1)}, bf16[1024,1024]{1,0:T(8,128)(2,1)}, u32[]{:S(2)}) copy-start(bf16[1024,1024]{1,0:T(8,128)(2,1)} %param.8) | copy-start | bytes 6291460
  106.0 2.8 %copy-start.9 = (bf16[128,1024]{1,0:T(8,128)(2,1)S(1)}, bf16[128,1024]{1,0:T(8,128)(2,1)}, u32[]{:S(2)}) copy-start(bf16[128,1024]{1,0:T(8,128)(2,1)} %get-tuple-element.7) | copy-start | bytes 786436
  107.4 15.1 %copy-start.15 = (bf16[6,6,1024]{2,1,0:T(8,128)(2,1)S(1)}, bf16[6,6,1024]{2,1,0:T(8,128)(2,1)}, u32[]{:S(2)}) copy-start(bf16[6,6,1024]{2,1,0:T(8,128)(2,1)} %get-tuple-element.14) | copy-start | bytes 221188
  107.4 19.1 %copy-start.14 = (bf16[6,6,1024]{2,1,0:T(8,128)(2,1)S(1)}, bf16[6,6,1024]{2,1,0:T(8,128)(2,1)}, u32[]{:S(2)}) copy-start(bf16[6,6,1024]{2,1,0:T(8,128)(2,1)} %get-tuple-element.15) | copy-start | bytes 221188
  107.4 20.4 %copy-start.13 = (bf16[6,6,1024]{2,1,0:T(8,128)(2,1)S(1)}, bf16[6,6,1024]{2,1,0:T(8,128)(2,1)}, u32[]{:S(2)}) copy-start(bf16[6,6,1024]{2,1,0:T(8,128)(2,1)} %get-tuple-element.16) | copy-start | bytes 221188
  107.4 24.8 %copy-start.12 = (bf16[6,6,1024]{2,1,0:T(8,128)(2,1)S(1)}, bf16[6,6,1024]{2,1,0:T(8,128)(2,1)}, u32[]{:S(2)}) copy-start(bf16[6,6,1024]{2,1,0:T(8,128)(2,1)} %get-tuple-element.17) | copy-start | bytes 221188
  107.4 26.1 %copy-start.11 = (bf16[6,16,1024]{2,1,0:T(8,128)(2,1)S(1)}, bf16[6,16,1024]{2,1,0:T(8,128)(2,1)}, u32[]{:S(2)}) copy-start(bf16[6,16,1024]{2,1,0:T(8,128)(2,1)} %get-tuple-element.10) | copy-start | bytes 589828
  107.4 30.0 %copy-start.10 = (bf16[6,16,1024]{2,1,0:T(8,128)(2,1)S(1)}, bf16[6,16,1024]{2,1,0:T(8,128)(2,1)}, u32[]{:S(2)}) copy-start(bf16[6,16,1024]{2,1,0:T(8,128)(2,1)} %get-tuple-element.11) | copy-start | bytes 589828
  107.4 3.9 %collective-permute-start.29 = (f32[2,8,2048]{2,1,0:T(8,128)S(1)}, f32[2,8,2048]{2,1,0:T(8,128)S(1)}, u32[]{:S(2)}, u32[]{:S(2)}) collective-permute-start(f32[2,8,2048]{2,1,0:T(8,128)S(1)} %select_bitcast_fusion), channel_id=1, source_target_pairs={{0,16},{8,24},{16,0},{24,8},{1,17},{9,25},{17,1},{25,9},{2,18},{10... | collective-permute-start | bytes 393224 | tf_op jit(solution)/shard_map/ppermute | solution.py:113
  111.4 16.4 %collective-permute-start.30 = (f32[1,8,2048]{2,1,0:T(8,128)S(1)}, f32[1,8,2048]{2,1,0:T(8,128)S(1)}, u32[]{:S(2)}, u32[]{:S(2)}) collective-permute-start(f32[1,8,2048]{2,1,0:T(8,128)S(1)} %slice_select_fusion), channel_id=1, source_target_pairs={{0,8},{8,0},{16,24},{24,16},{1,9},{9,1},{17,25},{25,17},{2,10},{10... | collective-permute-start | bytes 196616 | tf_op jit(solution)/shard_map/ppermute | solution.py:113
  112.6 31.9 %collective-permute-start.15 = (bf16[8,6,1024]{2,1,0:T(8,128)(2,1)S(1)}, bf16[8,6,1024]{2,1,0:T(8,128)(2,1)S(1)}, u32[]{:S(2)}, u32[]{:S(2)}) collective-permute-start(bf16[8,6,1024]{2,1,0:T(8,128)(2,1)S(1)} %get-tuple-element.12), channel_id=1, source_target_pairs={{1,0},{2,1},{3,2},{4,3},{5,4},{6,5},{7,6},{9,8},{10,9},{11,10},{12... | collective-permute-start | bytes 294920 | tf_op jit(solution)/shard_map/ppermute | solution.py:29
  121.2 24.6 %collective-permute-start.16 = (bf16[8,6,1024]{2,1,0:T(8,128)(2,1)S(1)}, bf16[8,6,1024]{2,1,0:T(8,128)(2,1)S(1)}, u32[]{:S(2)}, u32[]{:S(2)}) collective-permute-start(bf16[8,6,1024]{2,1,0:T(8,128)(2,1)S(1)} %get-tuple-element.13), channel_id=1, source_target_pairs={{0,1},{1,2},{2,3},{3,4},{4,5},{5,6},{6,7},{8,9},{9,10},{10,11},{11... | collective-permute-start | bytes 294920 | tf_op jit(solution)/shard_map/ppermute | solution.py:29
  122.5 9.6 %collective-permute-start.17 = (bf16[6,6,1024]{2,1,0:T(8,128)(2,1)S(1)}, bf16[6,6,1024]{2,1,0:T(8,128)(2,1)S(1)}, u32[]{:S(2)}, u32[]{:S(2)}) collective-permute-start(bf16[6,6,1024]{2,1,0:T(8,128)(2,1)S(1)} %copy-done.15), channel_id=1, source_target_pairs={{9,0},{10,1},{11,2},{12,3},{13,4},{14,5},{15,6},{17,8},{18,9},{19,... | collective-permute-start | bytes 221192 | tf_op jit(solution)/shard_map/ppermute | solution.py:29
  126.4 7.0 %collective-permute-start.20 = (bf16[6,6,1024]{2,1,0:T(8,128)(2,1)S(1)}, bf16[6,6,1024]{2,1,0:T(8,128)(2,1)S(1)}, u32[]{:S(2)}, u32[]{:S(2)}) collective-permute-start(bf16[6,6,1024]{2,1,0:T(8,128)(2,1)S(1)} %copy-done.14), channel_id=1, source_target_pairs={{0,9},{1,10},{2,11},{3,12},{4,13},{5,14},{6,15},{8,17},{9,18},{10,... | collective-permute-start | bytes 221192 | tf_op jit(solution)/shard_map/ppermute | solution.py:29
  127.8 9.6 %collective-permute-start.19 = (bf16[6,6,1024]{2,1,0:T(8,128)(2,1)S(1)}, bf16[6,6,1024]{2,1,0:T(8,128)(2,1)S(1)}, u32[]{:S(2)}, u32[]{:S(2)}) collective-permute-start(bf16[6,6,1024]{2,1,0:T(8,128)(2,1)S(1)} %copy-done.13), channel_id=1, source_target_pairs={{1,8},{2,9},{3,10},{4,11},{5,12},{6,13},{7,14},{9,16},{10,17},{11,... | collective-permute-start | bytes 221192 | tf_op jit(solution)/shard_map/ppermute | solution.py:29
  132.1 8.0 %collective-permute-start.18 = (bf16[6,6,1024]{2,1,0:T(8,128)(2,1)S(1)}, bf16[6,6,1024]{2,1,0:T(8,128)(2,1)S(1)}, u32[]{:S(2)}, u32[]{:S(2)}) collective-permute-start(bf16[6,6,1024]{2,1,0:T(8,128)(2,1)S(1)} %copy-done.12), channel_id=1, source_target_pairs={{8,1},{9,2},{10,3},{11,4},{12,5},{13,6},{14,7},{16,9},{17,10},{18,... | collective-permute-start | bytes 221192 | tf_op jit(solution)/shard_map/ppermute | solution.py:29
  133.5 18.8 %collective-permute-start.13 = (bf16[6,16,1024]{2,1,0:T(8,128)(2,1)S(1)}, bf16[6,16,1024]{2,1,0:T(8,128)(2,1)S(1)}, u32[]{:S(2)}, u32[]{:S(2)}) collective-permute-start(bf16[6,16,1024]{2,1,0:T(8,128)(2,1)S(1)} %copy-done.11), channel_id=1, source_target_pairs={{8,0},{16,8},{24,16},{9,1},{17,9},{25,17},{10,2},{18,10},{26,18},{... | collective-permute-start | bytes 589832 | tf_op jit(solution)/shard_map/ppermute | solution.py:29
  137.4 16.1 %collective-permute-start.14 = (bf16[6,16,1024]{2,1,0:T(8,128)(2,1)S(1)}, bf16[6,16,1024]{2,1,0:T(8,128)(2,1)S(1)}, u32[]{:S(2)}, u32[]{:S(2)}) collective-permute-start(bf16[6,16,1024]{2,1,0:T(8,128)(2,1)S(1)} %copy-done.10), channel_id=1, source_target_pairs={{0,8},{8,16},{16,24},{1,9},{9,17},{17,25},{2,10},{10,18},{18,26},{... | collective-permute-start | bytes 589832 | tf_op jit(solution)/shard_map/ppermute | solution.py:29
  140.1 33.6 %collective-permute-start.23 = (bf16[8,6,1024]{2,1,0:T(8,128)(2,1)S(1)}, bf16[8,6,1024]{2,1,0:T(8,128)(2,1)S(1)}, u32[]{:S(2)}, u32[]{:S(2)}) collective-permute-start(bf16[8,6,1024]{2,1,0:T(8,128)(2,1)S(1)} %get-tuple-element.20), channel_id=1, source_target_pairs={{1,0},{2,1},{3,2},{4,3},{5,4},{6,5},{7,6},{9,8},{10,9},{11,10},{12... | collective-permute-start | bytes 294920 | tf_op jit(solution)/shard_map/ppermute | solution.py:29
  144.5 29.3 %collective-permute-start.24 = (bf16[8,6,1024]{2,1,0:T(8,128)(2,1)S(1)}, bf16[8,6,1024]{2,1,0:T(8,128)(2,1)S(1)}, u32[]{:S(2)}, u32[]{:S(2)}) collective-permute-start(bf16[8,6,1024]{2,1,0:T(8,128)(2,1)S(1)} %get-tuple-element.21), channel_id=1, source_target_pairs={{0,1},{1,2},{2,3},{3,4},{4,5},{5,6},{6,7},{8,9},{9,10},{10,11},{11... | collective-permute-start | bytes 294920 | tf_op jit(solution)/shard_map/ppermute | solution.py:29
  145.8 16.1 %collective-permute-start.25 = (bf16[6,6,1024]{2,1,0:T(8,128)(2,1)S(1)}, bf16[6,6,1024]{2,1,0:T(8,128)(2,1)S(1)}, u32[]{:S(2)}, u32[]{:S(2)}) collective-permute-start(bf16[6,6,1024]{2,1,0:T(8,128)(2,1)S(1)} %get-tuple-element.22), channel_id=1, source_target_pairs={{9,0},{10,1},{11,2},{12,3},{13,4},{14,5},{15,6},{17,8},{18,9},{19,... | collective-permute-start | bytes 221192 | tf_op jit(solution)/shard_map/ppermute | solution.py:29
  152.2 11.0 %collective-permute-start.28 = (bf16[6,6,1024]{2,1,0:T(8,128)(2,1)S(1)}, bf16[6,6,1024]{2,1,0:T(8,128)(2,1)S(1)}, u32[]{:S(2)}, u32[]{:S(2)}) collective-permute-start(bf16[6,6,1024]{2,1,0:T(8,128)(2,1)S(1)} %get-tuple-element.23), channel_id=1, source_target_pairs={{0,9},{1,10},{2,11},{3,12},{4,13},{5,14},{6,15},{8,17},{9,18},{10,... | collective-permute-start | bytes 221192 | tf_op jit(solution)/shard_map/ppermute | solution.py:29
  153.6 5.2 %collective-permute-start.31 = (f32[4,1,2048]{2,0,1:T(4,128)S(1)}, f32[4,1,2048]{2,0,1:T(4,128)S(1)}, u32[]{:S(2)}, u32[]{:S(2)}) collective-permute-start(f32[4,1,2048]{2,0,1:T(4,128)S(1)} %select_bitcast_fusion.1), channel_id=1, source_target_pairs={{0,4},{1,5},{2,6},{3,7},{4,0},{5,1},{6,2},{7,3},{8,12},{9,13},{10,... | collective-permute-start | bytes 98312 | tf_op jit(solution)/shard_map/ppermute | solution.py:113
  158.8 9.8 %collective-permute-start.27 = (bf16[6,6,1024]{2,1,0:T(8,128)(2,1)S(1)}, bf16[6,6,1024]{2,1,0:T(8,128)(2,1)S(1)}, u32[]{:S(2)}, u32[]{:S(2)}) collective-permute-start(bf16[6,6,1024]{2,1,0:T(8,128)(2,1)S(1)} %get-tuple-element.24), channel_id=1, source_target_pairs={{1,8},{2,9},{3,10},{4,11},{5,12},{6,13},{7,14},{9,16},{10,17},{11,... | collective-permute-start | bytes 221192 | tf_op jit(solution)/shard_map/ppermute | solution.py:29
  161.9 8.7 %collective-permute-start.26 = (bf16[6,6,1024]{2,1,0:T(8,128)(2,1)S(1)}, bf16[6,6,1024]{2,1,0:T(8,128)(2,1)S(1)}, u32[]{:S(2)}, u32[]{:S(2)}) collective-permute-start(bf16[6,6,1024]{2,1,0:T(8,128)(2,1)S(1)} %get-tuple-element.25), channel_id=1, source_target_pairs={{8,1},{9,2},{10,3},{11,4},{12,5},{13,6},{14,7},{16,9},{17,10},{18,... | collective-permute-start | bytes 221192 | tf_op jit(solution)/shard_map/ppermute | solution.py:29
  163.2 10.7 %collective-permute-start.21 = (bf16[6,16,1024]{2,1,0:T(8,128)(2,1)S(1)}, bf16[6,16,1024]{2,1,0:T(8,128)(2,1)S(1)}, u32[]{:S(2)}, u32[]{:S(2)}) collective-permute-start(bf16[6,16,1024]{2,1,0:T(8,128)(2,1)S(1)} %get-tuple-element.18), channel_id=1, source_target_pairs={{8,0},{16,8},{24,16},{9,1},{17,9},{25,17},{10,2},{18,10},{26,18},{... | collective-permute-start | bytes 589832 | tf_op jit(solution)/shard_map/ppermute | solution.py:29
  168.6 10.8 %collective-permute-start.22 = (bf16[6,16,1024]{2,1,0:T(8,128)(2,1)S(1)}, bf16[6,16,1024]{2,1,0:T(8,128)(2,1)S(1)}, u32[]{:S(2)}, u32[]{:S(2)}) collective-permute-start(bf16[6,16,1024]{2,1,0:T(8,128)(2,1)S(1)} %get-tuple-element.19), channel_id=1, source_target_pairs={{0,8},{8,16},{16,24},{1,9},{9,17},{17,25},{2,10},{10,18},{18,26},{... | collective-permute-start | bytes 589832 | tf_op jit(solution)/shard_map/ppermute | solution.py:29
  170.6 10.3 %collective-permute-start.32 = (f32[2,1,2048]{2,0,1:T(2,128)S(1)}, f32[2,1,2048]{2,0,1:T(2,128)S(1)}, u32[]{:S(2)}, u32[]{:S(2)}) collective-permute-start(f32[2,1,2048]{2,0,1:T(2,128)S(1)} %broadcast_select_fusion), channel_id=1, source_target_pairs={{0,2},{1,3},{2,0},{3,1},{4,6},{5,7},{6,4},{7,5},{8,10},{9,11},{10,... | collective-permute-start | bytes 49160 | tf_op jit(solution)/shard_map/ppermute | solution.py:113
  180.9 1.8 collective-permute-start.33
  (4 other events, 8.7 us)

commit v4 on v3

v4 whole, which is shorter than its diff:
```python
import math

import jax
import jax.numpy as jnp
import numpy as np
from jax import lax
from jax.experimental import pallas as pl
from jax.sharding import PartitionSpec as P

HEADS = 16
KW = 13
RAD = 6


def bits(n):
    return n.bit_length() - 1


def device_bit(position):
    col_bits = bits(lax.axis_size("cols"))
    if position < col_bits:
        return "cols", position
    return "rows", position - col_bits


def own_bit(position):
    axis, bit = device_bit(position)
    return (lax.axis_index(axis) >> bit) % 2


def partner(x, position):
    axis, bit = device_bit(position)
    size = lax.axis_size(axis)
    return lax.ppermute(x, axis, [(i, i ^ (1 << bit)) for i in range(size)])


def exchange(to_lower, to_higher, axis, rider=None, rider_dim=0):
    size = lax.axis_size(axis)
    even = lax.axis_index(axis) % 2 == 0
    first = jnp.where(even, to_higher, to_lower)
    length = first.shape[rider_dim]
    if rider is not None:
        first = jnp.concatenate([first, rider], axis=rider_dim)
    got_first = lax.ppermute(first, axis, [(i, i ^ 1) for i in range(size)])
    links = [(i, i + 1) for i in range(1, size - 1, 2)] + [(i, i - 1) for i in range(2, size, 2)]
    got_second = lax.ppermute(jnp.where(even, to_lower, to_higher), axis, links)
    rider_got = None
    if rider is not None:
        rider_got = lax.slice_in_dim(got_first, length, None, axis=rider_dim)
        got_first = lax.slice_in_dim(got_first, 0, length, axis=rider_dim)
    from_lower = jnp.where(even, got_second, got_first)
    from_higher = jnp.where(even, got_first, got_second)
    return from_lower, from_higher, rider_got


def gather_step(x, other, position):
    low = own_bit(position) == 0
    return jnp.where(low, jnp.concatenate([x, other]), jnp.concatenate([other, x]))


def gather_order(order, count):
    where = np.zeros(count, np.int32)
    for l in range(count):
        where[l] = sum(((l >> bit) & 1) << step for step, bit in enumerate(order))
    return where


def scatter_split(x, order_left, position):
    axis = 1 + order_left.index(position)
    high = own_bit(position) == 1
    lower = lax.index_in_dim(x, 0, axis, keepdims=False)
    upper = lax.index_in_dim(x, 1, axis, keepdims=False)
    order_left.remove(position)
    return jnp.where(high, upper, lower), jnp.where(high, lower, upper)


def attention_kernel(q_ref, k_ref, v_ref, g_ref, mask_ref, o_ref, dq_ref, dkv_ref):
    head_size = q_ref.shape[1] // 2
    score_scale = 1.0 / math.sqrt(head_size)
    q = q_ref[...]
    k = k_ref[...]
    v = v_ref[...]
    g = g_ref[...]
    keep = mask_ref[...] > 0
    lane_head = lax.broadcasted_iota(jnp.int32, q.shape, 1) // head_size
    lane_head_keys = lax.broadcasted_iota(jnp.int32, k.shape, 1) // head_size
    rows = (((1,), (1,)), ((), ()))
    cols = (((0,), (0,)), ((), ()))
    out = jnp.zeros(q.shape, jnp.float32)
    dq = jnp.zeros(q.shape, jnp.float32)
    dk = jnp.zeros(k.shape, jnp.float32)
    dv = jnp.zeros(k.shape, jnp.float32)
    for head in range(2):
        mine = lane_head == head
        mine_keys = lane_head_keys == head
        q_head = jnp.where(mine, q, jnp.zeros_like(q))
        g_head = jnp.where(mine, g, jnp.zeros_like(g))
        scores = lax.dot_general(q_head, k, rows, preferred_element_type=jnp.float32) * score_scale
        scores = jnp.where(keep, scores, -1e30)
        row_max = jnp.max(scores, axis=1, keepdims=True)
        exps = jnp.exp(scores - row_max)
        probs = exps / jnp.sum(exps, axis=1, keepdims=True)
        rounded = probs.astype(jnp.bfloat16)
        attended = jnp.dot(rounded, v, preferred_element_type=jnp.float32)
        attended = attended.astype(jnp.bfloat16).astype(jnp.float32)
        out = jnp.where(mine, attended, out)
        delta = jnp.sum(
            jnp.where(mine, g.astype(jnp.float32) * attended, 0.0), axis=1, keepdims=True
        )
        dots = lax.dot_general(g_head, v, rows, preferred_element_type=jnp.float32)
        slopes = (probs * (dots - delta) * score_scale).astype(jnp.bfloat16)
        dq = jnp.where(mine, jnp.dot(slopes, k, preferred_element_type=jnp.float32), dq)
        dk = jnp.where(
            mine_keys, lax.dot_general(slopes, q, cols, preferred_element_type=jnp.float32), dk
        )
        dv = jnp.where(
            mine_keys, lax.dot_general(rounded, g, cols, preferred_element_type=jnp.float32), dv
        )
    o_ref[...] = out.astype(o_ref.dtype)
    dq_ref[...] = dq.astype(dq_ref.dtype)
    dkv_ref[0] = dk
    dkv_ref[1] = dv


def attention(queries, all_kv, grad_attended, keep):
    tokens, model_width = queries.shape
    key_count = all_kv.shape[0]
    lanes = 2 * (model_width // HEADS)
    steps = model_width // lanes
    token_block = pl.BlockSpec((tokens, lanes), lambda i: (0, i))
    key_block = pl.BlockSpec((key_count, lanes), lambda i: (0, i))
    value_block = pl.BlockSpec((key_count, lanes), lambda i: (0, i + steps))
    mask_block = pl.BlockSpec((tokens, key_count), lambda i: (0, 0))
    grads_block = pl.BlockSpec((2, key_count, lanes), lambda i: (0, 0, i))
    flops = 2 * 2 * 6 * tokens * key_count * model_width
    moved = 2 * (3 * tokens * model_width + 2 * key_count * model_width) + 4 * (
        tokens * key_count + 2 * key_count * model_width
    )
    return pl.pallas_call(
        attention_kernel,
        grid=(steps,),
        in_specs=[token_block, key_block, value_block, token_block, mask_block],
        out_specs=[token_block, token_block, grads_block],
        out_shape=[
            jax.ShapeDtypeStruct((tokens, model_width), jnp.bfloat16),
            jax.ShapeDtypeStruct((tokens, model_width), jnp.bfloat16),
            jax.ShapeDtypeStruct((2, key_count, model_width), jnp.float32),
        ],
        cost_estimate=pl.CostEstimate(
            flops=flops, transcendentals=HEADS * tokens * key_count, bytes_accessed=moved
        ),
    )(queries, all_kv, all_kv, grad_attended, keep)


def shards(features, w_query, w_key, w_value, w_out, reg_pos, grad_out):
    tile_rows, tile_cols, model_width = features.shape
    row_count = lax.axis_size("rows")
    col_count = lax.axis_size("cols")
    row_index = lax.axis_index("rows")
    col_index = lax.axis_index("cols")
    band_rows = tile_rows * row_count
    band_cols = tile_cols * col_count
    first_row = row_index * tile_rows
    first_col = col_index * tile_cols
    tokens = tile_rows * tile_cols
    device_count = row_count * col_count
    col_bits = bits(col_count)
    all_bits = col_bits + bits(row_count)
    ext_rows = tile_rows + 2 * RAD
    width = 2 * model_width

    flat_tokens = features.reshape(-1, model_width)
    queries = jnp.dot(flat_tokens, w_query, preferred_element_type=jnp.float32).astype(jnp.bfloat16)
    keys_local = jnp.dot(flat_tokens, w_key, preferred_element_type=jnp.float32).astype(
        jnp.bfloat16
    )
    values_local = jnp.dot(flat_tokens, w_value, preferred_element_type=jnp.float32).astype(
        jnp.bfloat16
    )
    key_value = jnp.concatenate([keys_local, values_local], axis=1)
    tile_kv = key_value.reshape(tile_rows, tile_cols, width)

    own_index = row_index * col_count + col_index
    own_place = lax.dynamic_index_in_dim(reg_pos, own_index, 0, keepdims=False)
    own_local = (own_place // band_cols - first_row) * tile_cols + (own_place % band_cols - first_col)
    gathered = lax.dynamic_slice_in_dim(key_value, own_local, 1, 0)
    order = [col_bits, 0] + list(range(1, col_bits)) + list(range(col_bits + 1, all_bits))

    from_above, from_below, got = exchange(
        tile_kv[:RAD].reshape(-1, width),
        tile_kv[tile_rows - RAD :].reshape(-1, width),
        "rows",
        gathered,
    )
    gathered = gather_step(gathered, got, order[0])
    extended = jnp.concatenate(
        [
            from_above.reshape(RAD, tile_cols, width),
            tile_kv,
            from_below.reshape(RAD, tile_cols, width),
        ],
        axis=0,
    )
    from_left, from_right, got = exchange(
        extended[:, :RAD].reshape(-1, width),
        extended[:, tile_cols - RAD :].reshape(-1, width),
        "cols",
        gathered,
    )
    gathered = gather_step(gathered, got, order[1])
    for position in order[2:]:
        gathered = gather_step(gathered, partner(gathered, position), position)
    global_kv = jnp.take(gathered, jnp.asarray(gather_order(order, device_count)), axis=0)

    own_keys = ext_rows * tile_cols
    strip_keys = ext_rows * RAD
    frame_keys = own_keys + 2 * strip_keys
    used = frame_keys + device_count
    key_count = -(-used // 128) * 128
    all_kv = jnp.concatenate(
        [
            extended.reshape(own_keys, width),
            from_left,
            from_right,
            global_kv,
            jnp.zeros((key_count - used, width), key_value.dtype),
        ],
        axis=0,
    )

    a, b = np.meshgrid(np.arange(ext_rows), np.arange(tile_cols), indexing="ij")
    s, t = np.meshgrid(np.arange(ext_rows), np.arange(RAD), indexing="ij")
    key_rows = np.zeros(key_count, np.int32)
    key_cols = np.zeros(key_count, np.int32)
    key_rows[:frame_keys] = np.concatenate([a.reshape(-1), s.reshape(-1), s.reshape(-1)])
    key_cols[:frame_keys] = np.concatenate(
        [b.reshape(-1) + RAD, t.reshape(-1), t.reshape(-1) + RAD + tile_cols]
    )
    kind = np.full(key_count, 2, np.int32)
    kind[:frame_keys] = 0
    kind[frame_keys:used] = 1

    query_rows = first_row + jnp.repeat(jnp.arange(tile_rows, dtype=jnp.int32), tile_cols)
    query_cols = first_col + jnp.tile(jnp.arange(tile_cols, dtype=jnp.int32), tile_rows)
    start_rows = jnp.clip(query_rows - RAD, 0, band_rows - KW)[:, None]
    start_cols = jnp.clip(query_cols - RAD, 0, band_cols - KW)[:, None]
    cell_rows = (first_row - RAD + jnp.asarray(key_rows))[None, :]
    cell_cols = (first_col - RAD + jnp.asarray(key_cols))[None, :]
    inside = (
        (cell_rows >= start_rows)
        & (cell_rows < start_rows + KW)
        & (cell_cols >= start_cols)
        & (cell_cols < start_cols + KW)
    )
    key_kind = jnp.asarray(kind)[None, :]
    keep = ((inside & (key_kind == 0)) | (key_kind == 1)).astype(jnp.float32)

    grad_attended = jnp.dot(
        grad_out.reshape(-1, model_width), w_out.T, preferred_element_type=jnp.float32
    ).astype(jnp.bfloat16)
    attended, query_grads, kv_grads_all = attention(queries, all_kv, grad_attended, keep)
    layer_out = (
        jnp.dot(attended, w_out, preferred_element_type=jnp.float32)
        .astype(jnp.bfloat16)
        .reshape(features.shape)
    )

    scatter = kv_grads_all[:, frame_keys:used].reshape((2,) + (2,) * all_bits + (model_width,))
    left = list(range(all_bits - 1, -1, -1))
    back_order = [0, col_bits] + list(range(1, col_bits)) + list(range(col_bits + 1, all_bits))

    keep_part, send_part = scatter_split(scatter, left, back_order[0])
    strip_shape = (2, ext_rows, RAD, model_width)
    from_left, from_right, got = exchange(
        kv_grads_all[:, own_keys : own_keys + strip_keys],
        kv_grads_all[:, own_keys + strip_keys : frame_keys],
        "cols",
        send_part.reshape(2, -1, model_width),
        rider_dim=1,
    )
    scatter = keep_part + got.reshape(keep_part.shape)
    extended_grads = kv_grads_all[:, :own_keys].reshape(2, ext_rows, tile_cols, model_width)
    extended_grads = extended_grads + jnp.pad(
        from_left.reshape(strip_shape), ((0, 0), (0, 0), (0, tile_cols - RAD), (0, 0))
    )
    extended_grads = extended_grads + jnp.pad(
        from_right.reshape(strip_shape), ((0, 0), (0, 0), (tile_cols - RAD, 0), (0, 0))
    )
    keep_part, send_part = scatter_split(scatter, left, back_order[1])
    band_shape = (2, RAD, tile_cols, model_width)
    from_above, from_below, got = exchange(
        extended_grads[:, :RAD].reshape(2, -1, model_width),
        extended_grads[:, RAD + tile_rows :].reshape(2, -1, model_width),
        "rows",
        send_part.reshape(2, -1, model_width),
        rider_dim=1,
    )
    scatter = keep_part + got.reshape(keep_part.shape)
    centre = extended_grads[:, RAD : RAD + tile_rows]
    centre = centre + jnp.pad(
        from_above.reshape(band_shape), ((0, 0), (0, tile_rows - RAD), (0, 0), (0, 0))
    )
    centre = centre + jnp.pad(
        from_below.reshape(band_shape), ((0, 0), (tile_rows - RAD, 0), (0, 0), (0, 0))
    )
    for position in back_order[2:]:
        keep_part, send_part = scatter_split(scatter, left, position)
        scatter = keep_part + partner(send_part, position)
    own_grads = scatter.reshape(2, 1, model_width)

    middle = centre.reshape(2, tokens, model_width)
    own_row = lax.dynamic_slice_in_dim(middle, own_local, 1, 1) + own_grads
    kv_grads = lax.dynamic_update_slice_in_dim(middle, own_row, own_local, 1).astype(jnp.bfloat16)

    grad_in = (
        jnp.dot(query_grads, w_query.T, preferred_element_type=jnp.float32)
        + jnp.dot(kv_grads[0], w_key.T, preferred_element_type=jnp.float32)
        + jnp.dot(kv_grads[1], w_value.T, preferred_element_type=jnp.float32)
    )
    grad_in = grad_in.astype(jnp.bfloat16).reshape(features.shape)
    return (layer_out, grad_in)


def solution(mesh):
    placed = (P("rows", "cols", None), P(), P(), P(), P(), P(), P("rows", "cols", None))
    return jax.shard_map(
        shards,
        mesh=mesh,
        in_specs=placed,
        out_specs=(P("rows", "cols", None), P("rows", "cols", None)),
        check_vma=False,
    )
```

time: 189 us -> 164 us (0.87)
  the two profiles are of different devices: /device:TPU:29 before, /device:TPU:16 now
where the time goes in v4:
time: 164 us; the launch traced here: 163 us
  waiting for transfers between devices  49 us (30%)
  starting transfers between devices  31.9 us (19%)
  local copies, waits for them, and re-layouts  24.4 us (15%)
  other arithmetic  24.4 us (15%)
  Pallas kernels  16.6 us (10%)
  matrix products  12.5 us (8%)
  between operations  3.9 us (2%)
    ppermute x4, waiting for transfers between devices, exchange(): got_first = lax.ppermute(first, axis, [(i, i ^ 1) for i in range(size)])  24.8 us
    ppermute x6, starting transfers between devices, partner(): return lax.ppermute(x, axis, [(i, i ^ 1 << bit) for i in range(size)])  21 us
    pallas_call x1, Pallas kernels, attention(): pl.pallas_call(attention_kernel, grid=(steps,), in_specs=[token_block, ke...  16.6 us
    ppermute x6, waiting for transfers between devices, partner(): return lax.ppermute(x, axis, [(i, i ^ 1 << bit) for i in range(size)])  15.4 us
    ppermute x4, waiting for transfers between devices, exchange(): got_second = lax.ppermute(jnp.where(even, to_lower, to_higher), axis, links)  8.8 us
    ppermute x4, starting transfers between devices, exchange(): got_second = lax.ppermute(jnp.where(even, to_lower, to_higher), axis, links)  6.67 us
    select_n x4, other arithmetic, exchange(): first = jnp.where(even, to_higher, to_lower)  6.59 us
    select_n x3, other arithmetic, exchange(): from_lower = jnp.where(even, got_second, got_first)  4.83 us
  transfers between devices with their start and end apart: 14, of which 7 were waited for; matrix products, arithmetic and copies ran while one was open for 15% of the time, Pallas kernels for 0%

profile of v4, /device:TPU:16, one launch (start us, length us, event | category | flops | bytes accessed | tf_op | source)
XLA Modules:
  0.0 162.9 jit_solution(14894301565776392724)
XLA Ops:
  0.7 1.4 dynamic_slice.10
  4.7 2.3 %convolution_convert_fusion.2 = bf16[128,1024]{1,0:T(8,128)(2,1)S(1)} fusion(bf16[128,1024]{1,0:T(8,128)(2,1)} %bitcast.103, bf16[1024,1024]{1,0:T(8,128)(2,1)} %param.14), kind=kOutput, calls=%fused_computation.8 | convolution fusion | flops 268566528 | bytes 2621440 | tf_op jit(solution)/shard_map/dot_general | solution.py:177
  7.5 0.9 broadcast_select_fusion.8
  8.5 1.6 collective-permute-start.1
  10.0 1.4 collective-permute-start
  12.6 1.2 convolution_convert_fusion.4.q_ref
  13.7 7.6 %collective-permute-done.1 = bf16[97,2048]{1,0:T(8,128)(2,1)} collective-permute-done((bf16[97,2048]{1,0:T(8,128)(2,1)S(1)}, bf16[97,2048]{1,0:T(8,128)(2,1)}, u32[]{:S(2)}, u32[]{:S(2)}) %collective-permute-start.1) | collective-permute-done | bytes 397344 | tf_op jit(solution)/shard_map/ppermute | solution.py:44
  21.3 1.2 broadcast_select_fusion.7
  22.7 1.3 broadcast_select_fusion.4
  24.0 2.0 %select_n.315 = bf16[120,2048]{1,0:T(8,128)(2,1)} reshape(bf16[20,6,2048]{2,1,0:T(8,128)(2,1)} %get-tuple-element.16) | data formatting | bytes 983040 | tf_op jit(solution)/shard_map/jit(_where)/select_n | solution.py:40
  26.8 1.9 %pad_maximum_fusion.4 = bf16[122,2048]{1,0:T(8,128)(2,1)} fusion(bf16[2,2048]{1,0:T(2,128)(2,1)S(1)} %broadcast_select_fusion.12, bf16[120,2048]{1,0:T(8,128)(2,1)} %select_n.315), kind=kLoop, calls=%fused_computation.33 | loop fusion | flops 999424 | bytes 999424 | tf_op jit(solution)/shard_map/concatenate | solution.py:43
  28.7 1.0 or_convert_fusion.mask_ref
  29.7 3.2 %convolution_convert_fusion.1.g_ref = bf16[128,1024]{1,0:T(8,128)(2,1)} fusion(bf16[128,1024]{1,0:T(8,128)(2,1)} %bitcast.110, bf16[1024,1024]{1,0:T(8,128)(2,1)} %param.15), kind=kOutput, calls=%fused_computation.7 | convolution fusion | flops 268566528 | bytes 2621440 | tf_op jit(solution)/shard_map/dot_general | solution.py:258
  32.9 2.1 %select_n.313 = bf16[120,2048]{1,0:T(8,128)(2,1)} reshape(bf16[20,6,2048]{2,1,0:T(8,128)(2,1)} %get-tuple-element.17) | data formatting | bytes 983040 | tf_op jit(solution)/shard_map/jit(_where)/select_n | solution.py:46
  35.0 2.5 %collective-permute-start.2 = (bf16[120,2048]{1,0:T(8,128)(2,1)}, bf16[120,2048]{1,0:T(8,128)(2,1)S(1)}, u32[]{:S(2)}, u32[]{:S(2)}) collective-permute-start(bf16[120,2048]{1,0:T(8,128)(2,1)} %select_n.313), channel_id=1, source_target_pairs={{1,2},{3,4},{5,6},{2,1},{4,3},{6,5},{9,10},{11,12},{13,14},{10,9},... | collective-permute-start | bytes 1474568 | tf_op jit(solution)/shard_map/ppermute | solution.py:46
  38.3 1.6 %collective-permute-start.4 = (bf16[4,2048]{1,0:T(4,128)(2,1)S(1)}, bf16[4,2048]{1,0:T(4,128)(2,1)S(1)}, u32[]{:S(2)}, u32[]{:S(2)}) collective-permute-start(bf16[4,2048]{1,0:T(4,128)(2,1)S(1)} %maximum_select_fusion.3), channel_id=1, source_target_pairs={{0,2},{1,3},{2,0},{3,1},{4,6},{5,7},{6,4},{7,5},{8,10},{9,11},{10,... | collective-permute-start | bytes 49160 | tf_op jit(solution)/shard_map/ppermute | solution.py:34
  40.0 6.4 %collective-permute-done.4 = bf16[4,2048]{1,0:T(4,128)(2,1)S(1)} collective-permute-done((bf16[4,2048]{1,0:T(4,128)(2,1)S(1)}, bf16[4,2048]{1,0:T(4,128)(2,1)S(1)}, u32[]{:S(2)}, u32[]{:S(2)}) %collective-permute-start.4) | collective-permute-done | bytes 16416 | tf_op jit(solution)/shard_map/ppermute | solution.py:34
  46.5 1.2 select_dynamic-update-slice_fusion.1
  47.6 3.6 %collective-permute-done.5 = bf16[8,2048]{1,0:T(8,128)(2,1)S(1)} collective-permute-done((bf16[8,2048]{1,0:T(8,128)(2,1)S(1)}, bf16[8,2048]{1,0:T(8,128)(2,1)S(1)}, u32[]{:S(2)}, u32[]{:S(2)}) %collective-permute-start.5) | collective-permute-done | bytes 32800 | tf_op jit(solution)/shard_map/ppermute | solution.py:34
  51.3 8.8 %collective-permute-start.6 = (bf16[16,2048]{1,0:T(8,128)(2,1)S(1)}, bf16[16,2048]{1,0:T(8,128)(2,1)S(1)}, u32[]{:S(2)}, u32[]{:S(2)}) collective-permute-start(bf16[16,2048]{1,0:T(8,128)(2,1)S(1)} %maximum_select_fusion.1), channel_id=1, source_target_pairs={{0,16},{8,24},{16,0},{24,8},{1,17},{9,25},{17,1},{25,9},{2,18},{10... | collective-permute-start | bytes 196616 | tf_op jit(solution)/shard_map/ppermute | solution.py:34
  60.1 1.1 select_dynamic-update-slice_fusion
  61.3 1.5 copy-done.10
  64.8 16.6 %shard_map.122 = (bf16[128,1024]{1,0:T(8,128)(2,1)}, bf16[128,1024]{1,0:T(8,128)(2,1)}, f32[2,640,1024]{2,1,0:T(8,128)}) custom-call(bf16[128,1024]{1,0:T(8,128)(2,1)} %convolution_convert_fusion.4.q_ref, bf16[640,2048]{1,0:T(8,128)(2,1)} %broadcast_dynamic-update-slice_fusion.k_ref.v_ref, bf16[640,2048]{1,0:T(8,128)(2,1)} %broadcast_dynamic-update-slice_fusion.k_ref.v_ref, ...), custom_call_target="tpu_custom_call" | custom-call | flops 2013265920 | bytes 8978432 | tf_op jit(solution)/shard_map/pallas_call | solution.py:139
  81.4 1.0 slice.106
  82.4 2.7 %slice_select_fusion.2 = (f32[2,120,1024]{2,1,0:T(8,128)S(1)}, f32[2,120,1024]{2,1,0:T(8,128)}) fusion(f32[2,640,1024]{2,1,0:T(8,128)} %get-tuple-element.7, pred[]{:T(512)S(6)} %eq.69), kind=kLoop, calls=%fused_computation.17 | loop fusion | flops 491520 | bytes 3932161 | tf_op jit(solution)/shard_map/jit(_where)/select_n | solution.py:40
  85.1 0.8 reshape.160
  85.9 1.3 fusion.18
  88.1 1.0 select_n.340
  89.1 1.1 pad_maximum_fusion.1
  90.2 2.1 %collective-permute-start.7 = (f32[2,120,1024]{2,1,0:T(8,128)}, f32[2,120,1024]{2,1,0:T(8,128)}, u32[]{:S(2)}, u32[]{:S(2)}) collective-permute-start(f32[2,120,1024]{2,1,0:T(8,128)} %get-tuple-element.9), channel_id=1, source_target_pairs={{1,2},{3,4},{5,6},{2,1},{4,3},{6,5},{9,10},{11,12},{13,14},{10,9},... | collective-permute-start | bytes 2949128 | tf_op jit(solution)/shard_map/ppermute | solution.py:46
  92.3 3.6 %slice.103 = f32[2,320,1024]{2,1,0:T(8,128)} slice(f32[2,640,1024]{2,1,0:T(8,128)} %get-tuple-element.7), slice={[0:2], [0:320], [0:1024]} | slice | bytes 5242880 | tf_op jit(solution)/shard_map/slice | solution.py:282
  95.9 0.9 slice.144
  97.2 8.8 %collective-permute-done.7 = f32[2,120,1024]{2,1,0:T(8,128)} collective-permute-done((f32[2,120,1024]{2,1,0:T(8,128)}, f32[2,120,1024]{2,1,0:T(8,128)}, u32[]{:S(2)}, u32[]{:S(2)}) %collective-permute-start.7) | collective-permute-done | bytes 983072 | tf_op jit(solution)/shard_map/ppermute | solution.py:46
  105.9 1.7 %slice_select_fusion.1 = (f32[2,120,1024]{2,1,0:T(8,128)S(1)}, f32[2,120,1024]{2,1,0:T(8,128)S(1)}) fusion(f32[2,120,1024]{2,1,0:T(8,128)} %collective-permute-done.7, f32[2,136,1024]{2,1,0:T(8,128)} %collective-permute-done.8, pred[]{:T(512)S(6)} %eq.69), kind=kLoop, calls=%fused_computation.16 | loop fusion | flops 491520 | bytes 3932161 | tf_op jit(solution)/shard_map/jit(_where)/select_n | solution.py:51
  109.4 2.0 %fusion = f32[2,20,16,1024]{3,0,2,1:T(2,128)S(1)} fusion(f32[2,20,16,1024]{3,2,1,0:T(8,128)S(1)} %bitcast.96, f32[2,20,6,1024]{3,0,2,1:T(2,128)S(1)} %bitcast.98, f32[2,20,6,1024]{3,0,2,1:T(2,128)S(1)} %bitcast.99), kind=kLoop, calls=%fused_computation.2 | loop fusion | flops 1310720 | bytes 7208960 | tf_op jit(solution)/shard_map/add | solution.py:286
  111.5 1.8 %broadcast_select_fusion = (f32[2,6,16,1024]{3,0,2,1:T(2,128)S(1)}, f32[2,6,16,1024]{3,0,2,1:T(2,128)}) fusion(pred[]{:T(512)S(6)} %eq.68, f32[2,20,16,1024]{3,0,2,1:T(2,128)S(1)} %fusion), kind=kLoop, calls=%fused_computation.20 | loop fusion | flops 393216 | bytes 3145729 | tf_op jit(solution)/shard_map/jit(_where)/select_n | solution.py:40
  113.7 2.7 %collective-permute-start.10 = (f32[2,104,1024]{2,0,1:T(2,128)S(1)}, f32[2,104,1024]{2,0,1:T(2,128)}, u32[]{:S(2)}, u32[]{:S(2)}) collective-permute-start(f32[2,104,1024]{2,0,1:T(2,128)S(1)} %pad_maximum_fusion.2), channel_id=1, source_target_pairs={{0,8},{8,0},{16,24},{24,16},{1,9},{9,1},{17,25},{25,17},{2,10},{10... | collective-permute-start | bytes 2555912 | tf_op jit(solution)/shard_map/ppermute | solution.py:44
  116.3 1.9 %fusion.19 = f32[128,1024]{1,0:T(8,128)S(1)} fusion(bf16[128,1024]{1,0:T(8,128)(2,1)} %get-tuple-element.6, bf16[1024,1024]{1,0:T(8,128)(2,1)S(1)} %copy-done), kind=kOutput, calls=%fused_computation.84 | convolution fusion | flops 268435456 | bytes 2883584 | tf_op jit(solution)/shard_map/dot_general | solution.py:316
  119.0 17.2 %collective-permute-done.10 = f32[2,104,1024]{2,0,1:T(2,128)} collective-permute-done((f32[2,104,1024]{2,0,1:T(2,128)S(1)}, f32[2,104,1024]{2,0,1:T(2,128)}, u32[]{:S(2)}, u32[]{:S(2)}) %collective-permute-start.10) | collective-permute-done | bytes 852000 | tf_op jit(solution)/shard_map/ppermute | solution.py:44
  136.2 0.8 slice.148
  137.3 1.2 convolution_convert_fusion
  138.4 2.7 %collective-permute-done.11 = f32[2,2,2,1024]{3,0,2,1:T(2,128)S(1)} collective-permute-done((f32[2,2,2,1024]{3,0,2,1:T(2,128)S(1)}, f32[2,2,2,1024]{3,0,2,1:T(2,128)S(1)}, u32[]{:S(2)}, u32[]{:S(2)}) %collective-permute-start.11) | collective-permute-done | bytes 32800 | tf_op jit(solution)/shard_map/ppermute | solution.py:34
  141.3 1.9 %broadcast_select_fusion.3 = (f32[2,96,1024]{2,0,1:T(2,128)S(1)}, f32[2,96,1024]{2,0,1:T(2,128)S(1)}) fusion(f32[2,96,1024]{2,0,1:T(2,128)S(1)} %collective-permute-done.9, pred[]{:T(512)S(6)} %eq.68, f32[2,104,1024]{2,0,1:T(2,128)} %collective-permute-done.10), kind=kLoop, calls=%fused_computation.23 | loop fusion | flops 393216 | bytes 3145729 | tf_op jit(solution)/shard_map/jit(_where)/select_n | solution.py:51
  143.2 2.7 %collective-permute-done.12 = f32[2,2,1024]{2,0,1:T(2,128)S(1)} collective-permute-done((f32[2,2,1024]{2,0,1:T(2,128)S(1)}, f32[2,2,1024]{2,0,1:T(2,128)S(1)}, u32[]{:S(2)}, u32[]{:S(2)}) %collective-permute-start.12) | collective-permute-done | bytes 16416 | tf_op jit(solution)/shard_map/ppermute | solution.py:34
  145.9 10.4 %collective-permute-start.13 = (f32[2,1024]{1,0:T(2,128)S(1)}, f32[2,1024]{1,0:T(2,128)S(1)}, u32[]{:S(2)}, u32[]{:S(2)}) collective-permute-start(f32[2,1024]{1,0:T(2,128)S(1)} %select_bitcast_fusion), channel_id=1, source_target_pairs={{0,16},{8,24},{16,0},{24,8},{1,17},{9,25},{17,1},{25,9},{2,18},{10... | collective-permute-start | bytes 24584 | tf_op jit(solution)/shard_map/ppermute | solution.py:34
  156.3 2.2 %fusion.2 = f32[2,8,16,1024]{3,0,2,1:T(2,128)S(1)} fusion(f32[2,20,16,1024]{3,0,2,1:T(2,128)} %copy-done.1, f32[2,6,16,1024]{3,0,2,1:T(2,128)S(1)} %bitcast.101, f32[2,6,16,1024]{3,0,2,1:T(2,128)S(1)} %bitcast.100), kind=kLoop, calls=%fused_computation.14 | loop fusion | flops 524288 | bytes 3670016 | tf_op jit(solution)/shard_map/add | solution.py:303
  160.1 0.8 convolution_add_fusion.1
  161.4 1.5 fusion.1
  (86 shorter events, 12.0 us)
Async XLA Ops:
  0.6 11.9 %copy-start = (bf16[1024,1024]{1,0:T(8,128)(2,1)S(1)}, bf16[1024,1024]{1,0:T(8,128)(2,1)}, u32[]{:S(2)}) copy-start(bf16[1024,1024]{1,0:T(8,128)(2,1)} %param.12) | copy-start | bytes 6291460
  0.6 6.3 %copy-start.7 = (bf16[8,16,1024]{2,1,0:T(8,128)(2,1)S(1)}, bf16[8,16,1024]{2,1,0:T(8,128)(2,1)}, u32[]{:S(2)}) copy-start(bf16[8,16,1024]{2,1,0:T(8,128)(2,1)} %param.11) | copy-start | bytes 786436
  4.7 2.3 %copy-start.5 = (bf16[1024,1024]{1,0:T(8,128)(2,1)S(1)}, bf16[1024,1024]{1,0:T(8,128)(2,1)}, u32[]{:S(2)}) copy-start(bf16[1024,1024]{1,0:T(8,128)(2,1)} %param.13) | copy-start | bytes 6291460
  7.5 5.0 %copy-start.12 = (s32[640]{0:T(1024)S(1)}, s32[640]{0:T(1024)}, u32[]{:S(2)}) copy-start(s32[640]{0:T(1024)} %constant.134.clone) | copy-start | bytes 7684
  7.5 5.0 %copy-start.13 = (s32[640]{0:T(1024)S(1)}, s32[640]{0:T(1024)}, u32[]{:S(2)}) copy-start(s32[640]{0:T(1024)} %constant.135.clone) | copy-start | bytes 7684
  7.5 5.0 %copy-start.16 = (s32[32]{0:T(128)S(1)}, s32[32]{0:T(128)}, u32[]{:S(2)}) copy-start(s32[32]{0:T(128)} %constant.155) | copy-start | bytes 388
  8.5 12.9 %collective-permute-start.1 = (bf16[97,2048]{1,0:T(8,128)(2,1)S(1)}, bf16[97,2048]{1,0:T(8,128)(2,1)}, u32[]{:S(2)}, u32[]{:S(2)}) collective-permute-start(bf16[97,2048]{1,0:T(8,128)(2,1)S(1)} %pad_maximum_fusion.5), channel_id=1, source_target_pairs={{0,8},{8,0},{16,24},{24,16},{1,9},{9,1},{17,25},{25,17},{2,10},{10... | collective-permute-start | bytes 1191944 | tf_op jit(solution)/shard_map/ppermute | solution.py:44
  10.0 3.7 %collective-permute-start = (bf16[96,2048]{1,0:T(8,128)(2,1)}, bf16[96,2048]{1,0:T(8,128)(2,1)}, u32[]{:S(2)}, u32[]{:S(2)}) collective-permute-start(bf16[96,2048]{1,0:T(8,128)(2,1)} %get-tuple-element.23), channel_id=1, source_target_pairs={{8,16},{16,8},{9,17},{17,9},{10,18},{18,10},{11,19},{19,11},{12,20... | collective-permute-start | bytes 1179656 | tf_op jit(solution)/shard_map/ppermute | solution.py:46
  12.6 9.9 %copy-start.8 = (bf16[128,2048]{1,0:T(8,128)(2,1)S(1)}, bf16[128,2048]{1,0:T(8,128)(2,1)}, u32[]{:S(2)}) copy-start(bf16[128,2048]{1,0:T(8,128)(2,1)} %pad_maximum_fusion.3) | copy-start | bytes 1572868
  22.7 6.1 %copy-start.14 = (pred[640]{0:T(1024)(128)(4,1)S(1)}, pred[640]{0:T(1024)(128)(4,1)}, u32[]{:S(2)}) copy-start(pred[640]{0:T(1024)(128)(4,1)} %constant.152) | copy-start | bytes 1924
  22.7 6.0 %copy-start.15 = (pred[640]{0:T(1024)(128)(4,1)S(1)}, pred[640]{0:T(1024)(128)(4,1)}, u32[]{:S(2)}) copy-start(pred[640]{0:T(1024)(128)(4,1)} %constant.153) | copy-start | bytes 1924
  28.7 8.7 %collective-permute-start.3 = (bf16[122,2048]{1,0:T(8,128)(2,1)}, bf16[122,2048]{1,0:T(8,128)(2,1)}, u32[]{:S(2)}, u32[]{:S(2)}) collective-permute-start(bf16[122,2048]{1,0:T(8,128)(2,1)} %pad_maximum_fusion.4), channel_id=1, source_target_pairs={{0,1},{1,0},{2,3},{3,2},{4,5},{5,4},{6,7},{7,6},{8,9},{9,8},{10,11... | collective-permute-start | bytes 1499144 | tf_op jit(solution)/shard_map/ppermute | solution.py:44
  35.0 11.5 %collective-permute-start.2 = (bf16[120,2048]{1,0:T(8,128)(2,1)}, bf16[120,2048]{1,0:T(8,128)(2,1)S(1)}, u32[]{:S(2)}, u32[]{:S(2)}) collective-permute-start(bf16[120,2048]{1,0:T(8,128)(2,1)} %select_n.313), channel_id=1, source_target_pairs={{1,2},{3,4},{5,6},{2,1},{4,3},{6,5},{9,10},{11,12},{13,14},{10,9},... | collective-permute-start | bytes 1474568 | tf_op jit(solution)/shard_map/ppermute | solution.py:46
  38.3 8.1 %collective-permute-start.4 = (bf16[4,2048]{1,0:T(4,128)(2,1)S(1)}, bf16[4,2048]{1,0:T(4,128)(2,1)S(1)}, u32[]{:S(2)}, u32[]{:S(2)}) collective-permute-start(bf16[4,2048]{1,0:T(4,128)(2,1)S(1)} %maximum_select_fusion.3), channel_id=1, source_target_pairs={{0,2},{1,3},{2,0},{3,1},{4,6},{5,7},{6,4},{7,5},{8,10},{9,11},{10,... | collective-permute-start | bytes 49160 | tf_op jit(solution)/shard_map/ppermute | solution.py:34
  46.4 4.9 %collective-permute-start.5 = (bf16[8,2048]{1,0:T(8,128)(2,1)S(1)}, bf16[8,2048]{1,0:T(8,128)(2,1)S(1)}, u32[]{:S(2)}, u32[]{:S(2)}) collective-permute-start(bf16[8,2048]{1,0:T(8,128)(2,1)S(1)} %maximum_select_fusion.2), channel_id=1, source_target_pairs={{0,4},{1,5},{2,6},{3,7},{4,0},{5,1},{6,2},{7,3},{8,12},{9,13},{10,... | collective-permute-start | bytes 98312 | tf_op jit(solution)/shard_map/ppermute | solution.py:34
  51.3 11.5 %collective-permute-start.6 = (bf16[16,2048]{1,0:T(8,128)(2,1)S(1)}, bf16[16,2048]{1,0:T(8,128)(2,1)S(1)}, u32[]{:S(2)}, u32[]{:S(2)}) collective-permute-start(bf16[16,2048]{1,0:T(8,128)(2,1)S(1)} %maximum_select_fusion.1), channel_id=1, source_target_pairs={{0,16},{8,24},{16,0},{24,8},{1,17},{9,25},{17,1},{25,9},{2,18},{10... | collective-permute-start | bytes 196616 | tf_op jit(solution)/shard_map/ppermute | solution.py:34
  61.3 1.5 copy-start.10
  90.2 5.7 %collective-permute-start.8 = (f32[2,136,1024]{2,1,0:T(8,128)}, f32[2,136,1024]{2,1,0:T(8,128)}, u32[]{:S(2)}, u32[]{:S(2)}) collective-permute-start(f32[2,136,1024]{2,1,0:T(8,128)} %pad_maximum_fusion.1), channel_id=1, source_target_pairs={{0,1},{1,0},{2,3},{3,2},{4,5},{5,4},{6,7},{7,6},{8,9},{9,8},{10,11... | collective-permute-start | bytes 3342344 | tf_op jit(solution)/shard_map/ppermute | solution.py:44
  90.2 15.7 %collective-permute-start.7 = (f32[2,120,1024]{2,1,0:T(8,128)}, f32[2,120,1024]{2,1,0:T(8,128)}, u32[]{:S(2)}, u32[]{:S(2)}) collective-permute-start(f32[2,120,1024]{2,1,0:T(8,128)} %get-tuple-element.9), channel_id=1, source_target_pairs={{1,2},{3,4},{5,6},{2,1},{4,3},{6,5},{9,10},{11,12},{13,14},{10,9},... | collective-permute-start | bytes 2949128 | tf_op jit(solution)/shard_map/ppermute | solution.py:46
  107.7 1.7 %copy-start.2 = (f32[2,320,1024]{2,1,0:T(8,128)S(1)}, f32[2,320,1024]{2,1,0:T(8,128)}, u32[]{:S(2)}) copy-start(f32[2,320,1024]{2,1,0:T(8,128)} %slice.103) | copy-start | bytes 7864324
  111.4 2.2 %copy-start.1 = (f32[2,20,16,1024]{3,0,2,1:T(2,128)}, f32[2,20,16,1024]{3,0,2,1:T(2,128)S(1)}, u32[]{:S(2)}) copy-start(f32[2,20,16,1024]{3,0,2,1:T(2,128)S(1)} %fusion) | copy-start | bytes 7864324
  113.3 24.0 %copy-start.11 = (bf16[128,1024]{1,0:T(8,128)(2,1)S(1)}, bf16[128,1024]{1,0:T(8,128)(2,1)}, u32[]{:S(2)}) copy-start(bf16[128,1024]{1,0:T(8,128)(2,1)} %get-tuple-element.5) | copy-start | bytes 786436
  113.7 22.6 %collective-permute-start.10 = (f32[2,104,1024]{2,0,1:T(2,128)S(1)}, f32[2,104,1024]{2,0,1:T(2,128)}, u32[]{:S(2)}, u32[]{:S(2)}) collective-permute-start(f32[2,104,1024]{2,0,1:T(2,128)S(1)} %pad_maximum_fusion.2), channel_id=1, source_target_pairs={{0,8},{8,0},{16,24},{24,16},{1,9},{9,1},{17,25},{25,17},{2,10},{10... | collective-permute-start | bytes 2555912 | tf_op jit(solution)/shard_map/ppermute | solution.py:44
  116.3 1.9 %copy-start.9 = (f32[2,6,16,1024]{3,0,2,1:T(2,128)S(1)}, f32[2,6,16,1024]{3,0,2,1:T(2,128)}, u32[]{:S(2)}) copy-start(f32[2,6,16,1024]{3,0,2,1:T(2,128)} %get-tuple-element.11) | copy-start | bytes 2359300
  116.3 20.9 %copy-start.3 = (bf16[1024,1024]{1,0:T(8,128)(2,1)S(1)}, bf16[1024,1024]{1,0:T(8,128)(2,1)}, u32[]{:S(2)}) copy-start(bf16[1024,1024]{1,0:T(8,128)(2,1)} %param.15) | copy-start | bytes 6291460
  118.3 23.0 %collective-permute-start.9 = (f32[2,96,1024]{2,0,1:T(2,128)S(1)}, f32[2,96,1024]{2,0,1:T(2,128)S(1)}, u32[]{:S(2)}, u32[]{:S(2)}) collective-permute-start(f32[2,96,1024]{2,0,1:T(2,128)S(1)} %bitcast.109), channel_id=1, source_target_pairs={{8,16},{16,8},{9,17},{17,9},{10,18},{18,10},{11,19},{19,11},{12,20... | collective-permute-start | bytes 2359304 | tf_op jit(solution)/shard_map/ppermute | solution.py:46
  137.2 4.0 %collective-permute-start.11 = (f32[2,2,2,1024]{3,0,2,1:T(2,128)S(1)}, f32[2,2,2,1024]{3,0,2,1:T(2,128)S(1)}, u32[]{:S(2)}, u32[]{:S(2)}) collective-permute-start(f32[2,2,2,1024]{3,0,2,1:T(2,128)S(1)} %fusion.9), channel_id=1, source_target_pairs={{0,2},{1,3},{2,0},{3,1},{4,6},{5,7},{6,4},{7,5},{8,10},{9,11},{10,... | collective-permute-start | bytes 98312 | tf_op jit(solution)/shard_map/ppermute | solution.py:34
  141.2 4.7 %collective-permute-start.12 = (f32[2,2,1024]{2,0,1:T(2,128)S(1)}, f32[2,2,1024]{2,0,1:T(2,128)S(1)}, u32[]{:S(2)}, u32[]{:S(2)}) collective-permute-start(f32[2,2,1024]{2,0,1:T(2,128)S(1)} %fusion.12), channel_id=1, source_target_pairs={{0,4},{1,5},{2,6},{3,7},{4,0},{5,1},{6,2},{7,3},{8,12},{9,13},{10,... | collective-permute-start | bytes 49160 | tf_op jit(solution)/shard_map/ppermute | solution.py:34
  145.9 12.6 %collective-permute-start.13 = (f32[2,1024]{1,0:T(2,128)S(1)}, f32[2,1024]{1,0:T(2,128)S(1)}, u32[]{:S(2)}, u32[]{:S(2)}) collective-permute-start(f32[2,1024]{1,0:T(2,128)S(1)} %select_bitcast_fusion), channel_id=1, source_target_pairs={{0,16},{8,24},{16,0},{24,8},{1,17},{9,25},{17,1},{25,9},{2,18},{10... | collective-permute-start | bytes 24584 | tf_op jit(solution)/shard_map/ppermute | solution.py:34
  158.5 1.6 copy-start.6
  159.7 1.7 %copy-start.4 = (bf16[1024,1024]{1,0:T(8,128)(2,1)S(1)}, bf16[1024,1024]{1,0:T(8,128)(2,1)}, u32[]{:S(2)}) copy-start(bf16[1024,1024]{1,0:T(8,128)(2,1)} %param.14) | copy-start | bytes 6291460

commit v5 on v4

--- a/solution.py
+++ b/solution.py
@@ -122,14 +122,13 @@
     dkv_ref[1] = dv
 
 
-def attention(queries, all_kv, grad_attended, keep):
+def attention(queries, keys, values, grad_attended, keep):
     tokens, model_width = queries.shape
-    key_count = all_kv.shape[0]
+    key_count = keys.shape[0]
     lanes = 2 * (model_width // HEADS)
     steps = model_width // lanes
     token_block = pl.BlockSpec((tokens, lanes), lambda i: (0, i))
     key_block = pl.BlockSpec((key_count, lanes), lambda i: (0, i))
-    value_block = pl.BlockSpec((key_count, lanes), lambda i: (0, i + steps))
     mask_block = pl.BlockSpec((tokens, key_count), lambda i: (0, 0))
     grads_block = pl.BlockSpec((2, key_count, lanes), lambda i: (0, 0, i))
     flops = 2 * 2 * 6 * tokens * key_count * model_width
@@ -139,7 +138,7 @@
     return pl.pallas_call(
         attention_kernel,
         grid=(steps,),
-        in_specs=[token_block, key_block, value_block, token_block, mask_block],
+        in_specs=[token_block, key_block, key_block, token_block, mask_block],
         out_specs=[token_block, token_block, grads_block],
         out_shape=[
             jax.ShapeDtypeStruct((tokens, model_width), jnp.bfloat16),
@@ -149,7 +148,18 @@
         cost_estimate=pl.CostEstimate(
             flops=flops, transcendentals=HEADS * tokens * key_count, bytes_accessed=moved
         ),
-    )(queries, all_kv, all_kv, grad_attended, keep)
+    )(queries, keys, values, grad_attended, keep)
+
+
+def split_wide(x):
+    high = x.astype(jnp.bfloat16)
+    low = (x - high.astype(jnp.float32)).astype(jnp.bfloat16)
+    return jnp.concatenate([high, low], axis=0)
+
+
+def join_wide(pair):
+    half = pair.shape[0] // 2
+    return pair[:half].astype(jnp.float32) + pair[half:].astype(jnp.float32)
 
 
 def shards(features, w_query, w_key, w_value, w_out, reg_pos, grad_out):
@@ -167,65 +177,65 @@
     col_bits = bits(col_count)
     all_bits = col_bits + bits(row_count)
     ext_rows = tile_rows + 2 * RAD
-    width = 2 * model_width
 
     flat_tokens = features.reshape(-1, model_width)
-    queries = jnp.dot(flat_tokens, w_query, preferred_element_type=jnp.float32).astype(jnp.bfloat16)
-    keys_local = jnp.dot(flat_tokens, w_key, preferred_element_type=jnp.float32).astype(
-        jnp.bfloat16
-    )
-    values_local = jnp.dot(flat_tokens, w_value, preferred_element_type=jnp.float32).astype(
-        jnp.bfloat16
-    )
-    key_value = jnp.concatenate([keys_local, values_local], axis=1)
-    tile_kv = key_value.reshape(tile_rows, tile_cols, width)
 
     own_index = row_index * col_count + col_index
     own_place = lax.dynamic_index_in_dim(reg_pos, own_index, 0, keepdims=False)
     own_local = (own_place // band_cols - first_row) * tile_cols + (own_place % band_cols - first_col)
-    gathered = lax.dynamic_slice_in_dim(key_value, own_local, 1, 0)
+    gathered = lax.dynamic_slice_in_dim(flat_tokens, own_local, 1, 0)
     order = [col_bits, 0] + list(range(1, col_bits)) + list(range(col_bits + 1, all_bits))
 
     from_above, from_below, got = exchange(
-        tile_kv[:RAD].reshape(-1, width),
-        tile_kv[tile_rows - RAD :].reshape(-1, width),
+        features[:RAD].reshape(-1, model_width),
+        features[tile_rows - RAD :].reshape(-1, model_width),
         "rows",
         gathered,
     )
     gathered = gather_step(gathered, got, order[0])
     extended = jnp.concatenate(
         [
-            from_above.reshape(RAD, tile_cols, width),
-            tile_kv,
-            from_below.reshape(RAD, tile_cols, width),
+            from_above.reshape(RAD, tile_cols, model_width),
+            features,
+            from_below.reshape(RAD, tile_cols, model_width),
         ],
         axis=0,
     )
     from_left, from_right, got = exchange(
-        extended[:, :RAD].reshape(-1, width),
-        extended[:, tile_cols - RAD :].reshape(-1, width),
+        extended[:, :RAD].reshape(-1, model_width),
+        extended[:, tile_cols - RAD :].reshape(-1, model_width),
         "cols",
         gathered,
     )
     gathered = gather_step(gathered, got, order[1])
+
+    queries = jnp.dot(flat_tokens, w_query, preferred_element_type=jnp.float32).astype(jnp.bfloat16)
+    grad_attended = jnp.dot(
+        grad_out.reshape(-1, model_width), w_out.T, preferred_element_type=jnp.float32
+    ).astype(jnp.bfloat16)
+
     for position in order[2:]:
         gathered = gather_step(gathered, partner(gathered, position), position)
-    global_kv = jnp.take(gathered, jnp.asarray(gather_order(order, device_count)), axis=0)
+    global_features = jnp.take(gathered, jnp.asarray(gather_order(order, device_count)), axis=0)
 
     own_keys = ext_rows * tile_cols
     strip_keys = ext_rows * RAD
     frame_keys = own_keys + 2 * strip_keys
     used = frame_keys + device_count
     key_count = -(-used // 128) * 128
-    all_kv = jnp.concatenate(
+    key_features = jnp.concatenate(
         [
-            extended.reshape(own_keys, width),
+            extended.reshape(own_keys, model_width),
             from_left,
             from_right,
-            global_kv,
-            jnp.zeros((key_count - used, width), key_value.dtype),
+            global_features,
+            jnp.zeros((key_count - used, model_width), features.dtype),
         ],
         axis=0,
+    )
+    keys = jnp.dot(key_features, w_key, preferred_element_type=jnp.float32).astype(jnp.bfloat16)
+    values = jnp.dot(key_features, w_value, preferred_element_type=jnp.float32).astype(
+        jnp.bfloat16
     )
 
     a, b = np.meshgrid(np.arange(ext_rows), np.arange(tile_cols), indexing="ij")
@@ -255,67 +265,71 @@
     key_kind = jnp.asarray(kind)[None, :]
     keep = ((inside & (key_kind == 0)) | (key_kind == 1)).astype(jnp.float32)
 
-    grad_attended = jnp.dot(
-        grad_out.reshape(-1, model_width), w_out.T, preferred_element_type=jnp.float32
-    ).astype(jnp.bfloat16)
-    attended, query_grads, kv_grads_all = attention(queries, all_kv, grad_attended, keep)
+    attended, query_grads, kv_grads_all = attention(queries, keys, values, grad_attended, keep)
     layer_out = (
         jnp.dot(attended, w_out, preferred_element_type=jnp.float32)
         .astype(jnp.bfloat16)
         .reshape(features.shape)
     )
 
+    rounded_grads = kv_grads_all.astype(jnp.bfloat16)
+    given = jnp.dot(rounded_grads[0], w_key.T, preferred_element_type=jnp.float32) + jnp.dot(
+        rounded_grads[1], w_value.T, preferred_element_type=jnp.float32
+    )
+
     scatter = kv_grads_all[:, frame_keys:used].reshape((2,) + (2,) * all_bits + (model_width,))
     left = list(range(all_bits - 1, -1, -1))
     back_order = [0, col_bits] + list(range(1, col_bits)) + list(range(col_bits + 1, all_bits))
 
     keep_part, send_part = scatter_split(scatter, left, back_order[0])
-    strip_shape = (2, ext_rows, RAD, model_width)
+    strip_shape = (ext_rows, RAD, model_width)
     from_left, from_right, got = exchange(
-        kv_grads_all[:, own_keys : own_keys + strip_keys],
-        kv_grads_all[:, own_keys + strip_keys : frame_keys],
+        given[own_keys : own_keys + strip_keys].astype(jnp.bfloat16),
+        given[own_keys + strip_keys : frame_keys].astype(jnp.bfloat16),
         "cols",
-        send_part.reshape(2, -1, model_width),
-        rider_dim=1,
-    )
-    scatter = keep_part + got.reshape(keep_part.shape)
-    extended_grads = kv_grads_all[:, :own_keys].reshape(2, ext_rows, tile_cols, model_width)
-    extended_grads = extended_grads + jnp.pad(
-        from_left.reshape(strip_shape), ((0, 0), (0, 0), (0, tile_cols - RAD), (0, 0))
-    )
-    extended_grads = extended_grads + jnp.pad(
-        from_right.reshape(strip_shape), ((0, 0), (0, 0), (tile_cols - RAD, 0), (0, 0))
-    )
+        split_wide(send_part.reshape(-1, model_width)),
+    )
+    scatter = keep_part + join_wide(got).reshape(keep_part.shape)
+    received = jnp.pad(
+        from_left.astype(jnp.float32).reshape(strip_shape), ((0, 0), (0, tile_cols - RAD), (0, 0))
+    ) + jnp.pad(
+        from_right.astype(jnp.float32).reshape(strip_shape), ((0, 0), (tile_cols - RAD, 0), (0, 0))
+    )
+    extended_given = given[:own_keys].reshape(ext_rows, tile_cols, model_width) + received
     keep_part, send_part = scatter_split(scatter, left, back_order[1])
-    band_shape = (2, RAD, tile_cols, model_width)
+    band_shape = (RAD, tile_cols, model_width)
     from_above, from_below, got = exchange(
-        extended_grads[:, :RAD].reshape(2, -1, model_width),
-        extended_grads[:, RAD + tile_rows :].reshape(2, -1, model_width),
+        extended_given[:RAD].reshape(-1, model_width).astype(jnp.bfloat16),
+        extended_given[RAD + tile_rows :].reshape(-1, model_width).astype(jnp.bfloat16),
         "rows",
-        send_part.reshape(2, -1, model_width),
-        rider_dim=1,
-    )
-    scatter = keep_part + got.reshape(keep_part.shape)
-    centre = extended_grads[:, RAD : RAD + tile_rows]
-    centre = centre + jnp.pad(
-        from_above.reshape(band_shape), ((0, 0), (0, tile_rows - RAD), (0, 0), (0, 0))
-    )
-    centre = centre + jnp.pad(
-        from_below.reshape(band_shape), ((0, 0), (tile_rows - RAD, 0), (0, 0), (0, 0))
+        split_wide(send_part.reshape(-1, model_width)),
+    )
+    scatter = keep_part + join_wide(got).reshape(keep_part.shape)
+    received = received[RAD : RAD + tile_rows]
+    received = received + jnp.pad(
+        from_above.astype(jnp.float32).reshape(band_shape), ((0, tile_rows - RAD), (0, 0), (0, 0))
+    )
+    received = received + jnp.pad(
+        from_below.astype(jnp.float32).reshape(band_shape), ((tile_rows - RAD, 0), (0, 0), (0, 0))
     )
     for position in back_order[2:]:
         keep_part, send_part = scatter_split(scatter, left, position)
         scatter = keep_part + partner(send_part, position)
     own_grads = scatter.reshape(2, 1, model_width)
 
-    middle = centre.reshape(2, tokens, model_width)
-    own_row = lax.dynamic_slice_in_dim(middle, own_local, 1, 1) + own_grads
-    kv_grads = lax.dynamic_update_slice_in_dim(middle, own_row, own_local, 1).astype(jnp.bfloat16)
+    own_given = given[RAD * tile_cols : (RAD + tile_rows) * tile_cols]
+    own_row = (
+        lax.dynamic_slice_in_dim(kv_grads_all, RAD * tile_cols + own_local, 1, 1) + own_grads
+    ).astype(jnp.bfloat16)
+    own_row_given = jnp.dot(own_row[0], w_key.T, preferred_element_type=jnp.float32) + jnp.dot(
+        own_row[1], w_value.T, preferred_element_type=jnp.float32
+    )
+    own_given = lax.dynamic_update_slice_in_dim(own_given, own_row_given, own_local, 0)
 
     grad_in = (
         jnp.dot(query_grads, w_query.T, preferred_element_type=jnp.float32)
-        + jnp.dot(kv_grads[0], w_key.T, preferred_element_type=jnp.float32)
-        + jnp.dot(kv_grads[1], w_value.T, preferred_element_type=jnp.float32)
+        + own_given
+        + received.reshape(tokens, model_width)
     )
     grad_in = grad_in.astype(jnp.bfloat16).reshape(features.shape)
     return (layer_out, grad_in)

time: 164 us -> 134 us (0.82)
  the two profiles are of different devices: /device:TPU:16 before, /device:TPU:0 now
where the time goes in v5:
time: 134 us; the launch traced here: 133 us
  starting transfers between devices  27.9 us (21%)
  matrix products  25.3 us (19%)
  other arithmetic  20.8 us (16%)
  waiting for transfers between devices  19.6 us (15%)
  local copies, waits for them, and re-layouts  19.4 us (14%)
  Pallas kernels  16.5 us (12%)
  between operations  3.84 us (3%)
    ppermute x6, starting transfers between devices, partner(): return lax.ppermute(x, axis, [(i, i ^ 1 << bit) for i in range(size)])  17 us
    pallas_call x1, Pallas kernels, attention(): pl.pallas_call(attention_kernel, grid=(steps,), in_specs=[token_block, ke...  16.5 us
    ppermute x6, waiting for transfers between devices, partner(): return lax.ppermute(x, axis, [(i, i ^ 1 << bit) for i in range(size)])  12.3 us
    ppermute x4, starting transfers between devices, exchange(): got_first = lax.ppermute(first, axis, [(i, i ^ 1) for i in range(size)])  7.53 us
    ppermute x4, waiting for transfers between devices, exchange(): got_first = lax.ppermute(first, axis, [(i, i ^ 1) for i in range(size)])  7.33 us
    convert_element_type x1, other arithmetic, shards(): rounded_grads = kv_grads_all.astype(jnp.bfloat16)  4.41 us
    dot_general x1, matrix products, shards(): jnp.dot(key_features, w_value, preferred_element_type=jnp.float32)  4.09 us
    dot_general x1, matrix products, shards(): jnp.dot(rounded_grads[0], w_key.T, preferred_element_type=jnp.float32)  3.68 us
  transfers between devices with their start and end apart: 14, of which 7 were waited for; matrix products, arithmetic and copies ran while one was open for 16% of the time, Pallas kernels for 0%

profile of v5, /device:TPU:0, one launch (start us, length us, event | category | flops | bytes accessed | tf_op | source)
XLA Modules:
  0.0 133.3 jit_solution(13849702396555728343)
XLA Ops:
  0.7 1.2 broadcast_select_fusion.8
  2.6 1.2 dynamic_slice.10
  6.5 0.7 constant_dynamic-slice_fusion
  7.2 5.7 %collective-permute-start.1 = (bf16[97,1024]{1,0:T(8,128)(2,1)S(1)}, bf16[97,1024]{1,0:T(8,128)(2,1)S(1)}, u32[]{:S(2)}, u32[]{:S(2)}) collective-permute-start(bf16[97,1024]{1,0:T(8,128)(2,1)S(1)} %pad_maximum_fusion.4), channel_id=1, source_target_pairs={{0,8},{8,0},{16,24},{24,16},{1,9},{9,1},{17,25},{25,17},{2,10},{10... | collective-permute-start | bytes 595976 | tf_op jit(solution)/shard_map/ppermute | solution.py:44
  13.2 3.0 %convolution_convert_fusion.4.q_ref = bf16[128,1024]{1,0:T(8,128)(2,1)} fusion(bf16[128,1024]{1,0:T(8,128)(2,1)} %bitcast.72, bf16[1024,1024]{1,0:T(8,128)(2,1)} %param.12), kind=kOutput, calls=%fused_computation.14 | convolution fusion | flops 268566528 | bytes 2621440 | tf_op jit(solution)/shard_map/dot_general | solution.py:212
  16.1 1.6 %convolution_convert_fusion.3.g_ref = bf16[128,1024]{1,0:T(8,128)(2,1)} fusion(bf16[128,1024]{1,0:T(8,128)(2,1)S(1)} %bitcast.81, bf16[1024,1024]{1,0:T(8,128)(2,1)S(1)} %copy-done.1), kind=kOutput, calls=%fused_computation.13 | convolution fusion | flops 268566528 | bytes 2621440 | tf_op jit(solution)/shard_map/dot_general | solution.py:213
  18.8 0.8 select_n.318
  19.6 0.7 slice.159
  20.3 1.7 %pad_maximum_fusion.2 = bf16[122,1024]{1,0:T(8,128)(2,1)} fusion(bf16[2,1024]{1,0:T(2,128)(2,1)S(1)} %broadcast_select_fusion.16, bf16[120,1024]{1,0:T(8,128)(2,1)} %select_n.318), kind=kLoop, calls=%fused_computation.22 | loop fusion | flops 499712 | bytes 499712 | tf_op jit(solution)/shard_map/concatenate | solution.py:43
  22.1 0.9 or_convert_fusion.mask_ref
  23.0 0.8 select_n.316
  24.5 3.4 %collective-permute-start.4 = (bf16[4,1024]{1,0:T(4,128)(2,1)S(1)}, bf16[4,1024]{1,0:T(4,128)(2,1)S(1)}, u32[]{:S(2)}, u32[]{:S(2)}) collective-permute-start(bf16[4,1024]{1,0:T(4,128)(2,1)S(1)} %maximum_select_fusion.3), channel_id=1, source_target_pairs={{0,2},{1,3},{2,0},{3,1},{4,6},{5,7},{6,4},{7,5},{8,10},{9,11},{10,... | collective-permute-start | bytes 24584 | tf_op jit(solution)/shard_map/ppermute | solution.py:34
  28.0 4.4 %collective-permute-done.4 = bf16[4,1024]{1,0:T(4,128)(2,1)S(1)} collective-permute-done((bf16[4,1024]{1,0:T(4,128)(2,1)S(1)}, bf16[4,1024]{1,0:T(4,128)(2,1)S(1)}, u32[]{:S(2)}, u32[]{:S(2)}) %collective-permute-start.4) | collective-permute-done | bytes 8224 | tf_op jit(solution)/shard_map/ppermute | solution.py:34
  32.4 2.7 %collective-permute-start.5 = (bf16[8,1024]{1,0:T(8,128)(2,1)S(1)}, bf16[8,1024]{1,0:T(8,128)(2,1)S(1)}, u32[]{:S(2)}, u32[]{:S(2)}) collective-permute-start(bf16[8,1024]{1,0:T(8,128)(2,1)S(1)} %maximum_select_fusion.2), channel_id=1, source_target_pairs={{0,4},{1,5},{2,6},{3,7},{4,0},{5,1},{6,2},{7,3},{8,12},{9,13},{10,... | collective-permute-start | bytes 49160 | tf_op jit(solution)/shard_map/ppermute | solution.py:34
  35.1 2.0 %collective-permute-done.5 = bf16[8,1024]{1,0:T(8,128)(2,1)S(1)} collective-permute-done((bf16[8,1024]{1,0:T(8,128)(2,1)S(1)}, bf16[8,1024]{1,0:T(8,128)(2,1)S(1)}, u32[]{:S(2)}, u32[]{:S(2)}) %collective-permute-start.5) | collective-permute-done | bytes 16416 | tf_op jit(solution)/shard_map/ppermute | solution.py:34
  37.1 1.8 %collective-permute-start.6 = (bf16[16,1024]{1,0:T(8,128)(2,1)S(1)}, bf16[16,1024]{1,0:T(8,128)(2,1)S(1)}, u32[]{:S(2)}, u32[]{:S(2)}) collective-permute-start(bf16[16,1024]{1,0:T(8,128)(2,1)S(1)} %maximum_select_fusion.1), channel_id=1, source_target_pairs={{0,16},{8,24},{16,0},{24,8},{1,17},{9,25},{17,1},{25,9},{2,18},{10... | collective-permute-start | bytes 98312 | tf_op jit(solution)/shard_map/ppermute | solution.py:34
  39.0 1.1 copy-done.8
  40.1 1.0 collective-permute-done.6
  43.0 4.1 %convolution_convert_fusion.v_ref = bf16[640,1024]{1,0:T(8,128)(2,1)} fusion(bf16[640,1024]{1,0:T(8,128)(2,1)} %broadcast_dynamic-update-slice_fusion, bf16[1024,1024]{1,0:T(8,128)(2,1)S(1)} %copy-done), kind=kOutput, calls=%fused_computation.2 | convolution fusion | flops 1342832640 | bytes 4718592 | tf_op jit(solution)/shard_map/dot_general | solution.py:237
  47.1 2.6 %convolution_convert_fusion.1.k_ref = bf16[640,1024]{1,0:T(8,128)(2,1)} fusion(bf16[640,1024]{1,0:T(8,128)(2,1)S(1)} %copy-done.9, bf16[1024,1024]{1,0:T(8,128)(2,1)S(1)} %copy-done.4), kind=kOutput, calls=%fused_computation.3 | convolution fusion | flops 1342832640 | bytes 4718592 | tf_op jit(solution)/shard_map/dot_general | solution.py:236
  49.7 16.5 %shard_map.122 = (bf16[128,1024]{1,0:T(8,128)(2,1)}, bf16[128,1024]{1,0:T(8,128)(2,1)}, f32[2,640,1024]{2,1,0:T(8,128)}) custom-call(bf16[128,1024]{1,0:T(8,128)(2,1)} %convolution_convert_fusion.4.q_ref, bf16[640,1024]{1,0:T(8,128)(2,1)} %convolution_convert_fusion.1.k_ref, bf16[640,1024]{1,0:T(8,128)(2,1)} %convolution_convert_fusion.v_ref, ...), custom_call_target="tpu_custom_call" | custom-call | flops 2013265920 | bytes 8978432 | tf_op jit(solution)/shard_map/pallas_call | solution.py:138
  66.2 1.0 slice.129
  67.2 4.4 %convert_element_type.81 = bf16[2,640,1024]{2,1,0:T(8,128)(2,1)} convert(f32[2,640,1024]{2,1,0:T(8,128)} %get-tuple-element.7) | non-fusion elementwise | flops 1310720 | bytes 7864320 | tf_op jit(solution)/shard_map/convert_element_type | solution.py:275
  73.1 3.7 %fusion = f32[640,1024]{1,0:T(8,128)S(1)} fusion(bf16[1024,1024]{1,0:T(8,128)(2,1)} %param.13, bf16[2,640,1024]{2,1,0:T(8,128)(2,1)} %convert_element_type.81), kind=kOutput, calls=%fused_computation.6 | convolution fusion | flops 1342177280 | bytes 6029312 | tf_op jit(solution)/shard_map/dot_general | solution.py:276
  76.8 3.1 %fusion.7 = (bf16[640,1024]{1,0:T(8,128)(2,1)S(1)}, f32[640,1024]{1,0:T(8,128)}) fusion(f32[640,1024]{1,0:T(8,128)S(1)} %fusion, bf16[1024,1024]{1,0:T(8,128)(2,1)S(1)} %copy-done, bf16[2,640,1024]{2,1,0:T(8,128)(2,1)S(1)} %copy-done.2), kind=kOutput, calls=%fused_computation.75 | convolution fusion | flops 1343488000 | bytes 9961472 | tf_op jit(solution)/shard_map/dot_general | solution.py:276
  79.9 0.7 broadcast_select_fusion.5
  80.6 0.8 pad_maximum_fusion.1
  81.5 1.4 %collective-permute-start.8 = (bf16[120,1024]{1,0:T(8,128)(2,1)}, bf16[120,1024]{1,0:T(8,128)(2,1)}, u32[]{:S(2)}, u32[]{:S(2)}) collective-permute-start(bf16[120,1024]{1,0:T(8,128)(2,1)} %get-tuple-element.13), channel_id=1, source_target_pairs={{1,2},{3,4},{5,6},{2,1},{4,3},{6,5},{9,10},{11,12},{13,14},{10,9},... | collective-permute-start | bytes 737288 | tf_op jit(solution)/shard_map/ppermute | solution.py:46
  82.8 1.4 %slice.173 = f32[320,1024]{1,0:T(8,128)S(1)} slice(f32[640,1024]{1,0:T(8,128)} %get-tuple-element.31), slice={[0:320], [0:1024]} | slice | bytes 2621440 | tf_op jit(solution)/shard_map/slice | solution.py:298
  84.2 0.9 convert_add_fusion.1
  85.1 0.7 reshape.173
  85.8 1.3 bitcast_add_fusion
  87.8 1.5 %select_n.357 = f32[16,1024]{1,0:T(8,128)} reshape(f32[2,2,1,2,2,1024]{5,4,3,1,0,2:T(2,128)} %copy.19) | data formatting | bytes 131072 | tf_op jit(solution)/shard_map/jit(_where)/select_n | solution.py:74
  89.4 1.5 %subtract_convert_fusion.1 = (bf16[16,1024]{1,0:T(8,128)(2,1)}, bf16[16,1024]{1,0:T(8,128)(2,1)}) fusion(f32[16,1024]{1,0:T(8,128)} %select_n.357), kind=kLoop, calls=%fused_computation.46 | loop fusion | flops 65536 | bytes 131072 | tf_op jit(solution)/shard_map/convert_element_type | solution.py:156
  90.9 1.9 %broadcast_select_fusion.3 = (bf16[120,1024]{1,0:T(8,128)(2,1)}, bf16[120,1024]{1,0:T(8,128)(2,1)}) fusion(bf16[120,1024]{1,0:T(8,128)(2,1)} %collective-permute-done.8, pred[]{:T(512)S(6)} %eq.69, bf16[184,1024]{1,0:T(8,128)(2,1)} %collective-permute-done.7), kind=kLoop, calls=%fused_computation.27 | loop fusion | flops 245760 | bytes 983041 | tf_op jit(solution)/shard_map/jit(_where)/select_n | solution.py:51
  92.8 1.8 %reshape.175 = bf16[20,6,1024]{2,1,0:T(8,128)(2,1)} reshape(bf16[120,1024]{1,0:T(8,128)(2,1)} %get-tuple-element.20) | data formatting | bytes 491520 | tf_op jit(solution)/shard_map/reshape | solution.py:294
  94.5 1.8 %reshape.176 = bf16[20,6,1024]{2,1,0:T(8,128)(2,1)} reshape(bf16[120,1024]{1,0:T(8,128)(2,1)} %get-tuple-element.21) | data formatting | bytes 491520 | tf_op jit(solution)/shard_map/reshape | solution.py:296
  96.3 2.5 %add_convert_fusion = (bf16[20,16,1024]{2,1,0:T(8,128)(2,1)S(1)}, f32[20,16,1024]{2,1,0:T(8,128)}) fusion(f32[20,16,1024]{2,1,0:T(8,128)S(1)} %bitcast.70, bf16[20,6,1024]{2,1,0:T(8,128)(2,1)} %reshape.176, bf16[20,6,1024]{2,1,0:T(8,128)(2,1)} %reshape.175), kind=kLoop, calls=%fused_computation.7 | loop fusion | flops 1638400 | bytes 3768320 | tf_op jit(solution)/shard_map/convert.13
  98.9 1.8 %collective-permute-start.9 = (bf16[128,1024]{1,0:T(8,128)(2,1)S(1)}, bf16[128,1024]{1,0:T(8,128)(2,1)S(1)}, u32[]{:S(2)}, u32[]{:S(2)}) collective-permute-start(bf16[128,1024]{1,0:T(8,128)(2,1)S(1)} %pad_maximum_fusion.3), channel_id=1, source_target_pairs={{0,8},{8,0},{16,24},{24,16},{1,9},{9,1},{17,25},{25,17},{2,10},{10... | collective-permute-start | bytes 786440 | tf_op jit(solution)/shard_map/ppermute | solution.py:44
  100.7 7.2 %collective-permute-done.9 = bf16[128,1024]{1,0:T(8,128)(2,1)S(1)} collective-permute-done((bf16[128,1024]{1,0:T(8,128)(2,1)S(1)}, bf16[128,1024]{1,0:T(8,128)(2,1)S(1)}, u32[]{:S(2)}, u32[]{:S(2)}) %collective-permute-start.9) | collective-permute-done | bytes 262176 | tf_op jit(solution)/shard_map/ppermute | solution.py:44
  108.0 3.0 %collective-permute-start.10 = (f32[2,2,2,1024]{3,0,1,2:T(2,128)S(1)}, f32[2,2,2,1024]{3,0,1,2:T(2,128)S(1)}, u32[]{:S(2)}, u32[]{:S(2)}) collective-permute-start(f32[2,2,2,1024]{3,0,1,2:T(2,128)S(1)} %select_bitcast_fusion), channel_id=1, source_target_pairs={{0,2},{1,3},{2,0},{3,1},{4,6},{5,7},{6,4},{7,5},{8,10},{9,11},{10,... | collective-permute-start | bytes 98312 | tf_op jit(solution)/shard_map/ppermute | solution.py:34
  111.1 2.7 %convolution_convert_fusion.2 = bf16[128,1024]{1,0:T(8,128)(2,1)} fusion(bf16[128,1024]{1,0:T(8,128)(2,1)S(1)} %copy-done.12, bf16[1024,1024]{1,0:T(8,128)(2,1)} %param.15), kind=kOutput, calls=%fused_computation.12 | convolution fusion | flops 268566528 | bytes 2621440 | tf_op jit(solution)/shard_map/dot_general | solution.py:270
  113.8 1.1 slice.164
  115.9 4.4 %collective-permute-done.11 = f32[2,2,1024]{2,0,1:T(2,128)S(1)} collective-permute-done((f32[2,2,1024]{2,0,1:T(2,128)S(1)}, f32[2,2,1024]{2,0,1:T(2,128)S(1)}, u32[]{:S(2)}, u32[]{:S(2)}) %collective-permute-start.11) | collective-permute-done | bytes 16416 | tf_op jit(solution)/shard_map/ppermute | solution.py:34
  120.4 5.8 %collective-permute-start.12 = (f32[2,1024]{1,0:T(2,128)S(1)}, f32[2,1024]{1,0:T(2,128)S(1)}, u32[]{:S(2)}, u32[]{:S(2)}) collective-permute-start(f32[2,1024]{1,0:T(2,128)S(1)} %select_bitcast_fusion.2), channel_id=1, source_target_pairs={{0,16},{8,24},{16,0},{24,8},{1,17},{9,25},{17,1},{25,9},{2,18},{10... | collective-permute-start | bytes 24584 | tf_op jit(solution)/shard_map/ppermute | solution.py:34
  126.2 1.1 fusion.3
  127.8 0.9 add_convert_fusion.1
  130.1 3.1 %fusion.2 = bf16[128,1024]{1,0:T(8,128)(2,1)} fusion(f32[128,1024]{1,0:T(8,128)S(1)} %bitcast.73, f32[128,1024]{1,0:T(8,128)S(1)} %dynamic_update_slice.3, bf16[128,1024]{1,0:T(8,128)(2,1)S(1)} %copy-done.10, bf16[1024,1024]{1,0:T(8,128)(2,1)} %param.12), kind=kOutput, calls=%fused_computation.11 | convolution fusion | flops 268828672 | bytes 3670016 | tf_op jit(solution)/shard_map/dot_general | solution.py:330
  (103 shorter events, 10.1 us)
Async XLA Ops:
  0.6 42.4 %copy-start = (bf16[1024,1024]{1,0:T(8,128)(2,1)S(1)}, bf16[1024,1024]{1,0:T(8,128)(2,1)}, u32[]{:S(2)}) copy-start(bf16[1024,1024]{1,0:T(8,128)(2,1)} %param.14) | copy-start | bytes 6291460
  0.6 15.5 %copy-start.11 = (bf16[8,16,1024]{2,1,0:T(8,128)(2,1)S(1)}, bf16[8,16,1024]{2,1,0:T(8,128)(2,1)}, u32[]{:S(2)}) copy-start(bf16[8,16,1024]{2,1,0:T(8,128)(2,1)} %param.17) | copy-start | bytes 786436
  1.9 15.9 %collective-permute-start = (bf16[96,1024]{1,0:T(8,128)(2,1)S(1)}, bf16[96,1024]{1,0:T(8,128)(2,1)S(1)}, u32[]{:S(2)}, u32[]{:S(2)}) collective-permute-start(bf16[96,1024]{1,0:T(8,128)(2,1)S(1)} %bitcast.83), channel_id=1, source_target_pairs={{8,16},{16,8},{9,17},{17,9},{10,18},{18,10},{11,19},{19,11},{12,20... | collective-permute-start | bytes 589832 | tf_op jit(solution)/shard_map/ppermute | solution.py:46
  7.2 10.7 %collective-permute-start.1 = (bf16[97,1024]{1,0:T(8,128)(2,1)S(1)}, bf16[97,1024]{1,0:T(8,128)(2,1)S(1)}, u32[]{:S(2)}, u32[]{:S(2)}) collective-permute-start(bf16[97,1024]{1,0:T(8,128)(2,1)S(1)} %pad_maximum_fusion.4), channel_id=1, source_target_pairs={{0,8},{8,0},{16,24},{24,16},{1,9},{9,1},{17,25},{25,17},{2,10},{10... | collective-permute-start | bytes 595976 | tf_op jit(solution)/shard_map/ppermute | solution.py:44
  13.1 3.0 %copy-start.1 = (bf16[1024,1024]{1,0:T(8,128)(2,1)S(1)}, bf16[1024,1024]{1,0:T(8,128)(2,1)}, u32[]{:S(2)}) copy-start(bf16[1024,1024]{1,0:T(8,128)(2,1)} %param.15) | copy-start | bytes 6291460
  13.1 4.6 %copy-start.16 = (s32[640]{0:T(1024)S(1)}, s32[640]{0:T(1024)}, u32[]{:S(2)}) copy-start(s32[640]{0:T(1024)} %constant.140.clone) | copy-start | bytes 7684
  13.1 4.6 %copy-start.17 = (s32[640]{0:T(1024)S(1)}, s32[640]{0:T(1024)}, u32[]{:S(2)}) copy-start(s32[640]{0:T(1024)} %constant.139.clone) | copy-start | bytes 7684
  16.1 2.5 %copy-start.3 = (bf16[8,16,1024]{2,1,0:T(8,128)(2,1)S(1)}, bf16[8,16,1024]{2,1,0:T(8,128)(2,1)}, u32[]{:S(2)}) copy-start(bf16[8,16,1024]{2,1,0:T(8,128)(2,1)} %param.11) | copy-start | bytes 786436
  17.7 4.3 %copy-start.20 = (s32[32]{0:T(128)S(1)}, s32[32]{0:T(128)}, u32[]{:S(2)}) copy-start(s32[32]{0:T(128)} %constant.160) | copy-start | bytes 388
  17.9 0.7 copy-start.13
  18.0 4.1 %copy-start.18 = (pred[640]{0:T(1024)(128)(4,1)S(1)}, pred[640]{0:T(1024)(128)(4,1)}, u32[]{:S(2)}) copy-start(pred[640]{0:T(1024)(128)(4,1)} %constant.158) | copy-start | bytes 1924
  18.0 4.1 %copy-start.19 = (pred[640]{0:T(1024)(128)(4,1)S(1)}, pred[640]{0:T(1024)(128)(4,1)}, u32[]{:S(2)}) copy-start(pred[640]{0:T(1024)(128)(4,1)} %constant.157) | copy-start | bytes 1924
  22.0 2.5 %collective-permute-start.3 = (bf16[122,1024]{1,0:T(8,128)(2,1)}, bf16[122,1024]{1,0:T(8,128)(2,1)S(1)}, u32[]{:S(2)}, u32[]{:S(2)}) collective-permute-start(bf16[122,1024]{1,0:T(8,128)(2,1)} %pad_maximum_fusion.2), channel_id=1, source_target_pairs={{0,1},{1,0},{2,3},{3,2},{4,5},{5,4},{6,7},{7,6},{8,9},{9,8},{10,11... | collective-permute-start | bytes 749576 | tf_op jit(solution)/shard_map/ppermute | solution.py:44
  23.8 11.3 %collective-permute-start.2 = (bf16[120,1024]{1,0:T(8,128)(2,1)}, bf16[120,1024]{1,0:T(8,128)(2,1)S(1)}, u32[]{:S(2)}, u32[]{:S(2)}) collective-permute-start(bf16[120,1024]{1,0:T(8,128)(2,1)} %select_n.316), channel_id=1, source_target_pairs={{1,2},{3,4},{5,6},{2,1},{4,3},{6,5},{9,10},{11,12},{13,14},{10,9},... | collective-permute-start | bytes 737288 | tf_op jit(solution)/shard_map/ppermute | solution.py:46
  24.5 7.8 %collective-permute-start.4 = (bf16[4,1024]{1,0:T(4,128)(2,1)S(1)}, bf16[4,1024]{1,0:T(4,128)(2,1)S(1)}, u32[]{:S(2)}, u32[]{:S(2)}) collective-permute-start(bf16[4,1024]{1,0:T(4,128)(2,1)S(1)} %maximum_select_fusion.3), channel_id=1, source_target_pairs={{0,2},{1,3},{2,0},{3,1},{4,6},{5,7},{6,4},{7,5},{8,10},{9,11},{10,... | collective-permute-start | bytes 24584 | tf_op jit(solution)/shard_map/ppermute | solution.py:34
  32.4 4.7 %collective-permute-start.5 = (bf16[8,1024]{1,0:T(8,128)(2,1)S(1)}, bf16[8,1024]{1,0:T(8,128)(2,1)S(1)}, u32[]{:S(2)}, u32[]{:S(2)}) collective-permute-start(bf16[8,1024]{1,0:T(8,128)(2,1)S(1)} %maximum_select_fusion.2), channel_id=1, source_target_pairs={{0,4},{1,5},{2,6},{3,7},{4,0},{5,1},{6,2},{7,3},{8,12},{9,13},{10,... | collective-permute-start | bytes 49160 | tf_op jit(solution)/shard_map/ppermute | solution.py:34
  37.1 4.0 %collective-permute-start.6 = (bf16[16,1024]{1,0:T(8,128)(2,1)S(1)}, bf16[16,1024]{1,0:T(8,128)(2,1)S(1)}, u32[]{:S(2)}, u32[]{:S(2)}) collective-permute-start(bf16[16,1024]{1,0:T(8,128)(2,1)S(1)} %maximum_select_fusion.1), channel_id=1, source_target_pairs={{0,16},{8,24},{16,0},{24,8},{1,17},{9,25},{17,1},{25,9},{2,18},{10... | collective-permute-start | bytes 98312 | tf_op jit(solution)/shard_map/ppermute | solution.py:34
  38.9 1.1 copy-start.8
  43.0 4.1 %copy-start.4 = (bf16[1024,1024]{1,0:T(8,128)(2,1)S(1)}, bf16[1024,1024]{1,0:T(8,128)(2,1)}, u32[]{:S(2)}) copy-start(bf16[1024,1024]{1,0:T(8,128)(2,1)} %param.13) | copy-start | bytes 6291460
  43.0 4.1 %copy-start.9 = (bf16[640,1024]{1,0:T(8,128)(2,1)S(1)}, bf16[640,1024]{1,0:T(8,128)(2,1)}, u32[]{:S(2)}) copy-start(bf16[640,1024]{1,0:T(8,128)(2,1)} %broadcast_dynamic-update-slice_fusion) | copy-start | bytes 3932164
  72.0 0.7 copy-start.6
  72.0 0.8 copy-start.7
  73.1 3.7 %copy-start.2 = (bf16[2,640,1024]{2,1,0:T(8,128)(2,1)S(1)}, bf16[2,640,1024]{2,1,0:T(8,128)(2,1)}, u32[]{:S(2)}) copy-start(bf16[2,640,1024]{2,1,0:T(8,128)(2,1)} %convert_element_type.81) | copy-start | bytes 7864324
  81.4 2.8 %collective-permute-start.7 = (bf16[184,1024]{1,0:T(8,128)(2,1)}, bf16[184,1024]{1,0:T(8,128)(2,1)}, u32[]{:S(2)}, u32[]{:S(2)}) collective-permute-start(bf16[184,1024]{1,0:T(8,128)(2,1)} %pad_maximum_fusion.1), channel_id=1, source_target_pairs={{0,1},{1,0},{2,3},{3,2},{4,5},{5,4},{6,7},{7,6},{8,9},{9,8},{10,11... | collective-permute-start | bytes 1130504 | tf_op jit(solution)/shard_map/ppermute | solution.py:44
  81.5 9.4 %collective-permute-start.8 = (bf16[120,1024]{1,0:T(8,128)(2,1)}, bf16[120,1024]{1,0:T(8,128)(2,1)}, u32[]{:S(2)}, u32[]{:S(2)}) collective-permute-start(bf16[120,1024]{1,0:T(8,128)(2,1)} %get-tuple-element.13), channel_id=1, source_target_pairs={{1,2},{3,4},{5,6},{2,1},{4,3},{6,5},{9,10},{11,12},{13,14},{10,9},... | collective-permute-start | bytes 737288 | tf_op jit(solution)/shard_map/ppermute | solution.py:46
  96.3 2.5 %copy-start.14 = (bf16[16,1024]{1,0:T(8,128)(2,1)S(1)}, bf16[16,1024]{1,0:T(8,128)(2,1)}, u32[]{:S(2)}) copy-start(bf16[16,1024]{1,0:T(8,128)(2,1)} %get-tuple-element.8) | copy-start | bytes 98308
  96.3 2.6 %copy-start.15 = (bf16[16,1024]{1,0:T(8,128)(2,1)S(1)}, bf16[16,1024]{1,0:T(8,128)(2,1)}, u32[]{:S(2)}) copy-start(bf16[16,1024]{1,0:T(8,128)(2,1)} %get-tuple-element.9) | copy-start | bytes 98308
  98.8 12.3 %copy-start.12 = (bf16[128,1024]{1,0:T(8,128)(2,1)S(1)}, bf16[128,1024]{1,0:T(8,128)(2,1)}, u32[]{:S(2)}) copy-start(bf16[128,1024]{1,0:T(8,128)(2,1)} %get-tuple-element.5) | copy-start | bytes 786436
  98.9 9.0 %collective-permute-start.9 = (bf16[128,1024]{1,0:T(8,128)(2,1)S(1)}, bf16[128,1024]{1,0:T(8,128)(2,1)S(1)}, u32[]{:S(2)}, u32[]{:S(2)}) collective-permute-start(bf16[128,1024]{1,0:T(8,128)(2,1)S(1)} %pad_maximum_fusion.3), channel_id=1, source_target_pairs={{0,8},{8,0},{16,24},{24,16},{1,9},{9,1},{17,25},{25,17},{2,10},{10... | collective-permute-start | bytes 786440 | tf_op jit(solution)/shard_map/ppermute | solution.py:44
  108.0 7.6 %collective-permute-start.10 = (f32[2,2,2,1024]{3,0,1,2:T(2,128)S(1)}, f32[2,2,2,1024]{3,0,1,2:T(2,128)S(1)}, u32[]{:S(2)}, u32[]{:S(2)}) collective-permute-start(f32[2,2,2,1024]{3,0,1,2:T(2,128)S(1)} %select_bitcast_fusion), channel_id=1, source_target_pairs={{0,2},{1,3},{2,0},{3,1},{4,6},{5,7},{6,4},{7,5},{8,10},{9,11},{10,... | collective-permute-start | bytes 98312 | tf_op jit(solution)/shard_map/ppermute | solution.py:34
  114.9 1.0 collective-permute-start.13
  115.6 13.7 %copy-start.5 = (bf16[1024,1024]{1,0:T(8,128)(2,1)S(1)}, bf16[1024,1024]{1,0:T(8,128)(2,1)}, u32[]{:S(2)}) copy-start(bf16[1024,1024]{1,0:T(8,128)(2,1)} %param.13) | copy-start | bytes 6291460
  115.6 4.7 %collective-permute-start.11 = (f32[2,2,1024]{2,0,1:T(2,128)S(1)}, f32[2,2,1024]{2,0,1:T(2,128)S(1)}, u32[]{:S(2)}, u32[]{:S(2)}) collective-permute-start(f32[2,2,1024]{2,0,1:T(2,128)S(1)} %select_bitcast_fusion.1), channel_id=1, source_target_pairs={{0,4},{1,5},{2,6},{3,7},{4,0},{5,1},{6,2},{7,3},{8,12},{9,13},{10,... | collective-permute-start | bytes 49160 | tf_op jit(solution)/shard_map/ppermute | solution.py:34
  120.4 7.4 %collective-permute-start.12 = (f32[2,1024]{1,0:T(2,128)S(1)}, f32[2,1024]{1,0:T(2,128)S(1)}, u32[]{:S(2)}, u32[]{:S(2)}) collective-permute-start(f32[2,1024]{1,0:T(2,128)S(1)} %select_bitcast_fusion.2), channel_id=1, source_target_pairs={{0,16},{8,24},{16,0},{24,8},{1,17},{9,25},{17,1},{25,9},{2,18},{10... | collective-permute-start | bytes 24584 | tf_op jit(solution)/shard_map/ppermute | solution.py:34
  128.7 1.4 %copy-start.10 = (bf16[128,1024]{1,0:T(8,128)(2,1)S(1)}, bf16[128,1024]{1,0:T(8,128)(2,1)}, u32[]{:S(2)}) copy-start(bf16[128,1024]{1,0:T(8,128)(2,1)} %get-tuple-element.6) | copy-start | bytes 786436

commit v6 on v5

--- a/solution.py
+++ b/solution.py
@@ -1,3 +1,4 @@
+import functools
 import math
 
 import jax
@@ -74,7 +75,7 @@
     return jnp.where(high, upper, lower), jnp.where(high, lower, upper)
 
 
-def attention_kernel(q_ref, k_ref, v_ref, g_ref, mask_ref, o_ref, dq_ref, dkv_ref):
+def attention_kernel(own, first, last, q_ref, k_ref, v_ref, g_ref, mask_ref, o_ref, dq_ref, dkv_ref, wide_ref):
     head_size = q_ref.shape[1] // 2
     score_scale = 1.0 / math.sqrt(head_size)
     q = q_ref[...]
@@ -118,11 +119,15 @@
         )
     o_ref[...] = out.astype(o_ref.dtype)
     dq_ref[...] = dq.astype(dq_ref.dtype)
-    dkv_ref[0] = dk
-    dkv_ref[1] = dv
-
-
-def attention(queries, keys, values, grad_attended, keep):
+    dkv_ref[0] = dk.astype(dkv_ref.dtype)
+    dkv_ref[1] = dv.astype(dkv_ref.dtype)
+    wide_ref[0, :own] = dk[:own]
+    wide_ref[1, :own] = dv[:own]
+    wide_ref[0, own:] = dk[first:last]
+    wide_ref[1, own:] = dv[first:last]
+
+
+def attention(queries, keys, values, grad_attended, keep, first, last):
     tokens, model_width = queries.shape
     key_count = keys.shape[0]
     lanes = 2 * (model_width // HEADS)
@@ -131,19 +136,22 @@
     key_block = pl.BlockSpec((key_count, lanes), lambda i: (0, i))
     mask_block = pl.BlockSpec((tokens, key_count), lambda i: (0, 0))
     grads_block = pl.BlockSpec((2, key_count, lanes), lambda i: (0, 0, i))
+    wide_rows = tokens + last - first
+    wide_block = pl.BlockSpec((2, wide_rows, lanes), lambda i: (0, 0, i))
     flops = 2 * 2 * 6 * tokens * key_count * model_width
     moved = 2 * (3 * tokens * model_width + 2 * key_count * model_width) + 4 * (
         tokens * key_count + 2 * key_count * model_width
     )
     return pl.pallas_call(
-        attention_kernel,
+        functools.partial(attention_kernel, tokens, first, last),
         grid=(steps,),
         in_specs=[token_block, key_block, key_block, token_block, mask_block],
-        out_specs=[token_block, token_block, grads_block],
+        out_specs=[token_block, token_block, grads_block, wide_block],
         out_shape=[
             jax.ShapeDtypeStruct((tokens, model_width), jnp.bfloat16),
             jax.ShapeDtypeStruct((tokens, model_width), jnp.bfloat16),
-            jax.ShapeDtypeStruct((2, key_count, model_width), jnp.float32),
+            jax.ShapeDtypeStruct((2, key_count, model_width), jnp.bfloat16),
+            jax.ShapeDtypeStruct((2, wide_rows, model_width), jnp.float32),
         ],
         cost_estimate=pl.CostEstimate(
             flops=flops, transcendentals=HEADS * tokens * key_count, bytes_accessed=moved
@@ -177,6 +185,11 @@
     col_bits = bits(col_count)
     all_bits = col_bits + bits(row_count)
     ext_rows = tile_rows + 2 * RAD
+    band_keys = RAD * tile_cols
+    strip_keys = ext_rows * RAD
+    frame_keys = tokens + 2 * band_keys + 2 * strip_keys
+    used = frame_keys + device_count
+    key_count = -(-used // 128) * 128
 
     flat_tokens = features.reshape(-1, model_width)
 
@@ -214,38 +227,47 @@
         grad_out.reshape(-1, model_width), w_out.T, preferred_element_type=jnp.float32
     ).astype(jnp.bfloat16)
 
+    key_features = jnp.concatenate(
+        [
+            flat_tokens,
+            from_above,
+            from_below,
+            from_left,
+            from_right,
+            jnp.zeros((key_count - frame_keys, model_width), features.dtype),
+        ],
+        axis=0,
+    )
+    keys = jnp.dot(key_features, w_key, preferred_element_type=jnp.float32).astype(jnp.bfloat16)
+    values = jnp.dot(key_features, w_value, preferred_element_type=jnp.float32).astype(
+        jnp.bfloat16
+    )
+
     for position in order[2:]:
         gathered = gather_step(gathered, partner(gathered, position), position)
     global_features = jnp.take(gathered, jnp.asarray(gather_order(order, device_count)), axis=0)
-
-    own_keys = ext_rows * tile_cols
-    strip_keys = ext_rows * RAD
-    frame_keys = own_keys + 2 * strip_keys
-    used = frame_keys + device_count
-    key_count = -(-used // 128) * 128
-    key_features = jnp.concatenate(
-        [
-            extended.reshape(own_keys, model_width),
-            from_left,
-            from_right,
-            global_features,
-            jnp.zeros((key_count - used, model_width), features.dtype),
-        ],
-        axis=0,
-    )
-    keys = jnp.dot(key_features, w_key, preferred_element_type=jnp.float32).astype(jnp.bfloat16)
-    values = jnp.dot(key_features, w_value, preferred_element_type=jnp.float32).astype(
-        jnp.bfloat16
-    )
-
-    a, b = np.meshgrid(np.arange(ext_rows), np.arange(tile_cols), indexing="ij")
-    s, t = np.meshgrid(np.arange(ext_rows), np.arange(RAD), indexing="ij")
+    global_keys = jnp.dot(global_features, w_key, preferred_element_type=jnp.float32)
+    global_values = jnp.dot(global_features, w_value, preferred_element_type=jnp.float32)
+    keys = lax.dynamic_update_slice_in_dim(keys, global_keys.astype(jnp.bfloat16), frame_keys, 0)
+    values = lax.dynamic_update_slice_in_dim(
+        values, global_values.astype(jnp.bfloat16), frame_keys, 0
+    )
+
+    def grid(height, width, row0, col0):
+        a, b = np.meshgrid(np.arange(height) + row0, np.arange(width) + col0, indexing="ij")
+        return a.reshape(-1), b.reshape(-1)
+
+    parts = [
+        grid(tile_rows, tile_cols, RAD, RAD),
+        grid(RAD, tile_cols, 0, RAD),
+        grid(RAD, tile_cols, RAD + tile_rows, RAD),
+        grid(ext_rows, RAD, 0, 0),
+        grid(ext_rows, RAD, 0, RAD + tile_cols),
+    ]
     key_rows = np.zeros(key_count, np.int32)
     key_cols = np.zeros(key_count, np.int32)
-    key_rows[:frame_keys] = np.concatenate([a.reshape(-1), s.reshape(-1), s.reshape(-1)])
-    key_cols[:frame_keys] = np.concatenate(
-        [b.reshape(-1) + RAD, t.reshape(-1), t.reshape(-1) + RAD + tile_cols]
-    )
+    key_rows[:frame_keys] = np.concatenate([p[0] for p in parts])
+    key_cols[:frame_keys] = np.concatenate([p[1] for p in parts])
     kind = np.full(key_count, 2, np.int32)
     kind[:frame_keys] = 0
     kind[frame_keys:used] = 1
@@ -265,27 +287,32 @@
     key_kind = jnp.asarray(kind)[None, :]
     keep = ((inside & (key_kind == 0)) | (key_kind == 1)).astype(jnp.float32)
 
-    attended, query_grads, kv_grads_all = attention(queries, keys, values, grad_attended, keep)
+    attended, query_grads, rounded_grads, wide_grads = attention(
+        queries, keys, values, grad_attended, keep, frame_keys, used
+    )
     layer_out = (
         jnp.dot(attended, w_out, preferred_element_type=jnp.float32)
         .astype(jnp.bfloat16)
         .reshape(features.shape)
     )
 
-    rounded_grads = kv_grads_all.astype(jnp.bfloat16)
-    given = jnp.dot(rounded_grads[0], w_key.T, preferred_element_type=jnp.float32) + jnp.dot(
-        rounded_grads[1], w_value.T, preferred_element_type=jnp.float32
-    )
-
-    scatter = kv_grads_all[:, frame_keys:used].reshape((2,) + (2,) * all_bits + (model_width,))
+    def given(lo, hi):
+        return jnp.dot(rounded_grads[0, lo:hi], w_key.T, preferred_element_type=jnp.float32) + jnp.dot(
+            rounded_grads[1, lo:hi], w_value.T, preferred_element_type=jnp.float32
+        )
+
+    scatter = wide_grads[:, tokens:].reshape(
+        (2,) + (2,) * all_bits + (model_width,)
+    )
     left = list(range(all_bits - 1, -1, -1))
     back_order = [0, col_bits] + list(range(1, col_bits)) + list(range(col_bits + 1, all_bits))
 
+    strips_from = tokens + 2 * band_keys
     keep_part, send_part = scatter_split(scatter, left, back_order[0])
     strip_shape = (ext_rows, RAD, model_width)
     from_left, from_right, got = exchange(
-        given[own_keys : own_keys + strip_keys].astype(jnp.bfloat16),
-        given[own_keys + strip_keys : frame_keys].astype(jnp.bfloat16),
+        given(strips_from, strips_from + strip_keys).astype(jnp.bfloat16),
+        given(strips_from + strip_keys, frame_keys).astype(jnp.bfloat16),
         "cols",
         split_wide(send_part.reshape(-1, model_width)),
     )
@@ -295,12 +322,15 @@
     ) + jnp.pad(
         from_right.astype(jnp.float32).reshape(strip_shape), ((0, 0), (tile_cols - RAD, 0), (0, 0))
     )
-    extended_given = given[:own_keys].reshape(ext_rows, tile_cols, model_width) + received
+    band_shape = (RAD, tile_cols, model_width)
     keep_part, send_part = scatter_split(scatter, left, back_order[1])
-    band_shape = (RAD, tile_cols, model_width)
     from_above, from_below, got = exchange(
-        extended_given[:RAD].reshape(-1, model_width).astype(jnp.bfloat16),
-        extended_given[RAD + tile_rows :].reshape(-1, model_width).astype(jnp.bfloat16),
+        (given(tokens, tokens + band_keys).reshape(band_shape) + received[:RAD])
+        .reshape(-1, model_width)
+        .astype(jnp.bfloat16),
+        (given(tokens + band_keys, strips_from).reshape(band_shape) + received[RAD + tile_rows :])
+        .reshape(-1, model_width)
+        .astype(jnp.bfloat16),
         "rows",
         split_wide(send_part.reshape(-1, model_width)),
     )
@@ -317,10 +347,10 @@
         scatter = keep_part + partner(send_part, position)
     own_grads = scatter.reshape(2, 1, model_width)
 
-    own_given = given[RAD * tile_cols : (RAD + tile_rows) * tile_cols]
-    own_row = (
-        lax.dynamic_slice_in_dim(kv_grads_all, RAD * tile_cols + own_local, 1, 1) + own_grads
-    ).astype(jnp.bfloat16)
+    own_given = given(0, tokens)
+    own_row = (lax.dynamic_slice_in_dim(wide_grads, own_local, 1, 1) + own_grads).astype(
+        jnp.bfloat16
+    )
     own_row_given = jnp.dot(own_row[0], w_key.T, preferred_element_type=jnp.float32) + jnp.dot(
         own_row[1], w_value.T, preferred_element_type=jnp.float32
     )

time: 134 us -> 130 us (0.970)
  matrix products: 25.3 us -> 44.1 us
  waiting for transfers between devices: 19.6 us -> 10.6 us
  other arithmetic: 20.8 us -> 11.9 us
  local copies, waits for them, and re-layouts: 19.4 us -> 12.1 us
  starting transfers between devices: 27.9 us -> 30.2 us
    dot_general x2 -> x12, matrix products: 6.8 us -> 26.4 us  [the longest x5 11.5 us: given(): jnp.dot(rounded_grads[1, lo:hi], w_value.T, preferred_element_type=jnp.fl...]
    ppermute x6, waiting for transfers between devices: 12.3 us -> 6.08 us  [partner(): return lax.ppermute(x, axis, [(i, i ^ 1 << bit) for i in range(size)])]
    convert_element_type x2 -> x1, other arithmetic: 5.27 us -> 0.86 us  [shards(): (lax.dynamic_slice_in_dim(wide_grads, own_local, 1, 1) + own_grads).astyp...]
    unnamed x2 -> x4, other arithmetic: 0.12 us -> 2.99 us
    ppermute x4, waiting for transfers between devices: 7.33 us -> 4.48 us  [exchange(): got_first = lax.ppermute(first, axis, [(i, i ^ 1) for i in range(size)])]
    another operation x1 -> x0, other arithmetic: 2.51 us -> none
    concatenate x4, other arithmetic: 2.52 us -> 0.08 us  [exchange(): first = jnp.concatenate([first, rider], axis=rider_dim)]
    select_n x4, local copies, waits for them, and re-layouts: 2.39 us -> 0.3 us  [scatter_split(): return (jnp.where(high, upper, lower), jnp.where(high, lower, upper))]
  transfers between devices with their start and end apart: 14 -> 14, of which waited for: 7 -> 6; matrix products, arithmetic and copies ran while one was open for 16% -> 20% of each run, Pallas kernels for 0% -> 0%
where the time goes in v6:
time: 130 us; the launch traced here: 129 us
  matrix products  44.1 us (34%)
  starting transfers between devices  30.2 us (23%)
  Pallas kernels  16.5 us (13%)
  local copies, waits for them, and re-layouts  12.1 us (9%)
  other arithmetic  11.9 us (9%)
  waiting for transfers between devices  10.6 us (8%)
  between operations  3.84 us (3%)
    ppermute x6, starting transfers between devices, partner(): return lax.ppermute(x, axis, [(i, i ^ 1 << bit) for i in range(size)])  17.1 us
    pallas_call x1, Pallas kernels, attention(): pl.pallas_call(functools.partial(attention_kernel, tokens, first, last),...  16.5 us
    dot_general x5, matrix products, given(): jnp.dot(rounded_grads[1, lo:hi], w_value.T, preferred_element_type=jnp.fl...  11.5 us
    dot_general x5, matrix products, given(): jnp.dot(rounded_grads[0, lo:hi], w_key.T, preferred_element_type=jnp.floa...  11.2 us
    ppermute x4, starting transfers between devices, exchange(): got_first = lax.ppermute(first, axis, [(i, i ^ 1) for i in range(size)])  9.56 us
    ppermute x6, waiting for transfers between devices, partner(): return lax.ppermute(x, axis, [(i, i ^ 1 << bit) for i in range(size)])  6.08 us
    ppermute x4, waiting for transfers between devices, exchange(): got_first = lax.ppermute(first, axis, [(i, i ^ 1) for i in range(size)])  4.48 us
    dot_general x1, matrix products, shards(): jnp.dot(key_features, w_value, preferred_element_type=jnp.float32)  3.96 us
  transfers between devices with their start and end apart: 14, of which 6 were waited for; matrix products, arithmetic and copies ran while one was open for 20% of the time, Pallas kernels for 0%

profile of v6, /device:TPU:0, one launch (start us, length us, event | category | flops | bytes accessed | tf_op | source)
XLA Modules:
  0.0 129.1 jit_solution(10104946714966093575)
XLA Ops:
  0.7 1.2 broadcast_select_fusion.8
  2.6 1.2 dynamic_slice.10
  7.2 5.7 %collective-permute-start.1 = (bf16[97,1024]{1,0:T(8,128)(2,1)S(1)}, bf16[97,1024]{1,0:T(8,128)(2,1)S(1)}, u32[]{:S(2)}, u32[]{:S(2)}) collective-permute-start(bf16[97,1024]{1,0:T(8,128)(2,1)S(1)} %pad_maximum_fusion.4), channel_id=1, source_target_pairs={{0,8},{8,0},{16,24},{24,16},{1,9},{9,1},{17,25},{25,17},{2,10},{10... | collective-permute-start | bytes 595976 | tf_op jit(solution)/shard_map/ppermute | solution.py:45
  13.0 1.7 %constant_dynamic-update-slice_fusion.2 = bf16[640,1024]{1,0:T(8,128)(2,1)} fusion(bf16[128,1024]{1,0:T(8,128)(2,1)} %bitcast.106), kind=kLoop, calls=%fused_computation.90 | loop fusion | bytes 524288
  14.8 3.0 %convolution_convert_fusion.4.q_ref = bf16[128,1024]{1,0:T(8,128)(2,1)} fusion(bf16[128,1024]{1,0:T(8,128)(2,1)} %bitcast.107, bf16[1024,1024]{1,0:T(8,128)(2,1)} %param.12), kind=kOutput, calls=%fused_computation.13 | convolution fusion | flops 268566528 | bytes 2621440 | tf_op jit(solution)/shard_map/dot_general | solution.py:225
  17.8 1.6 %convolution_convert_fusion.3.g_ref = bf16[128,1024]{1,0:T(8,128)(2,1)} fusion(bf16[128,1024]{1,0:T(8,128)(2,1)S(1)} %bitcast.118, bf16[1024,1024]{1,0:T(8,128)(2,1)S(1)} %copy-done.5), kind=kOutput, calls=%fused_computation.12 | convolution fusion | flops 268566528 | bytes 2621440 | tf_op jit(solution)/shard_map/dot_general | solution.py:226
  19.4 0.7 constant_dynamic-update-slice_fusion.1
  20.1 0.7 constant_dynamic-update-slice_fusion
  22.0 3.0 %collective-permute-start.3 = (bf16[122,1024]{1,0:T(8,128)(2,1)S(1)}, bf16[122,1024]{1,0:T(8,128)(2,1)S(1)}, u32[]{:S(2)}, u32[]{:S(2)}) collective-permute-start(bf16[122,1024]{1,0:T(8,128)(2,1)S(1)} %pad_maximum_fusion.2), channel_id=1, source_target_pairs={{0,1},{1,0},{2,3},{3,2},{4,5},{5,4},{6,7},{7,6},{8,9},{9,8},{10,11... | collective-permute-start | bytes 749576 | tf_op jit(solution)/shard_map/ppermute | solution.py:45
  25.0 0.9 or_convert_fusion.mask_ref
  26.2 1.7 %collective-permute-start.4 = (bf16[4,1024]{1,0:T(4,128)(2,1)S(1)}, bf16[4,1024]{1,0:T(4,128)(2,1)S(1)}, u32[]{:S(2)}, u32[]{:S(2)}) collective-permute-start(bf16[4,1024]{1,0:T(4,128)(2,1)S(1)} %maximum_select_fusion.3), channel_id=1, source_target_pairs={{0,2},{1,3},{2,0},{3,1},{4,6},{5,7},{6,4},{7,5},{8,10},{9,11},{10,... | collective-permute-start | bytes 24584 | tf_op jit(solution)/shard_map/ppermute | solution.py:35
  27.9 0.8 select_dynamic-update-slice_fusion.1
  28.6 0.8 select_dynamic-update-slice_fusion
  30.1 3.6 %collective-permute-start.5 = (bf16[8,1024]{1,0:T(8,128)(2,1)S(1)}, bf16[8,1024]{1,0:T(8,128)(2,1)S(1)}, u32[]{:S(2)}, u32[]{:S(2)}) collective-permute-start(bf16[8,1024]{1,0:T(8,128)(2,1)S(1)} %maximum_select_fusion.2), channel_id=1, source_target_pairs={{0,4},{1,5},{2,6},{3,7},{4,0},{5,1},{6,2},{7,3},{8,12},{9,13},{10,... | collective-permute-start | bytes 49160 | tf_op jit(solution)/shard_map/ppermute | solution.py:35
  33.7 4.0 %convolution_convert_fusion = bf16[640,1024]{1,0:T(8,128)(2,1)} fusion(bf16[640,1024]{1,0:T(8,128)(2,1)} %broadcast_dynamic-update-slice_fusion, bf16[1024,1024]{1,0:T(8,128)(2,1)S(1)} %copy-done), kind=kOutput, calls=%fused_computation.1 | convolution fusion | flops 1342832640 | bytes 4718592 | tf_op jit(solution)/shard_map/dot_general | solution.py:242
  37.9 2.6 %convolution_convert_fusion.1 = bf16[640,1024]{1,0:T(8,128)(2,1)} fusion(bf16[640,1024]{1,0:T(8,128)(2,1)S(1)} %copy-done.18, bf16[1024,1024]{1,0:T(8,128)(2,1)S(1)} %copy-done.1), kind=kOutput, calls=%fused_computation.2 | convolution fusion | flops 1342832640 | bytes 4718592 | tf_op jit(solution)/shard_map/dot_general | solution.py:241
  40.6 1.0 collective-permute-done.6
  42.3 2.7 %fusion.5.k_ref = bf16[640,1024]{1,0:T(8,128)(2,1)} fusion(bf16[640,1024]{1,0:T(8,128)(2,1)} %convolution_convert_fusion.1, bf16[32,1024]{1,0:T(8,128)(2,1)S(1)} %gather_fusion, bf16[1024,1024]{1,0:T(8,128)(2,1)} %param.13), kind=kOutput, calls=%fused_computation.19 | convolution fusion | flops 67141632 | bytes 2228224 | tf_op jit(solution)/shard_map/dot_general | solution.py:249
  44.9 1.1 fusion.4.v_ref
  46.0 16.5 %shard_map.122 = (bf16[128,1024]{1,0:T(8,128)(2,1)}, bf16[128,1024]{1,0:T(8,128)(2,1)}, bf16[2,640,1024]{2,1,0:T(8,128)(2,1)}, f32[2,160,1024]{2,1,0:T(8,128)}) custom-call(bf16[128,1024]{1,0:T(8,128)(2,1)} %convolution_convert_fusion.4.q_ref, bf16[640,1024]{1,0:T(8,128)(2,1)} %fusion.5.k_ref, bf16[640,1024]{1,0:T(8,128)(2,1)} %fusion.4.v_ref, ...), custom_call_target="tpu_custom_call" | custom-call | flops 2013265920 | bytes 8978432 | tf_op jit(solution)/shard_map/pallas_call | solution.py:145
  62.5 3.4 %fusion.24 = f32[96,1024]{1,0:T(8,128)} fusion(bf16[1024,1024]{1,0:T(8,128)(2,1)} %param.13, bf16[2,640,1024]{2,1,0:T(8,128)(2,1)} %get-tuple-element.8), kind=kOutput, calls=%fused_computation.55 | convolution fusion | flops 201326592 | bytes 2686976 | tf_op jit(solution)/shard_map/dot_general | solution.py:300
  65.9 2.5 %fusion.27 = f32[96,1024]{1,0:T(8,128)} fusion(bf16[1024,1024]{1,0:T(8,128)(2,1)S(1)} %copy-done.2, bf16[2,640,1024]{2,1,0:T(8,128)(2,1)} %get-tuple-element.8), kind=kOutput, calls=%fused_computation.58 | convolution fusion | flops 201326592 | bytes 2686976 | tf_op jit(solution)/shard_map/dot_general | solution.py:300
  68.4 1.8 %fusion.14 = f32[120,1024]{1,0:T(8,128)S(1)} fusion(bf16[1024,1024]{1,0:T(8,128)(2,1)S(1)} %copy-done.2, bf16[2,640,1024]{2,1,0:T(8,128)(2,1)} %get-tuple-element.8), kind=kOutput, calls=%fused_computation.38 | convolution fusion | flops 251658240 | bytes 2834432 | tf_op jit(solution)/shard_map/dot_general | solution.py:300
  70.1 1.8 %fusion.17 = f32[120,1024]{1,0:T(8,128)S(1)} fusion(bf16[1024,1024]{1,0:T(8,128)(2,1)S(1)} %copy-done.2, bf16[2,640,1024]{2,1,0:T(8,128)(2,1)} %get-tuple-element.8), kind=kOutput, calls=%fused_computation.41 | convolution fusion | flops 251658240 | bytes 2834432 | tf_op jit(solution)/shard_map/dot_general | solution.py:300
  71.9 1.7 %slice.136 = f32[2,32,1024]{2,1,0:T(8,128)} slice(f32[2,160,1024]{2,1,0:T(8,128)} %get-tuple-element.9), slice={[0:2], [128:160], [0:1024]} | slice | bytes 524288 | tf_op jit(solution)/shard_map/slice | solution.py:304
  73.6 1.1 reshape.171
  76.0 1.9 %convolution_add_fusion.4 = f32[96,1024]{1,0:T(8,128)S(1)} fusion(f32[96,1024]{1,0:T(8,128)} %fusion.24, bf16[1024,1024]{1,0:T(8,128)(2,1)S(1)} %copy-done, bf16[2,640,1024]{2,1,0:T(8,128)(2,1)} %get-tuple-element.8), kind=kOutput, calls=%fused_computation.9 | convolution fusion | flops 201424896 | bytes 3080192 | tf_op jit(solution)/shard_map/dot_general | solution.py:300
  77.9 2.6 %convolution_add_fusion.5 = f32[96,1024]{1,0:T(8,128)} fusion(f32[96,1024]{1,0:T(8,128)} %fusion.27, bf16[1024,1024]{1,0:T(8,128)(2,1)S(1)} %copy-done, bf16[2,640,1024]{2,1,0:T(8,128)(2,1)} %get-tuple-element.8), kind=kOutput, calls=%fused_computation.10 | convolution fusion | flops 201424896 | bytes 3080192 | tf_op jit(solution)/shard_map/dot_general | solution.py:300
  80.5 1.8 %fusion.3 = bf16[120,1024]{1,0:T(8,128)(2,1)S(1)} fusion(f32[120,1024]{1,0:T(8,128)S(1)} %fusion.14, bf16[1024,1024]{1,0:T(8,128)(2,1)S(1)} %copy-done, bf16[2,640,1024]{2,1,0:T(8,128)(2,1)} %get-tuple-element.8), kind=kOutput, calls=%fused_computation.15 | convolution fusion | flops 251904000 | bytes 3080192 | tf_op jit(solution)/shard_map/dot_general | solution.py:300
  82.3 2.6 %broadcast_select_fusion.5 = (bf16[120,1024]{1,0:T(8,128)(2,1)S(1)}, bf16[120,1024]{1,0:T(8,128)(2,1)}) fusion(bf16[120,1024]{1,0:T(8,128)(2,1)S(1)} %fusion.3, pred[]{:T(512)S(6)} %eq.69, f32[120,1024]{1,0:T(8,128)S(1)} %fusion.17, bf16[1024,1024]{1,0:T(8,128)(2,1)S(1)} %copy-done, bf16[2,640,1024]{2,1,0:T(8,128)(2,1)} %get-tuple-element.8), kind=kOutput, calls=%fused_computation.52 | convolution fusion | flops 252149760 | bytes 3571713 | tf_op jit(solution)/shard_map/dot_general | solution.py:300
  85.0 1.8 %fusion.9 = f32[128,1024]{1,0:T(8,128)S(1)} fusion(bf16[1024,1024]{1,0:T(8,128)(2,1)S(1)} %copy-done.3, bf16[2,640,1024]{2,1,0:T(8,128)(2,1)} %get-tuple-element.8), kind=kOutput, calls=%fused_computation.33 | convolution fusion | flops 268435456 | bytes 2883584 | tf_op jit(solution)/shard_map/dot_general | solution.py:300
  86.9 1.5 %collective-permute-start.8 = (bf16[120,1024]{1,0:T(8,128)(2,1)}, bf16[120,1024]{1,0:T(8,128)(2,1)}, u32[]{:S(2)}, u32[]{:S(2)}) collective-permute-start(bf16[120,1024]{1,0:T(8,128)(2,1)} %get-tuple-element.26), channel_id=1, source_target_pairs={{1,2},{3,4},{5,6},{2,1},{4,3},{6,5},{9,10},{11,12},{13,14},{10,9},... | collective-permute-start | bytes 737288 | tf_op jit(solution)/shard_map/ppermute | solution.py:47
  88.4 2.6 %convolution_add_fusion = f32[128,1024]{1,0:T(8,128)} fusion(f32[128,1024]{1,0:T(8,128)S(1)} %fusion.9, bf16[1024,1024]{1,0:T(8,128)(2,1)S(1)} %copy-done, bf16[2,640,1024]{2,1,0:T(8,128)(2,1)} %get-tuple-element.8), kind=kOutput, calls=%fused_computation.3 | convolution fusion | flops 268566528 | bytes 3407872 | tf_op jit(solution)/shard_map/dot_general | solution.py:300
  92.3 1.8 %broadcast_select_fusion.3 = (bf16[120,1024]{1,0:T(8,128)(2,1)S(1)}, bf16[120,1024]{1,0:T(8,128)(2,1)}) fusion(bf16[120,1024]{1,0:T(8,128)(2,1)} %collective-permute-done.8, pred[]{:T(512)S(6)} %eq.69, bf16[184,1024]{1,0:T(8,128)(2,1)} %copy-done.14), kind=kLoop, calls=%fused_computation.50 | loop fusion | flops 245760 | bytes 983041 | tf_op jit(solution)/shard_map/jit(_where)/select_n | solution.py:52
  94.2 1.0 reshape.175
  95.2 2.0 %broadcast_select_fusion.7 = (bf16[6,16,1024]{2,1,0:T(8,128)(2,1)S(1)}, bf16[6,16,1024]{2,1,0:T(8,128)(2,1)S(1)}, bf16[6,16,1024]{2,1,0:T(8,128)(2,1)}) fusion(pred[]{:T(512)S(6)} %eq.68, f32[6,16,1024]{2,1,0:T(8,128)} %bitcast.110, bf16[20,6,1024]{2,1,0:T(8,128)(2,1)S(1)} %reshape.175, bf16[20,6,1024]{2,1,0:T(8,128)(2,1)S(1)} %reshape.174, ...), kind=kLoop, calls=%fused_computation.65 | loop fusion | flops 1081344 | bytes 1867777 | tf_op jit(solution)/shard_map/jit(_where)/select_n | solution.py:41
  97.2 0.8 collective-permute-start.9
  98.0 2.1 %convolution_convert_fusion.2 = bf16[128,1024]{1,0:T(8,128)(2,1)} fusion(bf16[128,1024]{1,0:T(8,128)(2,1)} %get-tuple-element.6, bf16[1024,1024]{1,0:T(8,128)(2,1)S(1)} %copy-done.6), kind=kOutput, calls=%fused_computation.11 | convolution fusion | flops 268566528 | bytes 2621440 | tf_op jit(solution)/shard_map/dot_general | solution.py:294
  100.1 4.2 %collective-permute-done.9 = bf16[128,1024]{1,0:T(8,128)(2,1)S(1)} collective-permute-done((bf16[128,1024]{1,0:T(8,128)(2,1)S(1)}, bf16[128,1024]{1,0:T(8,128)(2,1)S(1)}, u32[]{:S(2)}, u32[]{:S(2)}) %collective-permute-start.9) | collective-permute-done | bytes 262176 | tf_op jit(solution)/shard_map/ppermute | solution.py:45
  105.2 5.9 %collective-permute-start.10 = (f32[2,2,2,1024]{3,0,1,2:T(2,128)S(1)}, f32[2,2,2,1024]{3,0,1,2:T(2,128)S(1)}, u32[]{:S(2)}, u32[]{:S(2)}) collective-permute-start(f32[2,2,2,1024]{3,0,1,2:T(2,128)S(1)} %select_bitcast_fusion), channel_id=1, source_target_pairs={{0,2},{1,3},{2,0},{3,1},{4,6},{5,7},{6,4},{7,5},{8,10},{9,11},{10,... | collective-permute-start | bytes 98312 | tf_op jit(solution)/shard_map/ppermute | solution.py:35
  111.8 1.2 collective-permute-done.10
  113.1 1.4 %collective-permute-start.11 = (f32[2,2,1024]{2,0,1:T(2,128)S(1)}, f32[2,2,1024]{2,0,1:T(2,128)S(1)}, u32[]{:S(2)}, u32[]{:S(2)}) collective-permute-start(f32[2,2,1024]{2,0,1:T(2,128)S(1)} %select_bitcast_fusion.1), channel_id=1, source_target_pairs={{0,4},{1,5},{2,6},{3,7},{4,0},{5,1},{6,2},{7,3},{8,12},{9,13},{10,... | collective-permute-start | bytes 49160 | tf_op jit(solution)/shard_map/ppermute | solution.py:35
  114.4 1.0 broadcast_select_fusion.11
  115.4 2.3 %collective-permute-done.11 = f32[2,2,1024]{2,0,1:T(2,128)S(1)} collective-permute-done((f32[2,2,1024]{2,0,1:T(2,128)S(1)}, f32[2,2,1024]{2,0,1:T(2,128)S(1)}, u32[]{:S(2)}, u32[]{:S(2)}) %collective-permute-start.11) | collective-permute-done | bytes 16416 | tf_op jit(solution)/shard_map/ppermute | solution.py:35
  117.8 4.2 %collective-permute-start.12 = (f32[2,1024]{1,0:T(2,128)S(1)}, f32[2,1024]{1,0:T(2,128)S(1)}, u32[]{:S(2)}, u32[]{:S(2)}) collective-permute-start(f32[2,1024]{1,0:T(2,128)S(1)} %select_bitcast_fusion.2), channel_id=1, source_target_pairs={{0,16},{8,24},{16,0},{24,8},{1,17},{9,25},{17,1},{25,9},{2,18},{10... | collective-permute-start | bytes 24584 | tf_op jit(solution)/shard_map/ppermute | solution.py:35
  122.1 1.5 %collective-permute-done.12 = f32[2,1024]{1,0:T(2,128)S(1)} collective-permute-done((f32[2,1024]{1,0:T(2,128)S(1)}, f32[2,1024]{1,0:T(2,128)S(1)}, u32[]{:S(2)}, u32[]{:S(2)}) %collective-permute-start.12) | collective-permute-done | bytes 8224 | tf_op jit(solution)/shard_map/ppermute | solution.py:35
  123.7 0.9 add_convert_fusion
  126.0 3.1 %fusion.1 = bf16[128,1024]{1,0:T(8,128)(2,1)} fusion(f32[128,1024]{1,0:T(8,128)S(1)} %bitcast.108, f32[128,1024]{1,0:T(8,128)S(1)} %dynamic_update_slice.11, bf16[128,1024]{1,0:T(8,128)(2,1)S(1)} %copy-done.15, bf16[1024,1024]{1,0:T(8,128)(2,1)} %param.12), kind=kOutput, calls=%fused_computation.8 | convolution fusion | flops 268828672 | bytes 3670016 | tf_op jit(solution)/shard_map/dot_general | solution.py:360
  (115 shorter events, 10.5 us)
Async XLA Ops:
  0.6 33.0 %copy-start = (bf16[1024,1024]{1,0:T(8,128)(2,1)S(1)}, bf16[1024,1024]{1,0:T(8,128)(2,1)}, u32[]{:S(2)}) copy-start(bf16[1024,1024]{1,0:T(8,128)(2,1)} %param.14) | copy-start | bytes 6291460
  0.7 17.1 %copy-start.16 = (bf16[8,16,1024]{2,1,0:T(8,128)(2,1)S(1)}, bf16[8,16,1024]{2,1,0:T(8,128)(2,1)}, u32[]{:S(2)}) copy-start(bf16[8,16,1024]{2,1,0:T(8,128)(2,1)} %param.17) | copy-start | bytes 786436
  1.9 17.5 %collective-permute-start = (bf16[96,1024]{1,0:T(8,128)(2,1)S(1)}, bf16[96,1024]{1,0:T(8,128)(2,1)S(1)}, u32[]{:S(2)}, u32[]{:S(2)}) collective-permute-start(bf16[96,1024]{1,0:T(8,128)(2,1)S(1)} %bitcast.120), channel_id=1, source_target_pairs={{8,16},{16,8},{9,17},{17,9},{10,18},{18,10},{11,19},{19,11},{12,20... | collective-permute-start | bytes 589832 | tf_op jit(solution)/shard_map/ppermute | solution.py:47
  7.2 12.2 %collective-permute-start.1 = (bf16[97,1024]{1,0:T(8,128)(2,1)S(1)}, bf16[97,1024]{1,0:T(8,128)(2,1)S(1)}, u32[]{:S(2)}, u32[]{:S(2)}) collective-permute-start(bf16[97,1024]{1,0:T(8,128)(2,1)S(1)} %pad_maximum_fusion.4), channel_id=1, source_target_pairs={{0,8},{8,0},{16,24},{24,16},{1,9},{9,1},{17,25},{25,17},{2,10},{10... | collective-permute-start | bytes 595976 | tf_op jit(solution)/shard_map/ppermute | solution.py:45
  14.8 3.0 %copy-start.5 = (bf16[1024,1024]{1,0:T(8,128)(2,1)S(1)}, bf16[1024,1024]{1,0:T(8,128)(2,1)}, u32[]{:S(2)}) copy-start(bf16[1024,1024]{1,0:T(8,128)(2,1)} %param.15) | copy-start | bytes 6291460
  14.8 4.6 %copy-start.19 = (s32[640]{0:T(1024)S(1)}, s32[640]{0:T(1024)}, u32[]{:S(2)}) copy-start(s32[640]{0:T(1024)} %constant.139.clone) | copy-start | bytes 7684
  14.8 4.6 %copy-start.20 = (s32[640]{0:T(1024)S(1)}, s32[640]{0:T(1024)}, u32[]{:S(2)}) copy-start(s32[640]{0:T(1024)} %constant.138.clone) | copy-start | bytes 7684
  17.8 3.1 %copy-start.7 = (bf16[8,16,1024]{2,1,0:T(8,128)(2,1)S(1)}, bf16[8,16,1024]{2,1,0:T(8,128)(2,1)}, u32[]{:S(2)}) copy-start(bf16[8,16,1024]{2,1,0:T(8,128)(2,1)} %param.11) | copy-start | bytes 786436
  20.9 4.1 %copy-start.21 = (pred[640]{0:T(1024)(128)(4,1)S(1)}, pred[640]{0:T(1024)(128)(4,1)}, u32[]{:S(2)}) copy-start(pred[640]{0:T(1024)(128)(4,1)} %constant.157) | copy-start | bytes 1924
  20.9 4.1 %copy-start.22 = (pred[640]{0:T(1024)(128)(4,1)S(1)}, pred[640]{0:T(1024)(128)(4,1)}, u32[]{:S(2)}) copy-start(pred[640]{0:T(1024)(128)(4,1)} %constant.156) | copy-start | bytes 1924
  20.9 5.0 %copy-start.23 = (s32[32]{0:T(128)S(1)}, s32[32]{0:T(128)}, u32[]{:S(2)}) copy-start(s32[32]{0:T(128)} %constant.159) | copy-start | bytes 388
  21.3 6.6 %collective-permute-start.2 = (bf16[120,1024]{1,0:T(8,128)(2,1)S(1)}, bf16[120,1024]{1,0:T(8,128)(2,1)S(1)}, u32[]{:S(2)}, u32[]{:S(2)}) collective-permute-start(bf16[120,1024]{1,0:T(8,128)(2,1)S(1)} %select_n.316), channel_id=1, source_target_pairs={{1,2},{3,4},{5,6},{2,1},{4,3},{6,5},{9,10},{11,12},{13,14},{10,9},... | collective-permute-start | bytes 737288 | tf_op jit(solution)/shard_map/ppermute | solution.py:47
  22.0 4.2 %collective-permute-start.3 = (bf16[122,1024]{1,0:T(8,128)(2,1)S(1)}, bf16[122,1024]{1,0:T(8,128)(2,1)S(1)}, u32[]{:S(2)}, u32[]{:S(2)}) collective-permute-start(bf16[122,1024]{1,0:T(8,128)(2,1)S(1)} %pad_maximum_fusion.2), channel_id=1, source_target_pairs={{0,1},{1,0},{2,3},{3,2},{4,5},{5,4},{6,7},{7,6},{8,9},{9,8},{10,11... | collective-permute-start | bytes 749576 | tf_op jit(solution)/shard_map/ppermute | solution.py:45
  26.2 3.8 %collective-permute-start.4 = (bf16[4,1024]{1,0:T(4,128)(2,1)S(1)}, bf16[4,1024]{1,0:T(4,128)(2,1)S(1)}, u32[]{:S(2)}, u32[]{:S(2)}) collective-permute-start(bf16[4,1024]{1,0:T(4,128)(2,1)S(1)} %maximum_select_fusion.3), channel_id=1, source_target_pairs={{0,2},{1,3},{2,0},{3,1},{4,6},{5,7},{6,4},{7,5},{8,10},{9,11},{10,... | collective-permute-start | bytes 24584 | tf_op jit(solution)/shard_map/ppermute | solution.py:35
  30.1 7.9 %copy-start.1 = (bf16[1024,1024]{1,0:T(8,128)(2,1)S(1)}, bf16[1024,1024]{1,0:T(8,128)(2,1)}, u32[]{:S(2)}) copy-start(bf16[1024,1024]{1,0:T(8,128)(2,1)} %param.13) | copy-start | bytes 6291460
  30.1 7.9 %copy-start.18 = (bf16[640,1024]{1,0:T(8,128)(2,1)S(1)}, bf16[640,1024]{1,0:T(8,128)(2,1)}, u32[]{:S(2)}) copy-start(bf16[640,1024]{1,0:T(8,128)(2,1)} %broadcast_dynamic-update-slice_fusion) | copy-start | bytes 3932164
  30.1 7.5 %collective-permute-start.5 = (bf16[8,1024]{1,0:T(8,128)(2,1)S(1)}, bf16[8,1024]{1,0:T(8,128)(2,1)S(1)}, u32[]{:S(2)}, u32[]{:S(2)}) collective-permute-start(bf16[8,1024]{1,0:T(8,128)(2,1)S(1)} %maximum_select_fusion.2), channel_id=1, source_target_pairs={{0,4},{1,5},{2,6},{3,7},{4,0},{5,1},{6,2},{7,3},{8,12},{9,13},{10,... | collective-permute-start | bytes 49160 | tf_op jit(solution)/shard_map/ppermute | solution.py:35
  37.6 4.0 %collective-permute-start.6 = (bf16[16,1024]{1,0:T(8,128)(2,1)S(1)}, bf16[16,1024]{1,0:T(8,128)(2,1)S(1)}, u32[]{:S(2)}, u32[]{:S(2)}) collective-permute-start(bf16[16,1024]{1,0:T(8,128)(2,1)S(1)} %maximum_select_fusion.1), channel_id=1, source_target_pairs={{0,16},{8,24},{16,0},{24,8},{1,17},{9,25},{17,1},{25,9},{2,18},{10... | collective-permute-start | bytes 98312 | tf_op jit(solution)/shard_map/ppermute | solution.py:35
  62.5 3.4 %copy-start.2 = (bf16[1024,1024]{1,0:T(8,128)(2,1)S(1)}, bf16[1024,1024]{1,0:T(8,128)(2,1)}, u32[]{:S(2)}) copy-start(bf16[1024,1024]{1,0:T(8,128)(2,1)} %param.13) | copy-start | bytes 6291460
  74.9 0.7 copy-start.9
  74.9 0.8 copy-start.11
  82.3 2.7 %copy-start.3 = (bf16[1024,1024]{1,0:T(8,128)(2,1)S(1)}, bf16[1024,1024]{1,0:T(8,128)(2,1)}, u32[]{:S(2)}) copy-start(bf16[1024,1024]{1,0:T(8,128)(2,1)} %param.13) | copy-start | bytes 6291460
  85.0 6.0 %collective-permute-start.7 = (bf16[184,1024]{1,0:T(8,128)(2,1)S(1)}, bf16[184,1024]{1,0:T(8,128)(2,1)S(1)}, u32[]{:S(2)}, u32[]{:S(2)}) collective-permute-start(bf16[184,1024]{1,0:T(8,128)(2,1)S(1)} %pad_maximum_fusion.1), channel_id=1, source_target_pairs={{0,1},{1,0},{2,3},{3,2},{4,5},{5,4},{6,7},{7,6},{8,9},{9,8},{10,11... | collective-permute-start | bytes 1130504 | tf_op jit(solution)/shard_map/ppermute | solution.py:45
  86.8 5.0 %copy-start.10 = (f32[2,2,2,2,2,1,1024]{6,5,4,3,2,1,0:T(1,128)S(1)}, f32[2,2,2,2,2,1,1024]{6,5,4,3,2,1,0:T(1,128)}, u32[]{:S(2)}) copy-start(f32[2,2,2,2,2,1,1024]{6,5,4,3,2,1,0:T(1,128)} %copy-done.9) | copy-start | bytes 393220
  86.9 5.0 %copy-start.12 = (f32[2,2,2,2,2,1,1024]{6,5,4,3,2,1,0:T(1,128)S(1)}, f32[2,2,2,2,2,1,1024]{6,5,4,3,2,1,0:T(1,128)}, u32[]{:S(2)}) copy-start(f32[2,2,2,2,2,1,1024]{6,5,4,3,2,1,0:T(1,128)} %copy-done.11) | copy-start | bytes 393220
  86.9 5.4 %collective-permute-start.8 = (bf16[120,1024]{1,0:T(8,128)(2,1)}, bf16[120,1024]{1,0:T(8,128)(2,1)}, u32[]{:S(2)}, u32[]{:S(2)}) collective-permute-start(bf16[120,1024]{1,0:T(8,128)(2,1)} %get-tuple-element.26), channel_id=1, source_target_pairs={{1,2},{3,4},{5,6},{2,1},{4,3},{6,5},{9,10},{11,12},{13,14},{10,9},... | collective-permute-start | bytes 737288 | tf_op jit(solution)/shard_map/ppermute | solution.py:47
  91.0 0.7 copy-start.14
  95.2 2.8 %copy-start.6 = (bf16[1024,1024]{1,0:T(8,128)(2,1)S(1)}, bf16[1024,1024]{1,0:T(8,128)(2,1)}, u32[]{:S(2)}) copy-start(bf16[1024,1024]{1,0:T(8,128)(2,1)} %param.15) | copy-start | bytes 6291460
  97.2 13.9 %copy-start.13 = (bf16[6,16,1024]{2,1,0:T(8,128)(2,1)S(1)}, bf16[6,16,1024]{2,1,0:T(8,128)(2,1)}, u32[]{:S(2)}) copy-start(bf16[6,16,1024]{2,1,0:T(8,128)(2,1)} %get-tuple-element.12) | copy-start | bytes 589828
  97.2 7.1 %collective-permute-start.9 = (bf16[128,1024]{1,0:T(8,128)(2,1)S(1)}, bf16[128,1024]{1,0:T(8,128)(2,1)S(1)}, u32[]{:S(2)}, u32[]{:S(2)}) collective-permute-start(bf16[128,1024]{1,0:T(8,128)(2,1)S(1)} %pad_maximum_fusion.3), channel_id=1, source_target_pairs={{0,8},{8,0},{16,24},{24,16},{1,9},{9,1},{17,25},{25,17},{2,10},{10... | collective-permute-start | bytes 786440 | tf_op jit(solution)/shard_map/ppermute | solution.py:45
  104.3 0.7 copy-start.17
  105.2 7.8 %collective-permute-start.10 = (f32[2,2,2,1024]{3,0,1,2:T(2,128)S(1)}, f32[2,2,2,1024]{3,0,1,2:T(2,128)S(1)}, u32[]{:S(2)}, u32[]{:S(2)}) collective-permute-start(f32[2,2,2,1024]{3,0,1,2:T(2,128)S(1)} %select_bitcast_fusion), channel_id=1, source_target_pairs={{0,2},{1,3},{2,0},{3,1},{4,6},{5,7},{6,4},{7,5},{8,10},{9,11},{10,... | collective-permute-start | bytes 98312 | tf_op jit(solution)/shard_map/ppermute | solution.py:35
  111.1 3.3 %collective-permute-start.13 = (bf16[96,1024]{1,0:T(8,128)(2,1)S(1)}, bf16[96,1024]{1,0:T(8,128)(2,1)S(1)}, u32[]{:S(2)}, u32[]{:S(2)}) collective-permute-start(bf16[96,1024]{1,0:T(8,128)(2,1)S(1)} %bitcast.121), channel_id=1, source_target_pairs={{8,16},{16,8},{9,17},{17,9},{10,18},{18,10},{11,19},{19,11},{12,20... | collective-permute-start | bytes 589832 | tf_op jit(solution)/shard_map/ppermute | solution.py:47
  113.1 4.7 %collective-permute-start.11 = (f32[2,2,1024]{2,0,1:T(2,128)S(1)}, f32[2,2,1024]{2,0,1:T(2,128)S(1)}, u32[]{:S(2)}, u32[]{:S(2)}) collective-permute-start(f32[2,2,1024]{2,0,1:T(2,128)S(1)} %select_bitcast_fusion.1), channel_id=1, source_target_pairs={{0,4},{1,5},{2,6},{3,7},{4,0},{5,1},{6,2},{7,3},{8,12},{9,13},{10,... | collective-permute-start | bytes 49160 | tf_op jit(solution)/shard_map/ppermute | solution.py:35
  115.4 9.8 %copy-start.4 = (bf16[1024,1024]{1,0:T(8,128)(2,1)S(1)}, bf16[1024,1024]{1,0:T(8,128)(2,1)}, u32[]{:S(2)}) copy-start(bf16[1024,1024]{1,0:T(8,128)(2,1)} %param.13) | copy-start | bytes 6291460
  117.8 5.9 %collective-permute-start.12 = (f32[2,1024]{1,0:T(2,128)S(1)}, f32[2,1024]{1,0:T(2,128)S(1)}, u32[]{:S(2)}, u32[]{:S(2)}) collective-permute-start(f32[2,1024]{1,0:T(2,128)S(1)} %select_bitcast_fusion.2), channel_id=1, source_target_pairs={{0,16},{8,24},{16,0},{24,8},{1,17},{9,25},{17,1},{25,9},{2,18},{10... | collective-permute-start | bytes 24584 | tf_op jit(solution)/shard_map/ppermute | solution.py:35
  124.5 1.3 %copy-start.8 = (f32[128,1024]{1,0:T(8,128)S(1)}, f32[128,1024]{1,0:T(8,128)}, u32[]{:S(2)}) copy-start(f32[128,1024]{1,0:T(8,128)} %convolution_add_fusion) | copy-start | bytes 1572868
  124.5 1.4 %copy-start.15 = (bf16[128,1024]{1,0:T(8,128)(2,1)S(1)}, bf16[128,1024]{1,0:T(8,128)(2,1)}, u32[]{:S(2)}) copy-start(bf16[128,1024]{1,0:T(8,128)(2,1)} %get-tuple-element.7) | copy-start | bytes 786436

commit v7 on v6

--- a/solution.py
+++ b/solution.py
@@ -75,12 +75,14 @@
     return jnp.where(high, upper, lower), jnp.where(high, lower, upper)
 
 
-def attention_kernel(own, first, last, q_ref, k_ref, v_ref, g_ref, mask_ref, o_ref, dq_ref, dkv_ref, wide_ref):
+def attention_kernel(
+    own, first, last, q_ref, kf_ref, kg_ref, vf_ref, vg_ref, g_ref, mask_ref, o_ref, dq_ref, dkv_ref, wide_ref
+):
     head_size = q_ref.shape[1] // 2
     score_scale = 1.0 / math.sqrt(head_size)
     q = q_ref[...]
-    k = k_ref[...]
-    v = v_ref[...]
+    k = jnp.concatenate([kf_ref[...], kg_ref[...]], axis=0)
+    v = jnp.concatenate([vf_ref[...], vg_ref[...]], axis=0)
     g = g_ref[...]
     keep = mask_ref[...] > 0
     lane_head = lax.broadcasted_iota(jnp.int32, q.shape, 1) // head_size
@@ -100,7 +102,7 @@
         scores = jnp.where(keep, scores, -1e30)
         row_max = jnp.max(scores, axis=1, keepdims=True)
         exps = jnp.exp(scores - row_max)
-        probs = exps / jnp.sum(exps, axis=1, keepdims=True)
+        probs = exps * (1.0 / jnp.sum(exps, axis=1, keepdims=True))
         rounded = probs.astype(jnp.bfloat16)
         attended = jnp.dot(rounded, v, preferred_element_type=jnp.float32)
         attended = attended.astype(jnp.bfloat16).astype(jnp.float32)
@@ -127,13 +129,17 @@
     wide_ref[1, own:] = dv[first:last]
 
 
-def attention(queries, keys, values, grad_attended, keep, first, last):
+def attention(queries, keys, values, global_keys, global_values, grad_attended, keep):
     tokens, model_width = queries.shape
-    key_count = keys.shape[0]
+    first = keys.shape[0]
+    last = first + global_keys.shape[0]
+    key_count = last
     lanes = 2 * (model_width // HEADS)
     steps = model_width // lanes
     token_block = pl.BlockSpec((tokens, lanes), lambda i: (0, i))
     key_block = pl.BlockSpec((key_count, lanes), lambda i: (0, i))
+    frame_block = pl.BlockSpec((first, lanes), lambda i: (0, i))
+    global_block = pl.BlockSpec((last - first, lanes), lambda i: (0, i))
     mask_block = pl.BlockSpec((tokens, key_count), lambda i: (0, 0))
     grads_block = pl.BlockSpec((2, key_count, lanes), lambda i: (0, 0, i))
     wide_rows = tokens + last - first
@@ -145,7 +151,15 @@
     return pl.pallas_call(
         functools.partial(attention_kernel, tokens, first, last),
         grid=(steps,),
-        in_specs=[token_block, key_block, key_block, token_block, mask_block],
+        in_specs=[
+            token_block,
+            frame_block,
+            global_block,
+            frame_block,
+            global_block,
+            token_block,
+            mask_block,
+        ],
         out_specs=[token_block, token_block, grads_block, wide_block],
         out_shape=[
             jax.ShapeDtypeStruct((tokens, model_width), jnp.bfloat16),
@@ -156,7 +170,7 @@
         cost_estimate=pl.CostEstimate(
             flops=flops, transcendentals=HEADS * tokens * key_count, bytes_accessed=moved
         ),
-    )(queries, keys, values, grad_attended, keep)
+    )(queries, keys, global_keys, values, global_values, grad_attended, keep)
 
 
 def split_wide(x):
@@ -234,7 +248,7 @@
             from_below,
             from_left,
             from_right,
-            jnp.zeros((key_count - frame_keys, model_width), features.dtype),
+            jnp.zeros((key_count - used, model_width), features.dtype),
         ],
         axis=0,
     )
@@ -246,12 +260,12 @@
     for position in order[2:]:
         gathered = gather_step(gathered, partner(gathered, position), position)
     global_features = jnp.take(gathered, jnp.asarray(gather_order(order, device_count)), axis=0)
-    global_keys = jnp.dot(global_features, w_key, preferred_element_type=jnp.float32)
-    global_values = jnp.dot(global_features, w_value, preferred_element_type=jnp.float32)
-    keys = lax.dynamic_update_slice_in_dim(keys, global_keys.astype(jnp.bfloat16), frame_keys, 0)
-    values = lax.dynamic_update_slice_in_dim(
-        values, global_values.astype(jnp.bfloat16), frame_keys, 0
-    )
+    global_keys = jnp.dot(global_features, w_key, preferred_element_type=jnp.float32).astype(
+        jnp.bfloat16
+    )
+    global_values = jnp.dot(
+        global_features, w_value, preferred_element_type=jnp.float32
+    ).astype(jnp.bfloat16)
 
     def grid(height, width, row0, col0):
         a, b = np.meshgrid(np.arange(height) + row0, np.arange(width) + col0, indexing="ij")
@@ -270,7 +284,7 @@
     key_cols[:frame_keys] = np.concatenate([p[1] for p in parts])
     kind = np.full(key_count, 2, np.int32)
     kind[:frame_keys] = 0
-    kind[frame_keys:used] = 1
+    kind[key_count - device_count :] = 1
 
     query_rows = first_row + jnp.repeat(jnp.arange(tile_rows, dtype=jnp.int32), tile_cols)
     query_cols = first_col + jnp.tile(jnp.arange(tile_cols, dtype=jnp.int32), tile_rows)
@@ -288,7 +302,7 @@
     keep = ((inside & (key_kind == 0)) | (key_kind == 1)).astype(jnp.float32)
 
     attended, query_grads, rounded_grads, wide_grads = attention(
-        queries, keys, values, grad_attended, keep, frame_keys, used
+        queries, keys, values, global_keys, global_values, grad_attended, keep
     )
     layer_out = (
         jnp.dot(attended, w_out, preferred_element_type=jnp.float32)
@@ -296,10 +310,12 @@
         .reshape(features.shape)
     )
 
+    given_all = jnp.dot(
+        rounded_grads[0, :frame_keys], w_key.T, preferred_element_type=jnp.float32
+    ) + jnp.dot(rounded_grads[1, :frame_keys], w_value.T, preferred_element_type=jnp.float32)
+
     def given(lo, hi):
-        return jnp.dot(rounded_grads[0, lo:hi], w_key.T, preferred_element_type=jnp.float32) + jnp.dot(
-            rounded_grads[1, lo:hi], w_value.T, preferred_element_type=jnp.float32
-        )
+        return given_all[lo:hi]
 
     scatter = wide_grads[:, tokens:].reshape(
         (2,) + (2,) * all_bits + (model_width,)

time: 130 us -> 126 us (0.969)
  matrix products: 44.1 us -> 29.8 us
  local copies, waits for them, and re-layouts: 12.1 us -> 17.1 us
  other arithmetic: 11.9 us -> 15.6 us
    dot_general x10 -> x2, matrix products: 22.7 us -> 7.37 us  [the longest x1 4.04 us: shards(): jnp.dot(rounded_grads[1, :frame_keys], w_value.T, preferred_element_type=...]
    slice x0 -> x2, local copies, waits for them, and re-layouts: none -> 3.07 us  [given(): return given_all[lo:hi]]
    select_n x4, local copies, waits for them, and re-layouts: 0.3 us -> 2.39 us  [scatter_split(): return (jnp.where(high, upper, lower), jnp.where(high, lower, upper))]
    dot_general x1, matrix products: 2.63 us -> 4.5 us  [shards(): jnp.dot(key_features, w_key, preferred_element_type=jnp.float32)]
    dot_general x1, matrix products: 1.56 us -> 3.17 us  [shards(): jnp.dot(grad_out.reshape(-1, model_width), w_out.T, preferred_element_typ...]
    reshape x2, local copies, waits for them, and re-layouts: 0.11 us -> 1.67 us  [shards(): scatter = keep_part + join_wide(got).reshape(keep_part.shape)]
    add x2, other arithmetic: 0.03 us -> 1.55 us  [join_wide(): return pair[:half].astype(jnp.float32) + pair[half:].astype(jnp.float32)]
    dot_general x1, matrix products: 3.96 us -> 2.54 us  [shards(): jnp.dot(key_features, w_value, preferred_element_type=jnp.float32)]
  transfers between devices with their start and end apart: 14 -> 14, of which waited for: 6 -> 6; matrix products, arithmetic and copies ran while one was open for 20% -> 21% of each run, Pallas kernels for 0% -> 0%
where the time goes in v7:
time: 126 us; the launch traced here: 125 us
  starting transfers between devices  30.3 us (24%)
  matrix products  29.8 us (24%)
  local copies, waits for them, and re-layouts  17.1 us (14%)
  Pallas kernels  16.6 us (13%)
  other arithmetic  15.6 us (12%)
  waiting for transfers between devices  11.7 us (9%)
  between operations  3.84 us (3%)
    ppermute x6, starting transfers between devices, partner(): return lax.ppermute(x, axis, [(i, i ^ 1 << bit) for i in range(size)])  17.9 us
    pallas_call x1, Pallas kernels, attention(): pl.pallas_call(functools.partial(attention_kernel, tokens, first, last),...  16.6 us
    ppermute x4, starting transfers between devices, exchange(): got_first = lax.ppermute(first, axis, [(i, i ^ 1) for i in range(size)])  9.49 us
    ppermute x6, waiting for transfers between devices, partner(): return lax.ppermute(x, axis, [(i, i ^ 1 << bit) for i in range(size)])  6.92 us
    ppermute x4, waiting for transfers between devices, exchange(): got_first = lax.ppermute(first, axis, [(i, i ^ 1) for i in range(size)])  4.8 us
    dot_general x1, matrix products, shards(): jnp.dot(key_features, w_key, preferred_element_type=jnp.float32)  4.5 us
    dot_general x1, matrix products, shards(): jnp.dot(rounded_grads[1, :frame_keys], w_value.T, preferred_element_type=...  4.04 us
    unnamed x51, local copies, waits for them, and re-layouts  3.76 us
  transfers between devices with their start and end apart: 14, of which 6 were waited for; matrix products, arithmetic and copies ran while one was open for 21% of the time, Pallas kernels for 0%

profile of v7, /device:TPU:0, one launch (start us, length us, event | category | flops | bytes accessed | tf_op | source)
XLA Modules:
  0.0 124.9 jit_solution(704131800720333935)
XLA Ops:
  0.7 1.2 broadcast_select_fusion.8
  2.6 1.2 dynamic_slice.10
  6.4 0.7 constant_dynamic-slice_fusion
  7.2 5.7 %collective-permute-start.1 = (bf16[97,1024]{1,0:T(8,128)(2,1)S(1)}, bf16[97,1024]{1,0:T(8,128)(2,1)S(1)}, u32[]{:S(2)}, u32[]{:S(2)}) collective-permute-start(bf16[97,1024]{1,0:T(8,128)(2,1)S(1)} %pad_maximum_fusion.4), channel_id=1, source_target_pairs={{0,8},{8,0},{16,24},{24,16},{1,9},{9,1},{17,25},{25,17},{2,10},{10... | collective-permute-start | bytes 595976 | tf_op jit(solution)/shard_map/ppermute | solution.py:45
  12.9 1.7 %constant_dynamic-update-slice_fusion.2 = bf16[608,1024]{1,0:T(8,128)(2,1)} fusion(bf16[128,1024]{1,0:T(8,128)(2,1)} %bitcast.74), kind=kLoop, calls=%fused_computation.62 | loop fusion | bytes 524288
  14.6 2.9 %convolution_convert_fusion.4.q_ref = bf16[128,1024]{1,0:T(8,128)(2,1)} fusion(bf16[128,1024]{1,0:T(8,128)(2,1)} %bitcast.75, bf16[1024,1024]{1,0:T(8,128)(2,1)} %param.12), kind=kOutput, calls=%fused_computation.9 | convolution fusion | flops 268566528 | bytes 2621440 | tf_op jit(solution)/shard_map/dot_general | solution.py:239
  17.7 3.2 %convolution_convert_fusion.3.g_ref = bf16[128,1024]{1,0:T(8,128)(2,1)} fusion(bf16[128,1024]{1,0:T(8,128)(2,1)S(1)} %bitcast.86, bf16[1024,1024]{1,0:T(8,128)(2,1)} %param.15), kind=kOutput, calls=%fused_computation.8 | convolution fusion | flops 268566528 | bytes 2621440 | tf_op jit(solution)/shard_map/dot_general | solution.py:240
  21.4 0.7 constant_dynamic-update-slice_fusion.1
  22.2 0.8 constant_dynamic-update-slice_fusion
  24.1 3.0 %collective-permute-start.3 = (bf16[122,1024]{1,0:T(8,128)(2,1)S(1)}, bf16[122,1024]{1,0:T(8,128)(2,1)S(1)}, u32[]{:S(2)}, u32[]{:S(2)}) collective-permute-start(bf16[122,1024]{1,0:T(8,128)(2,1)S(1)} %pad_maximum_fusion.2), channel_id=1, source_target_pairs={{0,1},{1,0},{2,3},{3,2},{4,5},{5,4},{6,7},{7,6},{8,9},{9,8},{10,11... | collective-permute-start | bytes 749576 | tf_op jit(solution)/shard_map/ppermute | solution.py:45
  27.1 0.9 or_convert_fusion.mask_ref
  28.3 1.7 %collective-permute-start.4 = (bf16[4,1024]{1,0:T(4,128)(2,1)S(1)}, bf16[4,1024]{1,0:T(4,128)(2,1)S(1)}, u32[]{:S(2)}, u32[]{:S(2)}) collective-permute-start(bf16[4,1024]{1,0:T(4,128)(2,1)S(1)} %maximum_select_fusion.3), channel_id=1, source_target_pairs={{0,2},{1,3},{2,0},{3,1},{4,6},{5,7},{6,4},{7,5},{8,10},{9,11},{10,... | collective-permute-start | bytes 24584 | tf_op jit(solution)/shard_map/ppermute | solution.py:35
  30.0 0.8 select_dynamic-update-slice_fusion.1
  30.7 0.8 select_dynamic-update-slice_fusion
  32.2 3.5 %collective-permute-start.5 = (bf16[8,1024]{1,0:T(8,128)(2,1)S(1)}, bf16[8,1024]{1,0:T(8,128)(2,1)S(1)}, u32[]{:S(2)}, u32[]{:S(2)}) collective-permute-start(bf16[8,1024]{1,0:T(8,128)(2,1)S(1)} %maximum_select_fusion.2), channel_id=1, source_target_pairs={{0,4},{1,5},{2,6},{3,7},{4,0},{5,1},{6,2},{7,3},{8,12},{9,13},{10,... | collective-permute-start | bytes 49160 | tf_op jit(solution)/shard_map/ppermute | solution.py:35
  35.6 4.5 %convolution_convert_fusion.1.kf_ref = bf16[608,1024]{1,0:T(8,128)(2,1)} fusion(bf16[608,1024]{1,0:T(8,128)(2,1)} %broadcast_dynamic-update-slice_fusion, bf16[1024,1024]{1,0:T(8,128)(2,1)} %param.13), kind=kOutput, calls=%fused_computation.2 | convolution fusion | flops 1275691008 | bytes 4587520 | tf_op jit(solution)/shard_map/dot_general | solution.py:255
  40.2 2.5 %convolution_convert_fusion.vf_ref = bf16[608,1024]{1,0:T(8,128)(2,1)} fusion(bf16[608,1024]{1,0:T(8,128)(2,1)S(1)} %copy-done.15, bf16[1024,1024]{1,0:T(8,128)(2,1)S(1)} %copy-done), kind=kOutput, calls=%fused_computation.1 | convolution fusion | flops 1275691008 | bytes 4587520 | tf_op jit(solution)/shard_map/dot_general | solution.py:256
  42.8 1.3 %collective-permute-done.6 = bf16[16,1024]{1,0:T(8,128)(2,1)S(1)} collective-permute-done((bf16[16,1024]{1,0:T(8,128)(2,1)S(1)}, bf16[16,1024]{1,0:T(8,128)(2,1)S(1)}, u32[]{:S(2)}, u32[]{:S(2)}) %collective-permute-start.6) | collective-permute-done | bytes 32800 | tf_op jit(solution)/shard_map/ppermute | solution.py:35
  44.8 2.7 %convolution_convert_fusion.6.kg_ref = bf16[32,1024]{1,0:T(8,128)(2,1)} fusion(bf16[32,1024]{1,0:T(8,128)(2,1)S(1)} %gather_fusion, bf16[1024,1024]{1,0:T(8,128)(2,1)} %param.13), kind=kOutput, calls=%fused_computation.16 | convolution fusion | flops 67141632 | bytes 2228224 | tf_op jit(solution)/shard_map/dot_general | solution.py:263
  47.5 1.1 convolution_convert_fusion.5.vg_ref
  48.6 16.6 %shard_map.122 = (bf16[128,1024]{1,0:T(8,128)(2,1)}, bf16[128,1024]{1,0:T(8,128)(2,1)}, bf16[2,640,1024]{2,1,0:T(8,128)(2,1)}, f32[2,160,1024]{2,1,0:T(8,128)}) custom-call(bf16[128,1024]{1,0:T(8,128)(2,1)} %convolution_convert_fusion.4.q_ref, bf16[608,1024]{1,0:T(8,128)(2,1)} %convolution_convert_fusion.1.kf_ref, ...), custom_call_target="tpu_custom_call" | custom-call | flops 2013265920 | bytes 8978432 | tf_op jit(solution)/shard_map/pallas_call | solution.py:151
  65.1 3.3 %fusion.3 = f32[560,1024]{1,0:T(8,128)S(1)} fusion(bf16[1024,1024]{1,0:T(8,128)(2,1)} %param.13, bf16[2,640,1024]{2,1,0:T(8,128)(2,1)} %get-tuple-element.8), kind=kOutput, calls=%fused_computation.11 | convolution fusion | flops 1174405120 | bytes 5537792 | tf_op jit(solution)/shard_map/dot_general | solution.py:313
  68.5 4.0 %fusion.15 = (bf16[560,1024]{1,0:T(8,128)(2,1)S(1)}, f32[560,1024]{1,0:T(8,128)}) fusion(f32[560,1024]{1,0:T(8,128)S(1)} %fusion.3, bf16[1024,1024]{1,0:T(8,128)(2,1)S(1)} %copy-done, bf16[2,640,1024]{2,1,0:T(8,128)(2,1)} %get-tuple-element.8), kind=kOutput, calls=%fused_computation.82 | convolution fusion | flops 1175552000 | bytes 8978432 | tf_op jit(solution)/shard_map/dot_general | solution.py:315
  72.5 0.7 broadcast_select_fusion.5
  73.2 1.0 slice.130
  75.8 0.9 collective-permute-start.8
  76.7 1.9 %slice.164 = f32[128,1024]{1,0:T(8,128)} slice(f32[560,1024]{1,0:T(8,128)} %get-tuple-element.36), slice={[0:128], [0:1024]} | slice | bytes 1048576 | tf_op jit(solution)/shard_map/slice | solution.py:318
  78.6 1.2 fusion.13
  79.8 1.7 %broadcast_select_fusion.3 = (bf16[120,1024]{1,0:T(8,128)(2,1)}, bf16[120,1024]{1,0:T(8,128)(2,1)S(1)}) fusion(bf16[120,1024]{1,0:T(8,128)(2,1)S(1)} %collective-permute-done.8, pred[]{:T(512)S(6)} %eq.69, bf16[184,1024]{1,0:T(8,128)(2,1)} %collective-permute-done.7), kind=kLoop, calls=%fused_computation.32 | loop fusion | flops 245760 | bytes 983041 | tf_op jit(solution)/shard_map/jit(_where)/select_n | solution.py:52
  81.6 1.0 reshape.174
  82.6 1.5 %convert_add_fusion.1 = f32[32,1024]{1,0:T(8,128)} fusion(bf16[184,1024]{1,0:T(8,128)(2,1)} %collective-permute-done.7), kind=kLoop, calls=%fused_computation.45 | loop fusion | flops 98304 | bytes 262144 | tf_op jit(solution)/shard_map/add | solution.py:184
  84.2 1.6 %reshape.172 = f32[2,2,2,2,2,1024]{5,4,3,2,1,0:T(2,128)} reshape(f32[32,1024]{1,0:T(8,128)} %convert_add_fusion.1) | data formatting | bytes 262144 | tf_op jit(solution)/shard_map/reshape | solution.py:335
  85.8 1.3 %bitcast_add_fusion = f32[2,2,2,2,2,1024]{5,0,1,3,4,2:T(2,128)S(1)} fusion(f32[2,2,2,2,2,1024]{5,4,3,2,1,0:T(2,128)} %reshape.172, pred[]{:T(512)S(6)} %eq.83, f32[2,2,2,2,2,1,1024]{6,5,4,3,2,1,0:T(1,128)} %copy-done.8, f32[2,2,2,2,2,1,1024]{6,5,4,3,2,1,0:T(1,128)} %copy-done.7), kind=kLoop, calls=%fused_computation.44 | loop fusion | flops 65536 | bytes 524289 | tf_op jit(solution)/shard_map/add | solution.py:335
  88.4 1.5 %select_n.357 = f32[16,1024]{1,0:T(8,128)} reshape(f32[2,2,1,2,2,1024]{5,4,3,1,0,2:T(2,128)} %copy.19) | data formatting | bytes 131072 | tf_op jit(solution)/shard_map/jit(_where)/select_n | solution.py:75
  89.9 1.0 subtract_convert_fusion.1
  91.0 0.9 broadcast_select_fusion.7
  92.6 1.1 convolution_convert_fusion.2
  93.8 4.6 %collective-permute-done.9 = bf16[128,1024]{1,0:T(8,128)(2,1)S(1)} collective-permute-done((bf16[128,1024]{1,0:T(8,128)(2,1)S(1)}, bf16[128,1024]{1,0:T(8,128)(2,1)S(1)}, u32[]{:S(2)}, u32[]{:S(2)}) %collective-permute-start.9) | collective-permute-done | bytes 262176 | tf_op jit(solution)/shard_map/ppermute | solution.py:45
  98.3 0.7 copy-done.14
  99.2 7.8 %collective-permute-start.10 = (f32[2,2,2,1024]{3,0,1,2:T(2,128)S(1)}, f32[2,2,2,1024]{3,0,1,2:T(2,128)S(1)}, u32[]{:S(2)}, u32[]{:S(2)}) collective-permute-start(f32[2,2,2,1024]{3,0,1,2:T(2,128)S(1)} %select_bitcast_fusion), channel_id=1, source_target_pairs={{0,2},{1,3},{2,0},{3,1},{4,6},{5,7},{6,4},{7,5},{8,10},{9,11},{10,... | collective-permute-start | bytes 98312 | tf_op jit(solution)/shard_map/ppermute | solution.py:35
  107.7 1.2 collective-permute-done.10
  109.0 0.9 collective-permute-start.11
  109.8 1.0 broadcast_select_fusion.11
  110.8 2.9 %collective-permute-done.11 = f32[2,2,1024]{2,0,1:T(2,128)S(1)} collective-permute-done((f32[2,2,1024]{2,0,1:T(2,128)S(1)}, f32[2,2,1024]{2,0,1:T(2,128)S(1)}, u32[]{:S(2)}, u32[]{:S(2)}) %collective-permute-start.11) | collective-permute-done | bytes 16416 | tf_op jit(solution)/shard_map/ppermute | solution.py:35
  113.7 4.1 %collective-permute-start.12 = (f32[2,1024]{1,0:T(2,128)S(1)}, f32[2,1024]{1,0:T(2,128)S(1)}, u32[]{:S(2)}, u32[]{:S(2)}) collective-permute-start(f32[2,1024]{1,0:T(2,128)S(1)} %select_bitcast_fusion.2), channel_id=1, source_target_pairs={{0,16},{8,24},{16,0},{24,8},{1,17},{9,25},{17,1},{25,9},{2,18},{10... | collective-permute-start | bytes 24584 | tf_op jit(solution)/shard_map/ppermute | solution.py:35
  117.9 1.5 %collective-permute-done.12 = f32[2,1024]{1,0:T(2,128)S(1)} collective-permute-done((f32[2,1024]{1,0:T(2,128)S(1)}, f32[2,1024]{1,0:T(2,128)S(1)}, u32[]{:S(2)}, u32[]{:S(2)}) %collective-permute-start.12) | collective-permute-done | bytes 8224 | tf_op jit(solution)/shard_map/ppermute | solution.py:35
  119.4 0.9 add_convert_fusion
  121.8 3.1 %fusion.1 = bf16[128,1024]{1,0:T(8,128)(2,1)} fusion(f32[128,1024]{1,0:T(8,128)S(1)} %bitcast.76, f32[128,1024]{1,0:T(8,128)S(1)} %dynamic_update_slice.3, bf16[128,1024]{1,0:T(8,128)(2,1)S(1)} %copy-done.11, bf16[1024,1024]{1,0:T(8,128)(2,1)} %param.12), kind=kOutput, calls=%fused_computation.6 | convolution fusion | flops 268828672 | bytes 3670016 | tf_op jit(solution)/shard_map/dot_general | solution.py:376
  (112 shorter events, 10.4 us)
Async XLA Ops:
  0.6 39.6 %copy-start = (bf16[1024,1024]{1,0:T(8,128)(2,1)S(1)}, bf16[1024,1024]{1,0:T(8,128)(2,1)}, u32[]{:S(2)}) copy-start(bf16[1024,1024]{1,0:T(8,128)(2,1)} %param.14) | copy-start | bytes 6291460
  0.7 17.0 %copy-start.12 = (bf16[8,16,1024]{2,1,0:T(8,128)(2,1)S(1)}, bf16[8,16,1024]{2,1,0:T(8,128)(2,1)}, u32[]{:S(2)}) copy-start(bf16[8,16,1024]{2,1,0:T(8,128)(2,1)} %param.17) | copy-start | bytes 786436
  1.9 19.5 %collective-permute-start = (bf16[96,1024]{1,0:T(8,128)(2,1)S(1)}, bf16[96,1024]{1,0:T(8,128)(2,1)S(1)}, u32[]{:S(2)}, u32[]{:S(2)}) collective-permute-start(bf16[96,1024]{1,0:T(8,128)(2,1)S(1)} %bitcast.88), channel_id=1, source_target_pairs={{8,16},{16,8},{9,17},{17,9},{10,18},{18,10},{11,19},{19,11},{12,20... | collective-permute-start | bytes 589832 | tf_op jit(solution)/shard_map/ppermute | solution.py:47
  7.2 14.2 %collective-permute-start.1 = (bf16[97,1024]{1,0:T(8,128)(2,1)S(1)}, bf16[97,1024]{1,0:T(8,128)(2,1)S(1)}, u32[]{:S(2)}, u32[]{:S(2)}) collective-permute-start(bf16[97,1024]{1,0:T(8,128)(2,1)S(1)} %pad_maximum_fusion.4), channel_id=1, source_target_pairs={{0,8},{8,0},{16,24},{24,16},{1,9},{9,1},{17,25},{25,17},{2,10},{10... | collective-permute-start | bytes 595976 | tf_op jit(solution)/shard_map/ppermute | solution.py:45
  14.6 6.2 %copy-start.18 = (s32[640]{0:T(1024)S(1)}, s32[640]{0:T(1024)}, u32[]{:S(2)}) copy-start(s32[640]{0:T(1024)} %constant.137.clone) | copy-start | bytes 7684
  14.6 6.2 %copy-start.19 = (s32[640]{0:T(1024)S(1)}, s32[640]{0:T(1024)}, u32[]{:S(2)}) copy-start(s32[640]{0:T(1024)} %constant.136.clone) | copy-start | bytes 7684
  17.6 5.3 %copy-start.16 = (s32[128]{0:T(128)}, s32[128]{0:T(128)S(1)}, u32[]{:S(2)}) copy-start(s32[128]{0:T(128)S(1)} %min.20) | copy-start | bytes 1540
  17.7 5.3 %copy-start.3 = (bf16[8,16,1024]{2,1,0:T(8,128)(2,1)S(1)}, bf16[8,16,1024]{2,1,0:T(8,128)(2,1)}, u32[]{:S(2)}) copy-start(bf16[8,16,1024]{2,1,0:T(8,128)(2,1)} %param.11) | copy-start | bytes 786436
  22.9 4.2 %copy-start.17 = (s32[128]{0:T(128)S(1)}, s32[128]{0:T(128)}, u32[]{:S(2)}) copy-start(s32[128]{0:T(128)} %copy-done.16) | copy-start | bytes 1540
  22.9 4.2 %copy-start.20 = (s32[128]{0:T(128)S(1)}, s32[128]{0:T(128)}, u32[]{:S(2)}) copy-start(s32[128]{0:T(128)} %get-tuple-element.39) | copy-start | bytes 1540
  22.9 4.2 %copy-start.21 = (s32[128]{0:T(128)S(1)}, s32[128]{0:T(128)}, u32[]{:S(2)}) copy-start(s32[128]{0:T(128)} %get-tuple-element.40) | copy-start | bytes 1540
  22.9 4.2 %copy-start.22 = (pred[640]{0:T(1024)(128)(4,1)S(1)}, pred[640]{0:T(1024)(128)(4,1)}, u32[]{:S(2)}) copy-start(pred[640]{0:T(1024)(128)(4,1)} %constant.155) | copy-start | bytes 1924
  23.0 4.2 %copy-start.23 = (pred[640]{0:T(1024)(128)(4,1)S(1)}, pred[640]{0:T(1024)(128)(4,1)}, u32[]{:S(2)}) copy-start(pred[640]{0:T(1024)(128)(4,1)} %constant.154) | copy-start | bytes 1924
  23.0 5.1 %copy-start.24 = (s32[32]{0:T(128)S(1)}, s32[32]{0:T(128)}, u32[]{:S(2)}) copy-start(s32[32]{0:T(128)} %constant.157) | copy-start | bytes 388
  23.3 6.7 %collective-permute-start.2 = (bf16[120,1024]{1,0:T(8,128)(2,1)S(1)}, bf16[120,1024]{1,0:T(8,128)(2,1)S(1)}, u32[]{:S(2)}, u32[]{:S(2)}) collective-permute-start(bf16[120,1024]{1,0:T(8,128)(2,1)S(1)} %select_n.316), channel_id=1, source_target_pairs={{1,2},{3,4},{5,6},{2,1},{4,3},{6,5},{9,10},{11,12},{13,14},{10,9},... | collective-permute-start | bytes 737288 | tf_op jit(solution)/shard_map/ppermute | solution.py:47
  24.1 4.2 %collective-permute-start.3 = (bf16[122,1024]{1,0:T(8,128)(2,1)S(1)}, bf16[122,1024]{1,0:T(8,128)(2,1)S(1)}, u32[]{:S(2)}, u32[]{:S(2)}) collective-permute-start(bf16[122,1024]{1,0:T(8,128)(2,1)S(1)} %pad_maximum_fusion.2), channel_id=1, source_target_pairs={{0,1},{1,0},{2,3},{3,2},{4,5},{5,4},{6,7},{7,6},{8,9},{9,8},{10,11... | collective-permute-start | bytes 749576 | tf_op jit(solution)/shard_map/ppermute | solution.py:45
  28.3 3.8 %collective-permute-start.4 = (bf16[4,1024]{1,0:T(4,128)(2,1)S(1)}, bf16[4,1024]{1,0:T(4,128)(2,1)S(1)}, u32[]{:S(2)}, u32[]{:S(2)}) collective-permute-start(bf16[4,1024]{1,0:T(4,128)(2,1)S(1)} %maximum_select_fusion.3), channel_id=1, source_target_pairs={{0,2},{1,3},{2,0},{3,1},{4,6},{5,7},{6,4},{7,5},{8,10},{9,11},{10,... | collective-permute-start | bytes 24584 | tf_op jit(solution)/shard_map/ppermute | solution.py:35
  32.1 8.1 %copy-start.15 = (bf16[608,1024]{1,0:T(8,128)(2,1)S(1)}, bf16[608,1024]{1,0:T(8,128)(2,1)}, u32[]{:S(2)}) copy-start(bf16[608,1024]{1,0:T(8,128)(2,1)} %broadcast_dynamic-update-slice_fusion) | copy-start | bytes 3735556
  32.2 8.0 %collective-permute-start.5 = (bf16[8,1024]{1,0:T(8,128)(2,1)S(1)}, bf16[8,1024]{1,0:T(8,128)(2,1)S(1)}, u32[]{:S(2)}, u32[]{:S(2)}) collective-permute-start(bf16[8,1024]{1,0:T(8,128)(2,1)S(1)} %maximum_select_fusion.2), channel_id=1, source_target_pairs={{0,4},{1,5},{2,6},{3,7},{4,0},{5,1},{6,2},{7,3},{8,12},{9,13},{10,... | collective-permute-start | bytes 49160 | tf_op jit(solution)/shard_map/ppermute | solution.py:35
  40.1 4.0 %collective-permute-start.6 = (bf16[16,1024]{1,0:T(8,128)(2,1)S(1)}, bf16[16,1024]{1,0:T(8,128)(2,1)S(1)}, u32[]{:S(2)}, u32[]{:S(2)}) collective-permute-start(bf16[16,1024]{1,0:T(8,128)(2,1)S(1)} %maximum_select_fusion.1), channel_id=1, source_target_pairs={{0,16},{8,24},{16,0},{24,8},{1,17},{9,25},{17,1},{25,9},{2,18},{10... | collective-permute-start | bytes 98312 | tf_op jit(solution)/shard_map/ppermute | solution.py:35
  74.6 0.7 copy-start.7
  74.6 0.8 copy-start.8
  75.7 4.1 %collective-permute-start.7 = (bf16[184,1024]{1,0:T(8,128)(2,1)S(1)}, bf16[184,1024]{1,0:T(8,128)(2,1)}, u32[]{:S(2)}, u32[]{:S(2)}) collective-permute-start(bf16[184,1024]{1,0:T(8,128)(2,1)S(1)} %pad_maximum_fusion.1), channel_id=1, source_target_pairs={{0,1},{1,0},{2,3},{3,2},{4,5},{5,4},{6,7},{7,6},{8,9},{9,8},{10,11... | collective-permute-start | bytes 1130504 | tf_op jit(solution)/shard_map/ppermute | solution.py:45
  75.8 3.9 %collective-permute-start.8 = (bf16[120,1024]{1,0:T(8,128)(2,1)}, bf16[120,1024]{1,0:T(8,128)(2,1)S(1)}, u32[]{:S(2)}, u32[]{:S(2)}) collective-permute-start(bf16[120,1024]{1,0:T(8,128)(2,1)} %get-tuple-element.24), channel_id=1, source_target_pairs={{1,2},{3,4},{5,6},{2,1},{4,3},{6,5},{9,10},{11,12},{13,14},{10,9},... | collective-permute-start | bytes 737288 | tf_op jit(solution)/shard_map/ppermute | solution.py:47
  87.1 0.6 copy-start.5
  89.9 2.7 %copy-start.1 = (bf16[1024,1024]{1,0:T(8,128)(2,1)S(1)}, bf16[1024,1024]{1,0:T(8,128)(2,1)}, u32[]{:S(2)}) copy-start(bf16[1024,1024]{1,0:T(8,128)(2,1)} %param.15) | copy-start | bytes 6291460
  89.9 2.7 %copy-start.13 = (bf16[128,1024]{1,0:T(8,128)(2,1)S(1)}, bf16[128,1024]{1,0:T(8,128)(2,1)}, u32[]{:S(2)}) copy-start(bf16[128,1024]{1,0:T(8,128)(2,1)} %get-tuple-element.6) | copy-start | bytes 786436
  91.9 7.2 %copy-start.6 = (f32[2,2,2,2,2,1024]{5,0,1,3,4,2:T(2,128)S(1)}, f32[2,2,2,2,2,1024]{5,0,1,3,4,2:T(2,128)}, u32[]{:S(2)}) copy-start(f32[2,2,2,2,2,1024]{5,0,1,3,4,2:T(2,128)} %copy-done.5) | copy-start | bytes 393220
  91.9 15.2 %copy-start.9 = (bf16[6,16,1024]{2,1,0:T(8,128)(2,1)S(1)}, bf16[6,16,1024]{2,1,0:T(8,128)(2,1)}, u32[]{:S(2)}) copy-start(bf16[6,16,1024]{2,1,0:T(8,128)(2,1)} %get-tuple-element.11) | copy-start | bytes 589828
  91.9 15.2 %copy-start.10 = (bf16[6,16,1024]{2,1,0:T(8,128)(2,1)S(1)}, bf16[6,16,1024]{2,1,0:T(8,128)(2,1)}, u32[]{:S(2)}) copy-start(bf16[6,16,1024]{2,1,0:T(8,128)(2,1)} %get-tuple-element.12) | copy-start | bytes 589828
  91.9 6.4 %collective-permute-start.9 = (bf16[128,1024]{1,0:T(8,128)(2,1)S(1)}, bf16[128,1024]{1,0:T(8,128)(2,1)S(1)}, u32[]{:S(2)}, u32[]{:S(2)}) collective-permute-start(bf16[128,1024]{1,0:T(8,128)(2,1)S(1)} %pad_maximum_fusion.3), channel_id=1, source_target_pairs={{0,8},{8,0},{16,24},{24,16},{1,9},{9,1},{17,25},{25,17},{2,10},{10... | collective-permute-start | bytes 786440 | tf_op jit(solution)/shard_map/ppermute | solution.py:45
  98.3 0.7 copy-start.14
  99.1 21.2 %copy-start.2 = (bf16[1024,1024]{1,0:T(8,128)(2,1)S(1)}, bf16[1024,1024]{1,0:T(8,128)(2,1)}, u32[]{:S(2)}) copy-start(bf16[1024,1024]{1,0:T(8,128)(2,1)} %param.13) | copy-start | bytes 6291460
  99.2 9.7 %collective-permute-start.10 = (f32[2,2,2,1024]{3,0,1,2:T(2,128)S(1)}, f32[2,2,2,1024]{3,0,1,2:T(2,128)S(1)}, u32[]{:S(2)}, u32[]{:S(2)}) collective-permute-start(f32[2,2,2,1024]{3,0,1,2:T(2,128)S(1)} %select_bitcast_fusion), channel_id=1, source_target_pairs={{0,2},{1,3},{2,0},{3,1},{4,6},{5,7},{6,4},{7,5},{8,10},{9,11},{10,... | collective-permute-start | bytes 98312 | tf_op jit(solution)/shard_map/ppermute | solution.py:35
  107.1 2.8 %collective-permute-start.13 = (bf16[96,1024]{1,0:T(8,128)(2,1)S(1)}, bf16[96,1024]{1,0:T(8,128)(2,1)S(1)}, u32[]{:S(2)}, u32[]{:S(2)}) collective-permute-start(bf16[96,1024]{1,0:T(8,128)(2,1)S(1)} %bitcast.89), channel_id=1, source_target_pairs={{8,16},{16,8},{9,17},{17,9},{10,18},{18,10},{11,19},{19,11},{12,20... | collective-permute-start | bytes 589832 | tf_op jit(solution)/shard_map/ppermute | solution.py:47
  109.0 4.7 %collective-permute-start.11 = (f32[2,2,1024]{2,0,1:T(2,128)S(1)}, f32[2,2,1024]{2,0,1:T(2,128)S(1)}, u32[]{:S(2)}, u32[]{:S(2)}) collective-permute-start(f32[2,2,1024]{2,0,1:T(2,128)S(1)} %select_bitcast_fusion.1), channel_id=1, source_target_pairs={{0,4},{1,5},{2,6},{3,7},{4,0},{5,1},{6,2},{7,3},{8,12},{9,13},{10,... | collective-permute-start | bytes 49160 | tf_op jit(solution)/shard_map/ppermute | solution.py:35
  113.7 5.7 %collective-permute-start.12 = (f32[2,1024]{1,0:T(2,128)S(1)}, f32[2,1024]{1,0:T(2,128)S(1)}, u32[]{:S(2)}, u32[]{:S(2)}) collective-permute-start(f32[2,1024]{1,0:T(2,128)S(1)} %select_bitcast_fusion.2), channel_id=1, source_target_pairs={{0,16},{8,24},{16,0},{24,8},{1,17},{9,25},{17,1},{25,9},{2,18},{10... | collective-permute-start | bytes 24584 | tf_op jit(solution)/shard_map/ppermute | solution.py:35
  120.3 1.3 %copy-start.4 = (f32[128,1024]{1,0:T(8,128)S(1)}, f32[128,1024]{1,0:T(8,128)}, u32[]{:S(2)}) copy-start(f32[128,1024]{1,0:T(8,128)} %slice.164) | copy-start | bytes 1572868
  120.3 1.4 %copy-start.11 = (bf16[128,1024]{1,0:T(8,128)(2,1)S(1)}, bf16[128,1024]{1,0:T(8,128)(2,1)}, u32[]{:S(2)}) copy-start(bf16[128,1024]{1,0:T(8,128)(2,1)} %get-tuple-element.7) | copy-start | bytes 786436

commit v8 on v7

--- a/solution.py
+++ b/solution.py
@@ -76,13 +76,14 @@
 
 
 def attention_kernel(
-    own, first, last, q_ref, kf_ref, kg_ref, vf_ref, vg_ref, g_ref, mask_ref, o_ref, dq_ref, dkv_ref, wide_ref
+    own, first, last, q_ref, ko_ref, kh_ref, kg_ref, vo_ref, vh_ref, vg_ref, g_ref, mask_ref,
+    o_ref, dq_ref, dkv_ref, wide_ref,
 ):
     head_size = q_ref.shape[1] // 2
     score_scale = 1.0 / math.sqrt(head_size)
     q = q_ref[...]
-    k = jnp.concatenate([kf_ref[...], kg_ref[...]], axis=0)
-    v = jnp.concatenate([vf_ref[...], vg_ref[...]], axis=0)
+    k = jnp.concatenate([ko_ref[...], kh_ref[...], kg_ref[...]], axis=0)
+    v = jnp.concatenate([vo_ref[...], vh_ref[...], vg_ref[...]], axis=0)
     g = g_ref[...]
     keep = mask_ref[...] > 0
     lane_head = lax.broadcasted_iota(jnp.int32, q.shape, 1) // head_size
@@ -131,14 +132,15 @@
 
 def attention(queries, keys, values, global_keys, global_values, grad_attended, keep):
     tokens, model_width = queries.shape
-    first = keys.shape[0]
+    first = keys[0].shape[0] + keys[1].shape[0]
     last = first + global_keys.shape[0]
     key_count = last
     lanes = 2 * (model_width // HEADS)
     steps = model_width // lanes
     token_block = pl.BlockSpec((tokens, lanes), lambda i: (0, i))
     key_block = pl.BlockSpec((key_count, lanes), lambda i: (0, i))
-    frame_block = pl.BlockSpec((first, lanes), lambda i: (0, i))
+    own_block = pl.BlockSpec((keys[0].shape[0], lanes), lambda i: (0, i))
+    halo_block = pl.BlockSpec((keys[1].shape[0], lanes), lambda i: (0, i))
     global_block = pl.BlockSpec((last - first, lanes), lambda i: (0, i))
     mask_block = pl.BlockSpec((tokens, key_count), lambda i: (0, 0))
     grads_block = pl.BlockSpec((2, key_count, lanes), lambda i: (0, 0, i))
@@ -153,9 +155,11 @@
         grid=(steps,),
         in_specs=[
             token_block,
-            frame_block,
+            own_block,
+            halo_block,
             global_block,
-            frame_block,
+            own_block,
+            halo_block,
             global_block,
             token_block,
             mask_block,
@@ -170,7 +174,7 @@
         cost_estimate=pl.CostEstimate(
             flops=flops, transcendentals=HEADS * tokens * key_count, bytes_accessed=moved
         ),
-    )(queries, keys, global_keys, values, global_values, grad_attended, keep)
+    )(queries, *keys, global_keys, *values, global_values, grad_attended, keep)
 
 
 def split_wide(x):
@@ -206,20 +210,30 @@
     key_count = -(-used // 128) * 128
 
     flat_tokens = features.reshape(-1, model_width)
+    own_keys = jnp.dot(flat_tokens, w_key, preferred_element_type=jnp.float32).astype(jnp.bfloat16)
+    own_values = jnp.dot(flat_tokens, w_value, preferred_element_type=jnp.float32).astype(
+        jnp.bfloat16
+    )
 
     own_index = row_index * col_count + col_index
     own_place = lax.dynamic_index_in_dim(reg_pos, own_index, 0, keepdims=False)
     own_local = (own_place // band_cols - first_row) * tile_cols + (own_place % band_cols - first_col)
-    gathered = lax.dynamic_slice_in_dim(flat_tokens, own_local, 1, 0)
+    gathered = jnp.concatenate(
+        [
+            lax.dynamic_slice_in_dim(own_keys, own_local, 1, 0),
+            lax.dynamic_slice_in_dim(own_values, own_local, 1, 0),
+        ],
+        axis=1,
+    )
     order = [col_bits, 0] + list(range(1, col_bits)) + list(range(col_bits + 1, all_bits))
 
     from_above, from_below, got = exchange(
         features[:RAD].reshape(-1, model_width),
         features[tile_rows - RAD :].reshape(-1, model_width),
         "rows",
-        gathered,
-    )
-    gathered = gather_step(gathered, got, order[0])
+        gathered.reshape(-1, model_width),
+    )
+    gathered = gather_step(gathered, got.reshape(gathered.shape), order[0])
     extended = jnp.concatenate(
         [
             from_above.reshape(RAD, tile_cols, model_width),
@@ -232,18 +246,17 @@
         extended[:, :RAD].reshape(-1, model_width),
         extended[:, tile_cols - RAD :].reshape(-1, model_width),
         "cols",
-        gathered,
-    )
-    gathered = gather_step(gathered, got, order[1])
+        gathered.reshape(-1, model_width),
+    )
+    gathered = gather_step(gathered, got.reshape(gathered.shape), order[1])
 
     queries = jnp.dot(flat_tokens, w_query, preferred_element_type=jnp.float32).astype(jnp.bfloat16)
     grad_attended = jnp.dot(
         grad_out.reshape(-1, model_width), w_out.T, preferred_element_type=jnp.float32
     ).astype(jnp.bfloat16)
 
-    key_features = jnp.concatenate(
+    halo_features = jnp.concatenate(
         [
-            flat_tokens,
             from_above,
             from_below,
             from_left,
@@ -252,20 +265,18 @@
         ],
         axis=0,
     )
-    keys = jnp.dot(key_features, w_key, preferred_element_type=jnp.float32).astype(jnp.bfloat16)
-    values = jnp.dot(key_features, w_value, preferred_element_type=jnp.float32).astype(
+    halo_keys = jnp.dot(halo_features, w_key, preferred_element_type=jnp.float32).astype(
+        jnp.bfloat16
+    )
+    halo_values = jnp.dot(halo_features, w_value, preferred_element_type=jnp.float32).astype(
         jnp.bfloat16
     )
 
     for position in order[2:]:
         gathered = gather_step(gathered, partner(gathered, position), position)
-    global_features = jnp.take(gathered, jnp.asarray(gather_order(order, device_count)), axis=0)
-    global_keys = jnp.dot(global_features, w_key, preferred_element_type=jnp.float32).astype(
-        jnp.bfloat16
-    )
-    global_values = jnp.dot(
-        global_features, w_value, preferred_element_type=jnp.float32
-    ).astype(jnp.bfloat16)
+    global_kv = jnp.take(gathered, jnp.asarray(gather_order(order, device_count)), axis=0)
+    global_keys = global_kv[:, :model_width]
+    global_values = global_kv[:, model_width:]
 
     def grid(height, width, row0, col0):
         a, b = np.meshgrid(np.arange(height) + row0, np.arange(width) + col0, indexing="ij")
@@ -302,7 +313,13 @@
     keep = ((inside & (key_kind == 0)) | (key_kind == 1)).astype(jnp.float32)
 
     attended, query_grads, rounded_grads, wide_grads = attention(
-        queries, keys, values, global_keys, global_values, grad_attended, keep
+        queries,
+        (own_keys, halo_keys),
+        (own_values, halo_values),
+        global_keys,
+        global_values,
+        grad_attended,
+        keep,
     )
     layer_out = (
         jnp.dot(attended, w_out, preferred_element_type=jnp.float32)
@@ -325,7 +342,6 @@
 
     strips_from = tokens + 2 * band_keys
     keep_part, send_part = scatter_split(scatter, left, back_order[0])
-    strip_shape = (ext_rows, RAD, model_width)
     from_left, from_right, got = exchange(
         given(strips_from, strips_from + strip_keys).astype(jnp.bfloat16),
         given(strips_from + strip_keys, frame_keys).astype(jnp.bfloat16),
@@ -333,25 +349,36 @@
         split_wide(send_part.reshape(-1, model_width)),
     )
     scatter = keep_part + join_wide(got).reshape(keep_part.shape)
-    received = jnp.pad(
-        from_left.astype(jnp.float32).reshape(strip_shape), ((0, 0), (0, tile_cols - RAD), (0, 0))
-    ) + jnp.pad(
-        from_right.astype(jnp.float32).reshape(strip_shape), ((0, 0), (tile_cols - RAD, 0), (0, 0))
-    )
+    corner = RAD * RAD
+    lower_rows = (RAD + tile_rows) * RAD
+
+    def cols_placed(piece, height, at_right):
+        piece = piece.astype(jnp.float32).reshape(height, RAD, model_width)
+        pad = (tile_cols - RAD, 0) if at_right else (0, tile_cols - RAD)
+        return jnp.pad(piece, ((0, 0), pad, (0, 0)))
+
     band_shape = (RAD, tile_cols, model_width)
+    upper = (
+        given(tokens, tokens + band_keys).reshape(band_shape)
+        + cols_placed(from_left[:corner], RAD, False)
+        + cols_placed(from_right[:corner], RAD, True)
+    )
+    lower = (
+        given(tokens + band_keys, strips_from).reshape(band_shape)
+        + cols_placed(from_left[lower_rows:], RAD, False)
+        + cols_placed(from_right[lower_rows:], RAD, True)
+    )
     keep_part, send_part = scatter_split(scatter, left, back_order[1])
     from_above, from_below, got = exchange(
-        (given(tokens, tokens + band_keys).reshape(band_shape) + received[:RAD])
-        .reshape(-1, model_width)
-        .astype(jnp.bfloat16),
-        (given(tokens + band_keys, strips_from).reshape(band_shape) + received[RAD + tile_rows :])
-        .reshape(-1, model_width)
-        .astype(jnp.bfloat16),
+        upper.reshape(-1, model_width).astype(jnp.bfloat16),
+        lower.reshape(-1, model_width).astype(jnp.bfloat16),
         "rows",
         split_wide(send_part.reshape(-1, model_width)),
     )
     scatter = keep_part + join_wide(got).reshape(keep_part.shape)
-    received = received[RAD : RAD + tile_rows]
+    received = cols_placed(from_left[corner:lower_rows], tile_rows, False) + cols_placed(
+        from_right[corner:lower_rows], tile_rows, True
+    )
     received = received + jnp.pad(
         from_above.astype(jnp.float32).reshape(band_shape), ((0, tile_rows - RAD), (0, 0), (0, 0))
     )

time: 126 us -> 129 us (1.024)
  waiting for transfers between devices: 11.7 us -> 14.6 us
    reshape x2 -> x8, local copies, waits for them, and re-layouts: 1.12 us -> 5.41 us  [the longest x6 5.39 us: cols_placed(): piece = piece.astype(jnp.float32).reshape(height, RAD, model_width)]
    ppermute x6, starting transfers between devices: 17.9 us -> 21.4 us  [partner(): return lax.ppermute(x, axis, [(i, i ^ 1 << bit) for i in range(size)])]
    ppermute x4, starting transfers between devices: 9.49 us -> 6.48 us  [exchange(): got_first = lax.ppermute(first, axis, [(i, i ^ 1) for i in range(size)])]
    slice x0 -> x5, local copies, waits for them, and re-layouts: none -> 2.94 us  [the longest x1 0.93 us: shards(): from_right[corner:lower_rows]]
    select_n x4, local copies, waits for them, and re-layouts: 2.39 us -> 0.3 us  [scatter_split(): return (jnp.where(high, upper, lower), jnp.where(high, lower, upper))]
    dot_general x4, matrix products: 10.8 us -> 8.8 us  [the longest x1 4.07 us: shards(): jnp.dot(halo_features, w_key, preferred_element_type=jnp.float32)]
    unnamed x51 -> x34, local copies, waits for them, and re-layouts: 3.76 us -> 1.74 us
    ppermute x6, waiting for transfers between devices: 6.92 us -> 8.9 us  [partner(): return lax.ppermute(x, axis, [(i, i ^ 1 << bit) for i in range(size)])]
  transfers between devices with their start and end apart: 14 -> 14, of which waited for: 6 -> 5; matrix products, arithmetic and copies ran while one was open for 21% -> 22% of each run, Pallas kernels for 0% -> 0%
where the time goes in v8:
time: 129 us; the launch traced here: 128 us
  starting transfers between devices  31.4 us (24%)
  matrix products  29.5 us (23%)
  local copies, waits for them, and re-layouts  17.8 us (14%)
  Pallas kernels  16.6 us (13%)
  other arithmetic  14.6 us (11%)
  waiting for transfers between devices  14.6 us (11%)
  between operations  3.97 us (3%)
    ppermute x6, starting transfers between devices, partner(): return lax.ppermute(x, axis, [(i, i ^ 1 << bit) for i in range(size)])  21.4 us
    pallas_call x1, Pallas kernels, attention(): pl.pallas_call(functools.partial(attention_kernel, tokens, first, last),...  16.6 us
    ppermute x6, waiting for transfers between devices, partner(): return lax.ppermute(x, axis, [(i, i ^ 1 << bit) for i in range(size)])  8.9 us
    ppermute x4, starting transfers between devices, exchange(): got_first = lax.ppermute(first, axis, [(i, i ^ 1) for i in range(size)])  6.48 us
    ppermute x4, waiting for transfers between devices, exchange(): got_first = lax.ppermute(first, axis, [(i, i ^ 1) for i in range(size)])  5.7 us
    reshape x6, local copies, waits for them, and re-layouts, cols_placed(): piece = piece.astype(jnp.float32).reshape(height, RAD, model_width)  5.39 us
    dot_general x1, matrix products, shards(): jnp.dot(rounded_grads[1, :frame_keys], w_value.T, preferred_element_type=...  4.12 us
    dot_general x1, matrix products, shards(): jnp.dot(halo_features, w_key, preferred_element_type=jnp.float32)  4.07 us
  transfers between devices with their start and end apart: 14, of which 5 were waited for; matrix products, arithmetic and copies ran while one was open for 22% of the time, Pallas kernels for 0%

profile of v8, /device:TPU:0, one launch (start us, length us, event | category | flops | bytes accessed | tf_op | source)
XLA Modules:
  0.0 128.5 jit_solution(9664519188762412106)
XLA Ops:
  0.7 1.9 %broadcast_select_fusion.8 = (bf16[6,16,1024]{2,1,0:T(8,128)(2,1)S(1)}, bf16[6,16,1024]{2,1,0:T(8,128)(2,1)}) fusion(pred[]{:T(512)S(6)} %eq.68, bf16[8,16,1024]{2,1,0:T(8,128)(2,1)} %param.11), kind=kLoop, calls=%fused_computation.36 | loop fusion | flops 196608 | bytes 786433 | tf_op jit(solution)/shard_map/jit(_where)/select_n | solution.py:41
  3.2 1.2 dynamic_slice.13
  7.1 2.1 %convolution_convert_fusion.5.ko_ref = bf16[128,1024]{1,0:T(8,128)(2,1)S(1)} fusion(bf16[128,1024]{1,0:T(8,128)(2,1)} %bitcast.77, bf16[1024,1024]{1,0:T(8,128)(2,1)} %param.13), kind=kOutput, calls=%fused_computation.10 | convolution fusion | flops 268566528 | bytes 2621440 | tf_op jit(solution)/shard_map/dot_general | solution.py:213
  9.8 0.7 pad_maximum_fusion.4
  10.5 5.7 %collective-permute-start.1 = (bf16[98,1024]{1,0:T(8,128)(2,1)}, bf16[98,1024]{1,0:T(8,128)(2,1)S(1)}, u32[]{:S(2)}, u32[]{:S(2)}) collective-permute-start(bf16[98,1024]{1,0:T(8,128)(2,1)} %pad_maximum_fusion.4), channel_id=1, source_target_pairs={{0,8},{8,0},{16,24},{24,16},{1,9},{9,1},{17,25},{25,17},{2,10},{10... | collective-permute-start | bytes 602120 | tf_op jit(solution)/shard_map/ppermute | solution.py:45
  16.2 2.7 %convolution_convert_fusion.6.q_ref = bf16[128,1024]{1,0:T(8,128)(2,1)} fusion(bf16[128,1024]{1,0:T(8,128)(2,1)S(1)} %bitcast.79, bf16[1024,1024]{1,0:T(8,128)(2,1)} %param.12), kind=kOutput, calls=%fused_computation.11 | convolution fusion | flops 268566528 | bytes 2621440 | tf_op jit(solution)/shard_map/dot_general | solution.py:253
  19.1 3.2 %convolution_convert_fusion.3.g_ref = bf16[128,1024]{1,0:T(8,128)(2,1)} fusion(bf16[128,1024]{1,0:T(8,128)(2,1)} %bitcast.90, bf16[1024,1024]{1,0:T(8,128)(2,1)} %param.15), kind=kOutput, calls=%fused_computation.8 | convolution fusion | flops 268566528 | bytes 2621440 | tf_op jit(solution)/shard_map/dot_general | solution.py:254
  22.7 1.0 copy-done.9
  24.0 0.9 or_convert_fusion.mask_ref
  25.9 3.4 %collective-permute-start.4 = (bf16[4,2048]{1,0:T(4,128)(2,1)S(1)}, bf16[4,2048]{1,0:T(4,128)(2,1)S(1)}, u32[]{:S(2)}, u32[]{:S(2)}) collective-permute-start(bf16[4,2048]{1,0:T(4,128)(2,1)S(1)} %maximum_select_fusion.3), channel_id=1, source_target_pairs={{0,2},{1,3},{2,0},{3,1},{4,6},{5,7},{6,4},{7,5},{8,10},{9,11},{10,... | collective-permute-start | bytes 49160 | tf_op jit(solution)/shard_map/ppermute | solution.py:35
  29.3 0.8 select_dynamic-update-slice_fusion.1
  30.1 0.8 select_dynamic-update-slice_fusion
  31.5 2.1 %collective-permute-done.4 = bf16[4,2048]{1,0:T(4,128)(2,1)S(1)} collective-permute-done((bf16[4,2048]{1,0:T(4,128)(2,1)S(1)}, bf16[4,2048]{1,0:T(4,128)(2,1)S(1)}, u32[]{:S(2)}, u32[]{:S(2)}) %collective-permute-start.4) | collective-permute-done | bytes 16416 | tf_op jit(solution)/shard_map/ppermute | solution.py:35
  33.6 3.8 %collective-permute-start.5 = (bf16[8,2048]{1,0:T(8,128)(2,1)S(1)}, bf16[8,2048]{1,0:T(8,128)(2,1)S(1)}, u32[]{:S(2)}, u32[]{:S(2)}) collective-permute-start(bf16[8,2048]{1,0:T(8,128)(2,1)S(1)} %maximum_select_fusion.2), channel_id=1, source_target_pairs={{0,4},{1,5},{2,6},{3,7},{4,0},{5,1},{6,2},{7,3},{8,12},{9,13},{10,... | collective-permute-start | bytes 98312 | tf_op jit(solution)/shard_map/ppermute | solution.py:35
  37.4 4.1 %convolution_convert_fusion.1.kh_ref = bf16[480,1024]{1,0:T(8,128)(2,1)} fusion(bf16[480,1024]{1,0:T(8,128)(2,1)} %broadcast_dynamic-update-slice_fusion, bf16[1024,1024]{1,0:T(8,128)(2,1)} %param.13), kind=kOutput, calls=%fused_computation.3 | convolution fusion | flops 1007124480 | bytes 4063232 | tf_op jit(solution)/shard_map/dot_general | solution.py:268
  41.5 0.7 collective-permute-start.6
  42.3 2.2 %convolution_convert_fusion.vh_ref = bf16[480,1024]{1,0:T(8,128)(2,1)} fusion(bf16[480,1024]{1,0:T(8,128)(2,1)S(1)} %copy-done.10, bf16[1024,1024]{1,0:T(8,128)(2,1)S(1)} %copy-done), kind=kOutput, calls=%fused_computation.2 | convolution fusion | flops 1007124480 | bytes 4063232 | tf_op jit(solution)/shard_map/dot_general | solution.py:271
  44.4 1.5 %collective-permute-done.6 = bf16[16,2048]{1,0:T(8,128)(2,1)S(1)} collective-permute-done((bf16[16,2048]{1,0:T(8,128)(2,1)S(1)}, bf16[16,2048]{1,0:T(8,128)(2,1)S(1)}, u32[]{:S(2)}, u32[]{:S(2)}) %collective-permute-start.6) | collective-permute-done | bytes 65568 | tf_op jit(solution)/shard_map/ppermute | solution.py:35
  47.3 16.6 %shard_map.122 = (bf16[128,1024]{1,0:T(8,128)(2,1)}, bf16[128,1024]{1,0:T(8,128)(2,1)}, bf16[2,640,1024]{2,1,0:T(8,128)(2,1)}, f32[2,160,1024]{2,1,0:T(8,128)}) custom-call(bf16[128,1024]{1,0:T(8,128)(2,1)} %convolution_convert_fusion.6.q_ref, bf16[128,1024]{1,0:T(8,128)(2,1)} %copy-done.4, bf16[480,1024]{1,0:T(8,128)(2,1)} %convolution_convert_fusion.1.kh_ref, ...), custom_call_target="tpu_custom_call" | custom-call | flops 2013265920 | bytes 8978432 | tf_op jit(solution)/shard_map/pallas_call | solution.py:153
  63.9 3.3 %fusion.3 = f32[560,1024]{1,0:T(8,128)S(1)} fusion(bf16[1024,1024]{1,0:T(8,128)(2,1)} %param.13, bf16[2,640,1024]{2,1,0:T(8,128)(2,1)} %get-tuple-element.8), kind=kOutput, calls=%fused_computation.13 | convolution fusion | flops 1174405120 | bytes 5537792 | tf_op jit(solution)/shard_map/dot_general | solution.py:330
  67.3 4.1 %fusion.14 = (bf16[560,1024]{1,0:T(8,128)(2,1)S(1)}, f32[560,1024]{1,0:T(8,128)}) fusion(f32[560,1024]{1,0:T(8,128)S(1)} %fusion.3, bf16[1024,1024]{1,0:T(8,128)(2,1)S(1)} %copy-done, bf16[2,640,1024]{2,1,0:T(8,128)(2,1)} %get-tuple-element.8), kind=kOutput, calls=%fused_computation.85 | convolution fusion | flops 1175552000 | bytes 8978432 | tf_op jit(solution)/shard_map/dot_general | solution.py:332
  71.4 1.0 slice.147
  73.2 0.8 pad_maximum_fusion.1
  74.0 0.8 collective-permute-start.8
  74.9 1.2 fusion.9
  76.1 1.0 broadcast_select_fusion.3
  77.1 0.7 copy-done.3
  78.4 1.6 %reshape.208 = bf16[6,6,1024]{2,1,0:T(8,128)(2,1)} reshape(bf16[36,1024]{1,0:T(8,128)(2,1)} %get-tuple-element.37) | data formatting | bytes 147456 | tf_op jit(solution)/shard_map/reshape | solution.py:356
  80.7 1.6 %reshape.207 = bf16[6,6,1024]{2,1,0:T(8,128)(2,1)} reshape(bf16[36,1024]{1,0:T(8,128)(2,1)} %get-tuple-element.35) | data formatting | bytes 147456 | tf_op jit(solution)/shard_map/reshape | solution.py:356
  82.9 1.5 %reshape.210 = bf16[6,6,1024]{2,1,0:T(8,128)(2,1)} reshape(bf16[36,1024]{1,0:T(8,128)(2,1)} %get-tuple-element.34) | data formatting | bytes 147456 | tf_op jit(solution)/shard_map/reshape | solution.py:356
  84.4 0.9 convert_add_fusion.1
  85.3 0.7 reshape.205
  86.0 1.1 bitcast_add_fusion
  87.4 1.9 %broadcast_select_fusion.7 = (bf16[6,16,1024]{2,1,0:T(8,128)(2,1)S(1)}, bf16[6,16,1024]{2,1,0:T(8,128)(2,1)}) fusion(pred[]{:T(512)S(6)} %eq.68, bf16[6,6,1024]{2,1,0:T(8,128)(2,1)} %reshape.208, f32[6,16,1024]{2,1,0:T(8,128)S(1)} %bitcast.82, bf16[6,6,1024]{2,1,0:T(8,128)(2,1)} %reshape.207, bf16[6,6,1024]{2,1,0:T(8,128)(2,1)} %reshape.211, ...), kind=kLoop, calls=%fused_computation.35 | loop fusion | flops 1179648 | bytes 1474561 | tf_op jit(solution)/shard_map/jit(_where)/select_n | solution.py:41
  89.3 0.7 collective-permute-start.9
  90.0 5.7 %collective-permute-done.9 = bf16[128,1024]{1,0:T(8,128)(2,1)S(1)} collective-permute-done((bf16[128,1024]{1,0:T(8,128)(2,1)S(1)}, bf16[128,1024]{1,0:T(8,128)(2,1)S(1)}, u32[]{:S(2)}, u32[]{:S(2)}) %collective-permute-start.9) | collective-permute-done | bytes 262176 | tf_op jit(solution)/shard_map/ppermute | solution.py:45
  95.9 9.5 %collective-permute-start.10 = (f32[2,2,2,1024]{3,0,1,2:T(2,128)S(1)}, f32[2,2,2,1024]{3,0,1,2:T(2,128)}, u32[]{:S(2)}, u32[]{:S(2)}) collective-permute-start(f32[2,2,2,1024]{3,0,1,2:T(2,128)S(1)} %select_bitcast_fusion), channel_id=1, source_target_pairs={{0,2},{1,3},{2,0},{3,1},{4,6},{5,7},{6,4},{7,5},{8,10},{9,11},{10,... | collective-permute-start | bytes 98312 | tf_op jit(solution)/shard_map/ppermute | solution.py:35
  105.4 2.8 %convolution_convert_fusion.2 = bf16[128,1024]{1,0:T(8,128)(2,1)} fusion(bf16[128,1024]{1,0:T(8,128)(2,1)} %get-tuple-element.6, bf16[1024,1024]{1,0:T(8,128)(2,1)} %param.15), kind=kOutput, calls=%fused_computation.7 | convolution fusion | flops 268566528 | bytes 2621440 | tf_op jit(solution)/shard_map/dot_general | solution.py:325
  108.2 1.1 slice.186
  109.4 0.9 slice.213
  110.3 1.3 %collective-permute-start.13 = (bf16[96,1024]{1,0:T(8,128)(2,1)}, bf16[96,1024]{1,0:T(8,128)(2,1)}, u32[]{:S(2)}, u32[]{:S(2)}) collective-permute-start(bf16[96,1024]{1,0:T(8,128)(2,1)} %bitcast.24), channel_id=1, source_target_pairs={{8,16},{16,8},{9,17},{17,9},{10,18},{18,10},{11,19},{19,11},{12,20... | collective-permute-start | bytes 589832 | tf_op jit(solution)/shard_map/ppermute | solution.py:47
  111.8 0.9 bitcast_add_fusion.2
  112.8 1.0 broadcast_select_fusion.11
  113.8 3.7 %collective-permute-done.11 = f32[2,2,1024]{2,0,1:T(2,128)S(1)} collective-permute-done((f32[2,2,1024]{2,0,1:T(2,128)S(1)}, f32[2,2,1024]{2,0,1:T(2,128)S(1)}, u32[]{:S(2)}, u32[]{:S(2)}) %collective-permute-start.11) | collective-permute-done | bytes 16416 | tf_op jit(solution)/shard_map/ppermute | solution.py:35
  117.5 3.9 %collective-permute-start.12 = (f32[2,1024]{1,0:T(2,128)S(1)}, f32[2,1024]{1,0:T(2,128)S(1)}, u32[]{:S(2)}, u32[]{:S(2)}) collective-permute-start(f32[2,1024]{1,0:T(2,128)S(1)} %select_bitcast_fusion.2), channel_id=1, source_target_pairs={{0,16},{8,24},{16,0},{24,8},{1,17},{9,25},{17,1},{25,9},{2,18},{10... | collective-permute-start | bytes 24584 | tf_op jit(solution)/shard_map/ppermute | solution.py:35
  121.5 1.5 %collective-permute-done.12 = f32[2,1024]{1,0:T(2,128)S(1)} collective-permute-done((f32[2,1024]{1,0:T(2,128)S(1)}, f32[2,1024]{1,0:T(2,128)S(1)}, u32[]{:S(2)}, u32[]{:S(2)}) %collective-permute-start.12) | collective-permute-done | bytes 8224 | tf_op jit(solution)/shard_map/ppermute | solution.py:35
  123.1 0.9 add_convert_fusion.2
  125.4 3.1 %fusion.1 = bf16[128,1024]{1,0:T(8,128)(2,1)} fusion(f32[128,1024]{1,0:T(8,128)S(1)} %bitcast.80, f32[128,1024]{1,0:T(8,128)S(1)} %dynamic_update_slice.3, bf16[128,1024]{1,0:T(8,128)(2,1)S(1)} %copy-done.6, bf16[1024,1024]{1,0:T(8,128)(2,1)} %param.12), kind=kOutput, calls=%fused_computation.6 | convolution fusion | flops 268828672 | bytes 3670016 | tf_op jit(solution)/shard_map/dot_general | solution.py:403
  (106 shorter events, 9.7 us)
Async XLA Ops:
  0.6 8.6 %copy-start = (bf16[1024,1024]{1,0:T(8,128)(2,1)S(1)}, bf16[1024,1024]{1,0:T(8,128)(2,1)}, u32[]{:S(2)}) copy-start(bf16[1024,1024]{1,0:T(8,128)(2,1)} %param.14) | copy-start | bytes 6291460
  0.6 8.6 %copy-start.2 = (bf16[8,16,1024]{2,1,0:T(8,128)(2,1)S(1)}, bf16[8,16,1024]{2,1,0:T(8,128)(2,1)}, u32[]{:S(2)}) copy-start(bf16[8,16,1024]{2,1,0:T(8,128)(2,1)} %param.11) | copy-start | bytes 786436
  2.6 20.0 %collective-permute-start = (bf16[96,1024]{1,0:T(8,128)(2,1)}, bf16[96,1024]{1,0:T(8,128)(2,1)S(1)}, u32[]{:S(2)}, u32[]{:S(2)}) collective-permute-start(bf16[96,1024]{1,0:T(8,128)(2,1)} %bitcast.1), channel_id=1, source_target_pairs={{8,16},{16,8},{9,17},{17,9},{10,18},{18,10},{11,19},{19,11},{12,20... | collective-permute-start | bytes 589832 | tf_op jit(solution)/shard_map/ppermute | solution.py:47
  9.3 9.7 %copy-start.4 = (bf16[128,1024]{1,0:T(8,128)(2,1)}, bf16[128,1024]{1,0:T(8,128)(2,1)S(1)}, u32[]{:S(2)}) copy-start(bf16[128,1024]{1,0:T(8,128)(2,1)S(1)} %convolution_convert_fusion.5.ko_ref) | copy-start | bytes 786436
  9.7 12.6 %copy-start.5 = (bf16[128,1024]{1,0:T(8,128)(2,1)}, bf16[128,1024]{1,0:T(8,128)(2,1)S(1)}, u32[]{:S(2)}) copy-start(bf16[128,1024]{1,0:T(8,128)(2,1)S(1)} %convolution_convert_fusion.4.vo_ref) | copy-start | bytes 786436
  10.5 11.9 %collective-permute-start.1 = (bf16[98,1024]{1,0:T(8,128)(2,1)}, bf16[98,1024]{1,0:T(8,128)(2,1)S(1)}, u32[]{:S(2)}, u32[]{:S(2)}) collective-permute-start(bf16[98,1024]{1,0:T(8,128)(2,1)} %pad_maximum_fusion.4), channel_id=1, source_target_pairs={{0,8},{8,0},{16,24},{24,16},{1,9},{9,1},{17,25},{25,17},{2,10},{10... | collective-permute-start | bytes 602120 | tf_op jit(solution)/shard_map/ppermute | solution.py:45
  16.2 6.2 %copy-start.11 = (s32[640]{0:T(1024)S(1)}, s32[640]{0:T(1024)}, u32[]{:S(2)}) copy-start(s32[640]{0:T(1024)} %constant.137.clone) | copy-start | bytes 7684
  16.2 6.2 %copy-start.12 = (s32[640]{0:T(1024)S(1)}, s32[640]{0:T(1024)}, u32[]{:S(2)}) copy-start(s32[640]{0:T(1024)} %constant.136.clone) | copy-start | bytes 7684
  22.6 1.4 %copy-start.13 = (pred[640]{0:T(1024)(128)(4,1)S(1)}, pred[640]{0:T(1024)(128)(4,1)}, u32[]{:S(2)}) copy-start(pred[640]{0:T(1024)(128)(4,1)} %constant.163) | copy-start | bytes 1924
  22.6 1.4 %copy-start.14 = (pred[640]{0:T(1024)(128)(4,1)S(1)}, pred[640]{0:T(1024)(128)(4,1)}, u32[]{:S(2)}) copy-start(pred[640]{0:T(1024)(128)(4,1)} %constant.162) | copy-start | bytes 1924
  22.7 1.0 copy-start.9
  23.6 2.1 %copy-start.15 = (s32[32]{0:T(128)S(1)}, s32[32]{0:T(128)}, u32[]{:S(2)}) copy-start(s32[32]{0:T(128)} %constant.165) | copy-start | bytes 388
  23.9 1.9 %collective-permute-start.3 = (bf16[124,1024]{1,0:T(8,128)(2,1)S(1)}, bf16[124,1024]{1,0:T(8,128)(2,1)S(1)}, u32[]{:S(2)}, u32[]{:S(2)}) collective-permute-start(bf16[124,1024]{1,0:T(8,128)(2,1)S(1)} %pad_maximum_fusion.2), channel_id=1, source_target_pairs={{0,1},{1,0},{2,3},{3,2},{4,5},{5,4},{6,7},{7,6},{8,9},{9,8},{10,11... | collective-permute-start | bytes 761864 | tf_op jit(solution)/shard_map/ppermute | solution.py:45
  25.1 4.3 %collective-permute-start.2 = (bf16[120,1024]{1,0:T(8,128)(2,1)S(1)}, bf16[120,1024]{1,0:T(8,128)(2,1)S(1)}, u32[]{:S(2)}, u32[]{:S(2)}) collective-permute-start(bf16[120,1024]{1,0:T(8,128)(2,1)S(1)} %select_n.321), channel_id=1, source_target_pairs={{1,2},{3,4},{5,6},{2,1},{4,3},{6,5},{9,10},{11,12},{13,14},{10,9},... | collective-permute-start | bytes 737288 | tf_op jit(solution)/shard_map/ppermute | solution.py:47
  25.9 7.7 %collective-permute-start.4 = (bf16[4,2048]{1,0:T(4,128)(2,1)S(1)}, bf16[4,2048]{1,0:T(4,128)(2,1)S(1)}, u32[]{:S(2)}, u32[]{:S(2)}) collective-permute-start(bf16[4,2048]{1,0:T(4,128)(2,1)S(1)} %maximum_select_fusion.3), channel_id=1, source_target_pairs={{0,2},{1,3},{2,0},{3,1},{4,6},{5,7},{6,4},{7,5},{8,10},{9,11},{10,... | collective-permute-start | bytes 49160 | tf_op jit(solution)/shard_map/ppermute | solution.py:35
  33.6 8.6 %copy-start.10 = (bf16[480,1024]{1,0:T(8,128)(2,1)S(1)}, bf16[480,1024]{1,0:T(8,128)(2,1)}, u32[]{:S(2)}) copy-start(bf16[480,1024]{1,0:T(8,128)(2,1)} %broadcast_dynamic-update-slice_fusion) | copy-start | bytes 2949124
  33.6 7.9 %collective-permute-start.5 = (bf16[8,2048]{1,0:T(8,128)(2,1)S(1)}, bf16[8,2048]{1,0:T(8,128)(2,1)S(1)}, u32[]{:S(2)}, u32[]{:S(2)}) collective-permute-start(bf16[8,2048]{1,0:T(8,128)(2,1)S(1)} %maximum_select_fusion.2), channel_id=1, source_target_pairs={{0,4},{1,5},{2,6},{3,7},{4,0},{5,1},{6,2},{7,3},{8,12},{9,13},{10,... | collective-permute-start | bytes 98312 | tf_op jit(solution)/shard_map/ppermute | solution.py:35
  41.5 4.4 %collective-permute-start.6 = (bf16[16,2048]{1,0:T(8,128)(2,1)S(1)}, bf16[16,2048]{1,0:T(8,128)(2,1)S(1)}, u32[]{:S(2)}, u32[]{:S(2)}) collective-permute-start(bf16[16,2048]{1,0:T(8,128)(2,1)S(1)} %maximum_select_fusion.1), channel_id=1, source_target_pairs={{0,16},{8,24},{16,0},{24,8},{1,17},{9,25},{17,1},{25,9},{2,18},{10... | collective-permute-start | bytes 196616 | tf_op jit(solution)/shard_map/ppermute | solution.py:35
  74.0 2.0 %collective-permute-start.7 = (bf16[184,1024]{1,0:T(8,128)(2,1)}, bf16[184,1024]{1,0:T(8,128)(2,1)}, u32[]{:S(2)}, u32[]{:S(2)}) collective-permute-start(bf16[184,1024]{1,0:T(8,128)(2,1)} %pad_maximum_fusion.1), channel_id=1, source_target_pairs={{0,1},{1,0},{2,3},{3,2},{4,5},{5,4},{6,7},{7,6},{8,9},{9,8},{10,11... | collective-permute-start | bytes 1130504 | tf_op jit(solution)/shard_map/ppermute | solution.py:45
  74.0 2.0 %collective-permute-start.8 = (bf16[120,1024]{1,0:T(8,128)(2,1)S(1)}, bf16[120,1024]{1,0:T(8,128)(2,1)S(1)}, u32[]{:S(2)}, u32[]{:S(2)}) collective-permute-start(bf16[120,1024]{1,0:T(8,128)(2,1)S(1)} %get-tuple-element.23), channel_id=1, source_target_pairs={{1,2},{3,4},{5,6},{2,1},{4,3},{6,5},{9,10},{11,12},{13,14},{10,9},... | collective-permute-start | bytes 737288 | tf_op jit(solution)/shard_map/ppermute | solution.py:47
  77.1 0.7 copy-start.3
  89.3 6.4 %collective-permute-start.9 = (bf16[128,1024]{1,0:T(8,128)(2,1)S(1)}, bf16[128,1024]{1,0:T(8,128)(2,1)S(1)}, u32[]{:S(2)}, u32[]{:S(2)}) collective-permute-start(bf16[128,1024]{1,0:T(8,128)(2,1)S(1)} %pad_maximum_fusion.3), channel_id=1, source_target_pairs={{0,8},{8,0},{16,24},{24,16},{1,9},{9,1},{17,25},{25,17},{2,10},{10... | collective-permute-start | bytes 786440 | tf_op jit(solution)/shard_map/ppermute | solution.py:45
  95.7 9.7 %copy-start.7 = (bf16[128,1024]{1,0:T(8,128)(2,1)}, bf16[128,1024]{1,0:T(8,128)(2,1)S(1)}, u32[]{:S(2)}) copy-start(bf16[128,1024]{1,0:T(8,128)(2,1)S(1)} %collective-permute-done.9) | copy-start | bytes 786436
  95.9 15.9 %collective-permute-start.10 = (f32[2,2,2,1024]{3,0,1,2:T(2,128)S(1)}, f32[2,2,2,1024]{3,0,1,2:T(2,128)}, u32[]{:S(2)}, u32[]{:S(2)}) collective-permute-start(f32[2,2,2,1024]{3,0,1,2:T(2,128)S(1)} %select_bitcast_fusion), channel_id=1, source_target_pairs={{0,2},{1,3},{2,0},{3,1},{4,6},{5,7},{6,4},{7,5},{8,10},{9,11},{10,... | collective-permute-start | bytes 98312 | tf_op jit(solution)/shard_map/ppermute | solution.py:35
  108.2 4.6 %copy-start.8 = (bf16[128,1024]{1,0:T(8,128)(2,1)S(1)}, bf16[128,1024]{1,0:T(8,128)(2,1)}, u32[]{:S(2)}) copy-start(bf16[128,1024]{1,0:T(8,128)(2,1)} %copy-done.7) | copy-start | bytes 786436
  110.3 2.5 %collective-permute-start.13 = (bf16[96,1024]{1,0:T(8,128)(2,1)}, bf16[96,1024]{1,0:T(8,128)(2,1)}, u32[]{:S(2)}, u32[]{:S(2)}) collective-permute-start(bf16[96,1024]{1,0:T(8,128)(2,1)} %bitcast.24), channel_id=1, source_target_pairs={{8,16},{16,8},{9,17},{17,9},{10,18},{18,10},{11,19},{19,11},{12,20... | collective-permute-start | bytes 589832 | tf_op jit(solution)/shard_map/ppermute | solution.py:47
  111.7 12.2 %copy-start.1 = (bf16[1024,1024]{1,0:T(8,128)(2,1)S(1)}, bf16[1024,1024]{1,0:T(8,128)(2,1)}, u32[]{:S(2)}) copy-start(bf16[1024,1024]{1,0:T(8,128)(2,1)} %param.13) | copy-start | bytes 6291460
  112.7 4.8 %collective-permute-start.11 = (f32[2,2,1024]{2,0,1:T(2,128)S(1)}, f32[2,2,1024]{2,0,1:T(2,128)S(1)}, u32[]{:S(2)}, u32[]{:S(2)}) collective-permute-start(f32[2,2,1024]{2,0,1:T(2,128)S(1)} %select_bitcast_fusion.1), channel_id=1, source_target_pairs={{0,4},{1,5},{2,6},{3,7},{4,0},{5,1},{6,2},{7,3},{8,12},{9,13},{10,... | collective-permute-start | bytes 49160 | tf_op jit(solution)/shard_map/ppermute | solution.py:35
  117.5 5.5 %collective-permute-start.12 = (f32[2,1024]{1,0:T(2,128)S(1)}, f32[2,1024]{1,0:T(2,128)S(1)}, u32[]{:S(2)}, u32[]{:S(2)}) collective-permute-start(f32[2,1024]{1,0:T(2,128)S(1)} %select_bitcast_fusion.2), channel_id=1, source_target_pairs={{0,16},{8,24},{16,0},{24,8},{1,17},{9,25},{17,1},{25,9},{2,18},{10... | collective-permute-start | bytes 24584 | tf_op jit(solution)/shard_map/ppermute | solution.py:35
  123.9 1.4 %copy-start.6 = (bf16[128,1024]{1,0:T(8,128)(2,1)S(1)}, bf16[128,1024]{1,0:T(8,128)(2,1)}, u32[]{:S(2)}) copy-start(bf16[128,1024]{1,0:T(8,128)(2,1)} %get-tuple-element.7) | copy-start | bytes 786436

commit v9 on v8

--- a/solution.py
+++ b/solution.py
@@ -342,6 +342,7 @@
 
     strips_from = tokens + 2 * band_keys
     keep_part, send_part = scatter_split(scatter, left, back_order[0])
+    strip_shape = (ext_rows, RAD, model_width)
     from_left, from_right, got = exchange(
         given(strips_from, strips_from + strip_keys).astype(jnp.bfloat16),
         given(strips_from + strip_keys, frame_keys).astype(jnp.bfloat16),
@@ -349,36 +350,25 @@
         split_wide(send_part.reshape(-1, model_width)),
     )
     scatter = keep_part + join_wide(got).reshape(keep_part.shape)
-    corner = RAD * RAD
-    lower_rows = (RAD + tile_rows) * RAD
-
-    def cols_placed(piece, height, at_right):
-        piece = piece.astype(jnp.float32).reshape(height, RAD, model_width)
-        pad = (tile_cols - RAD, 0) if at_right else (0, tile_cols - RAD)
-        return jnp.pad(piece, ((0, 0), pad, (0, 0)))
-
+    received = jnp.pad(
+        from_left.astype(jnp.float32).reshape(strip_shape), ((0, 0), (0, tile_cols - RAD), (0, 0))
+    ) + jnp.pad(
+        from_right.astype(jnp.float32).reshape(strip_shape), ((0, 0), (tile_cols - RAD, 0), (0, 0))
+    )
     band_shape = (RAD, tile_cols, model_width)
-    upper = (
-        given(tokens, tokens + band_keys).reshape(band_shape)
-        + cols_placed(from_left[:corner], RAD, False)
-        + cols_placed(from_right[:corner], RAD, True)
-    )
-    lower = (
-        given(tokens + band_keys, strips_from).reshape(band_shape)
-        + cols_placed(from_left[lower_rows:], RAD, False)
-        + cols_placed(from_right[lower_rows:], RAD, True)
-    )
     keep_part, send_part = scatter_split(scatter, left, back_order[1])
     from_above, from_below, got = exchange(
-        upper.reshape(-1, model_width).astype(jnp.bfloat16),
-        lower.reshape(-1, model_width).astype(jnp.bfloat16),
+        (given(tokens, tokens + band_keys).reshape(band_shape) + received[:RAD])
+        .reshape(-1, model_width)
+        .astype(jnp.bfloat16),
+        (given(tokens + band_keys, strips_from).reshape(band_shape) + received[RAD + tile_rows :])
+        .reshape(-1, model_width)
+        .astype(jnp.bfloat16),
         "rows",
         split_wide(send_part.reshape(-1, model_width)),
     )
     scatter = keep_part + join_wide(got).reshape(keep_part.shape)
-    received = cols_placed(from_left[corner:lower_rows], tile_rows, False) + cols_placed(
-        from_right[corner:lower_rows], tile_rows, True
-    )
+    received = received[RAD : RAD + tile_rows]
     received = received + jnp.pad(
         from_above.astype(jnp.float32).reshape(band_shape), ((0, tile_rows - RAD), (0, 0), (0, 0))
     )

time: 129 us -> 125 us (0.969)
  matrix products: 29.5 us -> 27.8 us
  local copies, waits for them, and re-layouts: 17.8 us -> 16.4 us
  waiting for transfers between devices: 14.6 us -> 13.2 us
    reshape x6 -> x2, local copies, waits for them, and re-layouts: 5.39 us -> 1.12 us  [the longest x1 1.03 us: shards(): from_left.astype(jnp.float32).reshape(strip_shape)]
    slice x4 -> x0, local copies, waits for them, and re-layouts: 2.28 us -> none  [the longest x1 0.93 us: shards(): from_right[corner:lower_rows]]
    select_n x4, local copies, waits for them, and re-layouts: 0.3 us -> 2.39 us  [scatter_split(): return (jnp.where(high, upper, lower), jnp.where(high, lower, upper))]
    dot_general x1, matrix products: 2.84 us -> 1.15 us  [shards(): jnp.dot(attended, w_out, preferred_element_type=jnp.float32)]
    unnamed x34 -> x48, local copies, waits for them, and re-layouts: 1.74 us -> 3.06 us
  transfers between devices with their start and end apart: 14 -> 14, of which waited for: 5 -> 6; matrix products, arithmetic and copies ran while one was open for 22% -> 21% of each run, Pallas kernels for 0% -> 0%
where the time goes in v9:
time: 125 us; the launch traced here: 124 us
  starting transfers between devices  30.6 us (24%)
  matrix products  27.8 us (22%)
  Pallas kernels  16.6 us (13%)
  local copies, waits for them, and re-layouts  16.4 us (13%)
  other arithmetic  15.2 us (12%)
  waiting for transfers between devices  13.2 us (11%)
  between operations  3.98 us (3%)
    ppermute x6, starting transfers between devices, partner(): return lax.ppermute(x, axis, [(i, i ^ 1 << bit) for i in range(size)])  21.2 us
    pallas_call x1, Pallas kernels, attention(): pl.pallas_call(functools.partial(attention_kernel, tokens, first, last),...  16.6 us
    ppermute x6, waiting for transfers between devices, partner(): return lax.ppermute(x, axis, [(i, i ^ 1 << bit) for i in range(size)])  8.68 us
    ppermute x4, starting transfers between devices, exchange(): got_first = lax.ppermute(first, axis, [(i, i ^ 1) for i in range(size)])  6.55 us
    ppermute x4, waiting for transfers between devices, exchange(): got_first = lax.ppermute(first, axis, [(i, i ^ 1) for i in range(size)])  4.55 us
    dot_general x1, matrix products, shards(): jnp.dot(rounded_grads[1, :frame_keys], w_value.T, preferred_element_type=...  4.11 us
    dot_general x1, matrix products, shards(): jnp.dot(halo_features, w_key, preferred_element_type=jnp.float32)  4.08 us
    select_n x4, other arithmetic, exchange(): first = jnp.where(even, to_higher, to_lower)  3.65 us
  transfers between devices with their start and end apart: 14, of which 6 were waited for; matrix products, arithmetic and copies ran while one was open for 21% of the time, Pallas kernels for 0%

profile of v9, /device:TPU:0, one launch (start us, length us, event | category | flops | bytes accessed | tf_op | source)
XLA Modules:
  0.0 123.9 jit_solution(16630667052527545252)
XLA Ops:
  0.7 1.9 %broadcast_select_fusion.8 = (bf16[6,16,1024]{2,1,0:T(8,128)(2,1)S(1)}, bf16[6,16,1024]{2,1,0:T(8,128)(2,1)}) fusion(pred[]{:T(512)S(6)} %eq.68, bf16[8,16,1024]{2,1,0:T(8,128)(2,1)} %param.11), kind=kLoop, calls=%fused_computation.38 | loop fusion | flops 196608 | bytes 786433 | tf_op jit(solution)/shard_map/jit(_where)/select_n | solution.py:41
  3.2 1.2 %dynamic_slice.13 = s32[1]{0:T(128)} dynamic-slice(s32[32]{0:T(128)} %param.16, s32[]{:T(128)S(6)} %select_n.311), dynamic_slice_sizes={1} | dynamic-slice | bytes 12 | tf_op jit(solution)/shard_map/jit(dynamic_index_in_dim)/dynamic_slice | solution.py:219
  7.1 2.1 %convolution_convert_fusion.5.ko_ref = bf16[128,1024]{1,0:T(8,128)(2,1)S(1)} fusion(bf16[128,1024]{1,0:T(8,128)(2,1)} %bitcast.77, bf16[1024,1024]{1,0:T(8,128)(2,1)} %param.13), kind=kOutput, calls=%fused_computation.10 | convolution fusion | flops 268566528 | bytes 2621440 | tf_op jit(solution)/shard_map/dot_general | solution.py:213
  9.8 0.7 pad_maximum_fusion.4
  10.5 5.7 %collective-permute-start.1 = (bf16[98,1024]{1,0:T(8,128)(2,1)}, bf16[98,1024]{1,0:T(8,128)(2,1)S(1)}, u32[]{:S(2)}, u32[]{:S(2)}) collective-permute-start(bf16[98,1024]{1,0:T(8,128)(2,1)} %pad_maximum_fusion.4), channel_id=1, source_target_pairs={{0,8},{8,0},{16,24},{24,16},{1,9},{9,1},{17,25},{25,17},{2,10},{10... | collective-permute-start | bytes 602120 | tf_op jit(solution)/shard_map/ppermute | solution.py:45
  16.2 2.8 %convolution_convert_fusion.6.q_ref = bf16[128,1024]{1,0:T(8,128)(2,1)} fusion(bf16[128,1024]{1,0:T(8,128)(2,1)S(1)} %bitcast.79, bf16[1024,1024]{1,0:T(8,128)(2,1)} %param.12), kind=kOutput, calls=%fused_computation.11 | convolution fusion | flops 268566528 | bytes 2621440 | tf_op jit(solution)/shard_map/dot_general | solution.py:253
  19.1 3.2 %convolution_convert_fusion.3.g_ref = bf16[128,1024]{1,0:T(8,128)(2,1)} fusion(bf16[128,1024]{1,0:T(8,128)(2,1)} %bitcast.90, bf16[1024,1024]{1,0:T(8,128)(2,1)} %param.15), kind=kOutput, calls=%fused_computation.8 | convolution fusion | flops 268566528 | bytes 2621440 | tf_op jit(solution)/shard_map/dot_general | solution.py:254
  22.7 1.0 copy-done.16
  24.1 0.9 or_convert_fusion.mask_ref
  25.9 3.4 %collective-permute-start.4 = (bf16[4,2048]{1,0:T(4,128)(2,1)S(1)}, bf16[4,2048]{1,0:T(4,128)(2,1)S(1)}, u32[]{:S(2)}, u32[]{:S(2)}) collective-permute-start(bf16[4,2048]{1,0:T(4,128)(2,1)S(1)} %maximum_select_fusion.3), channel_id=1, source_target_pairs={{0,2},{1,3},{2,0},{3,1},{4,6},{5,7},{6,4},{7,5},{8,10},{9,11},{10,... | collective-permute-start | bytes 49160 | tf_op jit(solution)/shard_map/ppermute | solution.py:35
  29.3 0.8 select_dynamic-update-slice_fusion.1
  30.1 0.8 select_dynamic-update-slice_fusion
  31.5 2.1 %collective-permute-done.4 = bf16[4,2048]{1,0:T(4,128)(2,1)S(1)} collective-permute-done((bf16[4,2048]{1,0:T(4,128)(2,1)S(1)}, bf16[4,2048]{1,0:T(4,128)(2,1)S(1)}, u32[]{:S(2)}, u32[]{:S(2)}) %collective-permute-start.4) | collective-permute-done | bytes 16416 | tf_op jit(solution)/shard_map/ppermute | solution.py:35
  33.7 3.8 %collective-permute-start.5 = (bf16[8,2048]{1,0:T(8,128)(2,1)S(1)}, bf16[8,2048]{1,0:T(8,128)(2,1)S(1)}, u32[]{:S(2)}, u32[]{:S(2)}) collective-permute-start(bf16[8,2048]{1,0:T(8,128)(2,1)S(1)} %maximum_select_fusion.2), channel_id=1, source_target_pairs={{0,4},{1,5},{2,6},{3,7},{4,0},{5,1},{6,2},{7,3},{8,12},{9,13},{10,... | collective-permute-start | bytes 98312 | tf_op jit(solution)/shard_map/ppermute | solution.py:35
  37.5 4.1 %convolution_convert_fusion.1.kh_ref = bf16[480,1024]{1,0:T(8,128)(2,1)} fusion(bf16[480,1024]{1,0:T(8,128)(2,1)} %broadcast_dynamic-update-slice_fusion, bf16[1024,1024]{1,0:T(8,128)(2,1)} %param.13), kind=kOutput, calls=%fused_computation.3 | convolution fusion | flops 1007124480 | bytes 4063232 | tf_op jit(solution)/shard_map/dot_general | solution.py:268
  41.6 0.7 collective-permute-start.6
  42.3 2.1 %convolution_convert_fusion.vh_ref = bf16[480,1024]{1,0:T(8,128)(2,1)} fusion(bf16[480,1024]{1,0:T(8,128)(2,1)S(1)} %copy-done.17, bf16[1024,1024]{1,0:T(8,128)(2,1)S(1)} %copy-done), kind=kOutput, calls=%fused_computation.2 | convolution fusion | flops 1007124480 | bytes 4063232 | tf_op jit(solution)/shard_map/dot_general | solution.py:271
  44.5 1.6 %collective-permute-done.6 = bf16[16,2048]{1,0:T(8,128)(2,1)S(1)} collective-permute-done((bf16[16,2048]{1,0:T(8,128)(2,1)S(1)}, bf16[16,2048]{1,0:T(8,128)(2,1)S(1)}, u32[]{:S(2)}, u32[]{:S(2)}) %collective-permute-start.6) | collective-permute-done | bytes 65568 | tf_op jit(solution)/shard_map/ppermute | solution.py:35
  47.4 16.6 %shard_map.122 = (bf16[128,1024]{1,0:T(8,128)(2,1)}, bf16[128,1024]{1,0:T(8,128)(2,1)}, bf16[2,640,1024]{2,1,0:T(8,128)(2,1)}, f32[2,160,1024]{2,1,0:T(8,128)}) custom-call(bf16[128,1024]{1,0:T(8,128)(2,1)} %convolution_convert_fusion.6.q_ref, bf16[128,1024]{1,0:T(8,128)(2,1)} %copy-done.11, bf16[480,1024]{1,0:T(8,128)(2,1)} %convolution_convert_fusion.1.kh_ref, ...), custom_call_target="tpu_custom_call" | custom-call | flops 2013265920 | bytes 8978432 | tf_op jit(solution)/shard_map/pallas_call | solution.py:153
  64.0 3.3 %fusion.3 = f32[560,1024]{1,0:T(8,128)S(1)} fusion(bf16[1024,1024]{1,0:T(8,128)(2,1)} %param.13, bf16[2,640,1024]{2,1,0:T(8,128)(2,1)} %get-tuple-element.8), kind=kOutput, calls=%fused_computation.13 | convolution fusion | flops 1174405120 | bytes 5537792 | tf_op jit(solution)/shard_map/dot_general | solution.py:330
  67.3 4.1 %fusion.16 = (bf16[560,1024]{1,0:T(8,128)(2,1)S(1)}, f32[560,1024]{1,0:T(8,128)}) fusion(f32[560,1024]{1,0:T(8,128)S(1)} %fusion.3, bf16[1024,1024]{1,0:T(8,128)(2,1)S(1)} %copy-done, bf16[2,640,1024]{2,1,0:T(8,128)(2,1)} %get-tuple-element.8), kind=kOutput, calls=%fused_computation.85 | convolution fusion | flops 1175552000 | bytes 8978432 | tf_op jit(solution)/shard_map/dot_general | solution.py:332
  71.5 0.7 broadcast_select_fusion.5
  72.2 1.0 slice.138
  74.8 0.9 collective-permute-start.8
  75.7 1.9 %slice.174 = f32[128,1024]{1,0:T(8,128)} slice(f32[560,1024]{1,0:T(8,128)} %get-tuple-element.38), slice={[0:128], [0:1024]} | slice | bytes 1048576 | tf_op jit(solution)/shard_map/slice | solution.py:335
  77.5 1.2 fusion.13
  78.7 1.7 %broadcast_select_fusion.3 = (bf16[120,1024]{1,0:T(8,128)(2,1)}, bf16[120,1024]{1,0:T(8,128)(2,1)S(1)}) fusion(bf16[120,1024]{1,0:T(8,128)(2,1)S(1)} %collective-permute-done.8, pred[]{:T(512)S(6)} %eq.69, bf16[184,1024]{1,0:T(8,128)(2,1)} %collective-permute-done.7), kind=kLoop, calls=%fused_computation.32 | loop fusion | flops 245760 | bytes 983041 | tf_op jit(solution)/shard_map/jit(_where)/select_n | solution.py:52
  80.5 1.0 reshape.191
  81.6 1.5 %convert_add_fusion.1 = f32[32,1024]{1,0:T(8,128)} fusion(bf16[184,1024]{1,0:T(8,128)(2,1)} %collective-permute-done.7), kind=kLoop, calls=%fused_computation.46 | loop fusion | flops 98304 | bytes 262144 | tf_op jit(solution)/shard_map/add | solution.py:188
  83.1 1.6 %reshape.189 = f32[2,2,2,2,2,1024]{5,4,3,2,1,0:T(2,128)} reshape(f32[32,1024]{1,0:T(8,128)} %convert_add_fusion.1) | data formatting | bytes 262144 | tf_op jit(solution)/shard_map/reshape | solution.py:352
  84.7 1.3 %bitcast_add_fusion = f32[2,2,2,2,2,1024]{5,0,1,3,4,2:T(2,128)S(1)} fusion(f32[2,2,2,2,2,1024]{5,4,3,2,1,0:T(2,128)} %reshape.189, pred[]{:T(512)S(6)} %eq.83, f32[2,2,2,2,2,1,1024]{6,5,4,3,2,1,0:T(1,128)} %copy-done.8, f32[2,2,2,2,2,1,1024]{6,5,4,3,2,1,0:T(1,128)} %copy-done.7), kind=kLoop, calls=%fused_computation.45 | loop fusion | flops 65536 | bytes 524289 | tf_op jit(solution)/shard_map/add | solution.py:352
  86.7 0.7 copy.19
  87.4 1.5 %select_n.363 = f32[16,1024]{1,0:T(8,128)} reshape(f32[2,2,1,2,2,1024]{5,4,3,1,0,2:T(2,128)} %copy.19) | data formatting | bytes 131072 | tf_op jit(solution)/shard_map/jit(_where)/select_n | solution.py:75
  88.9 1.0 subtract_convert_fusion.1
  89.9 0.9 broadcast_select_fusion.7
  90.9 0.7 collective-permute-start.9
  91.6 1.2 convolution_convert_fusion.2
  92.8 4.5 %collective-permute-done.9 = bf16[128,1024]{1,0:T(8,128)(2,1)S(1)} collective-permute-done((bf16[128,1024]{1,0:T(8,128)(2,1)S(1)}, bf16[128,1024]{1,0:T(8,128)(2,1)S(1)}, u32[]{:S(2)}, u32[]{:S(2)}) %collective-permute-start.9) | collective-permute-done | bytes 262176 | tf_op jit(solution)/shard_map/ppermute | solution.py:45
  97.3 0.7 copy-done.15
  98.2 7.8 %collective-permute-start.10 = (f32[2,2,2,1024]{3,0,1,2:T(2,128)S(1)}, f32[2,2,2,1024]{3,0,1,2:T(2,128)S(1)}, u32[]{:S(2)}, u32[]{:S(2)}) collective-permute-start(f32[2,2,2,1024]{3,0,1,2:T(2,128)S(1)} %select_bitcast_fusion), channel_id=1, source_target_pairs={{0,2},{1,3},{2,0},{3,1},{4,6},{5,7},{6,4},{7,5},{8,10},{9,11},{10,... | collective-permute-start | bytes 98312 | tf_op jit(solution)/shard_map/ppermute | solution.py:35
  106.7 1.2 collective-permute-done.10
  107.9 1.4 %collective-permute-start.11 = (f32[2,2,1024]{2,0,1:T(2,128)S(1)}, f32[2,2,1024]{2,0,1:T(2,128)S(1)}, u32[]{:S(2)}, u32[]{:S(2)}) collective-permute-start(f32[2,2,1024]{2,0,1:T(2,128)S(1)} %select_bitcast_fusion.1), channel_id=1, source_target_pairs={{0,4},{1,5},{2,6},{3,7},{4,0},{5,1},{6,2},{7,3},{8,12},{9,13},{10,... | collective-permute-start | bytes 49160 | tf_op jit(solution)/shard_map/ppermute | solution.py:35
  109.4 1.0 broadcast_select_fusion.11
  110.3 2.3 %collective-permute-done.11 = f32[2,2,1024]{2,0,1:T(2,128)S(1)} collective-permute-done((f32[2,2,1024]{2,0,1:T(2,128)S(1)}, f32[2,2,1024]{2,0,1:T(2,128)S(1)}, u32[]{:S(2)}, u32[]{:S(2)}) %collective-permute-start.11) | collective-permute-done | bytes 16416 | tf_op jit(solution)/shard_map/ppermute | solution.py:35
  112.7 4.1 %collective-permute-start.12 = (f32[2,1024]{1,0:T(2,128)S(1)}, f32[2,1024]{1,0:T(2,128)S(1)}, u32[]{:S(2)}, u32[]{:S(2)}) collective-permute-start(f32[2,1024]{1,0:T(2,128)S(1)} %select_bitcast_fusion.2), channel_id=1, source_target_pairs={{0,16},{8,24},{16,0},{24,8},{1,17},{9,25},{17,1},{25,9},{2,18},{10... | collective-permute-start | bytes 24584 | tf_op jit(solution)/shard_map/ppermute | solution.py:35
  116.9 1.5 %collective-permute-done.12 = f32[2,1024]{1,0:T(2,128)S(1)} collective-permute-done((f32[2,1024]{1,0:T(2,128)S(1)}, f32[2,1024]{1,0:T(2,128)S(1)}, u32[]{:S(2)}, u32[]{:S(2)}) %collective-permute-start.12) | collective-permute-done | bytes 8224 | tf_op jit(solution)/shard_map/ppermute | solution.py:35
  118.4 0.9 add_convert_fusion
  120.7 3.1 %fusion.1 = bf16[128,1024]{1,0:T(8,128)(2,1)} fusion(f32[128,1024]{1,0:T(8,128)S(1)} %bitcast.80, f32[128,1024]{1,0:T(8,128)S(1)} %dynamic_update_slice.3, bf16[128,1024]{1,0:T(8,128)(2,1)S(1)} %copy-done.13, bf16[1024,1024]{1,0:T(8,128)(2,1)} %param.12), kind=kOutput, calls=%fused_computation.6 | convolution fusion | flops 268828672 | bytes 3670016 | tf_op jit(solution)/shard_map/dot_general | solution.py:393
  (113 shorter events, 9.6 us)
Async XLA Ops:
  0.6 8.6 %copy-start = (bf16[1024,1024]{1,0:T(8,128)(2,1)S(1)}, bf16[1024,1024]{1,0:T(8,128)(2,1)}, u32[]{:S(2)}) copy-start(bf16[1024,1024]{1,0:T(8,128)(2,1)} %param.14) | copy-start | bytes 6291460
  0.6 8.6 %copy-start.3 = (bf16[8,16,1024]{2,1,0:T(8,128)(2,1)S(1)}, bf16[8,16,1024]{2,1,0:T(8,128)(2,1)}, u32[]{:S(2)}) copy-start(bf16[8,16,1024]{2,1,0:T(8,128)(2,1)} %param.11) | copy-start | bytes 786436
  2.6 20.0 %collective-permute-start = (bf16[96,1024]{1,0:T(8,128)(2,1)}, bf16[96,1024]{1,0:T(8,128)(2,1)S(1)}, u32[]{:S(2)}, u32[]{:S(2)}) collective-permute-start(bf16[96,1024]{1,0:T(8,128)(2,1)} %bitcast.1), channel_id=1, source_target_pairs={{8,16},{16,8},{9,17},{17,9},{10,18},{18,10},{11,19},{19,11},{12,20... | collective-permute-start | bytes 589832 | tf_op jit(solution)/shard_map/ppermute | solution.py:47
  9.3 9.7 %copy-start.11 = (bf16[128,1024]{1,0:T(8,128)(2,1)}, bf16[128,1024]{1,0:T(8,128)(2,1)S(1)}, u32[]{:S(2)}) copy-start(bf16[128,1024]{1,0:T(8,128)(2,1)S(1)} %convolution_convert_fusion.5.ko_ref) | copy-start | bytes 786436
  9.7 12.6 %copy-start.12 = (bf16[128,1024]{1,0:T(8,128)(2,1)}, bf16[128,1024]{1,0:T(8,128)(2,1)S(1)}, u32[]{:S(2)}) copy-start(bf16[128,1024]{1,0:T(8,128)(2,1)S(1)} %convolution_convert_fusion.4.vo_ref) | copy-start | bytes 786436
  10.5 11.9 %collective-permute-start.1 = (bf16[98,1024]{1,0:T(8,128)(2,1)}, bf16[98,1024]{1,0:T(8,128)(2,1)S(1)}, u32[]{:S(2)}, u32[]{:S(2)}) collective-permute-start(bf16[98,1024]{1,0:T(8,128)(2,1)} %pad_maximum_fusion.4), channel_id=1, source_target_pairs={{0,8},{8,0},{16,24},{24,16},{1,9},{9,1},{17,25},{25,17},{2,10},{10... | collective-permute-start | bytes 602120 | tf_op jit(solution)/shard_map/ppermute | solution.py:45
  16.2 6.2 %copy-start.18 = (s32[640]{0:T(1024)S(1)}, s32[640]{0:T(1024)}, u32[]{:S(2)}) copy-start(s32[640]{0:T(1024)} %constant.137.clone) | copy-start | bytes 7684
  16.2 6.2 %copy-start.19 = (s32[640]{0:T(1024)S(1)}, s32[640]{0:T(1024)}, u32[]{:S(2)}) copy-start(s32[640]{0:T(1024)} %constant.136.clone) | copy-start | bytes 7684
  22.6 1.5 %copy-start.20 = (pred[640]{0:T(1024)(128)(4,1)S(1)}, pred[640]{0:T(1024)(128)(4,1)}, u32[]{:S(2)}) copy-start(pred[640]{0:T(1024)(128)(4,1)} %constant.155) | copy-start | bytes 1924
  22.6 1.5 %copy-start.21 = (pred[640]{0:T(1024)(128)(4,1)S(1)}, pred[640]{0:T(1024)(128)(4,1)}, u32[]{:S(2)}) copy-start(pred[640]{0:T(1024)(128)(4,1)} %constant.154) | copy-start | bytes 1924
  22.7 1.0 copy-start.16
  23.7 2.1 %copy-start.22 = (s32[32]{0:T(128)S(1)}, s32[32]{0:T(128)}, u32[]{:S(2)}) copy-start(s32[32]{0:T(128)} %constant.157) | copy-start | bytes 388
  24.0 1.9 %collective-permute-start.3 = (bf16[124,1024]{1,0:T(8,128)(2,1)S(1)}, bf16[124,1024]{1,0:T(8,128)(2,1)S(1)}, u32[]{:S(2)}, u32[]{:S(2)}) collective-permute-start(bf16[124,1024]{1,0:T(8,128)(2,1)S(1)} %pad_maximum_fusion.2), channel_id=1, source_target_pairs={{0,1},{1,0},{2,3},{3,2},{4,5},{5,4},{6,7},{7,6},{8,9},{9,8},{10,11... | collective-permute-start | bytes 761864 | tf_op jit(solution)/shard_map/ppermute | solution.py:45
  25.1 4.3 %collective-permute-start.2 = (bf16[120,1024]{1,0:T(8,128)(2,1)S(1)}, bf16[120,1024]{1,0:T(8,128)(2,1)S(1)}, u32[]{:S(2)}, u32[]{:S(2)}) collective-permute-start(bf16[120,1024]{1,0:T(8,128)(2,1)S(1)} %select_n.321), channel_id=1, source_target_pairs={{1,2},{3,4},{5,6},{2,1},{4,3},{6,5},{9,10},{11,12},{13,14},{10,9},... | collective-permute-start | bytes 737288 | tf_op jit(solution)/shard_map/ppermute | solution.py:47
  25.9 7.7 %collective-permute-start.4 = (bf16[4,2048]{1,0:T(4,128)(2,1)S(1)}, bf16[4,2048]{1,0:T(4,128)(2,1)S(1)}, u32[]{:S(2)}, u32[]{:S(2)}) collective-permute-start(bf16[4,2048]{1,0:T(4,128)(2,1)S(1)} %maximum_select_fusion.3), channel_id=1, source_target_pairs={{0,2},{1,3},{2,0},{3,1},{4,6},{5,7},{6,4},{7,5},{8,10},{9,11},{10,... | collective-permute-start | bytes 49160 | tf_op jit(solution)/shard_map/ppermute | solution.py:35
  33.6 8.7 %copy-start.17 = (bf16[480,1024]{1,0:T(8,128)(2,1)S(1)}, bf16[480,1024]{1,0:T(8,128)(2,1)}, u32[]{:S(2)}) copy-start(bf16[480,1024]{1,0:T(8,128)(2,1)} %broadcast_dynamic-update-slice_fusion) | copy-start | bytes 2949124
  33.7 7.9 %collective-permute-start.5 = (bf16[8,2048]{1,0:T(8,128)(2,1)S(1)}, bf16[8,2048]{1,0:T(8,128)(2,1)S(1)}, u32[]{:S(2)}, u32[]{:S(2)}) collective-permute-start(bf16[8,2048]{1,0:T(8,128)(2,1)S(1)} %maximum_select_fusion.2), channel_id=1, source_target_pairs={{0,4},{1,5},{2,6},{3,7},{4,0},{5,1},{6,2},{7,3},{8,12},{9,13},{10,... | collective-permute-start | bytes 98312 | tf_op jit(solution)/shard_map/ppermute | solution.py:35
  41.6 4.4 %collective-permute-start.6 = (bf16[16,2048]{1,0:T(8,128)(2,1)S(1)}, bf16[16,2048]{1,0:T(8,128)(2,1)S(1)}, u32[]{:S(2)}, u32[]{:S(2)}) collective-permute-start(bf16[16,2048]{1,0:T(8,128)(2,1)S(1)} %maximum_select_fusion.1), channel_id=1, source_target_pairs={{0,16},{8,24},{16,0},{24,8},{1,17},{9,25},{17,1},{25,9},{2,18},{10... | collective-permute-start | bytes 196616 | tf_op jit(solution)/shard_map/ppermute | solution.py:35
  73.6 0.7 copy-start.7
  73.6 0.8 copy-start.8
  74.7 4.0 %collective-permute-start.7 = (bf16[184,1024]{1,0:T(8,128)(2,1)S(1)}, bf16[184,1024]{1,0:T(8,128)(2,1)}, u32[]{:S(2)}, u32[]{:S(2)}) collective-permute-start(bf16[184,1024]{1,0:T(8,128)(2,1)S(1)} %pad_maximum_fusion.1), channel_id=1, source_target_pairs={{0,1},{1,0},{2,3},{3,2},{4,5},{5,4},{6,7},{7,6},{8,9},{9,8},{10,11... | collective-permute-start | bytes 1130504 | tf_op jit(solution)/shard_map/ppermute | solution.py:45
  74.8 3.9 %collective-permute-start.8 = (bf16[120,1024]{1,0:T(8,128)(2,1)}, bf16[120,1024]{1,0:T(8,128)(2,1)S(1)}, u32[]{:S(2)}, u32[]{:S(2)}) collective-permute-start(bf16[120,1024]{1,0:T(8,128)(2,1)} %get-tuple-element.24), channel_id=1, source_target_pairs={{1,2},{3,4},{5,6},{2,1},{4,3},{6,5},{9,10},{11,12},{13,14},{10,9},... | collective-permute-start | bytes 737288 | tf_op jit(solution)/shard_map/ppermute | solution.py:47
  86.0 0.6 copy-start.5
  88.9 2.7 %copy-start.1 = (bf16[1024,1024]{1,0:T(8,128)(2,1)S(1)}, bf16[1024,1024]{1,0:T(8,128)(2,1)}, u32[]{:S(2)}) copy-start(bf16[1024,1024]{1,0:T(8,128)(2,1)} %param.15) | copy-start | bytes 6291460
  88.9 2.7 %copy-start.14 = (bf16[128,1024]{1,0:T(8,128)(2,1)S(1)}, bf16[128,1024]{1,0:T(8,128)(2,1)}, u32[]{:S(2)}) copy-start(bf16[128,1024]{1,0:T(8,128)(2,1)} %get-tuple-element.6) | copy-start | bytes 786436
  90.9 7.2 %copy-start.6 = (f32[2,2,2,2,2,1024]{5,0,1,3,4,2:T(2,128)S(1)}, f32[2,2,2,2,2,1024]{5,0,1,3,4,2:T(2,128)}, u32[]{:S(2)}) copy-start(f32[2,2,2,2,2,1024]{5,0,1,3,4,2:T(2,128)} %copy-done.5) | copy-start | bytes 393220
  90.9 15.2 %copy-start.9 = (bf16[6,16,1024]{2,1,0:T(8,128)(2,1)S(1)}, bf16[6,16,1024]{2,1,0:T(8,128)(2,1)}, u32[]{:S(2)}) copy-start(bf16[6,16,1024]{2,1,0:T(8,128)(2,1)} %get-tuple-element.11) | copy-start | bytes 589828
  90.9 15.2 %copy-start.10 = (bf16[6,16,1024]{2,1,0:T(8,128)(2,1)S(1)}, bf16[6,16,1024]{2,1,0:T(8,128)(2,1)}, u32[]{:S(2)}) copy-start(bf16[6,16,1024]{2,1,0:T(8,128)(2,1)} %get-tuple-element.12) | copy-start | bytes 589828
  90.9 6.4 %collective-permute-start.9 = (bf16[128,1024]{1,0:T(8,128)(2,1)S(1)}, bf16[128,1024]{1,0:T(8,128)(2,1)S(1)}, u32[]{:S(2)}, u32[]{:S(2)}) collective-permute-start(bf16[128,1024]{1,0:T(8,128)(2,1)S(1)} %pad_maximum_fusion.3), channel_id=1, source_target_pairs={{0,8},{8,0},{16,24},{24,16},{1,9},{9,1},{17,25},{25,17},{2,10},{10... | collective-permute-start | bytes 786440 | tf_op jit(solution)/shard_map/ppermute | solution.py:45
  97.3 0.7 copy-start.15
  98.1 21.2 %copy-start.2 = (bf16[1024,1024]{1,0:T(8,128)(2,1)S(1)}, bf16[1024,1024]{1,0:T(8,128)(2,1)}, u32[]{:S(2)}) copy-start(bf16[1024,1024]{1,0:T(8,128)(2,1)} %param.13) | copy-start | bytes 6291460
  98.2 9.7 %collective-permute-start.10 = (f32[2,2,2,1024]{3,0,1,2:T(2,128)S(1)}, f32[2,2,2,1024]{3,0,1,2:T(2,128)S(1)}, u32[]{:S(2)}, u32[]{:S(2)}) collective-permute-start(f32[2,2,2,1024]{3,0,1,2:T(2,128)S(1)} %select_bitcast_fusion), channel_id=1, source_target_pairs={{0,2},{1,3},{2,0},{3,1},{4,6},{5,7},{6,4},{7,5},{8,10},{9,11},{10,... | collective-permute-start | bytes 98312 | tf_op jit(solution)/shard_map/ppermute | solution.py:35
  106.0 3.3 %collective-permute-start.13 = (bf16[96,1024]{1,0:T(8,128)(2,1)S(1)}, bf16[96,1024]{1,0:T(8,128)(2,1)S(1)}, u32[]{:S(2)}, u32[]{:S(2)}) collective-permute-start(bf16[96,1024]{1,0:T(8,128)(2,1)S(1)} %bitcast.92), channel_id=1, source_target_pairs={{8,16},{16,8},{9,17},{17,9},{10,18},{18,10},{11,19},{19,11},{12,20... | collective-permute-start | bytes 589832 | tf_op jit(solution)/shard_map/ppermute | solution.py:47
  107.9 4.7 %collective-permute-start.11 = (f32[2,2,1024]{2,0,1:T(2,128)S(1)}, f32[2,2,1024]{2,0,1:T(2,128)S(1)}, u32[]{:S(2)}, u32[]{:S(2)}) collective-permute-start(f32[2,2,1024]{2,0,1:T(2,128)S(1)} %select_bitcast_fusion.1), channel_id=1, source_target_pairs={{0,4},{1,5},{2,6},{3,7},{4,0},{5,1},{6,2},{7,3},{8,12},{9,13},{10,... | collective-permute-start | bytes 49160 | tf_op jit(solution)/shard_map/ppermute | solution.py:35
  112.7 5.7 %collective-permute-start.12 = (f32[2,1024]{1,0:T(2,128)S(1)}, f32[2,1024]{1,0:T(2,128)S(1)}, u32[]{:S(2)}, u32[]{:S(2)}) collective-permute-start(f32[2,1024]{1,0:T(2,128)S(1)} %select_bitcast_fusion.2), channel_id=1, source_target_pairs={{0,16},{8,24},{16,0},{24,8},{1,17},{9,25},{17,1},{25,9},{2,18},{10... | collective-permute-start | bytes 24584 | tf_op jit(solution)/shard_map/ppermute | solution.py:35
  119.3 1.3 %copy-start.4 = (f32[128,1024]{1,0:T(8,128)S(1)}, f32[128,1024]{1,0:T(8,128)}, u32[]{:S(2)}) copy-start(f32[128,1024]{1,0:T(8,128)} %slice.174) | copy-start | bytes 1572868
  119.3 1.4 %copy-start.13 = (bf16[128,1024]{1,0:T(8,128)(2,1)S(1)}, bf16[128,1024]{1,0:T(8,128)(2,1)}, u32[]{:S(2)}) copy-start(bf16[128,1024]{1,0:T(8,128)(2,1)} %get-tuple-element.7) | copy-start | bytes 786436

commit v10 on v9

--- a/solution.py
+++ b/solution.py
@@ -81,25 +81,23 @@
 ):
     head_size = q_ref.shape[1] // 2
     score_scale = 1.0 / math.sqrt(head_size)
-    q = q_ref[...]
+    q = (q_ref[...] * score_scale).astype(q_ref.dtype)
     k = jnp.concatenate([ko_ref[...], kh_ref[...], kg_ref[...]], axis=0)
     v = jnp.concatenate([vo_ref[...], vh_ref[...], vg_ref[...]], axis=0)
     g = g_ref[...]
     keep = mask_ref[...] > 0
     lane_head = lax.broadcasted_iota(jnp.int32, q.shape, 1) // head_size
-    lane_head_keys = lax.broadcasted_iota(jnp.int32, k.shape, 1) // head_size
     rows = (((1,), (1,)), ((), ()))
     cols = (((0,), (0,)), ((), ()))
     out = jnp.zeros(q.shape, jnp.float32)
     dq = jnp.zeros(q.shape, jnp.float32)
-    dk = jnp.zeros(k.shape, jnp.float32)
-    dv = jnp.zeros(k.shape, jnp.float32)
+    dk = None
+    dv = None
     for head in range(2):
         mine = lane_head == head
-        mine_keys = lane_head_keys == head
         q_head = jnp.where(mine, q, jnp.zeros_like(q))
         g_head = jnp.where(mine, g, jnp.zeros_like(g))
-        scores = lax.dot_general(q_head, k, rows, preferred_element_type=jnp.float32) * score_scale
+        scores = lax.dot_general(q_head, k, rows, preferred_element_type=jnp.float32)
         scores = jnp.where(keep, scores, -1e30)
         row_max = jnp.max(scores, axis=1, keepdims=True)
         exps = jnp.exp(scores - row_max)
@@ -112,14 +110,14 @@
             jnp.where(mine, g.astype(jnp.float32) * attended, 0.0), axis=1, keepdims=True
         )
         dots = lax.dot_general(g_head, v, rows, preferred_element_type=jnp.float32)
-        slopes = (probs * (dots - delta) * score_scale).astype(jnp.bfloat16)
-        dq = jnp.where(mine, jnp.dot(slopes, k, preferred_element_type=jnp.float32), dq)
-        dk = jnp.where(
-            mine_keys, lax.dot_general(slopes, q, cols, preferred_element_type=jnp.float32), dk
+        slopes = (probs * (dots - delta)).astype(jnp.bfloat16)
+        dq = jnp.where(
+            mine, jnp.dot(slopes, k, preferred_element_type=jnp.float32) * score_scale, dq
         )
-        dv = jnp.where(
-            mine_keys, lax.dot_general(rounded, g, cols, preferred_element_type=jnp.float32), dv
-        )
+        dk_head = lax.dot_general(slopes, q_head, cols, preferred_element_type=jnp.float32)
+        dv_head = lax.dot_general(rounded, g_head, cols, preferred_element_type=jnp.float32)
+        dk = dk_head if dk is None else dk + dk_head
+        dv = dv_head if dv is None else dv + dv_head
     o_ref[...] = out.astype(o_ref.dtype)
     dq_ref[...] = dq.astype(dq_ref.dtype)
     dkv_ref[0] = dk.astype(dkv_ref.dtype)

time: 125 us -> 124 us (level)
  no operation moved by 1% of the time
where the time goes in v10:
time: 124 us; the launch traced here: 123 us
  starting transfers between devices  30.6 us (25%)
  matrix products  27.8 us (22%)
  local copies, waits for them, and re-layouts  16.4 us (13%)
  Pallas kernels  15.9 us (13%)
  other arithmetic  15.2 us (12%)
  waiting for transfers between devices  13.3 us (11%)
  between operations  3.98 us (3%)
    ppermute x6, starting transfers between devices, partner(): return lax.ppermute(x, axis, [(i, i ^ 1 << bit) for i in range(size)])  21.2 us
    pallas_call x1, Pallas kernels, attention(): pl.pallas_call(functools.partial(attention_kernel, tokens, first, last),...  15.9 us
    ppermute x6, waiting for transfers between devices, partner(): return lax.ppermute(x, axis, [(i, i ^ 1 << bit) for i in range(size)])  8.68 us
    ppermute x4, starting transfers between devices, exchange(): got_first = lax.ppermute(first, axis, [(i, i ^ 1) for i in range(size)])  6.53 us
    ppermute x4, waiting for transfers between devices, exchange(): got_first = lax.ppermute(first, axis, [(i, i ^ 1) for i in range(size)])  4.57 us
    dot_general x1, matrix products, shards(): jnp.dot(rounded_grads[1, :frame_keys], w_value.T, preferred_element_type=...  4.11 us
    dot_general x1, matrix products, shards(): jnp.dot(halo_features, w_key, preferred_element_type=jnp.float32)  4.08 us
    select_n x4, other arithmetic, exchange(): first = jnp.where(even, to_higher, to_lower)  3.65 us
  transfers between devices with their start and end apart: 14, of which 6 were waited for; matrix products, arithmetic and copies ran while one was open for 21% of the time, Pallas kernels for 0%

profile of v10, /device:TPU:0, one launch (start us, length us, event | category | flops | bytes accessed | tf_op | source)
XLA Modules:
  0.0 123.1 jit_solution(7656175293706333684)
XLA Ops:
  0.7 1.9 %broadcast_select_fusion.8 = (bf16[6,16,1024]{2,1,0:T(8,128)(2,1)S(1)}, bf16[6,16,1024]{2,1,0:T(8,128)(2,1)}) fusion(pred[]{:T(512)S(6)} %eq.68, bf16[8,16,1024]{2,1,0:T(8,128)(2,1)} %param.11), kind=kLoop, calls=%fused_computation.38 | loop fusion | flops 196608 | bytes 786433 | tf_op jit(solution)/shard_map/jit(_where)/select_n | solution.py:41
  3.2 1.2 %dynamic_slice.13 = s32[1]{0:T(128)} dynamic-slice(s32[32]{0:T(128)} %param.16, s32[]{:T(128)S(6)} %select_n.311), dynamic_slice_sizes={1} | dynamic-slice | bytes 12 | tf_op jit(solution)/shard_map/jit(dynamic_index_in_dim)/dynamic_slice | solution.py:217
  7.1 2.1 %convolution_convert_fusion.5.ko_ref = bf16[128,1024]{1,0:T(8,128)(2,1)S(1)} fusion(bf16[128,1024]{1,0:T(8,128)(2,1)} %bitcast.77, bf16[1024,1024]{1,0:T(8,128)(2,1)} %param.13), kind=kOutput, calls=%fused_computation.10 | convolution fusion | flops 268566528 | bytes 2621440 | tf_op jit(solution)/shard_map/dot_general | solution.py:211
  9.8 0.7 pad_maximum_fusion.4
  10.5 5.7 %collective-permute-start.1 = (bf16[98,1024]{1,0:T(8,128)(2,1)}, bf16[98,1024]{1,0:T(8,128)(2,1)S(1)}, u32[]{:S(2)}, u32[]{:S(2)}) collective-permute-start(bf16[98,1024]{1,0:T(8,128)(2,1)} %pad_maximum_fusion.4), channel_id=1, source_target_pairs={{0,8},{8,0},{16,24},{24,16},{1,9},{9,1},{17,25},{25,17},{2,10},{10... | collective-permute-start | bytes 602120 | tf_op jit(solution)/shard_map/ppermute | solution.py:45
  16.2 2.8 %convolution_convert_fusion.6.q_ref = bf16[128,1024]{1,0:T(8,128)(2,1)} fusion(bf16[128,1024]{1,0:T(8,128)(2,1)S(1)} %bitcast.79, bf16[1024,1024]{1,0:T(8,128)(2,1)} %param.12), kind=kOutput, calls=%fused_computation.11 | convolution fusion | flops 268566528 | bytes 2621440 | tf_op jit(solution)/shard_map/dot_general | solution.py:251
  19.1 3.2 %convolution_convert_fusion.3.g_ref = bf16[128,1024]{1,0:T(8,128)(2,1)} fusion(bf16[128,1024]{1,0:T(8,128)(2,1)} %bitcast.90, bf16[1024,1024]{1,0:T(8,128)(2,1)} %param.15), kind=kOutput, calls=%fused_computation.8 | convolution fusion | flops 268566528 | bytes 2621440 | tf_op jit(solution)/shard_map/dot_general | solution.py:252
  22.7 1.0 copy-done.16
  24.1 0.9 or_convert_fusion.mask_ref
  25.9 3.4 %collective-permute-start.4 = (bf16[4,2048]{1,0:T(4,128)(2,1)S(1)}, bf16[4,2048]{1,0:T(4,128)(2,1)S(1)}, u32[]{:S(2)}, u32[]{:S(2)}) collective-permute-start(bf16[4,2048]{1,0:T(4,128)(2,1)S(1)} %maximum_select_fusion.3), channel_id=1, source_target_pairs={{0,2},{1,3},{2,0},{3,1},{4,6},{5,7},{6,4},{7,5},{8,10},{9,11},{10,... | collective-permute-start | bytes 49160 | tf_op jit(solution)/shard_map/ppermute | solution.py:35
  29.3 0.8 select_dynamic-update-slice_fusion.1
  30.1 0.8 select_dynamic-update-slice_fusion
  31.5 2.1 %collective-permute-done.4 = bf16[4,2048]{1,0:T(4,128)(2,1)S(1)} collective-permute-done((bf16[4,2048]{1,0:T(4,128)(2,1)S(1)}, bf16[4,2048]{1,0:T(4,128)(2,1)S(1)}, u32[]{:S(2)}, u32[]{:S(2)}) %collective-permute-start.4) | collective-permute-done | bytes 16416 | tf_op jit(solution)/shard_map/ppermute | solution.py:35
  33.7 3.8 %collective-permute-start.5 = (bf16[8,2048]{1,0:T(8,128)(2,1)S(1)}, bf16[8,2048]{1,0:T(8,128)(2,1)S(1)}, u32[]{:S(2)}, u32[]{:S(2)}) collective-permute-start(bf16[8,2048]{1,0:T(8,128)(2,1)S(1)} %maximum_select_fusion.2), channel_id=1, source_target_pairs={{0,4},{1,5},{2,6},{3,7},{4,0},{5,1},{6,2},{7,3},{8,12},{9,13},{10,... | collective-permute-start | bytes 98312 | tf_op jit(solution)/shard_map/ppermute | solution.py:35
  37.5 4.1 %convolution_convert_fusion.1.kh_ref = bf16[480,1024]{1,0:T(8,128)(2,1)} fusion(bf16[480,1024]{1,0:T(8,128)(2,1)} %broadcast_dynamic-update-slice_fusion, bf16[1024,1024]{1,0:T(8,128)(2,1)} %param.13), kind=kOutput, calls=%fused_computation.3 | convolution fusion | flops 1007124480 | bytes 4063232 | tf_op jit(solution)/shard_map/dot_general | solution.py:266
  41.6 0.7 collective-permute-start.6
  42.3 2.1 %convolution_convert_fusion.vh_ref = bf16[480,1024]{1,0:T(8,128)(2,1)} fusion(bf16[480,1024]{1,0:T(8,128)(2,1)S(1)} %copy-done.17, bf16[1024,1024]{1,0:T(8,128)(2,1)S(1)} %copy-done), kind=kOutput, calls=%fused_computation.2 | convolution fusion | flops 1007124480 | bytes 4063232 | tf_op jit(solution)/shard_map/dot_general | solution.py:269
  44.5 1.6 %collective-permute-done.6 = bf16[16,2048]{1,0:T(8,128)(2,1)S(1)} collective-permute-done((bf16[16,2048]{1,0:T(8,128)(2,1)S(1)}, bf16[16,2048]{1,0:T(8,128)(2,1)S(1)}, u32[]{:S(2)}, u32[]{:S(2)}) %collective-permute-start.6) | collective-permute-done | bytes 65568 | tf_op jit(solution)/shard_map/ppermute | solution.py:35
  47.4 15.9 %shard_map.122 = (bf16[128,1024]{1,0:T(8,128)(2,1)}, bf16[128,1024]{1,0:T(8,128)(2,1)}, bf16[2,640,1024]{2,1,0:T(8,128)(2,1)}, f32[2,160,1024]{2,1,0:T(8,128)}) custom-call(bf16[128,1024]{1,0:T(8,128)(2,1)} %convolution_convert_fusion.6.q_ref, bf16[128,1024]{1,0:T(8,128)(2,1)} %copy-done.11, bf16[480,1024]{1,0:T(8,128)(2,1)} %convolution_convert_fusion.1.kh_ref, ...), custom_call_target="tpu_custom_call" | custom-call | flops 2013265920 | bytes 8978432 | tf_op jit(solution)/shard_map/pallas_call | solution.py:151
  63.3 3.3 %fusion.3 = f32[560,1024]{1,0:T(8,128)S(1)} fusion(bf16[1024,1024]{1,0:T(8,128)(2,1)} %param.13, bf16[2,640,1024]{2,1,0:T(8,128)(2,1)} %get-tuple-element.8), kind=kOutput, calls=%fused_computation.13 | convolution fusion | flops 1174405120 | bytes 5537792 | tf_op jit(solution)/shard_map/dot_general | solution.py:328
  66.6 4.1 %fusion.16 = (bf16[560,1024]{1,0:T(8,128)(2,1)S(1)}, f32[560,1024]{1,0:T(8,128)}) fusion(f32[560,1024]{1,0:T(8,128)S(1)} %fusion.3, bf16[1024,1024]{1,0:T(8,128)(2,1)S(1)} %copy-done, bf16[2,640,1024]{2,1,0:T(8,128)(2,1)} %get-tuple-element.8), kind=kOutput, calls=%fused_computation.85 | convolution fusion | flops 1175552000 | bytes 8978432 | tf_op jit(solution)/shard_map/dot_general | solution.py:330
  70.7 0.7 broadcast_select_fusion.5
  71.5 1.0 slice.138
  74.1 0.9 collective-permute-start.8
  74.9 1.9 %slice.174 = f32[128,1024]{1,0:T(8,128)} slice(f32[560,1024]{1,0:T(8,128)} %get-tuple-element.38), slice={[0:128], [0:1024]} | slice | bytes 1048576 | tf_op jit(solution)/shard_map/slice | solution.py:333
  76.8 1.2 fusion.13
  78.0 1.7 %broadcast_select_fusion.3 = (bf16[120,1024]{1,0:T(8,128)(2,1)}, bf16[120,1024]{1,0:T(8,128)(2,1)S(1)}) fusion(bf16[120,1024]{1,0:T(8,128)(2,1)S(1)} %collective-permute-done.8, pred[]{:T(512)S(6)} %eq.69, bf16[184,1024]{1,0:T(8,128)(2,1)} %collective-permute-done.7), kind=kLoop, calls=%fused_computation.32 | loop fusion | flops 245760 | bytes 983041 | tf_op jit(solution)/shard_map/jit(_where)/select_n | solution.py:52
  79.8 1.0 reshape.191
  80.8 1.5 %convert_add_fusion.1 = f32[32,1024]{1,0:T(8,128)} fusion(bf16[184,1024]{1,0:T(8,128)(2,1)} %collective-permute-done.7), kind=kLoop, calls=%fused_computation.46 | loop fusion | flops 98304 | bytes 262144 | tf_op jit(solution)/shard_map/add | solution.py:186
  82.4 1.6 %reshape.189 = f32[2,2,2,2,2,1024]{5,4,3,2,1,0:T(2,128)} reshape(f32[32,1024]{1,0:T(8,128)} %convert_add_fusion.1) | data formatting | bytes 262144 | tf_op jit(solution)/shard_map/reshape | solution.py:350
  84.0 1.3 %bitcast_add_fusion = f32[2,2,2,2,2,1024]{5,0,1,3,4,2:T(2,128)S(1)} fusion(f32[2,2,2,2,2,1024]{5,4,3,2,1,0:T(2,128)} %reshape.189, pred[]{:T(512)S(6)} %eq.83, f32[2,2,2,2,2,1,1024]{6,5,4,3,2,1,0:T(1,128)} %copy-done.8, f32[2,2,2,2,2,1,1024]{6,5,4,3,2,1,0:T(1,128)} %copy-done.7), kind=kLoop, calls=%fused_computation.45 | loop fusion | flops 65536 | bytes 524289 | tf_op jit(solution)/shard_map/add | solution.py:350
  86.0 0.7 copy.19
  86.6 1.5 %select_n.363 = f32[16,1024]{1,0:T(8,128)} reshape(f32[2,2,1,2,2,1024]{5,4,3,1,0,2:T(2,128)} %copy.19) | data formatting | bytes 131072 | tf_op jit(solution)/shard_map/jit(_where)/select_n | solution.py:75
  88.2 1.0 subtract_convert_fusion.1
  89.2 0.9 broadcast_select_fusion.7
  90.2 0.7 collective-permute-start.9
  90.9 1.2 convolution_convert_fusion.2
  92.0 4.6 %collective-permute-done.9 = bf16[128,1024]{1,0:T(8,128)(2,1)S(1)} collective-permute-done((bf16[128,1024]{1,0:T(8,128)(2,1)S(1)}, bf16[128,1024]{1,0:T(8,128)(2,1)S(1)}, u32[]{:S(2)}, u32[]{:S(2)}) %collective-permute-start.9) | collective-permute-done | bytes 262176 | tf_op jit(solution)/shard_map/ppermute | solution.py:45
  96.6 0.7 copy-done.15
  97.5 7.8 %collective-permute-start.10 = (f32[2,2,2,1024]{3,0,1,2:T(2,128)S(1)}, f32[2,2,2,1024]{3,0,1,2:T(2,128)S(1)}, u32[]{:S(2)}, u32[]{:S(2)}) collective-permute-start(f32[2,2,2,1024]{3,0,1,2:T(2,128)S(1)} %select_bitcast_fusion), channel_id=1, source_target_pairs={{0,2},{1,3},{2,0},{3,1},{4,6},{5,7},{6,4},{7,5},{8,10},{9,11},{10,... | collective-permute-start | bytes 98312 | tf_op jit(solution)/shard_map/ppermute | solution.py:35
  106.0 1.2 collective-permute-done.10
  107.2 1.4 %collective-permute-start.11 = (f32[2,2,1024]{2,0,1:T(2,128)S(1)}, f32[2,2,1024]{2,0,1:T(2,128)S(1)}, u32[]{:S(2)}, u32[]{:S(2)}) collective-permute-start(f32[2,2,1024]{2,0,1:T(2,128)S(1)} %select_bitcast_fusion.1), channel_id=1, source_target_pairs={{0,4},{1,5},{2,6},{3,7},{4,0},{5,1},{6,2},{7,3},{8,12},{9,13},{10,... | collective-permute-start | bytes 49160 | tf_op jit(solution)/shard_map/ppermute | solution.py:35
  108.6 1.0 broadcast_select_fusion.11
  109.6 2.3 %collective-permute-done.11 = f32[2,2,1024]{2,0,1:T(2,128)S(1)} collective-permute-done((f32[2,2,1024]{2,0,1:T(2,128)S(1)}, f32[2,2,1024]{2,0,1:T(2,128)S(1)}, u32[]{:S(2)}, u32[]{:S(2)}) %collective-permute-start.11) | collective-permute-done | bytes 16416 | tf_op jit(solution)/shard_map/ppermute | solution.py:35
  112.0 4.1 %collective-permute-start.12 = (f32[2,1024]{1,0:T(2,128)S(1)}, f32[2,1024]{1,0:T(2,128)S(1)}, u32[]{:S(2)}, u32[]{:S(2)}) collective-permute-start(f32[2,1024]{1,0:T(2,128)S(1)} %select_bitcast_fusion.2), channel_id=1, source_target_pairs={{0,16},{8,24},{16,0},{24,8},{1,17},{9,25},{17,1},{25,9},{2,18},{10... | collective-permute-start | bytes 24584 | tf_op jit(solution)/shard_map/ppermute | solution.py:35
  116.1 1.5 %collective-permute-done.12 = f32[2,1024]{1,0:T(2,128)S(1)} collective-permute-done((f32[2,1024]{1,0:T(2,128)S(1)}, f32[2,1024]{1,0:T(2,128)S(1)}, u32[]{:S(2)}, u32[]{:S(2)}) %collective-permute-start.12) | collective-permute-done | bytes 8224 | tf_op jit(solution)/shard_map/ppermute | solution.py:35
  117.7 0.9 add_convert_fusion
  120.0 3.1 %fusion.1 = bf16[128,1024]{1,0:T(8,128)(2,1)} fusion(f32[128,1024]{1,0:T(8,128)S(1)} %bitcast.80, f32[128,1024]{1,0:T(8,128)S(1)} %dynamic_update_slice.3, bf16[128,1024]{1,0:T(8,128)(2,1)S(1)} %copy-done.13, bf16[1024,1024]{1,0:T(8,128)(2,1)} %param.12), kind=kOutput, calls=%fused_computation.6 | convolution fusion | flops 268828672 | bytes 3670016 | tf_op jit(solution)/shard_map/dot_general | solution.py:391
  (113 shorter events, 9.6 us)
Async XLA Ops:
  0.6 8.6 %copy-start = (bf16[1024,1024]{1,0:T(8,128)(2,1)S(1)}, bf16[1024,1024]{1,0:T(8,128)(2,1)}, u32[]{:S(2)}) copy-start(bf16[1024,1024]{1,0:T(8,128)(2,1)} %param.14) | copy-start | bytes 6291460
  0.6 8.6 %copy-start.3 = (bf16[8,16,1024]{2,1,0:T(8,128)(2,1)S(1)}, bf16[8,16,1024]{2,1,0:T(8,128)(2,1)}, u32[]{:S(2)}) copy-start(bf16[8,16,1024]{2,1,0:T(8,128)(2,1)} %param.11) | copy-start | bytes 786436
  2.6 20.0 %collective-permute-start = (bf16[96,1024]{1,0:T(8,128)(2,1)}, bf16[96,1024]{1,0:T(8,128)(2,1)S(1)}, u32[]{:S(2)}, u32[]{:S(2)}) collective-permute-start(bf16[96,1024]{1,0:T(8,128)(2,1)} %bitcast.1), channel_id=1, source_target_pairs={{8,16},{16,8},{9,17},{17,9},{10,18},{18,10},{11,19},{19,11},{12,20... | collective-permute-start | bytes 589832 | tf_op jit(solution)/shard_map/ppermute | solution.py:47
  9.3 9.7 %copy-start.11 = (bf16[128,1024]{1,0:T(8,128)(2,1)}, bf16[128,1024]{1,0:T(8,128)(2,1)S(1)}, u32[]{:S(2)}) copy-start(bf16[128,1024]{1,0:T(8,128)(2,1)S(1)} %convolution_convert_fusion.5.ko_ref) | copy-start | bytes 786436
  9.7 12.6 %copy-start.12 = (bf16[128,1024]{1,0:T(8,128)(2,1)}, bf16[128,1024]{1,0:T(8,128)(2,1)S(1)}, u32[]{:S(2)}) copy-start(bf16[128,1024]{1,0:T(8,128)(2,1)S(1)} %convolution_convert_fusion.4.vo_ref) | copy-start | bytes 786436
  10.5 11.9 %collective-permute-start.1 = (bf16[98,1024]{1,0:T(8,128)(2,1)}, bf16[98,1024]{1,0:T(8,128)(2,1)S(1)}, u32[]{:S(2)}, u32[]{:S(2)}) collective-permute-start(bf16[98,1024]{1,0:T(8,128)(2,1)} %pad_maximum_fusion.4), channel_id=1, source_target_pairs={{0,8},{8,0},{16,24},{24,16},{1,9},{9,1},{17,25},{25,17},{2,10},{10... | collective-permute-start | bytes 602120 | tf_op jit(solution)/shard_map/ppermute | solution.py:45
  16.2 6.2 %copy-start.18 = (s32[640]{0:T(1024)S(1)}, s32[640]{0:T(1024)}, u32[]{:S(2)}) copy-start(s32[640]{0:T(1024)} %constant.137.clone) | copy-start | bytes 7684
  16.2 6.2 %copy-start.19 = (s32[640]{0:T(1024)S(1)}, s32[640]{0:T(1024)}, u32[]{:S(2)}) copy-start(s32[640]{0:T(1024)} %constant.136.clone) | copy-start | bytes 7684
  22.6 1.5 %copy-start.20 = (pred[640]{0:T(1024)(128)(4,1)S(1)}, pred[640]{0:T(1024)(128)(4,1)}, u32[]{:S(2)}) copy-start(pred[640]{0:T(1024)(128)(4,1)} %constant.155) | copy-start | bytes 1924
  22.6 1.5 %copy-start.21 = (pred[640]{0:T(1024)(128)(4,1)S(1)}, pred[640]{0:T(1024)(128)(4,1)}, u32[]{:S(2)}) copy-start(pred[640]{0:T(1024)(128)(4,1)} %constant.154) | copy-start | bytes 1924
  22.7 1.0 copy-start.16
  23.7 2.1 %copy-start.22 = (s32[32]{0:T(128)S(1)}, s32[32]{0:T(128)}, u32[]{:S(2)}) copy-start(s32[32]{0:T(128)} %constant.157) | copy-start | bytes 388
  24.0 1.9 %collective-permute-start.3 = (bf16[124,1024]{1,0:T(8,128)(2,1)S(1)}, bf16[124,1024]{1,0:T(8,128)(2,1)S(1)}, u32[]{:S(2)}, u32[]{:S(2)}) collective-permute-start(bf16[124,1024]{1,0:T(8,128)(2,1)S(1)} %pad_maximum_fusion.2), channel_id=1, source_target_pairs={{0,1},{1,0},{2,3},{3,2},{4,5},{5,4},{6,7},{7,6},{8,9},{9,8},{10,11... | collective-permute-start | bytes 761864 | tf_op jit(solution)/shard_map/ppermute | solution.py:45
  25.1 4.3 %collective-permute-start.2 = (bf16[120,1024]{1,0:T(8,128)(2,1)S(1)}, bf16[120,1024]{1,0:T(8,128)(2,1)S(1)}, u32[]{:S(2)}, u32[]{:S(2)}) collective-permute-start(bf16[120,1024]{1,0:T(8,128)(2,1)S(1)} %select_n.321), channel_id=1, source_target_pairs={{1,2},{3,4},{5,6},{2,1},{4,3},{6,5},{9,10},{11,12},{13,14},{10,9},... | collective-permute-start | bytes 737288 | tf_op jit(solution)/shard_map/ppermute | solution.py:47
  25.9 7.7 %collective-permute-start.4 = (bf16[4,2048]{1,0:T(4,128)(2,1)S(1)}, bf16[4,2048]{1,0:T(4,128)(2,1)S(1)}, u32[]{:S(2)}, u32[]{:S(2)}) collective-permute-start(bf16[4,2048]{1,0:T(4,128)(2,1)S(1)} %maximum_select_fusion.3), channel_id=1, source_target_pairs={{0,2},{1,3},{2,0},{3,1},{4,6},{5,7},{6,4},{7,5},{8,10},{9,11},{10,... | collective-permute-start | bytes 49160 | tf_op jit(solution)/shard_map/ppermute | solution.py:35
  33.6 8.7 %copy-start.17 = (bf16[480,1024]{1,0:T(8,128)(2,1)S(1)}, bf16[480,1024]{1,0:T(8,128)(2,1)}, u32[]{:S(2)}) copy-start(bf16[480,1024]{1,0:T(8,128)(2,1)} %broadcast_dynamic-update-slice_fusion) | copy-start | bytes 2949124
  33.7 7.9 %collective-permute-start.5 = (bf16[8,2048]{1,0:T(8,128)(2,1)S(1)}, bf16[8,2048]{1,0:T(8,128)(2,1)S(1)}, u32[]{:S(2)}, u32[]{:S(2)}) collective-permute-start(bf16[8,2048]{1,0:T(8,128)(2,1)S(1)} %maximum_select_fusion.2), channel_id=1, source_target_pairs={{0,4},{1,5},{2,6},{3,7},{4,0},{5,1},{6,2},{7,3},{8,12},{9,13},{10,... | collective-permute-start | bytes 98312 | tf_op jit(solution)/shard_map/ppermute | solution.py:35
  41.6 4.4 %collective-permute-start.6 = (bf16[16,2048]{1,0:T(8,128)(2,1)S(1)}, bf16[16,2048]{1,0:T(8,128)(2,1)S(1)}, u32[]{:S(2)}, u32[]{:S(2)}) collective-permute-start(bf16[16,2048]{1,0:T(8,128)(2,1)S(1)} %maximum_select_fusion.1), channel_id=1, source_target_pairs={{0,16},{8,24},{16,0},{24,8},{1,17},{9,25},{17,1},{25,9},{2,18},{10... | collective-permute-start | bytes 196616 | tf_op jit(solution)/shard_map/ppermute | solution.py:35
  72.8 0.7 copy-start.7
  72.9 0.8 copy-start.8
  74.0 4.0 %collective-permute-start.7 = (bf16[184,1024]{1,0:T(8,128)(2,1)S(1)}, bf16[184,1024]{1,0:T(8,128)(2,1)}, u32[]{:S(2)}, u32[]{:S(2)}) collective-permute-start(bf16[184,1024]{1,0:T(8,128)(2,1)S(1)} %pad_maximum_fusion.1), channel_id=1, source_target_pairs={{0,1},{1,0},{2,3},{3,2},{4,5},{5,4},{6,7},{7,6},{8,9},{9,8},{10,11... | collective-permute-start | bytes 1130504 | tf_op jit(solution)/shard_map/ppermute | solution.py:45
  74.1 3.9 %collective-permute-start.8 = (bf16[120,1024]{1,0:T(8,128)(2,1)}, bf16[120,1024]{1,0:T(8,128)(2,1)S(1)}, u32[]{:S(2)}, u32[]{:S(2)}) collective-permute-start(bf16[120,1024]{1,0:T(8,128)(2,1)} %get-tuple-element.24), channel_id=1, source_target_pairs={{1,2},{3,4},{5,6},{2,1},{4,3},{6,5},{9,10},{11,12},{13,14},{10,9},... | collective-permute-start | bytes 737288 | tf_op jit(solution)/shard_map/ppermute | solution.py:47
  85.3 0.6 copy-start.5
  88.2 2.7 %copy-start.1 = (bf16[1024,1024]{1,0:T(8,128)(2,1)S(1)}, bf16[1024,1024]{1,0:T(8,128)(2,1)}, u32[]{:S(2)}) copy-start(bf16[1024,1024]{1,0:T(8,128)(2,1)} %param.15) | copy-start | bytes 6291460
  88.2 2.7 %copy-start.14 = (bf16[128,1024]{1,0:T(8,128)(2,1)S(1)}, bf16[128,1024]{1,0:T(8,128)(2,1)}, u32[]{:S(2)}) copy-start(bf16[128,1024]{1,0:T(8,128)(2,1)} %get-tuple-element.6) | copy-start | bytes 786436
  90.1 7.2 %copy-start.6 = (f32[2,2,2,2,2,1024]{5,0,1,3,4,2:T(2,128)S(1)}, f32[2,2,2,2,2,1024]{5,0,1,3,4,2:T(2,128)}, u32[]{:S(2)}) copy-start(f32[2,2,2,2,2,1024]{5,0,1,3,4,2:T(2,128)} %copy-done.5) | copy-start | bytes 393220
  90.1 15.1 %copy-start.9 = (bf16[6,16,1024]{2,1,0:T(8,128)(2,1)S(1)}, bf16[6,16,1024]{2,1,0:T(8,128)(2,1)}, u32[]{:S(2)}) copy-start(bf16[6,16,1024]{2,1,0:T(8,128)(2,1)} %get-tuple-element.11) | copy-start | bytes 589828
  90.1 15.1 %copy-start.10 = (bf16[6,16,1024]{2,1,0:T(8,128)(2,1)S(1)}, bf16[6,16,1024]{2,1,0:T(8,128)(2,1)}, u32[]{:S(2)}) copy-start(bf16[6,16,1024]{2,1,0:T(8,128)(2,1)} %get-tuple-element.12) | copy-start | bytes 589828
  90.2 6.4 %collective-permute-start.9 = (bf16[128,1024]{1,0:T(8,128)(2,1)S(1)}, bf16[128,1024]{1,0:T(8,128)(2,1)S(1)}, u32[]{:S(2)}, u32[]{:S(2)}) collective-permute-start(bf16[128,1024]{1,0:T(8,128)(2,1)S(1)} %pad_maximum_fusion.3), channel_id=1, source_target_pairs={{0,8},{8,0},{16,24},{24,16},{1,9},{9,1},{17,25},{25,17},{2,10},{10... | collective-permute-start | bytes 786440 | tf_op jit(solution)/shard_map/ppermute | solution.py:45
  96.6 0.7 copy-start.15
  97.4 21.2 %copy-start.2 = (bf16[1024,1024]{1,0:T(8,128)(2,1)S(1)}, bf16[1024,1024]{1,0:T(8,128)(2,1)}, u32[]{:S(2)}) copy-start(bf16[1024,1024]{1,0:T(8,128)(2,1)} %param.13) | copy-start | bytes 6291460
  97.5 9.7 %collective-permute-start.10 = (f32[2,2,2,1024]{3,0,1,2:T(2,128)S(1)}, f32[2,2,2,1024]{3,0,1,2:T(2,128)S(1)}, u32[]{:S(2)}, u32[]{:S(2)}) collective-permute-start(f32[2,2,2,1024]{3,0,1,2:T(2,128)S(1)} %select_bitcast_fusion), channel_id=1, source_target_pairs={{0,2},{1,3},{2,0},{3,1},{4,6},{5,7},{6,4},{7,5},{8,10},{9,11},{10,... | collective-permute-start | bytes 98312 | tf_op jit(solution)/shard_map/ppermute | solution.py:35
  105.3 3.3 %collective-permute-start.13 = (bf16[96,1024]{1,0:T(8,128)(2,1)S(1)}, bf16[96,1024]{1,0:T(8,128)(2,1)S(1)}, u32[]{:S(2)}, u32[]{:S(2)}) collective-permute-start(bf16[96,1024]{1,0:T(8,128)(2,1)S(1)} %bitcast.92), channel_id=1, source_target_pairs={{8,16},{16,8},{9,17},{17,9},{10,18},{18,10},{11,19},{19,11},{12,20... | collective-permute-start | bytes 589832 | tf_op jit(solution)/shard_map/ppermute | solution.py:47
  107.2 4.7 %collective-permute-start.11 = (f32[2,2,1024]{2,0,1:T(2,128)S(1)}, f32[2,2,1024]{2,0,1:T(2,128)S(1)}, u32[]{:S(2)}, u32[]{:S(2)}) collective-permute-start(f32[2,2,1024]{2,0,1:T(2,128)S(1)} %select_bitcast_fusion.1), channel_id=1, source_target_pairs={{0,4},{1,5},{2,6},{3,7},{4,0},{5,1},{6,2},{7,3},{8,12},{9,13},{10,... | collective-permute-start | bytes 49160 | tf_op jit(solution)/shard_map/ppermute | solution.py:35
  112.0 5.7 %collective-permute-start.12 = (f32[2,1024]{1,0:T(2,128)S(1)}, f32[2,1024]{1,0:T(2,128)S(1)}, u32[]{:S(2)}, u32[]{:S(2)}) collective-permute-start(f32[2,1024]{1,0:T(2,128)S(1)} %select_bitcast_fusion.2), channel_id=1, source_target_pairs={{0,16},{8,24},{16,0},{24,8},{1,17},{9,25},{17,1},{25,9},{2,18},{10... | collective-permute-start | bytes 24584 | tf_op jit(solution)/shard_map/ppermute | solution.py:35
  118.5 1.3 %copy-start.4 = (f32[128,1024]{1,0:T(8,128)S(1)}, f32[128,1024]{1,0:T(8,128)}, u32[]{:S(2)}) copy-start(f32[128,1024]{1,0:T(8,128)} %slice.174) | copy-start | bytes 1572868
  118.5 1.4 %copy-start.13 = (bf16[128,1024]{1,0:T(8,128)(2,1)S(1)}, bf16[128,1024]{1,0:T(8,128)(2,1)}, u32[]{:S(2)}) copy-start(bf16[128,1024]{1,0:T(8,128)(2,1)} %get-tuple-element.7) | copy-start | bytes 786436

commit v11 on v10

--- a/solution.py
+++ b/solution.py
@@ -38,19 +38,21 @@
 def exchange(to_lower, to_higher, axis, rider=None, rider_dim=0):
     size = lax.axis_size(axis)
     even = lax.axis_index(axis) % 2 == 0
-    first = jnp.where(even, to_higher, to_lower)
-    length = first.shape[rider_dim]
+    length = to_higher.shape[rider_dim]
     if rider is not None:
-        first = jnp.concatenate([first, rider], axis=rider_dim)
-    got_first = lax.ppermute(first, axis, [(i, i ^ 1) for i in range(size)])
-    links = [(i, i + 1) for i in range(1, size - 1, 2)] + [(i, i - 1) for i in range(2, size, 2)]
-    got_second = lax.ppermute(jnp.where(even, to_lower, to_higher), axis, links)
+        to_higher = jnp.concatenate([to_higher, rider], axis=rider_dim)
+        to_lower = jnp.concatenate([to_lower, rider], axis=rider_dim)
+    from_lower = lax.ppermute(to_higher, axis, [(i, i + 1) for i in range(size - 1)])
+    from_higher = lax.ppermute(to_lower, axis, [(i + 1, i) for i in range(size - 1)])
     rider_got = None
     if rider is not None:
-        rider_got = lax.slice_in_dim(got_first, length, None, axis=rider_dim)
-        got_first = lax.slice_in_dim(got_first, 0, length, axis=rider_dim)
-    from_lower = jnp.where(even, got_second, got_first)
-    from_higher = jnp.where(even, got_first, got_second)
+        rider_got = jnp.where(
+            even,
+            lax.slice_in_dim(from_higher, length, None, axis=rider_dim),
+            lax.slice_in_dim(from_lower, length, None, axis=rider_dim),
+        )
+        from_lower = lax.slice_in_dim(from_lower, 0, length, axis=rider_dim)
+        from_higher = lax.slice_in_dim(from_higher, 0, length, axis=rider_dim)
     return from_lower, from_higher, rider_got
 
 

time: 124 us -> 141 us (1.14)
  waiting for transfers between devices: 13.3 us -> 24.6 us
  local copies, waits for them, and re-layouts: 16.4 us -> 23.2 us
  other arithmetic: 15.2 us -> 11.5 us
  starting transfers between devices: 30.6 us -> 33.7 us
    ppermute x8, waiting for transfers between devices: 4.58 us -> 16.9 us  [the longest x4 14.2 us: exchange(): lax.ppermute(to_lower, axis, [(i + 1, i) for i in range(size - 1)])]
    ppermute x8, starting transfers between devices: 9.4 us -> 17.2 us  [the longest x4 11.8 us: exchange(): lax.ppermute(to_higher, axis, [(i, i + 1) for i in range(size - 1)])]
    slice x1 -> x8, local copies, waits for them, and re-layouts: 0.01 us -> 5.85 us  [the longest x3 3.55 us: exchange(): from_higher = lax.slice_in_dim(from_higher, 0, length, axis=rider_dim)]
    ppermute x6, starting transfers between devices: 21.2 us -> 16.5 us  [partner(): return lax.ppermute(x, axis, [(i, i ^ 1 << bit) for i in range(size)])]
    select_n x7 -> x3, other arithmetic: 6.35 us -> 1.84 us  [exchange(): jnp.where(even, lax.slice_in_dim(from_higher, length, None, axis=rider_di...]
    dot_general x1, matrix products: 4.08 us -> 2.14 us  [shards(): jnp.dot(halo_features, w_key, preferred_element_type=jnp.float32)]
    dot_general x1, matrix products: 2.13 us -> 0.45 us  [shards(): jnp.dot(flat_tokens, w_key, preferred_element_type=jnp.float32)]
    concatenate x4, other arithmetic: 0.77 us -> 2.42 us  [the longest x2 1.66 us: exchange(): to_higher = jnp.concatenate([to_higher, rider], axis=rider_dim)]
  transfers between devices with their start and end apart: 14 -> 14, of which waited for: 6 -> 8; matrix products, arithmetic and copies ran while one was open for 21% -> 16% of each run, Pallas kernels for 0% -> 0%
where the time goes in v11:
time: 141 us; the launch traced here: 140 us
  starting transfers between devices  33.7 us (24%)
  matrix products  27.3 us (19%)
  waiting for transfers between devices  24.6 us (17%)
  local copies, waits for them, and re-layouts  23.2 us (16%)
  Pallas kernels  15.9 us (11%)
  other arithmetic  11.5 us (8%)
  between operations  4.06 us (3%)
    ppermute x6, starting transfers between devices, partner(): return lax.ppermute(x, axis, [(i, i ^ 1 << bit) for i in range(size)])  16.5 us
    pallas_call x1, Pallas kernels, attention(): pl.pallas_call(functools.partial(attention_kernel, tokens, first, last),...  15.9 us
    ppermute x4, waiting for transfers between devices, exchange(): lax.ppermute(to_lower, axis, [(i + 1, i) for i in range(size - 1)])  14.2 us
    ppermute x4, starting transfers between devices, exchange(): lax.ppermute(to_higher, axis, [(i, i + 1) for i in range(size - 1)])  11.8 us
    ppermute x6, waiting for transfers between devices, partner(): return lax.ppermute(x, axis, [(i, i ^ 1 << bit) for i in range(size)])  7.68 us
    ppermute x4, starting transfers between devices, exchange(): lax.ppermute(to_lower, axis, [(i + 1, i) for i in range(size - 1)])  5.34 us
    dot_general x1, matrix products, shards(): jnp.dot(rounded_grads[1, :frame_keys], w_value.T, preferred_element_type=...  4.1 us
    unnamed x47, local copies, waits for them, and re-layouts  3.79 us
  transfers between devices with their start and end apart: 14, of which 8 were waited for; matrix products, arithmetic and copies ran while one was open for 16% of the time, Pallas kernels for 0%

profile of v11, /device:TPU:0, one launch (start us, length us, event | category | flops | bytes accessed | tf_op | source)
XLA Modules:
  0.0 140.3 jit_solution(6801036157078776194)
XLA Ops:
  0.7 1.4 dynamic_slice.13
  4.7 1.2 fusion.16
  5.9 1.4 convolution_convert_fusion.4.vo_ref
  8.6 4.8 %collective-permute-start = (bf16[98,1024]{1,0:T(8,128)(2,1)}, bf16[98,1024]{1,0:T(8,128)(2,1)S(1)}, u32[]{:S(2)}, u32[]{:S(2)}) collective-permute-start(bf16[98,1024]{1,0:T(8,128)(2,1)} %get-tuple-element.39), channel_id=1, source_target_pairs={{0,8},{8,16},{16,24},{1,9},{9,17},{17,25},{2,10},{10,18},{18,26},{... | collective-permute-start | bytes 602120 | tf_op jit(solution)/shard_map/ppermute | solution.py:45
  13.5 1.3 collective-permute-start.1
  15.0 2.9 %convolution_convert_fusion.6.q_ref = bf16[128,1024]{1,0:T(8,128)(2,1)} fusion(bf16[128,1024]{1,0:T(8,128)(2,1)S(1)} %bitcast.79, bf16[1024,1024]{1,0:T(8,128)(2,1)} %param.12), kind=kOutput, calls=%fused_computation.11 | convolution fusion | flops 268566528 | bytes 2621440 | tf_op jit(solution)/shard_map/dot_general | solution.py:253
  17.9 2.5 %convolution_convert_fusion.3.g_ref = bf16[128,1024]{1,0:T(8,128)(2,1)} fusion(bf16[128,1024]{1,0:T(8,128)(2,1)} %bitcast.92, bf16[1024,1024]{1,0:T(8,128)(2,1)S(1)} %copy-done.1), kind=kOutput, calls=%fused_computation.8 | convolution fusion | flops 268566528 | bytes 2621440 | tf_op jit(solution)/shard_map/dot_general | solution.py:254
  20.5 4.3 %collective-permute-done.1 = bf16[98,1024]{1,0:T(8,128)(2,1)} collective-permute-done((bf16[98,1024]{1,0:T(8,128)(2,1)S(1)}, bf16[98,1024]{1,0:T(8,128)(2,1)}, u32[]{:S(2)}, u32[]{:S(2)}) %collective-permute-start.1) | collective-permute-done | bytes 200736 | tf_op jit(solution)/shard_map/ppermute | solution.py:46
  24.8 1.0 fusion.18
  25.8 1.0 copy-done.15
  28.0 1.3 collective-permute-start.2
  29.3 1.3 collective-permute-start.3
  30.7 0.9 or_convert_fusion.mask_ref
  31.7 2.9 %collective-permute-done.3 = bf16[124,1024]{1,0:T(8,128)(2,1)S(1)} collective-permute-done((bf16[124,1024]{1,0:T(8,128)(2,1)S(1)}, bf16[124,1024]{1,0:T(8,128)(2,1)S(1)}, u32[]{:S(2)}, u32[]{:S(2)}) %collective-permute-start.3) | collective-permute-done | bytes 253984 | tf_op jit(solution)/shard_map/ppermute | solution.py:46
  34.6 4.5 %collective-permute-start.4 = (bf16[4,2048]{1,0:T(4,128)(2,1)S(1)}, bf16[4,2048]{1,0:T(4,128)(2,1)S(1)}, u32[]{:S(2)}, u32[]{:S(2)}) collective-permute-start(bf16[4,2048]{1,0:T(4,128)(2,1)S(1)} %maximum_select_fusion.3), channel_id=1, source_target_pairs={{0,2},{1,3},{2,0},{3,1},{4,6},{5,7},{6,4},{7,5},{8,10},{9,11},{10,... | collective-permute-start | bytes 49160 | tf_op jit(solution)/shard_map/ppermute | solution.py:35
  41.3 2.7 %collective-permute-start.5 = (bf16[8,2048]{1,0:T(8,128)(2,1)S(1)}, bf16[8,2048]{1,0:T(8,128)(2,1)S(1)}, u32[]{:S(2)}, u32[]{:S(2)}) collective-permute-start(bf16[8,2048]{1,0:T(8,128)(2,1)S(1)} %maximum_select_fusion.2), channel_id=1, source_target_pairs={{0,4},{1,5},{2,6},{3,7},{4,0},{5,1},{6,2},{7,3},{8,12},{9,13},{10,... | collective-permute-start | bytes 98312 | tf_op jit(solution)/shard_map/ppermute | solution.py:35
  44.0 3.4 %convolution_convert_fusion.vh_ref = bf16[480,1024]{1,0:T(8,128)(2,1)} fusion(bf16[480,1024]{1,0:T(8,128)(2,1)} %broadcast_dynamic-update-slice_fusion, bf16[1024,1024]{1,0:T(8,128)(2,1)S(1)} %copy-done), kind=kOutput, calls=%fused_computation.2 | convolution fusion | flops 1007124480 | bytes 4063232 | tf_op jit(solution)/shard_map/dot_general | solution.py:271
  47.5 2.1 %convolution_convert_fusion.1.kh_ref = bf16[480,1024]{1,0:T(8,128)(2,1)} fusion(bf16[480,1024]{1,0:T(8,128)(2,1)S(1)} %copy-done.16, bf16[1024,1024]{1,0:T(8,128)(2,1)S(1)} %copy-done.3), kind=kOutput, calls=%fused_computation.3 | convolution fusion | flops 1007124480 | bytes 4063232 | tf_op jit(solution)/shard_map/dot_general | solution.py:268
  49.7 2.3 %collective-permute-done.6 = bf16[16,2048]{1,0:T(8,128)(2,1)S(1)} collective-permute-done((bf16[16,2048]{1,0:T(8,128)(2,1)S(1)}, bf16[16,2048]{1,0:T(8,128)(2,1)S(1)}, u32[]{:S(2)}, u32[]{:S(2)}) %collective-permute-start.6) | collective-permute-done | bytes 65568 | tf_op jit(solution)/shard_map/ppermute | solution.py:35
  53.3 15.9 %shard_map.122 = (bf16[128,1024]{1,0:T(8,128)(2,1)}, bf16[128,1024]{1,0:T(8,128)(2,1)}, bf16[2,640,1024]{2,1,0:T(8,128)(2,1)}, f32[2,160,1024]{2,1,0:T(8,128)}) custom-call(bf16[128,1024]{1,0:T(8,128)(2,1)} %convolution_convert_fusion.6.q_ref, bf16[128,1024]{1,0:T(8,128)(2,1)} %copy-done.11, bf16[480,1024]{1,0:T(8,128)(2,1)} %convolution_convert_fusion.1.kh_ref, ...), custom_call_target="tpu_custom_call" | custom-call | flops 2013265920 | bytes 8978432 | tf_op jit(solution)/shard_map/pallas_call | solution.py:153
  69.2 3.3 %fusion.3 = f32[560,1024]{1,0:T(8,128)S(1)} fusion(bf16[1024,1024]{1,0:T(8,128)(2,1)} %param.13, bf16[2,640,1024]{2,1,0:T(8,128)(2,1)} %get-tuple-element.8), kind=kOutput, calls=%fused_computation.13 | convolution fusion | flops 1174405120 | bytes 5537792 | tf_op jit(solution)/shard_map/dot_general | solution.py:330
  72.5 4.1 %fusion.20 = (bf16[560,1024]{1,0:T(8,128)(2,1)S(1)}, f32[560,1024]{1,0:T(8,128)}) fusion(f32[560,1024]{1,0:T(8,128)S(1)} %fusion.3, bf16[1024,1024]{1,0:T(8,128)(2,1)S(1)} %copy-done, bf16[2,640,1024]{2,1,0:T(8,128)(2,1)} %get-tuple-element.8), kind=kOutput, calls=%fused_computation.88 | convolution fusion | flops 1175552000 | bytes 8978432 | tf_op jit(solution)/shard_map/dot_general | solution.py:332
  76.6 1.0 slice.166
  79.9 2.3 %collective-permute-start.8 = (bf16[184,1024]{1,0:T(8,128)(2,1)S(1)}, bf16[184,1024]{1,0:T(8,128)(2,1)}, u32[]{:S(2)}, u32[]{:S(2)}) collective-permute-start(bf16[184,1024]{1,0:T(8,128)(2,1)S(1)} %get-tuple-element.30), channel_id=1, source_target_pairs={{0,1},{1,2},{2,3},{3,4},{4,5},{5,6},{6,7},{8,9},{9,10},{10,11},{11... | collective-permute-start | bytes 1130504 | tf_op jit(solution)/shard_map/ppermute | solution.py:45
  82.2 1.3 collective-permute-start.7
  83.5 1.2 fusion.12
  84.7 1.0 slice.224
  85.7 1.0 collective-permute-done.7
  86.8 1.7 %slice.225 = bf16[120,1024]{1,0:T(8,128)(2,1)} slice(bf16[184,1024]{1,0:T(8,128)(2,1)} %collective-permute-done.7), slice={[0:120], [0:1024]} | slice | bytes 491520 | tf_op jit(solution)/shard_map/slice | solution.py:55
  88.4 1.0 reshape.192
  89.5 1.0 slice_select_fusion
  91.1 1.6 %reshape.189 = f32[2,2,2,2,2,1024]{5,4,3,2,1,0:T(2,128)} reshape(f32[32,1024]{1,0:T(8,128)} %convert_add_fusion.1) | data formatting | bytes 262144 | tf_op jit(solution)/shard_map/reshape | solution.py:352
  92.7 1.3 bitcast_add_fusion
  95.4 1.5 %select_n.286 = f32[16,1024]{1,0:T(8,128)} reshape(f32[2,2,1,2,2,1024]{5,4,3,1,0,2:T(2,128)} %copy.19) | data formatting | bytes 131072 | tf_op jit(solution)/shard_map/jit(_where)/select_n | solution.py:77
  96.9 0.9 subtract_convert_fusion.1
  98.8 3.4 %collective-permute-start.10 = (bf16[128,1024]{1,0:T(8,128)(2,1)}, bf16[128,1024]{1,0:T(8,128)(2,1)S(1)}, u32[]{:S(2)}, u32[]{:S(2)}) collective-permute-start(bf16[128,1024]{1,0:T(8,128)(2,1)} %get-tuple-element.34), channel_id=1, source_target_pairs={{0,8},{8,16},{16,24},{1,9},{9,17},{17,25},{2,10},{10,18},{18,26},{... | collective-permute-start | bytes 786440 | tf_op jit(solution)/shard_map/ppermute | solution.py:45
  102.2 1.5 %collective-permute-start.9 = (bf16[128,1024]{1,0:T(8,128)(2,1)}, bf16[128,1024]{1,0:T(8,128)(2,1)}, u32[]{:S(2)}, u32[]{:S(2)}) collective-permute-start(bf16[128,1024]{1,0:T(8,128)(2,1)} %get-tuple-element.35), channel_id=1, source_target_pairs={{8,0},{16,8},{24,16},{9,1},{17,9},{25,17},{10,2},{18,10},{26,18},{... | collective-permute-start | bytes 786440 | tf_op jit(solution)/shard_map/ppermute | solution.py:46
  103.7 2.7 %collective-permute-done.10 = bf16[128,1024]{1,0:T(8,128)(2,1)S(1)} collective-permute-done((bf16[128,1024]{1,0:T(8,128)(2,1)}, bf16[128,1024]{1,0:T(8,128)(2,1)S(1)}, u32[]{:S(2)}, u32[]{:S(2)}) %collective-permute-start.10) | collective-permute-done | bytes 262176 | tf_op jit(solution)/shard_map/ppermute | solution.py:45
  106.4 6.0 %collective-permute-done.9 = bf16[128,1024]{1,0:T(8,128)(2,1)} collective-permute-done((bf16[128,1024]{1,0:T(8,128)(2,1)}, bf16[128,1024]{1,0:T(8,128)(2,1)}, u32[]{:S(2)}, u32[]{:S(2)}) %collective-permute-start.9) | collective-permute-done | bytes 262176 | tf_op jit(solution)/shard_map/ppermute | solution.py:46
  113.3 1.0 bitcast_add_fusion.1
  114.3 8.4 %collective-permute-start.11 = (f32[2,2,2,1024]{3,0,1,2:T(2,128)S(1)}, f32[2,2,2,1024]{3,0,1,2:T(2,128)S(1)}, u32[]{:S(2)}, u32[]{:S(2)}) collective-permute-start(f32[2,2,2,1024]{3,0,1,2:T(2,128)S(1)} %select_bitcast_fusion), channel_id=1, source_target_pairs={{0,2},{1,3},{2,0},{3,1},{4,6},{5,7},{6,4},{7,5},{8,10},{9,11},{10,... | collective-permute-start | bytes 98312 | tf_op jit(solution)/shard_map/ppermute | solution.py:35
  122.7 1.9 %collective-permute-done.11 = f32[2,2,2,1024]{3,0,1,2:T(2,128)S(1)} collective-permute-done((f32[2,2,2,1024]{3,0,1,2:T(2,128)S(1)}, f32[2,2,2,1024]{3,0,1,2:T(2,128)S(1)}, u32[]{:S(2)}, u32[]{:S(2)}) %collective-permute-start.11) | collective-permute-done | bytes 32800 | tf_op jit(solution)/shard_map/ppermute | solution.py:35
  125.3 2.7 %convolution_convert_fusion.2 = bf16[128,1024]{1,0:T(8,128)(2,1)} fusion(bf16[128,1024]{1,0:T(8,128)(2,1)S(1)} %copy-done.13, bf16[1024,1024]{1,0:T(8,128)(2,1)} %param.15), kind=kOutput, calls=%fused_computation.7 | convolution fusion | flops 268566528 | bytes 2621440 | tf_op jit(solution)/shard_map/dot_general | solution.py:325
  128.1 2.0 %slice.212 = f32[128,1024]{1,0:T(8,128)} slice(f32[560,1024]{1,0:T(8,128)} %get-tuple-element.41), slice={[0:128], [0:1024]} | slice | bytes 1048576 | tf_op jit(solution)/shard_map/slice | solution.py:335
  130.1 0.9 slice.240
  131.3 3.5 %collective-permute-done.13 = f32[2,1024]{1,0:T(2,128)S(1)} collective-permute-done((f32[2,1024]{1,0:T(2,128)S(1)}, f32[2,1024]{1,0:T(2,128)S(1)}, u32[]{:S(2)}, u32[]{:S(2)}) %collective-permute-start.13) | collective-permute-done | bytes 8224 | tf_op jit(solution)/shard_map/ppermute | solution.py:35
  134.9 0.9 add_convert_fusion
  137.2 3.1 %fusion.1 = bf16[128,1024]{1,0:T(8,128)(2,1)} fusion(f32[128,1024]{1,0:T(8,128)S(1)} %bitcast.80, f32[128,1024]{1,0:T(8,128)S(1)} %dynamic_update_slice.3, bf16[128,1024]{1,0:T(8,128)(2,1)S(1)} %copy-done.12, bf16[1024,1024]{1,0:T(8,128)(2,1)} %param.12), kind=kOutput, calls=%fused_computation.6 | convolution fusion | flops 268828672 | bytes 3670016 | tf_op jit(solution)/shard_map/dot_general | solution.py:393
  (114 shorter events, 15.0 us)
Async XLA Ops:
  0.6 5.3 %copy-start = (bf16[1024,1024]{1,0:T(8,128)(2,1)S(1)}, bf16[1024,1024]{1,0:T(8,128)(2,1)}, u32[]{:S(2)}) copy-start(bf16[1024,1024]{1,0:T(8,128)(2,1)} %param.14) | copy-start | bytes 6291460
  0.6 6.7 %copy-start.5 = (bf16[8,16,1024]{2,1,0:T(8,128)(2,1)S(1)}, bf16[8,16,1024]{2,1,0:T(8,128)(2,1)}, u32[]{:S(2)}) copy-start(bf16[8,16,1024]{2,1,0:T(8,128)(2,1)} %param.11) | copy-start | bytes 786436
  4.7 2.6 %copy-start.2 = (bf16[1024,1024]{1,0:T(8,128)(2,1)S(1)}, bf16[1024,1024]{1,0:T(8,128)(2,1)}, u32[]{:S(2)}) copy-start(bf16[1024,1024]{1,0:T(8,128)(2,1)} %param.13) | copy-start | bytes 6291460
  7.3 10.6 %copy-start.10 = (bf16[128,1024]{1,0:T(8,128)(2,1)}, bf16[128,1024]{1,0:T(8,128)(2,1)S(1)}, u32[]{:S(2)}) copy-start(bf16[128,1024]{1,0:T(8,128)(2,1)S(1)} %convolution_convert_fusion.4.vo_ref) | copy-start | bytes 786436
  7.8 12.6 %copy-start.11 = (bf16[128,1024]{1,0:T(8,128)(2,1)}, bf16[128,1024]{1,0:T(8,128)(2,1)S(1)}, u32[]{:S(2)}) copy-start(bf16[128,1024]{1,0:T(8,128)(2,1)S(1)} %convolution_convert_fusion.5.ko_ref) | copy-start | bytes 786436
  8.6 11.8 %collective-permute-start = (bf16[98,1024]{1,0:T(8,128)(2,1)}, bf16[98,1024]{1,0:T(8,128)(2,1)S(1)}, u32[]{:S(2)}, u32[]{:S(2)}) collective-permute-start(bf16[98,1024]{1,0:T(8,128)(2,1)} %get-tuple-element.39), channel_id=1, source_target_pairs={{0,8},{8,16},{16,24},{1,9},{9,17},{17,25},{2,10},{10,18},{18,26},{... | collective-permute-start | bytes 602120 | tf_op jit(solution)/shard_map/ppermute | solution.py:45
  13.5 11.3 %collective-permute-start.1 = (bf16[98,1024]{1,0:T(8,128)(2,1)S(1)}, bf16[98,1024]{1,0:T(8,128)(2,1)}, u32[]{:S(2)}, u32[]{:S(2)}) collective-permute-start(bf16[98,1024]{1,0:T(8,128)(2,1)S(1)} %get-tuple-element.38), channel_id=1, source_target_pairs={{8,0},{16,8},{24,16},{9,1},{17,9},{25,17},{10,2},{18,10},{26,18},{... | collective-permute-start | bytes 602120 | tf_op jit(solution)/shard_map/ppermute | solution.py:46
  15.0 2.9 %copy-start.1 = (bf16[1024,1024]{1,0:T(8,128)(2,1)S(1)}, bf16[1024,1024]{1,0:T(8,128)(2,1)}, u32[]{:S(2)}) copy-start(bf16[1024,1024]{1,0:T(8,128)(2,1)} %param.15) | copy-start | bytes 6291460
  15.0 5.4 %copy-start.17 = (s32[640]{0:T(1024)S(1)}, s32[640]{0:T(1024)}, u32[]{:S(2)}) copy-start(s32[640]{0:T(1024)} %constant.136.clone) | copy-start | bytes 7684
  15.0 5.4 %copy-start.18 = (s32[640]{0:T(1024)S(1)}, s32[640]{0:T(1024)}, u32[]{:S(2)}) copy-start(s32[640]{0:T(1024)} %constant.137.clone) | copy-start | bytes 7684
  20.5 6.3 %copy-start.14 = (bf16[98,1024]{1,0:T(8,128)(2,1)}, bf16[98,1024]{1,0:T(8,128)(2,1)S(1)}, u32[]{:S(2)}) copy-start(bf16[98,1024]{1,0:T(8,128)(2,1)S(1)} %collective-permute-done) | copy-start | bytes 602116
  25.7 1.0 copy-start.15
  26.8 3.8 %copy-start.21 = (s32[32]{0:T(128)S(1)}, s32[32]{0:T(128)}, u32[]{:S(2)}) copy-start(s32[32]{0:T(128)} %constant.157) | copy-start | bytes 388
  26.8 3.9 %copy-start.19 = (pred[640]{0:T(1024)(128)(4,1)S(1)}, pred[640]{0:T(1024)(128)(4,1)}, u32[]{:S(2)}) copy-start(pred[640]{0:T(1024)(128)(4,1)} %constant.154) | copy-start | bytes 1924
  26.8 3.9 %copy-start.20 = (pred[640]{0:T(1024)(128)(4,1)S(1)}, pred[640]{0:T(1024)(128)(4,1)}, u32[]{:S(2)}) copy-start(pred[640]{0:T(1024)(128)(4,1)} %constant.155) | copy-start | bytes 1924
  28.0 3.7 %collective-permute-start.2 = (bf16[124,1024]{1,0:T(8,128)(2,1)S(1)}, bf16[124,1024]{1,0:T(8,128)(2,1)S(1)}, u32[]{:S(2)}, u32[]{:S(2)}) collective-permute-start(bf16[124,1024]{1,0:T(8,128)(2,1)S(1)} %get-tuple-element.37), channel_id=1, source_target_pairs={{0,1},{1,2},{2,3},{3,4},{4,5},{5,6},{6,7},{8,9},{9,10},{10,11},{11... | collective-permute-start | bytes 761864 | tf_op jit(solution)/shard_map/ppermute | solution.py:45
  29.3 5.2 %collective-permute-start.3 = (bf16[124,1024]{1,0:T(8,128)(2,1)S(1)}, bf16[124,1024]{1,0:T(8,128)(2,1)S(1)}, u32[]{:S(2)}, u32[]{:S(2)}) collective-permute-start(bf16[124,1024]{1,0:T(8,128)(2,1)S(1)} %get-tuple-element.36), channel_id=1, source_target_pairs={{1,0},{2,1},{3,2},{4,3},{5,4},{6,5},{7,6},{9,8},{10,9},{11,10},{12... | collective-permute-start | bytes 761864 | tf_op jit(solution)/shard_map/ppermute | solution.py:46
  34.6 6.6 %collective-permute-start.4 = (bf16[4,2048]{1,0:T(4,128)(2,1)S(1)}, bf16[4,2048]{1,0:T(4,128)(2,1)S(1)}, u32[]{:S(2)}, u32[]{:S(2)}) collective-permute-start(bf16[4,2048]{1,0:T(4,128)(2,1)S(1)} %maximum_select_fusion.3), channel_id=1, source_target_pairs={{0,2},{1,3},{2,0},{3,1},{4,6},{5,7},{6,4},{7,5},{8,10},{9,11},{10,... | collective-permute-start | bytes 49160 | tf_op jit(solution)/shard_map/ppermute | solution.py:35
  41.3 6.2 %copy-start.3 = (bf16[1024,1024]{1,0:T(8,128)(2,1)S(1)}, bf16[1024,1024]{1,0:T(8,128)(2,1)}, u32[]{:S(2)}) copy-start(bf16[1024,1024]{1,0:T(8,128)(2,1)} %param.13) | copy-start | bytes 6291460
  41.3 6.2 %copy-start.16 = (bf16[480,1024]{1,0:T(8,128)(2,1)S(1)}, bf16[480,1024]{1,0:T(8,128)(2,1)}, u32[]{:S(2)}) copy-start(bf16[480,1024]{1,0:T(8,128)(2,1)} %broadcast_dynamic-update-slice_fusion) | copy-start | bytes 2949124
  41.3 6.1 %collective-permute-start.5 = (bf16[8,2048]{1,0:T(8,128)(2,1)S(1)}, bf16[8,2048]{1,0:T(8,128)(2,1)S(1)}, u32[]{:S(2)}, u32[]{:S(2)}) collective-permute-start(bf16[8,2048]{1,0:T(8,128)(2,1)S(1)} %maximum_select_fusion.2), channel_id=1, source_target_pairs={{0,4},{1,5},{2,6},{3,7},{4,0},{5,1},{6,2},{7,3},{8,12},{9,13},{10,... | collective-permute-start | bytes 98312 | tf_op jit(solution)/shard_map/ppermute | solution.py:35
  47.4 4.5 %collective-permute-start.6 = (bf16[16,2048]{1,0:T(8,128)(2,1)S(1)}, bf16[16,2048]{1,0:T(8,128)(2,1)S(1)}, u32[]{:S(2)}, u32[]{:S(2)}) collective-permute-start(bf16[16,2048]{1,0:T(8,128)(2,1)S(1)} %maximum_select_fusion.1), channel_id=1, source_target_pairs={{0,16},{8,24},{16,0},{24,8},{1,17},{9,25},{17,1},{25,9},{2,18},{10... | collective-permute-start | bytes 196616 | tf_op jit(solution)/shard_map/ppermute | solution.py:35
  78.0 0.6 copy-start.8
  78.0 0.8 copy-start.9
  79.9 4.8 %collective-permute-start.8 = (bf16[184,1024]{1,0:T(8,128)(2,1)S(1)}, bf16[184,1024]{1,0:T(8,128)(2,1)}, u32[]{:S(2)}, u32[]{:S(2)}) collective-permute-start(bf16[184,1024]{1,0:T(8,128)(2,1)S(1)} %get-tuple-element.30), channel_id=1, source_target_pairs={{0,1},{1,2},{2,3},{3,4},{4,5},{5,6},{6,7},{8,9},{9,10},{10,11},{11... | collective-permute-start | bytes 1130504 | tf_op jit(solution)/shard_map/ppermute | solution.py:45
  82.2 4.6 %collective-permute-start.7 = (bf16[184,1024]{1,0:T(8,128)(2,1)}, bf16[184,1024]{1,0:T(8,128)(2,1)}, u32[]{:S(2)}, u32[]{:S(2)}) collective-permute-start(bf16[184,1024]{1,0:T(8,128)(2,1)} %get-tuple-element.31), channel_id=1, source_target_pairs={{1,0},{2,1},{3,2},{4,3},{5,4},{6,5},{7,6},{9,8},{10,9},{11,10},{12... | collective-permute-start | bytes 1130504 | tf_op jit(solution)/shard_map/ppermute | solution.py:46
  94.0 0.7 copy-start.7
  98.0 27.4 %copy-start.13 = (bf16[128,1024]{1,0:T(8,128)(2,1)S(1)}, bf16[128,1024]{1,0:T(8,128)(2,1)}, u32[]{:S(2)}) copy-start(bf16[128,1024]{1,0:T(8,128)(2,1)} %get-tuple-element.6) | copy-start | bytes 786436
  98.8 7.6 %collective-permute-start.10 = (bf16[128,1024]{1,0:T(8,128)(2,1)}, bf16[128,1024]{1,0:T(8,128)(2,1)S(1)}, u32[]{:S(2)}, u32[]{:S(2)}) collective-permute-start(bf16[128,1024]{1,0:T(8,128)(2,1)} %get-tuple-element.34), channel_id=1, source_target_pairs={{0,8},{8,16},{16,24},{1,9},{9,17},{17,25},{2,10},{10,18},{18,26},{... | collective-permute-start | bytes 786440 | tf_op jit(solution)/shard_map/ppermute | solution.py:45
  102.2 10.2 %collective-permute-start.9 = (bf16[128,1024]{1,0:T(8,128)(2,1)}, bf16[128,1024]{1,0:T(8,128)(2,1)}, u32[]{:S(2)}, u32[]{:S(2)}) collective-permute-start(bf16[128,1024]{1,0:T(8,128)(2,1)} %get-tuple-element.35), channel_id=1, source_target_pairs={{8,0},{16,8},{24,16},{9,1},{17,9},{25,17},{10,2},{18,10},{26,18},{... | collective-permute-start | bytes 786440 | tf_op jit(solution)/shard_map/ppermute | solution.py:46
  114.3 10.3 %collective-permute-start.11 = (f32[2,2,2,1024]{3,0,1,2:T(2,128)S(1)}, f32[2,2,2,1024]{3,0,1,2:T(2,128)S(1)}, u32[]{:S(2)}, u32[]{:S(2)}) collective-permute-start(f32[2,2,2,1024]{3,0,1,2:T(2,128)S(1)} %select_bitcast_fusion), channel_id=1, source_target_pairs={{0,2},{1,3},{2,0},{3,1},{4,6},{5,7},{6,4},{7,5},{8,10},{9,11},{10,... | collective-permute-start | bytes 98312 | tf_op jit(solution)/shard_map/ppermute | solution.py:35
  124.6 6.4 %collective-permute-start.12 = (f32[2,2,1024]{2,0,1:T(2,128)S(1)}, f32[2,2,1024]{2,0,1:T(2,128)S(1)}, u32[]{:S(2)}, u32[]{:S(2)}) collective-permute-start(f32[2,2,1024]{2,0,1:T(2,128)S(1)} %select_bitcast_fusion.1), channel_id=1, source_target_pairs={{0,4},{1,5},{2,6},{3,7},{4,0},{5,1},{6,2},{7,3},{8,12},{9,13},{10,... | collective-permute-start | bytes 49160 | tf_op jit(solution)/shard_map/ppermute | solution.py:35
  128.1 7.6 %copy-start.4 = (bf16[1024,1024]{1,0:T(8,128)(2,1)S(1)}, bf16[1024,1024]{1,0:T(8,128)(2,1)}, u32[]{:S(2)}) copy-start(bf16[1024,1024]{1,0:T(8,128)(2,1)} %param.13) | copy-start | bytes 6291460
  131.1 3.7 %collective-permute-start.13 = (f32[2,1024]{1,0:T(2,128)S(1)}, f32[2,1024]{1,0:T(2,128)S(1)}, u32[]{:S(2)}, u32[]{:S(2)}) collective-permute-start(f32[2,1024]{1,0:T(2,128)S(1)} %select_bitcast_fusion.2), channel_id=1, source_target_pairs={{0,16},{8,24},{16,0},{24,8},{1,17},{9,25},{17,1},{25,9},{2,18},{10... | collective-permute-start | bytes 24584 | tf_op jit(solution)/shard_map/ppermute | solution.py:35
  135.7 1.3 copy-start.6
  135.7 1.4 %copy-start.12 = (bf16[128,1024]{1,0:T(8,128)(2,1)S(1)}, bf16[128,1024]{1,0:T(8,128)(2,1)}, u32[]{:S(2)}) copy-start(bf16[128,1024]{1,0:T(8,128)(2,1)} %get-tuple-element.7) | copy-start | bytes 786436

commit v12 on v10

--- a/solution.py
+++ b/solution.py
@@ -325,12 +325,20 @@
         .reshape(features.shape)
     )
 
-    given_all = jnp.dot(
-        rounded_grads[0, :frame_keys], w_key.T, preferred_element_type=jnp.float32
-    ) + jnp.dot(rounded_grads[1, :frame_keys], w_value.T, preferred_element_type=jnp.float32)
+    strips_from = tokens + 2 * band_keys
+
+    def contribution(lo, hi):
+        return jnp.dot(
+            rounded_grads[0, lo:hi], w_key.T, preferred_element_type=jnp.float32
+        ) + jnp.dot(rounded_grads[1, lo:hi], w_value.T, preferred_element_type=jnp.float32)
+
+    strip_given = contribution(strips_from, frame_keys)
+    rest_given = contribution(0, strips_from)
 
     def given(lo, hi):
-        return given_all[lo:hi]
+        if lo >= strips_from:
+            return strip_given[lo - strips_from : hi - strips_from]
+        return rest_given[lo:hi]
 
     scatter = wide_grads[:, tokens:].reshape(
         (2,) + (2,) * all_bits + (model_width,)
@@ -338,7 +346,6 @@
     left = list(range(all_bits - 1, -1, -1))
     back_order = [0, col_bits] + list(range(1, col_bits)) + list(range(col_bits + 1, all_bits))
 
-    strips_from = tokens + 2 * band_keys
     keep_part, send_part = scatter_split(scatter, left, back_order[0])
     strip_shape = (ext_rows, RAD, model_width)
     from_left, from_right, got = exchange(

time: 124 us -> 121 us (0.976)
  starting transfers between devices: 30.6 us -> 26.2 us
  waiting for transfers between devices: 13.3 us -> 15.3 us
    ppermute x6, starting transfers between devices: 21.2 us -> 13.2 us  [partner(): return lax.ppermute(x, axis, [(i, i ^ 1 << bit) for i in range(size)])]
    ppermute x4, starting transfers between devices: 6.53 us -> 9.62 us  [exchange(): got_first = lax.ppermute(first, axis, [(i, i ^ 1) for i in range(size)])]
    dot_general x2 -> x4, matrix products: 7.45 us -> 9.57 us  [the longest x2 5.74 us: contribution(): jnp.dot(rounded_grads[0, lo:hi], w_key.T, preferred_element_type=jnp.floa...]
    slice x2 -> x3, local copies, waits for them, and re-layouts: 3.05 us -> 1.03 us  [given(): return rest_given[lo:hi]]
    dot_general x1, matrix products: 4.08 us -> 2.18 us  [shards(): jnp.dot(halo_features, w_key, preferred_element_type=jnp.float32)]
    dot_general x1, matrix products: 2.13 us -> 0.45 us  [shards(): jnp.dot(flat_tokens, w_key, preferred_element_type=jnp.float32)]
    ppermute x4, waiting for transfers between devices: 4.57 us -> 5.83 us  [exchange(): got_first = lax.ppermute(first, axis, [(i, i ^ 1) for i in range(size)])]
    unnamed x48 -> x62, local copies, waits for them, and re-layouts: 3.06 us -> 3.3 us
  transfers between devices with their start and end apart: 14 -> 14, of which waited for: 6 -> 6; matrix products, arithmetic and copies ran while one was open for 21% -> 23% of each run, Pallas kernels for 0% -> 0%
where the time goes in v12:
time: 121 us; the launch traced here: 120 us
  matrix products  28.1 us (23%)
  starting transfers between devices  26.2 us (22%)
  Pallas kernels  15.9 us (13%)
  local copies, waits for them, and re-layouts  15.8 us (13%)
  waiting for transfers between devices  15.3 us (13%)
  other arithmetic  14.8 us (12%)
  between operations  4.04 us (3%)
    pallas_call x1, Pallas kernels, attention(): pl.pallas_call(functools.partial(attention_kernel, tokens, first, last),...  15.9 us
    ppermute x6, starting transfers between devices, partner(): return lax.ppermute(x, axis, [(i, i ^ 1 << bit) for i in range(size)])  13.2 us
    ppermute x4, starting transfers between devices, exchange(): got_first = lax.ppermute(first, axis, [(i, i ^ 1) for i in range(size)])  9.62 us
    ppermute x6, waiting for transfers between devices, partner(): return lax.ppermute(x, axis, [(i, i ^ 1 << bit) for i in range(size)])  9.44 us
    ppermute x4, waiting for transfers between devices, exchange(): got_first = lax.ppermute(first, axis, [(i, i ^ 1) for i in range(size)])  5.83 us
    dot_general x2, matrix products, contribution(): jnp.dot(rounded_grads[0, lo:hi], w_key.T, preferred_element_type=jnp.floa...  5.74 us
    dot_general x2, matrix products, contribution(): jnp.dot(rounded_grads[1, lo:hi], w_value.T, preferred_element_type=jnp.fl...  3.83 us
    select_n x4, other arithmetic, exchange(): first = jnp.where(even, to_higher, to_lower)  3.61 us
  transfers between devices with their start and end apart: 14, of which 6 were waited for; matrix products, arithmetic and copies ran while one was open for 23% of the time, Pallas kernels for 0%

profile of v12, /device:TPU:0, one launch (start us, length us, event | category | flops | bytes accessed | tf_op | source)
XLA Modules:
  0.0 120.1 jit_solution(7341887492374828024)
XLA Ops:
  0.7 1.9 %broadcast_select_fusion.8 = (bf16[6,16,1024]{2,1,0:T(8,128)(2,1)S(1)}, bf16[6,16,1024]{2,1,0:T(8,128)(2,1)}) fusion(pred[]{:T(512)S(6)} %eq.68, bf16[8,16,1024]{2,1,0:T(8,128)(2,1)} %param.11), kind=kLoop, calls=%fused_computation.45 | loop fusion | flops 196608 | bytes 786433 | tf_op jit(solution)/shard_map/jit(_where)/select_n | solution.py:41
  3.2 1.2 %dynamic_slice.13 = s32[1]{0:T(128)} dynamic-slice(s32[32]{0:T(128)} %param.16, s32[]{:T(128)S(6)} %select_n.311), dynamic_slice_sizes={1} | dynamic-slice | bytes 12 | tf_op jit(solution)/shard_map/jit(dynamic_index_in_dim)/dynamic_slice | solution.py:217
  7.1 1.5 %convolution_convert_fusion.4.vo_ref = bf16[128,1024]{1,0:T(8,128)(2,1)S(1)} fusion(bf16[128,1024]{1,0:T(8,128)(2,1)} %bitcast.83, bf16[1024,1024]{1,0:T(8,128)(2,1)S(1)} %copy-done), kind=kOutput, calls=%fused_computation.11 | convolution fusion | flops 268566528 | bytes 2621440 | tf_op jit(solution)/shard_map/dot_general | solution.py:212
  10.0 5.7 %collective-permute-start.1 = (bf16[98,1024]{1,0:T(8,128)(2,1)}, bf16[98,1024]{1,0:T(8,128)(2,1)S(1)}, u32[]{:S(2)}, u32[]{:S(2)}) collective-permute-start(bf16[98,1024]{1,0:T(8,128)(2,1)} %pad_maximum_fusion.4), channel_id=1, source_target_pairs={{0,8},{8,0},{16,24},{24,16},{1,9},{9,1},{17,25},{25,17},{2,10},{10... | collective-permute-start | bytes 602120 | tf_op jit(solution)/shard_map/ppermute | solution.py:45
  15.9 2.9 %convolution_convert_fusion.6.q_ref = bf16[128,1024]{1,0:T(8,128)(2,1)} fusion(bf16[128,1024]{1,0:T(8,128)(2,1)S(1)} %bitcast.85, bf16[1024,1024]{1,0:T(8,128)(2,1)} %param.12), kind=kOutput, calls=%fused_computation.13 | convolution fusion | flops 268566528 | bytes 2621440 | tf_op jit(solution)/shard_map/dot_general | solution.py:251
  18.8 2.5 %convolution_convert_fusion.3.g_ref = bf16[128,1024]{1,0:T(8,128)(2,1)} fusion(bf16[128,1024]{1,0:T(8,128)(2,1)} %bitcast.96, bf16[1024,1024]{1,0:T(8,128)(2,1)S(1)} %copy-done.5), kind=kOutput, calls=%fused_computation.10 | convolution fusion | flops 268566528 | bytes 2621440 | tf_op jit(solution)/shard_map/dot_general | solution.py:252
  21.6 1.0 copy-done.23
  23.0 0.9 or_convert_fusion.mask_ref
  24.9 3.4 %collective-permute-start.4 = (bf16[4,2048]{1,0:T(4,128)(2,1)S(1)}, bf16[4,2048]{1,0:T(4,128)(2,1)S(1)}, u32[]{:S(2)}, u32[]{:S(2)}) collective-permute-start(bf16[4,2048]{1,0:T(4,128)(2,1)S(1)} %maximum_select_fusion.3), channel_id=1, source_target_pairs={{0,2},{1,3},{2,0},{3,1},{4,6},{5,7},{6,4},{7,5},{8,10},{9,11},{10,... | collective-permute-start | bytes 49160 | tf_op jit(solution)/shard_map/ppermute | solution.py:35
  28.3 0.8 select_dynamic-update-slice_fusion.1
  29.1 0.8 select_dynamic-update-slice_fusion
  30.4 2.1 %collective-permute-done.4 = bf16[4,2048]{1,0:T(4,128)(2,1)S(1)} collective-permute-done((bf16[4,2048]{1,0:T(4,128)(2,1)S(1)}, bf16[4,2048]{1,0:T(4,128)(2,1)S(1)}, u32[]{:S(2)}, u32[]{:S(2)}) %collective-permute-start.4) | collective-permute-done | bytes 16416 | tf_op jit(solution)/shard_map/ppermute | solution.py:35
  32.6 3.8 %collective-permute-start.5 = (bf16[8,2048]{1,0:T(8,128)(2,1)S(1)}, bf16[8,2048]{1,0:T(8,128)(2,1)S(1)}, u32[]{:S(2)}, u32[]{:S(2)}) collective-permute-start(bf16[8,2048]{1,0:T(8,128)(2,1)S(1)} %maximum_select_fusion.2), channel_id=1, source_target_pairs={{0,4},{1,5},{2,6},{3,7},{4,0},{5,1},{6,2},{7,3},{8,12},{9,13},{10,... | collective-permute-start | bytes 98312 | tf_op jit(solution)/shard_map/ppermute | solution.py:35
  36.4 3.4 %convolution_convert_fusion.vh_ref = bf16[480,1024]{1,0:T(8,128)(2,1)} fusion(bf16[480,1024]{1,0:T(8,128)(2,1)} %broadcast_dynamic-update-slice_fusion, bf16[1024,1024]{1,0:T(8,128)(2,1)S(1)} %copy-done), kind=kOutput, calls=%fused_computation.1 | convolution fusion | flops 1007124480 | bytes 4063232 | tf_op jit(solution)/shard_map/dot_general | solution.py:269
  39.8 1.3 %collective-permute-start.6 = (bf16[16,2048]{1,0:T(8,128)(2,1)S(1)}, bf16[16,2048]{1,0:T(8,128)(2,1)S(1)}, u32[]{:S(2)}, u32[]{:S(2)}) collective-permute-start(bf16[16,2048]{1,0:T(8,128)(2,1)S(1)} %maximum_select_fusion.1), channel_id=1, source_target_pairs={{0,16},{8,24},{16,0},{24,8},{1,17},{9,25},{17,1},{25,9},{2,18},{10... | collective-permute-start | bytes 196616 | tf_op jit(solution)/shard_map/ppermute | solution.py:35
  41.1 2.2 %convolution_convert_fusion.1.kh_ref = bf16[480,1024]{1,0:T(8,128)(2,1)} fusion(bf16[480,1024]{1,0:T(8,128)(2,1)S(1)} %copy-done.24, bf16[1024,1024]{1,0:T(8,128)(2,1)S(1)} %copy-done.2), kind=kOutput, calls=%fused_computation.2 | convolution fusion | flops 1007124480 | bytes 4063232 | tf_op jit(solution)/shard_map/dot_general | solution.py:266
  43.3 0.9 collective-permute-done.6
  45.6 15.9 %shard_map.122 = (bf16[128,1024]{1,0:T(8,128)(2,1)}, bf16[128,1024]{1,0:T(8,128)(2,1)}, bf16[2,640,1024]{2,1,0:T(8,128)(2,1)}, f32[2,160,1024]{2,1,0:T(8,128)}) custom-call(bf16[128,1024]{1,0:T(8,128)(2,1)} %convolution_convert_fusion.6.q_ref, bf16[128,1024]{1,0:T(8,128)(2,1)} %copy-done.19, bf16[480,1024]{1,0:T(8,128)(2,1)} %convolution_convert_fusion.1.kh_ref, ...), custom_call_target="tpu_custom_call" | custom-call | flops 2013265920 | bytes 8978432 | tf_op jit(solution)/shard_map/pallas_call | solution.py:151
  61.5 2.6 %fusion.9 = f32[240,1024]{1,0:T(8,128)S(1)} fusion(bf16[1024,1024]{1,0:T(8,128)(2,1)} %param.13, bf16[2,640,1024]{2,1,0:T(8,128)(2,1)} %get-tuple-element.8), kind=kOutput, calls=%fused_computation.22 | convolution fusion | flops 503316480 | bytes 3571712 | tf_op jit(solution)/shard_map/dot_general | solution.py:331
  64.2 3.1 %fusion.4 = f32[320,1024]{1,0:T(8,128)} fusion(bf16[1024,1024]{1,0:T(8,128)(2,1)S(1)} %copy-done.3, bf16[2,640,1024]{2,1,0:T(8,128)(2,1)} %get-tuple-element.8), kind=kOutput, calls=%fused_computation.16 | convolution fusion | flops 671088640 | bytes 4063232 | tf_op jit(solution)/shard_map/dot_general | solution.py:331
  67.3 1.0 slice.144
  68.2 0.8 reshape.188
  69.1 1.3 %fusion.20 = (f32[2,2,2,2,2,1,1024]{6,5,4,3,2,1,0:T(1,128)S(1)}, f32[2,2,2,2,2,1,1024]{6,5,4,3,2,1,0:T(1,128)S(1)}) fusion(f32[2,2,2,2,2,2,1024]{6,5,4,3,2,1,0:T(2,128)} %reshape.188), kind=kLoop, calls=%fused_computation.90 | loop fusion | bytes 524288 | tf_op jit(solution)/shard_map/slice | solution.py:73
  70.6 0.8 copy.17
  71.3 1.0 select_n.354
  72.4 1.9 %fusion = bf16[240,1024]{1,0:T(8,128)(2,1)S(1)} fusion(f32[240,1024]{1,0:T(8,128)S(1)} %fusion.9, bf16[1024,1024]{1,0:T(8,128)(2,1)S(1)} %copy-done, bf16[2,640,1024]{2,1,0:T(8,128)(2,1)} %get-tuple-element.8), kind=kOutput, calls=%fused_computation.5 | convolution fusion | flops 503808000 | bytes 4063232 | tf_op jit(solution)/shard_map/dot_general | solution.py:333
  75.0 1.3 %collective-permute-start.8 = (bf16[120,1024]{1,0:T(8,128)(2,1)}, bf16[120,1024]{1,0:T(8,128)(2,1)}, u32[]{:S(2)}, u32[]{:S(2)}) collective-permute-start(bf16[120,1024]{1,0:T(8,128)(2,1)} %get-tuple-element.28), channel_id=1, source_target_pairs={{1,2},{3,4},{5,6},{2,1},{4,3},{6,5},{9,10},{11,12},{13,14},{10,9},... | collective-permute-start | bytes 737288 | tf_op jit(solution)/shard_map/ppermute | solution.py:47
  76.4 2.6 %collective-permute-start.7 = (bf16[184,1024]{1,0:T(8,128)(2,1)S(1)}, bf16[184,1024]{1,0:T(8,128)(2,1)S(1)}, u32[]{:S(2)}, u32[]{:S(2)}) collective-permute-start(bf16[184,1024]{1,0:T(8,128)(2,1)S(1)} %pad_maximum_fusion.1), channel_id=1, source_target_pairs={{0,1},{1,0},{2,3},{3,2},{4,5},{5,4},{6,7},{7,6},{8,9},{9,8},{10,11... | collective-permute-start | bytes 1130504 | tf_op jit(solution)/shard_map/ppermute | solution.py:45
  78.9 2.0 %convolution_add_fusion = f32[320,1024]{1,0:T(8,128)S(1)} fusion(f32[320,1024]{1,0:T(8,128)S(1)} %copy-done.11, bf16[1024,1024]{1,0:T(8,128)(2,1)S(1)} %copy-done, bf16[2,640,1024]{2,1,0:T(8,128)(2,1)} %get-tuple-element.8), kind=kOutput, calls=%fused_computation.3 | convolution fusion | flops 671416320 | bytes 5373952 | tf_op jit(solution)/shard_map/dot_general | solution.py:333
  80.9 1.0 fusion.19
  81.9 0.8 copy-done.17
  83.4 1.6 %reshape.189 = f32[2,2,2,2,2,1024]{5,4,3,2,1,0:T(2,128)} reshape(f32[32,1024]{1,0:T(8,128)} %convert_add_fusion.1) | data formatting | bytes 262144 | tf_op jit(solution)/shard_map/reshape | solution.py:357
  85.0 1.2 %bitcast_add_fusion = f32[2,2,2,2,2,1024]{5,0,1,3,4,2:T(2,128)S(1)} fusion(f32[2,2,2,2,2,1024]{5,4,3,2,1,0:T(2,128)} %reshape.189, pred[]{:T(512)S(6)} %eq.83, f32[2,2,2,2,2,1,1024]{6,5,4,3,2,1,0:T(1,128)} %copy-done.14, f32[2,2,2,2,2,1,1024]{6,5,4,3,2,1,0:T(1,128)S(1)} %get-tuple-element.31), kind=kLoop, calls=%fused_computation.52 | loop fusion | flops 65536 | bytes 524289 | tf_op jit(solution)/shard_map/add | solution.py:357
  87.7 1.9 %broadcast_select_fusion.3 = (bf16[120,1024]{1,0:T(8,128)(2,1)S(1)}, bf16[120,1024]{1,0:T(8,128)(2,1)}) fusion(bf16[120,1024]{1,0:T(8,128)(2,1)} %collective-permute-done.8, pred[]{:T(512)S(6)} %eq.69, bf16[184,1024]{1,0:T(8,128)(2,1)} %copy-done.17), kind=kLoop, calls=%fused_computation.39 | loop fusion | flops 245760 | bytes 983041 | tf_op jit(solution)/shard_map/jit(_where)/select_n | solution.py:52
  89.6 1.0 reshape.192
  90.7 0.9 broadcast_select_fusion.7
  91.6 0.8 pad_maximum_fusion.3
  92.5 1.3 %collective-permute-start.9 = (bf16[128,1024]{1,0:T(8,128)(2,1)S(1)}, bf16[128,1024]{1,0:T(8,128)(2,1)S(1)}, u32[]{:S(2)}, u32[]{:S(2)}) collective-permute-start(bf16[128,1024]{1,0:T(8,128)(2,1)S(1)} %pad_maximum_fusion.3), channel_id=1, source_target_pairs={{0,8},{8,0},{16,24},{24,16},{1,9},{9,1},{17,25},{25,17},{2,10},{10... | collective-permute-start | bytes 786440 | tf_op jit(solution)/shard_map/ppermute | solution.py:45
  93.8 1.2 convolution_convert_fusion.2
  94.9 5.8 %collective-permute-done.9 = bf16[128,1024]{1,0:T(8,128)(2,1)S(1)} collective-permute-done((bf16[128,1024]{1,0:T(8,128)(2,1)S(1)}, bf16[128,1024]{1,0:T(8,128)(2,1)S(1)}, u32[]{:S(2)}, u32[]{:S(2)}) %collective-permute-start.9) | collective-permute-done | bytes 262176 | tf_op jit(solution)/shard_map/ppermute | solution.py:45
  102.8 2.8 %collective-permute-done.10 = f32[2,2,2,1024]{3,0,1,2:T(2,128)S(1)} collective-permute-done((f32[2,2,2,1024]{3,0,1,2:T(2,128)S(1)}, f32[2,2,2,1024]{3,0,1,2:T(2,128)S(1)}, u32[]{:S(2)}, u32[]{:S(2)}) %collective-permute-start.10) | collective-permute-done | bytes 32800 | tf_op jit(solution)/shard_map/ppermute | solution.py:35
  105.7 1.6 %collective-permute-start.11 = (f32[2,2,1024]{2,0,1:T(2,128)S(1)}, f32[2,2,1024]{2,0,1:T(2,128)S(1)}, u32[]{:S(2)}, u32[]{:S(2)}) collective-permute-start(f32[2,2,1024]{2,0,1:T(2,128)S(1)} %select_bitcast_fusion.1), channel_id=1, source_target_pairs={{0,4},{1,5},{2,6},{3,7},{4,0},{5,1},{6,2},{7,3},{8,12},{9,13},{10,... | collective-permute-start | bytes 49160 | tf_op jit(solution)/shard_map/ppermute | solution.py:35
  107.3 1.0 broadcast_select_fusion.11
  108.3 2.1 %collective-permute-done.11 = f32[2,2,1024]{2,0,1:T(2,128)S(1)} collective-permute-done((f32[2,2,1024]{2,0,1:T(2,128)S(1)}, f32[2,2,1024]{2,0,1:T(2,128)S(1)}, u32[]{:S(2)}, u32[]{:S(2)}) %collective-permute-start.11) | collective-permute-done | bytes 16416 | tf_op jit(solution)/shard_map/ppermute | solution.py:35
  110.4 2.6 %collective-permute-start.12 = (f32[2,1024]{1,0:T(2,128)S(1)}, f32[2,1024]{1,0:T(2,128)S(1)}, u32[]{:S(2)}, u32[]{:S(2)}) collective-permute-start(f32[2,1024]{1,0:T(2,128)S(1)} %select_bitcast_fusion.2), channel_id=1, source_target_pairs={{0,16},{8,24},{16,0},{24,8},{1,17},{9,25},{17,1},{25,9},{2,18},{10... | collective-permute-start | bytes 24584 | tf_op jit(solution)/shard_map/ppermute | solution.py:35
  113.2 1.5 %collective-permute-done.12 = f32[2,1024]{1,0:T(2,128)S(1)} collective-permute-done((f32[2,1024]{1,0:T(2,128)S(1)}, f32[2,1024]{1,0:T(2,128)S(1)}, u32[]{:S(2)}, u32[]{:S(2)}) %collective-permute-start.12) | collective-permute-done | bytes 8224 | tf_op jit(solution)/shard_map/ppermute | solution.py:35
  114.7 0.9 add_convert_fusion
  117.0 3.1 %fusion.2 = bf16[128,1024]{1,0:T(8,128)(2,1)} fusion(f32[128,1024]{1,0:T(8,128)S(1)} %bitcast.86, f32[128,1024]{1,0:T(8,128)S(1)} %dynamic_update_slice.3, bf16[128,1024]{1,0:T(8,128)(2,1)S(1)} %copy-done.20, bf16[1024,1024]{1,0:T(8,128)(2,1)} %param.12), kind=kOutput, calls=%fused_computation.8 | convolution fusion | flops 268828672 | bytes 3670016 | tf_op jit(solution)/shard_map/dot_general | solution.py:398
  (130 shorter events, 12.4 us)
Async XLA Ops:
  0.6 6.5 %copy-start = (bf16[1024,1024]{1,0:T(8,128)(2,1)S(1)}, bf16[1024,1024]{1,0:T(8,128)(2,1)}, u32[]{:S(2)}) copy-start(bf16[1024,1024]{1,0:T(8,128)(2,1)} %param.14) | copy-start | bytes 6291460
  0.6 8.0 %copy-start.7 = (bf16[8,16,1024]{2,1,0:T(8,128)(2,1)S(1)}, bf16[8,16,1024]{2,1,0:T(8,128)(2,1)}, u32[]{:S(2)}) copy-start(bf16[8,16,1024]{2,1,0:T(8,128)(2,1)} %param.11) | copy-start | bytes 786436
  2.5 18.9 %collective-permute-start = (bf16[96,1024]{1,0:T(8,128)(2,1)}, bf16[96,1024]{1,0:T(8,128)(2,1)S(1)}, u32[]{:S(2)}, u32[]{:S(2)}) collective-permute-start(bf16[96,1024]{1,0:T(8,128)(2,1)} %bitcast.1), channel_id=1, source_target_pairs={{8,16},{16,8},{9,17},{17,9},{10,18},{18,10},{11,19},{19,11},{12,20... | collective-permute-start | bytes 589832 | tf_op jit(solution)/shard_map/ppermute | solution.py:47
  7.1 1.7 %copy-start.1 = (bf16[1024,1024]{1,0:T(8,128)(2,1)S(1)}, bf16[1024,1024]{1,0:T(8,128)(2,1)}, u32[]{:S(2)}) copy-start(bf16[1024,1024]{1,0:T(8,128)(2,1)} %param.13) | copy-start | bytes 6291460
  8.8 10.0 %copy-start.18 = (bf16[128,1024]{1,0:T(8,128)(2,1)}, bf16[128,1024]{1,0:T(8,128)(2,1)S(1)}, u32[]{:S(2)}) copy-start(bf16[128,1024]{1,0:T(8,128)(2,1)S(1)} %convolution_convert_fusion.4.vo_ref) | copy-start | bytes 786436
  9.2 12.1 %copy-start.19 = (bf16[128,1024]{1,0:T(8,128)(2,1)}, bf16[128,1024]{1,0:T(8,128)(2,1)S(1)}, u32[]{:S(2)}) copy-start(bf16[128,1024]{1,0:T(8,128)(2,1)S(1)} %convolution_convert_fusion.5.ko_ref) | copy-start | bytes 786436
  10.0 11.3 %collective-permute-start.1 = (bf16[98,1024]{1,0:T(8,128)(2,1)}, bf16[98,1024]{1,0:T(8,128)(2,1)S(1)}, u32[]{:S(2)}, u32[]{:S(2)}) collective-permute-start(bf16[98,1024]{1,0:T(8,128)(2,1)} %pad_maximum_fusion.4), channel_id=1, source_target_pairs={{0,8},{8,0},{16,24},{24,16},{1,9},{9,1},{17,25},{25,17},{2,10},{10... | collective-permute-start | bytes 602120 | tf_op jit(solution)/shard_map/ppermute | solution.py:45
  15.9 2.9 %copy-start.5 = (bf16[1024,1024]{1,0:T(8,128)(2,1)S(1)}, bf16[1024,1024]{1,0:T(8,128)(2,1)}, u32[]{:S(2)}) copy-start(bf16[1024,1024]{1,0:T(8,128)(2,1)} %param.15) | copy-start | bytes 6291460
  15.9 5.4 %copy-start.25 = (s32[640]{0:T(1024)S(1)}, s32[640]{0:T(1024)}, u32[]{:S(2)}) copy-start(s32[640]{0:T(1024)} %constant.137.clone) | copy-start | bytes 7684
  15.9 5.4 %copy-start.26 = (s32[640]{0:T(1024)S(1)}, s32[640]{0:T(1024)}, u32[]{:S(2)}) copy-start(s32[640]{0:T(1024)} %constant.136.clone) | copy-start | bytes 7684
  21.5 1.5 %copy-start.27 = (pred[640]{0:T(1024)(128)(4,1)S(1)}, pred[640]{0:T(1024)(128)(4,1)}, u32[]{:S(2)}) copy-start(pred[640]{0:T(1024)(128)(4,1)} %constant.155) | copy-start | bytes 1924
  21.5 1.4 %copy-start.28 = (pred[640]{0:T(1024)(128)(4,1)S(1)}, pred[640]{0:T(1024)(128)(4,1)}, u32[]{:S(2)}) copy-start(pred[640]{0:T(1024)(128)(4,1)} %constant.154) | copy-start | bytes 1924
  21.6 1.0 copy-start.23
  22.6 2.1 %copy-start.29 = (s32[32]{0:T(128)S(1)}, s32[32]{0:T(128)}, u32[]{:S(2)}) copy-start(s32[32]{0:T(128)} %constant.157) | copy-start | bytes 388
  22.9 1.9 %collective-permute-start.3 = (bf16[124,1024]{1,0:T(8,128)(2,1)S(1)}, bf16[124,1024]{1,0:T(8,128)(2,1)S(1)}, u32[]{:S(2)}, u32[]{:S(2)}) collective-permute-start(bf16[124,1024]{1,0:T(8,128)(2,1)S(1)} %pad_maximum_fusion.2), channel_id=1, source_target_pairs={{0,1},{1,0},{2,3},{3,2},{4,5},{5,4},{6,7},{7,6},{8,9},{9,8},{10,11... | collective-permute-start | bytes 761864 | tf_op jit(solution)/shard_map/ppermute | solution.py:45
  24.0 4.3 %collective-permute-start.2 = (bf16[120,1024]{1,0:T(8,128)(2,1)S(1)}, bf16[120,1024]{1,0:T(8,128)(2,1)S(1)}, u32[]{:S(2)}, u32[]{:S(2)}) collective-permute-start(bf16[120,1024]{1,0:T(8,128)(2,1)S(1)} %select_n.321), channel_id=1, source_target_pairs={{1,2},{3,4},{5,6},{2,1},{4,3},{6,5},{9,10},{11,12},{13,14},{10,9},... | collective-permute-start | bytes 737288 | tf_op jit(solution)/shard_map/ppermute | solution.py:47
  24.9 7.7 %collective-permute-start.4 = (bf16[4,2048]{1,0:T(4,128)(2,1)S(1)}, bf16[4,2048]{1,0:T(4,128)(2,1)S(1)}, u32[]{:S(2)}, u32[]{:S(2)}) collective-permute-start(bf16[4,2048]{1,0:T(4,128)(2,1)S(1)} %maximum_select_fusion.3), channel_id=1, source_target_pairs={{0,2},{1,3},{2,0},{3,1},{4,6},{5,7},{6,4},{7,5},{8,10},{9,11},{10,... | collective-permute-start | bytes 49160 | tf_op jit(solution)/shard_map/ppermute | solution.py:35
  32.6 8.5 %copy-start.2 = (bf16[1024,1024]{1,0:T(8,128)(2,1)S(1)}, bf16[1024,1024]{1,0:T(8,128)(2,1)}, u32[]{:S(2)}) copy-start(bf16[1024,1024]{1,0:T(8,128)(2,1)} %param.13) | copy-start | bytes 6291460
  32.6 8.5 %copy-start.24 = (bf16[480,1024]{1,0:T(8,128)(2,1)S(1)}, bf16[480,1024]{1,0:T(8,128)(2,1)}, u32[]{:S(2)}) copy-start(bf16[480,1024]{1,0:T(8,128)(2,1)} %broadcast_dynamic-update-slice_fusion) | copy-start | bytes 2949124
  32.6 7.2 %collective-permute-start.5 = (bf16[8,2048]{1,0:T(8,128)(2,1)S(1)}, bf16[8,2048]{1,0:T(8,128)(2,1)S(1)}, u32[]{:S(2)}, u32[]{:S(2)}) collective-permute-start(bf16[8,2048]{1,0:T(8,128)(2,1)S(1)} %maximum_select_fusion.2), channel_id=1, source_target_pairs={{0,4},{1,5},{2,6},{3,7},{4,0},{5,1},{6,2},{7,3},{8,12},{9,13},{10,... | collective-permute-start | bytes 98312 | tf_op jit(solution)/shard_map/ppermute | solution.py:35
  39.8 4.4 %collective-permute-start.6 = (bf16[16,2048]{1,0:T(8,128)(2,1)S(1)}, bf16[16,2048]{1,0:T(8,128)(2,1)S(1)}, u32[]{:S(2)}, u32[]{:S(2)}) collective-permute-start(bf16[16,2048]{1,0:T(8,128)(2,1)S(1)} %maximum_select_fusion.1), channel_id=1, source_target_pairs={{0,16},{8,24},{16,0},{24,8},{1,17},{9,25},{17,1},{25,9},{2,18},{10... | collective-permute-start | bytes 196616 | tf_op jit(solution)/shard_map/ppermute | solution.py:35
  61.5 2.6 %copy-start.3 = (bf16[1024,1024]{1,0:T(8,128)(2,1)S(1)}, bf16[1024,1024]{1,0:T(8,128)(2,1)}, u32[]{:S(2)}) copy-start(bf16[1024,1024]{1,0:T(8,128)(2,1)} %param.13) | copy-start | bytes 6291460
  70.4 3.9 %copy-start.14 = (f32[2,2,2,2,2,1,1024]{6,5,4,3,2,1,0:T(1,128)}, f32[2,2,2,2,2,1,1024]{6,5,4,3,2,1,0:T(1,128)S(1)}, u32[]{:S(2)}) copy-start(f32[2,2,2,2,2,1,1024]{6,5,4,3,2,1,0:T(1,128)S(1)} %get-tuple-element.32) | copy-start | bytes 393220
  72.4 6.6 %copy-start.11 = (f32[320,1024]{1,0:T(8,128)S(1)}, f32[320,1024]{1,0:T(8,128)}, u32[]{:S(2)}) copy-start(f32[320,1024]{1,0:T(8,128)} %fusion.4) | copy-start | bytes 3932164
  75.0 12.7 %collective-permute-start.8 = (bf16[120,1024]{1,0:T(8,128)(2,1)}, bf16[120,1024]{1,0:T(8,128)(2,1)}, u32[]{:S(2)}, u32[]{:S(2)}) collective-permute-start(bf16[120,1024]{1,0:T(8,128)(2,1)} %get-tuple-element.28), channel_id=1, source_target_pairs={{1,2},{3,4},{5,6},{2,1},{4,3},{6,5},{9,10},{11,12},{13,14},{10,9},... | collective-permute-start | bytes 737288 | tf_op jit(solution)/shard_map/ppermute | solution.py:47
  76.4 5.6 %collective-permute-start.7 = (bf16[184,1024]{1,0:T(8,128)(2,1)S(1)}, bf16[184,1024]{1,0:T(8,128)(2,1)S(1)}, u32[]{:S(2)}, u32[]{:S(2)}) collective-permute-start(bf16[184,1024]{1,0:T(8,128)(2,1)S(1)} %pad_maximum_fusion.1), channel_id=1, source_target_pairs={{0,1},{1,0},{2,3},{3,2},{4,5},{5,4},{6,7},{7,6},{8,9},{9,8},{10,11... | collective-permute-start | bytes 1130504 | tf_op jit(solution)/shard_map/ppermute | solution.py:45
  80.9 6.7 %copy-start.8 = (f32[320,1024]{1,0:T(8,128)}, f32[320,1024]{1,0:T(8,128)S(1)}, u32[]{:S(2)}) copy-start(f32[320,1024]{1,0:T(8,128)S(1)} %convolution_add_fusion) | copy-start | bytes 3932164
  81.9 0.8 copy-start.17
  86.2 0.7 copy-start.12
  87.7 3.0 %copy-start.9 = (f32[96,1024]{1,0:T(8,128)S(1)}, f32[96,1024]{1,0:T(8,128)}, u32[]{:S(2)}) copy-start(f32[96,1024]{1,0:T(8,128)} %get-tuple-element.21) | copy-start | bytes 1179652
  87.7 3.0 %copy-start.10 = (f32[96,1024]{1,0:T(8,128)S(1)}, f32[96,1024]{1,0:T(8,128)}, u32[]{:S(2)}) copy-start(f32[96,1024]{1,0:T(8,128)} %get-tuple-element.22) | copy-start | bytes 1179652
  90.7 3.1 %copy-start.6 = (bf16[1024,1024]{1,0:T(8,128)(2,1)S(1)}, bf16[1024,1024]{1,0:T(8,128)(2,1)}, u32[]{:S(2)}) copy-start(bf16[1024,1024]{1,0:T(8,128)(2,1)} %param.15) | copy-start | bytes 6291460
  90.7 3.1 %copy-start.21 = (bf16[128,1024]{1,0:T(8,128)(2,1)S(1)}, bf16[128,1024]{1,0:T(8,128)(2,1)}, u32[]{:S(2)}) copy-start(bf16[128,1024]{1,0:T(8,128)(2,1)} %get-tuple-element.6) | copy-start | bytes 786436
  91.6 9.9 %copy-start.13 = (f32[2,2,2,2,2,1024]{5,0,1,3,4,2:T(2,128)S(1)}, f32[2,2,2,2,2,1024]{5,0,1,3,4,2:T(2,128)}, u32[]{:S(2)}) copy-start(f32[2,2,2,2,2,1024]{5,0,1,3,4,2:T(2,128)} %copy-done.12) | copy-start | bytes 393220
  91.6 10.5 %copy-start.15 = (bf16[6,16,1024]{2,1,0:T(8,128)(2,1)S(1)}, bf16[6,16,1024]{2,1,0:T(8,128)(2,1)}, u32[]{:S(2)}) copy-start(bf16[6,16,1024]{2,1,0:T(8,128)(2,1)} %get-tuple-element.11) | copy-start | bytes 589828
  91.6 10.5 %copy-start.16 = (bf16[6,16,1024]{2,1,0:T(8,128)(2,1)S(1)}, bf16[6,16,1024]{2,1,0:T(8,128)(2,1)}, u32[]{:S(2)}) copy-start(bf16[6,16,1024]{2,1,0:T(8,128)(2,1)} %get-tuple-element.12) | copy-start | bytes 589828
  92.5 8.3 %collective-permute-start.9 = (bf16[128,1024]{1,0:T(8,128)(2,1)S(1)}, bf16[128,1024]{1,0:T(8,128)(2,1)S(1)}, u32[]{:S(2)}, u32[]{:S(2)}) collective-permute-start(bf16[128,1024]{1,0:T(8,128)(2,1)S(1)} %pad_maximum_fusion.3), channel_id=1, source_target_pairs={{0,8},{8,0},{16,24},{24,16},{1,9},{9,1},{17,25},{25,17},{2,10},{10... | collective-permute-start | bytes 786440 | tf_op jit(solution)/shard_map/ppermute | solution.py:45
  100.8 0.7 copy-start.22
  101.6 4.0 %collective-permute-start.10 = (f32[2,2,2,1024]{3,0,1,2:T(2,128)S(1)}, f32[2,2,2,1024]{3,0,1,2:T(2,128)S(1)}, u32[]{:S(2)}, u32[]{:S(2)}) collective-permute-start(f32[2,2,2,1024]{3,0,1,2:T(2,128)S(1)} %select_bitcast_fusion), channel_id=1, source_target_pairs={{0,2},{1,3},{2,0},{3,1},{4,6},{5,7},{6,4},{7,5},{8,10},{9,11},{10,... | collective-permute-start | bytes 98312 | tf_op jit(solution)/shard_map/ppermute | solution.py:35
  102.1 5.2 %collective-permute-start.13 = (bf16[96,1024]{1,0:T(8,128)(2,1)S(1)}, bf16[96,1024]{1,0:T(8,128)(2,1)S(1)}, u32[]{:S(2)}, u32[]{:S(2)}) collective-permute-start(bf16[96,1024]{1,0:T(8,128)(2,1)S(1)} %bitcast.98), channel_id=1, source_target_pairs={{8,16},{16,8},{9,17},{17,9},{10,18},{18,10},{11,19},{19,11},{12,20... | collective-permute-start | bytes 589832 | tf_op jit(solution)/shard_map/ppermute | solution.py:47
  105.7 4.7 %collective-permute-start.11 = (f32[2,2,1024]{2,0,1:T(2,128)S(1)}, f32[2,2,1024]{2,0,1:T(2,128)S(1)}, u32[]{:S(2)}, u32[]{:S(2)}) collective-permute-start(f32[2,2,1024]{2,0,1:T(2,128)S(1)} %select_bitcast_fusion.1), channel_id=1, source_target_pairs={{0,4},{1,5},{2,6},{3,7},{4,0},{5,1},{6,2},{7,3},{8,12},{9,13},{10,... | collective-permute-start | bytes 49160 | tf_op jit(solution)/shard_map/ppermute | solution.py:35
  108.3 7.9 %copy-start.4 = (bf16[1024,1024]{1,0:T(8,128)(2,1)S(1)}, bf16[1024,1024]{1,0:T(8,128)(2,1)}, u32[]{:S(2)}) copy-start(bf16[1024,1024]{1,0:T(8,128)(2,1)} %param.13) | copy-start | bytes 6291460
  110.4 4.3 %collective-permute-start.12 = (f32[2,1024]{1,0:T(2,128)S(1)}, f32[2,1024]{1,0:T(2,128)S(1)}, u32[]{:S(2)}, u32[]{:S(2)}) collective-permute-start(f32[2,1024]{1,0:T(2,128)S(1)} %select_bitcast_fusion.2), channel_id=1, source_target_pairs={{0,16},{8,24},{16,0},{24,8},{1,17},{9,25},{17,1},{25,9},{2,18},{10... | collective-permute-start | bytes 24584 | tf_op jit(solution)/shard_map/ppermute | solution.py:35
  115.5 1.3 %slice-start = ((f32[320,1024]{1,0:T(8,128)}), f32[128,1024]{1,0:T(8,128)S(1)}, s32[]{:S(2)}) async-start(f32[320,1024]{1,0:T(8,128)} %copy-done.8), calls=%async_computation | async-start | bytes 1048576 | tf_op jit(solution)/shard_map/slice | solution.py:341
  115.6 1.4 %copy-start.20 = (bf16[128,1024]{1,0:T(8,128)(2,1)S(1)}, bf16[128,1024]{1,0:T(8,128)(2,1)}, u32[]{:S(2)}) copy-start(bf16[128,1024]{1,0:T(8,128)(2,1)} %get-tuple-element.7) | copy-start | bytes 786436

commit v13 on v12

--- a/solution.py
+++ b/solution.py
@@ -75,15 +75,15 @@
     return jnp.where(high, upper, lower), jnp.where(high, lower, upper)
 
 
-def attention_kernel(
-    own, first, last, q_ref, ko_ref, kh_ref, kg_ref, vo_ref, vh_ref, vg_ref, g_ref, mask_ref,
-    o_ref, dq_ref, dkv_ref, wide_ref,
-):
+def attention_kernel(own, first, last, pieces, q_ref, *refs):
+    key_refs = refs[:pieces]
+    value_refs = refs[pieces : 2 * pieces]
+    g_ref, mask_ref, o_ref, dq_ref, dkv_ref, wide_ref = refs[2 * pieces :]
     head_size = q_ref.shape[1] // 2
     score_scale = 1.0 / math.sqrt(head_size)
     q = (q_ref[...] * score_scale).astype(q_ref.dtype)
-    k = jnp.concatenate([ko_ref[...], kh_ref[...], kg_ref[...]], axis=0)
-    v = jnp.concatenate([vo_ref[...], vh_ref[...], vg_ref[...]], axis=0)
+    k = jnp.concatenate([r[...] for r in key_refs], axis=0)
+    v = jnp.concatenate([r[...] for r in value_refs], axis=0)
     g = g_ref[...]
     keep = mask_ref[...] > 0
     lane_head = lax.broadcasted_iota(jnp.int32, q.shape, 1) // head_size
@@ -130,15 +130,14 @@
 
 def attention(queries, keys, values, global_keys, global_values, grad_attended, keep):
     tokens, model_width = queries.shape
-    first = keys[0].shape[0] + keys[1].shape[0]
+    first = sum(piece.shape[0] for piece in keys)
     last = first + global_keys.shape[0]
     key_count = last
     lanes = 2 * (model_width // HEADS)
     steps = model_width // lanes
     token_block = pl.BlockSpec((tokens, lanes), lambda i: (0, i))
     key_block = pl.BlockSpec((key_count, lanes), lambda i: (0, i))
-    own_block = pl.BlockSpec((keys[0].shape[0], lanes), lambda i: (0, i))
-    halo_block = pl.BlockSpec((keys[1].shape[0], lanes), lambda i: (0, i))
+    piece_blocks = [pl.BlockSpec((piece.shape[0], lanes), lambda i: (0, i)) for piece in keys]
     global_block = pl.BlockSpec((last - first, lanes), lambda i: (0, i))
     mask_block = pl.BlockSpec((tokens, key_count), lambda i: (0, 0))
     grads_block = pl.BlockSpec((2, key_count, lanes), lambda i: (0, 0, i))
@@ -149,19 +148,13 @@
         tokens * key_count + 2 * key_count * model_width
     )
     return pl.pallas_call(
-        functools.partial(attention_kernel, tokens, first, last),
+        functools.partial(attention_kernel, tokens, first, last, len(keys) + 1),
         grid=(steps,),
-        in_specs=[
-            token_block,
-            own_block,
-            halo_block,
-            global_block,
-            own_block,
-            halo_block,
-            global_block,
-            token_block,
-            mask_block,
-        ],
+        in_specs=[token_block]
+        + piece_blocks
+        + [global_block]
+        + piece_blocks
+        + [global_block, token_block, mask_block],
         out_specs=[token_block, token_block, grads_block, wide_block],
         out_shape=[
             jax.ShapeDtypeStruct((tokens, model_width), jnp.bfloat16),
@@ -253,21 +246,18 @@
         grad_out.reshape(-1, model_width), w_out.T, preferred_element_type=jnp.float32
     ).astype(jnp.bfloat16)
 
-    halo_features = jnp.concatenate(
-        [
-            from_above,
-            from_below,
-            from_left,
-            from_right,
-            jnp.zeros((key_count - used, model_width), features.dtype),
-        ],
+    band_features = jnp.concatenate([from_above, from_below], axis=0)
+    band_keys_kv = (
+        jnp.dot(band_features, w_key, preferred_element_type=jnp.float32).astype(jnp.bfloat16),
+        jnp.dot(band_features, w_value, preferred_element_type=jnp.float32).astype(jnp.bfloat16),
+    )
+    strip_features = jnp.concatenate(
+        [from_left, from_right, jnp.zeros((key_count - used, model_width), features.dtype)],
         axis=0,
     )
-    halo_keys = jnp.dot(halo_features, w_key, preferred_element_type=jnp.float32).astype(
-        jnp.bfloat16
-    )
-    halo_values = jnp.dot(halo_features, w_value, preferred_element_type=jnp.float32).astype(
-        jnp.bfloat16
+    strip_keys_kv = (
+        jnp.dot(strip_features, w_key, preferred_element_type=jnp.float32).astype(jnp.bfloat16),
+        jnp.dot(strip_features, w_value, preferred_element_type=jnp.float32).astype(jnp.bfloat16),
     )
 
     for position in order[2:]:
@@ -312,8 +302,8 @@
 
     attended, query_grads, rounded_grads, wide_grads = attention(
         queries,
-        (own_keys, halo_keys),
-        (own_values, halo_values),
+        (own_keys, band_keys_kv[0], strip_keys_kv[0]),
+        (own_values, band_keys_kv[1], strip_keys_kv[1]),
         global_keys,
         global_values,
         grad_attended,

time: 121 us -> 126 us (1.041)
  waiting for transfers between devices: 15.3 us -> 17.6 us
  local copies, waits for them, and re-layouts: 15.8 us -> 17.6 us
    ppermute x6, starting transfers between devices: 13.2 us -> 10.6 us  [partner(): return lax.ppermute(x, axis, [(i, i ^ 1 << bit) for i in range(size)])]
    dot_general x2 -> x4, matrix products: 5.54 us -> 7.6 us  [the longest x1 2.94 us: shards(): jnp.dot(band_features, w_key, preferred_element_type=jnp.float32)]
    unnamed x4 -> x0, other arithmetic: 1.64 us -> none
    gather x1, other arithmetic: 0.01 us -> 1.41 us  [shards(): jnp.take(gathered, jnp.asarray(gather_order(order, device_count)), axis=0)]
    select_n x2 -> x4, other arithmetic: 2.84 us -> 3.93 us  [exchange(): from_lower = jnp.where(even, got_second, got_first)]
    unnamed x62 -> x68, local copies, waits for them, and re-layouts: 3.3 us -> 3.62 us
  transfers between devices with their start and end apart: 14 -> 14, of which waited for: 6 -> 7; matrix products, arithmetic and copies ran while one was open for 23% -> 23% of each run, Pallas kernels for 0% -> 0%
where the time goes in v13:
time: 126 us; the launch traced here: 125 us
  matrix products  29.1 us (23%)
  starting transfers between devices  25.3 us (20%)
  local copies, waits for them, and re-layouts  17.6 us (14%)
  waiting for transfers between devices  17.6 us (14%)
  Pallas kernels  15.9 us (13%)
  other arithmetic  15.7 us (12%)
  between operations  3.88 us (3%)
    pallas_call x1, Pallas kernels, attention(): pl.pallas_call(functools.partial(attention_kernel, tokens, first, last, l...  15.9 us
    ppermute x4, starting transfers between devices, exchange(): got_first = lax.ppermute(first, axis, [(i, i ^ 1) for i in range(size)])  10.7 us
    ppermute x6, waiting for transfers between devices, partner(): return lax.ppermute(x, axis, [(i, i ^ 1 << bit) for i in range(size)])  10.6 us
    ppermute x6, starting transfers between devices, partner(): return lax.ppermute(x, axis, [(i, i ^ 1 << bit) for i in range(size)])  10.6 us
    ppermute x4, waiting for transfers between devices, exchange(): got_first = lax.ppermute(first, axis, [(i, i ^ 1) for i in range(size)])  6.99 us
    dot_general x2, matrix products, contribution(): jnp.dot(rounded_grads[0, lo:hi], w_key.T, preferred_element_type=jnp.floa...  5.74 us
    ppermute x4, starting transfers between devices, exchange(): got_second = lax.ppermute(jnp.where(even, to_lower, to_higher), axis, links)  4.04 us
    select_n x4, other arithmetic, exchange(): from_lower = jnp.where(even, got_second, got_first)  3.93 us
  transfers between devices with their start and end apart: 14, of which 7 were waited for; matrix products, arithmetic and copies ran while one was open for 23% of the time, Pallas kernels for 0%

profile of v13, /device:TPU:0, one launch (start us, length us, event | category | flops | bytes accessed | tf_op | source)
XLA Modules:
  0.0 125.0 jit_solution(7264525995214667721)
XLA Ops:
  0.7 1.9 %broadcast_select_fusion.10 = (bf16[6,16,1024]{2,1,0:T(8,128)(2,1)S(1)}, bf16[6,16,1024]{2,1,0:T(8,128)(2,1)}) fusion(pred[]{:T(512)S(6)} %eq.68, bf16[8,16,1024]{2,1,0:T(8,128)(2,1)} %param.11), kind=kLoop, calls=%fused_computation.51 | loop fusion | flops 196608 | bytes 786433 | tf_op jit(solution)/shard_map/jit(_where)/select_n | solution.py:41
  2.6 1.3 %collective-permute-start = (bf16[96,1024]{1,0:T(8,128)(2,1)}, bf16[96,1024]{1,0:T(8,128)(2,1)}, u32[]{:S(2)}, u32[]{:S(2)}) collective-permute-start(bf16[96,1024]{1,0:T(8,128)(2,1)} %bitcast.1), channel_id=1, source_target_pairs={{8,16},{16,8},{9,17},{17,9},{10,18},{18,10},{11,19},{19,11},{12,20... | collective-permute-start | bytes 589832 | tf_op jit(solution)/shard_map/ppermute | solution.py:47
  3.9 1.2 dynamic_slice.13
  7.8 1.5 %convolution_convert_fusion.6.refs_4_ = bf16[128,1024]{1,0:T(8,128)(2,1)S(1)} fusion(bf16[128,1024]{1,0:T(8,128)(2,1)} %bitcast.83, bf16[1024,1024]{1,0:T(8,128)(2,1)S(1)} %copy-done), kind=kOutput, calls=%fused_computation.13 | convolution fusion | flops 268566528 | bytes 2621440 | tf_op jit(solution)/shard_map/dot_general | solution.py:205
  11.9 5.1 %collective-permute-start.1 = (bf16[98,1024]{1,0:T(8,128)(2,1)S(1)}, bf16[98,1024]{1,0:T(8,128)(2,1)}, u32[]{:S(2)}, u32[]{:S(2)}) collective-permute-start(bf16[98,1024]{1,0:T(8,128)(2,1)S(1)} %pad_maximum_fusion.7), channel_id=1, source_target_pairs={{0,8},{8,0},{16,24},{24,16},{1,9},{9,1},{17,25},{25,17},{2,10},{10... | collective-permute-start | bytes 602120 | tf_op jit(solution)/shard_map/ppermute | solution.py:45
  17.2 1.4 %pad_clamp_fusion = s32[1024]{0:T(1024)} fusion(s32[32]{0:T(128)} %constant.157), kind=kLoop, calls=%fused_computation.83 | loop fusion | flops 1024 | bytes 4224 | tf_op jit(solution)/shard_map/jit(_take)/gather | solution.py:265
  18.6 2.8 %convolution_convert_fusion.8.q_ref = bf16[128,1024]{1,0:T(8,128)(2,1)} fusion(bf16[128,1024]{1,0:T(8,128)(2,1)S(1)} %bitcast.85, bf16[1024,1024]{1,0:T(8,128)(2,1)} %param.12), kind=kOutput, calls=%fused_computation.15 | convolution fusion | flops 268566528 | bytes 2621440 | tf_op jit(solution)/shard_map/dot_general | solution.py:244
  22.1 1.5 %convolution_convert_fusion.5.refs_8_ = bf16[128,1024]{1,0:T(8,128)(2,1)} fusion(bf16[128,1024]{1,0:T(8,128)(2,1)S(1)} %bitcast.96, bf16[1024,1024]{1,0:T(8,128)(2,1)S(1)} %copy-done.5), kind=kOutput, calls=%fused_computation.12 | convolution fusion | flops 268566528 | bytes 2621440 | tf_op jit(solution)/shard_map/dot_general | solution.py:245
  23.7 0.9 or_convert_fusion.refs_9_
  25.4 1.1 broadcast_select_fusion.15
  26.5 1.3 %convolution_convert_fusion.2.refs_5_ = bf16[192,1024]{1,0:T(8,128)(2,1)} fusion(bf16[1024,1024]{1,0:T(8,128)(2,1)S(1)} %copy-done, bf16[96,1024]{1,0:T(8,128)(2,1)S(1)} %get-tuple-element.30, bf16[96,1024]{1,0:T(8,128)(2,1)S(1)} %get-tuple-element.29), kind=kOutput, calls=%fused_computation.6 | convolution fusion | flops 403636224 | bytes 2883584 | tf_op jit(solution)/shard_map/dot_general | solution.py:252
  29.6 3.0 %collective-permute-start.3 = (bf16[124,1024]{1,0:T(8,128)(2,1)S(1)}, bf16[124,1024]{1,0:T(8,128)(2,1)S(1)}, u32[]{:S(2)}, u32[]{:S(2)}) collective-permute-start(bf16[124,1024]{1,0:T(8,128)(2,1)S(1)} %pad_maximum_fusion.3), channel_id=1, source_target_pairs={{0,1},{1,0},{2,3},{3,2},{4,5},{5,4},{6,7},{7,6},{8,9},{9,8},{10,11... | collective-permute-start | bytes 761864 | tf_op jit(solution)/shard_map/ppermute | solution.py:45
  32.6 2.9 %convolution_convert_fusion.3.refs_1_ = bf16[192,1024]{1,0:T(8,128)(2,1)} fusion(bf16[1024,1024]{1,0:T(8,128)(2,1)} %param.13, bf16[96,1024]{1,0:T(8,128)(2,1)S(1)} %get-tuple-element.30, bf16[96,1024]{1,0:T(8,128)(2,1)S(1)} %get-tuple-element.29), kind=kOutput, calls=%fused_computation.7 | convolution fusion | flops 403636224 | bytes 2883584 | tf_op jit(solution)/shard_map/dot_general | solution.py:251
  35.6 1.6 %collective-permute-start.4 = (bf16[4,2048]{1,0:T(4,128)(2,1)S(1)}, bf16[4,2048]{1,0:T(4,128)(2,1)S(1)}, u32[]{:S(2)}, u32[]{:S(2)}) collective-permute-start(bf16[4,2048]{1,0:T(4,128)(2,1)S(1)} %maximum_select_fusion.3), channel_id=1, source_target_pairs={{0,2},{1,3},{2,0},{3,1},{4,6},{5,7},{6,4},{7,5},{8,10},{9,11},{10,... | collective-permute-start | bytes 49160 | tf_op jit(solution)/shard_map/ppermute | solution.py:35
  37.3 2.1 %collective-permute-done.4 = bf16[4,2048]{1,0:T(4,128)(2,1)S(1)} collective-permute-done((bf16[4,2048]{1,0:T(4,128)(2,1)S(1)}, bf16[4,2048]{1,0:T(4,128)(2,1)S(1)}, u32[]{:S(2)}, u32[]{:S(2)}) %collective-permute-start.4) | collective-permute-done | bytes 16416 | tf_op jit(solution)/shard_map/ppermute | solution.py:35
  39.4 2.7 %collective-permute-start.5 = (bf16[8,2048]{1,0:T(8,128)(2,1)S(1)}, bf16[8,2048]{1,0:T(8,128)(2,1)S(1)}, u32[]{:S(2)}, u32[]{:S(2)}) collective-permute-start(bf16[8,2048]{1,0:T(8,128)(2,1)S(1)} %maximum_select_fusion.2), channel_id=1, source_target_pairs={{0,4},{1,5},{2,6},{3,7},{4,0},{5,1},{6,2},{7,3},{8,12},{9,13},{10,... | collective-permute-start | bytes 98312 | tf_op jit(solution)/shard_map/ppermute | solution.py:35
  42.1 1.7 %convolution_convert_fusion.refs_6_ = bf16[288,1024]{1,0:T(8,128)(2,1)} fusion(bf16[1024,1024]{1,0:T(8,128)(2,1)S(1)} %copy-done, bf16[120,1024]{1,0:T(8,128)(2,1)S(1)} %get-tuple-element.24, bf16[120,1024]{1,0:T(8,128)(2,1)S(1)} %get-tuple-element.23, bf16[288]{0:T(512)(128)(2,1)S(1)} %copy-done.32), kind=kOutput, calls=%fused_computation.3 | convolution fusion | flops 606044160 | bytes 3179072 | tf_op jit(solution)/shard_map/dot_general | solution.py:260
  44.5 1.7 %convolution_convert_fusion.1.refs_2_ = bf16[288,1024]{1,0:T(8,128)(2,1)} fusion(bf16[1024,1024]{1,0:T(8,128)(2,1)S(1)} %copy-done.2, bf16[120,1024]{1,0:T(8,128)(2,1)S(1)} %get-tuple-element.24, bf16[120,1024]{1,0:T(8,128)(2,1)S(1)} %get-tuple-element.23, bf16[288]{0:T(512)(128)(2,1)S(1)} %copy-done.32), kind=kOutput, calls=%fused_computation.4 | convolution fusion | flops 606044160 | bytes 3179072 | tf_op jit(solution)/shard_map/dot_general | solution.py:259
  46.1 2.5 %collective-permute-done.6 = bf16[16,2048]{1,0:T(8,128)(2,1)S(1)} collective-permute-done((bf16[16,2048]{1,0:T(8,128)(2,1)S(1)}, bf16[16,2048]{1,0:T(8,128)(2,1)S(1)}, u32[]{:S(2)}, u32[]{:S(2)}) %collective-permute-start.6) | collective-permute-done | bytes 65568 | tf_op jit(solution)/shard_map/ppermute | solution.py:35
  50.2 15.9 %shard_map.122 = (bf16[128,1024]{1,0:T(8,128)(2,1)}, bf16[128,1024]{1,0:T(8,128)(2,1)}, bf16[2,640,1024]{2,1,0:T(8,128)(2,1)}, f32[2,160,1024]{2,1,0:T(8,128)}) custom-call(bf16[128,1024]{1,0:T(8,128)(2,1)} %convolution_convert_fusion.8.q_ref, bf16[128,1024]{1,0:T(8,128)(2,1)} %copy-done.19, bf16[192,1024]{1,0:T(8,128)(2,1)} %convolution_convert_fusion.3.refs_1_, ...), custom_call_target="tpu_custom_call" | custom-call | flops 2013265920 | bytes 8978432 | tf_op jit(solution)/shard_map/pallas_call | solution.py:150
  66.1 2.6 %fusion.9 = f32[240,1024]{1,0:T(8,128)S(1)} fusion(bf16[1024,1024]{1,0:T(8,128)(2,1)} %param.13, bf16[2,640,1024]{2,1,0:T(8,128)(2,1)} %get-tuple-element.8), kind=kOutput, calls=%fused_computation.25 | convolution fusion | flops 503316480 | bytes 3571712 | tf_op jit(solution)/shard_map/dot_general | solution.py:321
  68.7 3.1 %fusion.4 = f32[320,1024]{1,0:T(8,128)} fusion(bf16[1024,1024]{1,0:T(8,128)(2,1)S(1)} %copy-done.3, bf16[2,640,1024]{2,1,0:T(8,128)(2,1)} %get-tuple-element.8), kind=kOutput, calls=%fused_computation.18 | convolution fusion | flops 671088640 | bytes 4063232 | tf_op jit(solution)/shard_map/dot_general | solution.py:321
  71.9 1.0 slice.144
  72.8 0.8 reshape.188
  73.7 1.3 %fusion.26 = (f32[2,2,2,2,2,1,1024]{6,5,4,3,2,1,0:T(1,128)S(1)}, f32[2,2,2,2,2,1,1024]{6,5,4,3,2,1,0:T(1,128)S(1)}) fusion(f32[2,2,2,2,2,2,1024]{6,5,4,3,2,1,0:T(2,128)} %reshape.188), kind=kLoop, calls=%fused_computation.97 | loop fusion | bytes 524288 | tf_op jit(solution)/shard_map/slice | solution.py:73
  75.9 1.0 select_n.354
  76.9 1.9 %fusion = bf16[240,1024]{1,0:T(8,128)(2,1)S(1)} fusion(f32[240,1024]{1,0:T(8,128)S(1)} %fusion.9, bf16[1024,1024]{1,0:T(8,128)(2,1)S(1)} %copy-done, bf16[2,640,1024]{2,1,0:T(8,128)(2,1)} %get-tuple-element.8), kind=kOutput, calls=%fused_computation.5 | convolution fusion | flops 503808000 | bytes 4063232 | tf_op jit(solution)/shard_map/dot_general | solution.py:323
  79.6 1.4 %collective-permute-start.8 = (bf16[120,1024]{1,0:T(8,128)(2,1)}, bf16[120,1024]{1,0:T(8,128)(2,1)}, u32[]{:S(2)}, u32[]{:S(2)}) collective-permute-start(bf16[120,1024]{1,0:T(8,128)(2,1)} %get-tuple-element.26), channel_id=1, source_target_pairs={{1,2},{3,4},{5,6},{2,1},{4,3},{6,5},{9,10},{11,12},{13,14},{10,9},... | collective-permute-start | bytes 737288 | tf_op jit(solution)/shard_map/ppermute | solution.py:47
  81.0 2.5 %collective-permute-start.7 = (bf16[184,1024]{1,0:T(8,128)(2,1)S(1)}, bf16[184,1024]{1,0:T(8,128)(2,1)S(1)}, u32[]{:S(2)}, u32[]{:S(2)}) collective-permute-start(bf16[184,1024]{1,0:T(8,128)(2,1)S(1)} %pad_maximum_fusion.2), channel_id=1, source_target_pairs={{0,1},{1,0},{2,3},{3,2},{4,5},{5,4},{6,7},{7,6},{8,9},{9,8},{10,11... | collective-permute-start | bytes 1130504 | tf_op jit(solution)/shard_map/ppermute | solution.py:45
  83.4 2.0 %convolution_add_fusion = f32[320,1024]{1,0:T(8,128)S(1)} fusion(f32[320,1024]{1,0:T(8,128)S(1)} %copy-done.11, bf16[1024,1024]{1,0:T(8,128)(2,1)S(1)} %copy-done, bf16[2,640,1024]{2,1,0:T(8,128)(2,1)} %get-tuple-element.8), kind=kOutput, calls=%fused_computation.1 | convolution fusion | flops 671416320 | bytes 5373952 | tf_op jit(solution)/shard_map/dot_general | solution.py:323
  85.4 1.0 fusion.25
  87.9 1.6 %reshape.189 = f32[2,2,2,2,2,1024]{5,4,3,2,1,0:T(2,128)} reshape(f32[32,1024]{1,0:T(8,128)} %convert_add_fusion.1) | data formatting | bytes 262144 | tf_op jit(solution)/shard_map/reshape | solution.py:347
  89.5 1.2 bitcast_add_fusion
  92.2 1.9 %broadcast_select_fusion.3 = (bf16[120,1024]{1,0:T(8,128)(2,1)S(1)}, bf16[120,1024]{1,0:T(8,128)(2,1)}) fusion(bf16[120,1024]{1,0:T(8,128)(2,1)} %collective-permute-done.8, pred[]{:T(512)S(6)} %eq.69, bf16[184,1024]{1,0:T(8,128)(2,1)} %copy-done.17), kind=kLoop, calls=%fused_computation.43 | loop fusion | flops 245760 | bytes 983041 | tf_op jit(solution)/shard_map/jit(_where)/select_n | solution.py:52
  94.1 1.0 reshape.192
  95.2 0.9 broadcast_select_fusion.9
  96.1 0.8 pad_maximum_fusion.4
  97.1 1.2 convolution_convert_fusion.4
  98.3 7.0 %collective-permute-done.9 = bf16[128,1024]{1,0:T(8,128)(2,1)S(1)} collective-permute-done((bf16[128,1024]{1,0:T(8,128)(2,1)S(1)}, bf16[128,1024]{1,0:T(8,128)(2,1)S(1)}, u32[]{:S(2)}, u32[]{:S(2)}) %collective-permute-start.9) | collective-permute-done | bytes 262176 | tf_op jit(solution)/shard_map/ppermute | solution.py:45
  106.1 1.6 %collective-permute-start.10 = (f32[2,2,2,1024]{3,0,1,2:T(2,128)S(1)}, f32[2,2,2,1024]{3,0,1,2:T(2,128)S(1)}, u32[]{:S(2)}, u32[]{:S(2)}) collective-permute-start(f32[2,2,2,1024]{3,0,1,2:T(2,128)S(1)} %select_bitcast_fusion), channel_id=1, source_target_pairs={{0,2},{1,3},{2,0},{3,1},{4,6},{5,7},{6,4},{7,5},{8,10},{9,11},{10,... | collective-permute-start | bytes 98312 | tf_op jit(solution)/shard_map/ppermute | solution.py:35
  108.5 1.6 %collective-permute-done.10 = f32[2,2,2,1024]{3,0,1,2:T(2,128)S(1)} collective-permute-done((f32[2,2,2,1024]{3,0,1,2:T(2,128)S(1)}, f32[2,2,2,1024]{3,0,1,2:T(2,128)S(1)}, u32[]{:S(2)}, u32[]{:S(2)}) %collective-permute-start.10) | collective-permute-done | bytes 32800 | tf_op jit(solution)/shard_map/ppermute | solution.py:35
  110.2 1.5 %collective-permute-start.11 = (f32[2,2,1024]{2,0,1:T(2,128)S(1)}, f32[2,2,1024]{2,0,1:T(2,128)S(1)}, u32[]{:S(2)}, u32[]{:S(2)}) collective-permute-start(f32[2,2,1024]{2,0,1:T(2,128)S(1)} %select_bitcast_fusion.1), channel_id=1, source_target_pairs={{0,4},{1,5},{2,6},{3,7},{4,0},{5,1},{6,2},{7,3},{8,12},{9,13},{10,... | collective-permute-start | bytes 49160 | tf_op jit(solution)/shard_map/ppermute | solution.py:35
  111.7 1.0 broadcast_select_fusion.13
  112.7 2.2 %collective-permute-done.11 = f32[2,2,1024]{2,0,1:T(2,128)S(1)} collective-permute-done((f32[2,2,1024]{2,0,1:T(2,128)S(1)}, f32[2,2,1024]{2,0,1:T(2,128)S(1)}, u32[]{:S(2)}, u32[]{:S(2)}) %collective-permute-start.11) | collective-permute-done | bytes 16416 | tf_op jit(solution)/shard_map/ppermute | solution.py:35
  114.9 3.0 %collective-permute-start.12 = (f32[2,1024]{1,0:T(2,128)S(1)}, f32[2,1024]{1,0:T(2,128)S(1)}, u32[]{:S(2)}, u32[]{:S(2)}) collective-permute-start(f32[2,1024]{1,0:T(2,128)S(1)} %select_bitcast_fusion.2), channel_id=1, source_target_pairs={{0,16},{8,24},{16,0},{24,8},{1,17},{9,25},{17,1},{25,9},{2,18},{10... | collective-permute-start | bytes 24584 | tf_op jit(solution)/shard_map/ppermute | solution.py:35
  118.0 1.5 %collective-permute-done.12 = f32[2,1024]{1,0:T(2,128)S(1)} collective-permute-done((f32[2,1024]{1,0:T(2,128)S(1)}, f32[2,1024]{1,0:T(2,128)S(1)}, u32[]{:S(2)}, u32[]{:S(2)}) %collective-permute-start.12) | collective-permute-done | bytes 8224 | tf_op jit(solution)/shard_map/ppermute | solution.py:35
  119.5 0.9 add_convert_fusion
  121.9 3.1 %fusion.2 = bf16[128,1024]{1,0:T(8,128)(2,1)} fusion(f32[128,1024]{1,0:T(8,128)S(1)} %bitcast.86, f32[128,1024]{1,0:T(8,128)S(1)} %dynamic_update_slice.3, bf16[128,1024]{1,0:T(8,128)(2,1)S(1)} %copy-done.20, bf16[1024,1024]{1,0:T(8,128)(2,1)} %param.12), kind=kOutput, calls=%fused_computation.10 | convolution fusion | flops 268828672 | bytes 3670016 | tf_op jit(solution)/shard_map/dot_general | solution.py:388
  (137 shorter events, 16.2 us)
Async XLA Ops:
  0.6 7.1 %copy-start = (bf16[1024,1024]{1,0:T(8,128)(2,1)S(1)}, bf16[1024,1024]{1,0:T(8,128)(2,1)}, u32[]{:S(2)}) copy-start(bf16[1024,1024]{1,0:T(8,128)(2,1)} %param.14) | copy-start | bytes 6291460
  0.6 8.7 %copy-start.7 = (bf16[8,16,1024]{2,1,0:T(8,128)(2,1)S(1)}, bf16[8,16,1024]{2,1,0:T(8,128)(2,1)}, u32[]{:S(2)}) copy-start(bf16[8,16,1024]{2,1,0:T(8,128)(2,1)} %param.11) | copy-start | bytes 786436
  2.6 22.9 %collective-permute-start = (bf16[96,1024]{1,0:T(8,128)(2,1)}, bf16[96,1024]{1,0:T(8,128)(2,1)}, u32[]{:S(2)}, u32[]{:S(2)}) collective-permute-start(bf16[96,1024]{1,0:T(8,128)(2,1)} %bitcast.1), channel_id=1, source_target_pairs={{8,16},{16,8},{9,17},{17,9},{10,18},{18,10},{11,19},{19,11},{12,20... | collective-permute-start | bytes 589832 | tf_op jit(solution)/shard_map/ppermute | solution.py:47
  7.8 1.7 %copy-start.1 = (bf16[1024,1024]{1,0:T(8,128)(2,1)S(1)}, bf16[1024,1024]{1,0:T(8,128)(2,1)}, u32[]{:S(2)}) copy-start(bf16[1024,1024]{1,0:T(8,128)(2,1)} %param.13) | copy-start | bytes 6291460
  9.4 12.0 %copy-start.18 = (bf16[128,1024]{1,0:T(8,128)(2,1)}, bf16[128,1024]{1,0:T(8,128)(2,1)S(1)}, u32[]{:S(2)}) copy-start(bf16[128,1024]{1,0:T(8,128)(2,1)S(1)} %convolution_convert_fusion.6.refs_4_) | copy-start | bytes 786436
  9.9 13.7 %copy-start.19 = (bf16[128,1024]{1,0:T(8,128)(2,1)}, bf16[128,1024]{1,0:T(8,128)(2,1)S(1)}, u32[]{:S(2)}) copy-start(bf16[128,1024]{1,0:T(8,128)(2,1)S(1)} %convolution_convert_fusion.7.refs_0_) | copy-start | bytes 786436
  9.9 12.2 %copy-start.21 = (bf16[8,16,1024]{2,1,0:T(8,128)(2,1)S(1)}, bf16[8,16,1024]{2,1,0:T(8,128)(2,1)}, u32[]{:S(2)}) copy-start(bf16[8,16,1024]{2,1,0:T(8,128)(2,1)} %param.17) | copy-start | bytes 786436
  9.9 0.6 copy-start.24
  10.0 0.6 copy-start.26
  11.9 12.7 %collective-permute-start.1 = (bf16[98,1024]{1,0:T(8,128)(2,1)S(1)}, bf16[98,1024]{1,0:T(8,128)(2,1)}, u32[]{:S(2)}, u32[]{:S(2)}) collective-permute-start(bf16[98,1024]{1,0:T(8,128)(2,1)S(1)} %pad_maximum_fusion.7), channel_id=1, source_target_pairs={{0,8},{8,0},{16,24},{24,16},{1,9},{9,1},{17,25},{25,17},{2,10},{10... | collective-permute-start | bytes 602120 | tf_op jit(solution)/shard_map/ppermute | solution.py:45
  17.2 4.9 %copy-start.5 = (bf16[1024,1024]{1,0:T(8,128)(2,1)S(1)}, bf16[1024,1024]{1,0:T(8,128)(2,1)}, u32[]{:S(2)}) copy-start(bf16[1024,1024]{1,0:T(8,128)(2,1)} %param.15) | copy-start | bytes 6291460
  18.6 5.0 %copy-start.28 = (s32[640]{0:T(1024)S(1)}, s32[640]{0:T(1024)}, u32[]{:S(2)}) copy-start(s32[640]{0:T(1024)} %constant.137.clone) | copy-start | bytes 7684
  18.6 5.0 %copy-start.29 = (s32[640]{0:T(1024)S(1)}, s32[640]{0:T(1024)}, u32[]{:S(2)}) copy-start(s32[640]{0:T(1024)} %constant.136.clone) | copy-start | bytes 7684
  18.6 5.1 %copy-start.30 = (pred[640]{0:T(1024)(128)(4,1)S(1)}, pred[640]{0:T(1024)(128)(4,1)}, u32[]{:S(2)}) copy-start(pred[640]{0:T(1024)(128)(4,1)} %constant.155) | copy-start | bytes 1924
  18.6 5.1 %copy-start.31 = (pred[640]{0:T(1024)(128)(4,1)S(1)}, pred[640]{0:T(1024)(128)(4,1)}, u32[]{:S(2)}) copy-start(pred[640]{0:T(1024)(128)(4,1)} %constant.154) | copy-start | bytes 1924
  21.4 3.9 %copy-start.25 = (bf16[1,1024]{1,0:T(2,128)(2,1)S(1)}, bf16[1,1024]{1,0:T(2,128)(2,1)}, u32[]{:S(2)}) copy-start(bf16[1,1024]{1,0:T(2,128)(2,1)} %copy-done.24) | copy-start | bytes 6148
  21.4 4.0 %copy-start.27 = (bf16[1,1024]{1,0:T(2,128)(2,1)S(1)}, bf16[1,1024]{1,0:T(2,128)(2,1)}, u32[]{:S(2)}) copy-start(bf16[1,1024]{1,0:T(2,128)(2,1)} %copy-done.26) | copy-start | bytes 6148
  28.9 8.4 %collective-permute-start.2 = (bf16[120,1024]{1,0:T(8,128)(2,1)}, bf16[120,1024]{1,0:T(8,128)(2,1)S(1)}, u32[]{:S(2)}, u32[]{:S(2)}) collective-permute-start(bf16[120,1024]{1,0:T(8,128)(2,1)} %select_n.321), channel_id=1, source_target_pairs={{1,2},{3,4},{5,6},{2,1},{4,3},{6,5},{9,10},{11,12},{13,14},{10,9},... | collective-permute-start | bytes 737288 | tf_op jit(solution)/shard_map/ppermute | solution.py:47
  29.6 12.5 %copy-start.32 = (bf16[288]{0:T(512)(128)(2,1)S(1)}, bf16[288]{0:T(512)(128)(2,1)}, u32[]{:S(2)}) copy-start(bf16[288]{0:T(512)(128)(2,1)} %pad.60.clone) | copy-start | bytes 1732
  29.6 5.9 %collective-permute-start.3 = (bf16[124,1024]{1,0:T(8,128)(2,1)S(1)}, bf16[124,1024]{1,0:T(8,128)(2,1)S(1)}, u32[]{:S(2)}, u32[]{:S(2)}) collective-permute-start(bf16[124,1024]{1,0:T(8,128)(2,1)S(1)} %pad_maximum_fusion.3), channel_id=1, source_target_pairs={{0,1},{1,0},{2,3},{3,2},{4,5},{5,4},{6,7},{7,6},{8,9},{9,8},{10,11... | collective-permute-start | bytes 761864 | tf_op jit(solution)/shard_map/ppermute | solution.py:45
  35.6 3.8 %collective-permute-start.4 = (bf16[4,2048]{1,0:T(4,128)(2,1)S(1)}, bf16[4,2048]{1,0:T(4,128)(2,1)S(1)}, u32[]{:S(2)}, u32[]{:S(2)}) collective-permute-start(bf16[4,2048]{1,0:T(4,128)(2,1)S(1)} %maximum_select_fusion.3), channel_id=1, source_target_pairs={{0,2},{1,3},{2,0},{3,1},{4,6},{5,7},{6,4},{7,5},{8,10},{9,11},{10,... | collective-permute-start | bytes 49160 | tf_op jit(solution)/shard_map/ppermute | solution.py:35
  39.4 4.9 %collective-permute-start.5 = (bf16[8,2048]{1,0:T(8,128)(2,1)S(1)}, bf16[8,2048]{1,0:T(8,128)(2,1)S(1)}, u32[]{:S(2)}, u32[]{:S(2)}) collective-permute-start(bf16[8,2048]{1,0:T(8,128)(2,1)S(1)} %maximum_select_fusion.2), channel_id=1, source_target_pairs={{0,4},{1,5},{2,6},{3,7},{4,0},{5,1},{6,2},{7,3},{8,12},{9,13},{10,... | collective-permute-start | bytes 98312 | tf_op jit(solution)/shard_map/ppermute | solution.py:35
  42.1 2.4 %copy-start.2 = (bf16[1024,1024]{1,0:T(8,128)(2,1)S(1)}, bf16[1024,1024]{1,0:T(8,128)(2,1)}, u32[]{:S(2)}) copy-start(bf16[1024,1024]{1,0:T(8,128)(2,1)} %param.13) | copy-start | bytes 6291460
  44.3 4.3 %collective-permute-start.6 = (bf16[16,2048]{1,0:T(8,128)(2,1)S(1)}, bf16[16,2048]{1,0:T(8,128)(2,1)S(1)}, u32[]{:S(2)}, u32[]{:S(2)}) collective-permute-start(bf16[16,2048]{1,0:T(8,128)(2,1)S(1)} %maximum_select_fusion.1), channel_id=1, source_target_pairs={{0,16},{8,24},{16,0},{24,8},{1,17},{9,25},{17,1},{25,9},{2,18},{10... | collective-permute-start | bytes 196616 | tf_op jit(solution)/shard_map/ppermute | solution.py:35
  66.1 2.6 %copy-start.3 = (bf16[1024,1024]{1,0:T(8,128)(2,1)S(1)}, bf16[1024,1024]{1,0:T(8,128)(2,1)}, u32[]{:S(2)}) copy-start(bf16[1024,1024]{1,0:T(8,128)(2,1)} %param.13) | copy-start | bytes 6291460
  75.0 3.9 %copy-start.14 = (f32[2,2,2,2,2,1,1024]{6,5,4,3,2,1,0:T(1,128)}, f32[2,2,2,2,2,1,1024]{6,5,4,3,2,1,0:T(1,128)S(1)}, u32[]{:S(2)}) copy-start(f32[2,2,2,2,2,1,1024]{6,5,4,3,2,1,0:T(1,128)S(1)} %get-tuple-element.32) | copy-start | bytes 393220
  76.9 6.5 %copy-start.11 = (f32[320,1024]{1,0:T(8,128)S(1)}, f32[320,1024]{1,0:T(8,128)}, u32[]{:S(2)}) copy-start(f32[320,1024]{1,0:T(8,128)} %fusion.4) | copy-start | bytes 3932164
  79.6 12.6 %collective-permute-start.8 = (bf16[120,1024]{1,0:T(8,128)(2,1)}, bf16[120,1024]{1,0:T(8,128)(2,1)}, u32[]{:S(2)}, u32[]{:S(2)}) collective-permute-start(bf16[120,1024]{1,0:T(8,128)(2,1)} %get-tuple-element.26), channel_id=1, source_target_pairs={{1,2},{3,4},{5,6},{2,1},{4,3},{6,5},{9,10},{11,12},{13,14},{10,9},... | collective-permute-start | bytes 737288 | tf_op jit(solution)/shard_map/ppermute | solution.py:47
  81.0 5.5 %collective-permute-start.7 = (bf16[184,1024]{1,0:T(8,128)(2,1)S(1)}, bf16[184,1024]{1,0:T(8,128)(2,1)S(1)}, u32[]{:S(2)}, u32[]{:S(2)}) collective-permute-start(bf16[184,1024]{1,0:T(8,128)(2,1)S(1)} %pad_maximum_fusion.2), channel_id=1, source_target_pairs={{0,1},{1,0},{2,3},{3,2},{4,5},{5,4},{6,7},{7,6},{8,9},{9,8},{10,11... | collective-permute-start | bytes 1130504 | tf_op jit(solution)/shard_map/ppermute | solution.py:45
  85.4 6.7 %copy-start.8 = (f32[320,1024]{1,0:T(8,128)}, f32[320,1024]{1,0:T(8,128)S(1)}, u32[]{:S(2)}) copy-start(f32[320,1024]{1,0:T(8,128)S(1)} %convolution_add_fusion) | copy-start | bytes 3932164
  86.5 0.7 copy-start.17
  90.7 0.6 copy-start.12
  92.2 3.0 %copy-start.9 = (f32[96,1024]{1,0:T(8,128)S(1)}, f32[96,1024]{1,0:T(8,128)}, u32[]{:S(2)}) copy-start(f32[96,1024]{1,0:T(8,128)} %get-tuple-element.17) | copy-start | bytes 1179652
  92.2 3.0 %copy-start.10 = (f32[96,1024]{1,0:T(8,128)S(1)}, f32[96,1024]{1,0:T(8,128)}, u32[]{:S(2)}) copy-start(f32[96,1024]{1,0:T(8,128)} %get-tuple-element.18) | copy-start | bytes 1179652
  95.2 2.0 %copy-start.6 = (bf16[1024,1024]{1,0:T(8,128)(2,1)S(1)}, bf16[1024,1024]{1,0:T(8,128)(2,1)}, u32[]{:S(2)}) copy-start(bf16[1024,1024]{1,0:T(8,128)(2,1)} %param.15) | copy-start | bytes 6291460
  95.2 2.0 %copy-start.22 = (bf16[128,1024]{1,0:T(8,128)(2,1)S(1)}, bf16[128,1024]{1,0:T(8,128)(2,1)}, u32[]{:S(2)}) copy-start(bf16[128,1024]{1,0:T(8,128)(2,1)} %get-tuple-element.6) | copy-start | bytes 786436
  96.1 9.9 %copy-start.13 = (f32[2,2,2,2,2,1024]{5,0,1,3,4,2:T(2,128)S(1)}, f32[2,2,2,2,2,1024]{5,0,1,3,4,2:T(2,128)}, u32[]{:S(2)}) copy-start(f32[2,2,2,2,2,1024]{5,0,1,3,4,2:T(2,128)} %copy-done.12) | copy-start | bytes 393220
  96.1 11.7 %copy-start.15 = (bf16[6,16,1024]{2,1,0:T(8,128)(2,1)S(1)}, bf16[6,16,1024]{2,1,0:T(8,128)(2,1)}, u32[]{:S(2)}) copy-start(bf16[6,16,1024]{2,1,0:T(8,128)(2,1)} %get-tuple-element.11) | copy-start | bytes 589828
  96.1 11.7 %copy-start.16 = (bf16[6,16,1024]{2,1,0:T(8,128)(2,1)S(1)}, bf16[6,16,1024]{2,1,0:T(8,128)(2,1)}, u32[]{:S(2)}) copy-start(bf16[6,16,1024]{2,1,0:T(8,128)(2,1)} %get-tuple-element.12) | copy-start | bytes 589828
  97.0 8.3 %collective-permute-start.9 = (bf16[128,1024]{1,0:T(8,128)(2,1)S(1)}, bf16[128,1024]{1,0:T(8,128)(2,1)S(1)}, u32[]{:S(2)}, u32[]{:S(2)}) collective-permute-start(bf16[128,1024]{1,0:T(8,128)(2,1)S(1)} %pad_maximum_fusion.4), channel_id=1, source_target_pairs={{0,8},{8,0},{16,24},{24,16},{1,9},{9,1},{17,25},{25,17},{2,10},{10... | collective-permute-start | bytes 786440 | tf_op jit(solution)/shard_map/ppermute | solution.py:45
  105.3 0.7 copy-start.23
  106.1 4.0 %collective-permute-start.10 = (f32[2,2,2,1024]{3,0,1,2:T(2,128)S(1)}, f32[2,2,2,1024]{3,0,1,2:T(2,128)S(1)}, u32[]{:S(2)}, u32[]{:S(2)}) collective-permute-start(f32[2,2,2,1024]{3,0,1,2:T(2,128)S(1)} %select_bitcast_fusion), channel_id=1, source_target_pairs={{0,2},{1,3},{2,0},{3,1},{4,6},{5,7},{6,4},{7,5},{8,10},{9,11},{10,... | collective-permute-start | bytes 98312 | tf_op jit(solution)/shard_map/ppermute | solution.py:35
  107.8 3.8 %collective-permute-start.13 = (bf16[96,1024]{1,0:T(8,128)(2,1)S(1)}, bf16[96,1024]{1,0:T(8,128)(2,1)S(1)}, u32[]{:S(2)}, u32[]{:S(2)}) collective-permute-start(bf16[96,1024]{1,0:T(8,128)(2,1)S(1)} %bitcast.98), channel_id=1, source_target_pairs={{8,16},{16,8},{9,17},{17,9},{10,18},{18,10},{11,19},{19,11},{12,20... | collective-permute-start | bytes 589832 | tf_op jit(solution)/shard_map/ppermute | solution.py:47
  110.2 4.7 %collective-permute-start.11 = (f32[2,2,1024]{2,0,1:T(2,128)S(1)}, f32[2,2,1024]{2,0,1:T(2,128)S(1)}, u32[]{:S(2)}, u32[]{:S(2)}) collective-permute-start(f32[2,2,1024]{2,0,1:T(2,128)S(1)} %select_bitcast_fusion.1), channel_id=1, source_target_pairs={{0,4},{1,5},{2,6},{3,7},{4,0},{5,1},{6,2},{7,3},{8,12},{9,13},{10,... | collective-permute-start | bytes 49160 | tf_op jit(solution)/shard_map/ppermute | solution.py:35
  112.6 8.4 %copy-start.4 = (bf16[1024,1024]{1,0:T(8,128)(2,1)S(1)}, bf16[1024,1024]{1,0:T(8,128)(2,1)}, u32[]{:S(2)}) copy-start(bf16[1024,1024]{1,0:T(8,128)(2,1)} %param.13) | copy-start | bytes 6291460
  114.9 4.6 %collective-permute-start.12 = (f32[2,1024]{1,0:T(2,128)S(1)}, f32[2,1024]{1,0:T(2,128)S(1)}, u32[]{:S(2)}, u32[]{:S(2)}) collective-permute-start(f32[2,1024]{1,0:T(2,128)S(1)} %select_bitcast_fusion.2), channel_id=1, source_target_pairs={{0,16},{8,24},{16,0},{24,8},{1,17},{9,25},{17,1},{25,9},{2,18},{10... | collective-permute-start | bytes 24584 | tf_op jit(solution)/shard_map/ppermute | solution.py:35
  120.4 1.3 %slice-start = ((f32[320,1024]{1,0:T(8,128)}), f32[128,1024]{1,0:T(8,128)S(1)}, s32[]{:S(2)}) async-start(f32[320,1024]{1,0:T(8,128)} %copy-done.8), calls=%async_computation | async-start | bytes 1048576 | tf_op jit(solution)/shard_map/slice | solution.py:331
  120.4 1.4 %copy-start.20 = (bf16[128,1024]{1,0:T(8,128)(2,1)S(1)}, bf16[128,1024]{1,0:T(8,128)(2,1)}, u32[]{:S(2)}) copy-start(bf16[128,1024]{1,0:T(8,128)(2,1)} %get-tuple-element.7) | copy-start | bytes 786436

commit v14 on v12

--- a/solution.py
+++ b/solution.py
@@ -76,10 +76,10 @@
 
 
 def attention_kernel(
-    own, first, last, q_ref, ko_ref, kh_ref, kg_ref, vo_ref, vh_ref, vg_ref, g_ref, mask_ref,
+    own, first, last, per_step, q_ref, ko_ref, kh_ref, kg_ref, vo_ref, vh_ref, vg_ref, g_ref, mask_ref,
     o_ref, dq_ref, dkv_ref, wide_ref,
 ):
-    head_size = q_ref.shape[1] // 2
+    head_size = q_ref.shape[1] // per_step
     score_scale = 1.0 / math.sqrt(head_size)
     q = (q_ref[...] * score_scale).astype(q_ref.dtype)
     k = jnp.concatenate([ko_ref[...], kh_ref[...], kg_ref[...]], axis=0)
@@ -93,7 +93,7 @@
     dq = jnp.zeros(q.shape, jnp.float32)
     dk = None
     dv = None
-    for head in range(2):
+    for head in range(per_step):
         mine = lane_head == head
         q_head = jnp.where(mine, q, jnp.zeros_like(q))
         g_head = jnp.where(mine, g, jnp.zeros_like(g))
@@ -133,7 +133,8 @@
     first = keys[0].shape[0] + keys[1].shape[0]
     last = first + global_keys.shape[0]
     key_count = last
-    lanes = 2 * (model_width // HEADS)
+    per_step = 4
+    lanes = per_step * (model_width // HEADS)
     steps = model_width // lanes
     token_block = pl.BlockSpec((tokens, lanes), lambda i: (0, i))
     key_block = pl.BlockSpec((key_count, lanes), lambda i: (0, i))
@@ -149,7 +150,7 @@
         tokens * key_count + 2 * key_count * model_width
     )
     return pl.pallas_call(
-        functools.partial(attention_kernel, tokens, first, last),
+        functools.partial(attention_kernel, tokens, first, last, per_step),
         grid=(steps,),
         in_specs=[
             token_block,

time: 121 us -> 123 us (1.017)
  Pallas kernels: 15.9 us -> 17.7 us
    pallas_call x1, Pallas kernels: 15.9 us -> 17.7 us  [attention(): pl.pallas_call(functools.partial(attention_kernel, tokens, first, last, p...]
where the time goes in v14:
time: 123 us; the launch traced here: 122 us
  matrix products  28.1 us (23%)
  starting transfers between devices  26.2 us (21%)
  Pallas kernels  17.7 us (14%)
  local copies, waits for them, and re-layouts  15.8 us (13%)
  waiting for transfers between devices  15.3 us (12%)
  other arithmetic  14.8 us (12%)
  between operations  4.04 us (3%)
    pallas_call x1, Pallas kernels, attention(): pl.pallas_call(functools.partial(attention_kernel, tokens, first, last, p...  17.7 us
    ppermute x6, starting transfers between devices, partner(): return lax.ppermute(x, axis, [(i, i ^ 1 << bit) for i in range(size)])  13.2 us
    ppermute x4, starting transfers between devices, exchange(): got_first = lax.ppermute(first, axis, [(i, i ^ 1) for i in range(size)])  9.62 us
    ppermute x6, waiting for transfers between devices, partner(): return lax.ppermute(x, axis, [(i, i ^ 1 << bit) for i in range(size)])  9.45 us
    ppermute x4, waiting for transfers between devices, exchange(): got_first = lax.ppermute(first, axis, [(i, i ^ 1) for i in range(size)])  5.83 us
    dot_general x2, matrix products, contribution(): jnp.dot(rounded_grads[0, lo:hi], w_key.T, preferred_element_type=jnp.floa...  5.73 us
    dot_general x2, matrix products, contribution(): jnp.dot(rounded_grads[1, lo:hi], w_value.T, preferred_element_type=jnp.fl...  3.84 us
    select_n x4, other arithmetic, exchange(): first = jnp.where(even, to_higher, to_lower)  3.61 us
  transfers between devices with their start and end apart: 14, of which 6 were waited for; matrix products, arithmetic and copies ran while one was open for 23% of the time, Pallas kernels for 0%

profile of v14, /device:TPU:0, one launch (start us, length us, event | category | flops | bytes accessed | tf_op | source)
XLA Modules:
  0.0 121.9 jit_solution(5541231410360832293)
XLA Ops:
  0.7 1.9 %broadcast_select_fusion.8 = (bf16[6,16,1024]{2,1,0:T(8,128)(2,1)S(1)}, bf16[6,16,1024]{2,1,0:T(8,128)(2,1)}) fusion(pred[]{:T(512)S(6)} %eq.68, bf16[8,16,1024]{2,1,0:T(8,128)(2,1)} %param.11), kind=kLoop, calls=%fused_computation.45 | loop fusion | flops 196608 | bytes 786433 | tf_op jit(solution)/shard_map/jit(_where)/select_n | solution.py:41
  3.2 1.2 %dynamic_slice.13 = s32[1]{0:T(128)} dynamic-slice(s32[32]{0:T(128)} %param.16, s32[]{:T(128)S(6)} %select_n.311), dynamic_slice_sizes={1} | dynamic-slice | bytes 12 | tf_op jit(solution)/shard_map/jit(dynamic_index_in_dim)/dynamic_slice | solution.py:218
  7.1 1.5 %convolution_convert_fusion.4.vo_ref = bf16[128,1024]{1,0:T(8,128)(2,1)S(1)} fusion(bf16[128,1024]{1,0:T(8,128)(2,1)} %bitcast.83, bf16[1024,1024]{1,0:T(8,128)(2,1)S(1)} %copy-done), kind=kOutput, calls=%fused_computation.11 | convolution fusion | flops 268566528 | bytes 2621440 | tf_op jit(solution)/shard_map/dot_general | solution.py:213
  10.0 5.7 %collective-permute-start.1 = (bf16[98,1024]{1,0:T(8,128)(2,1)}, bf16[98,1024]{1,0:T(8,128)(2,1)S(1)}, u32[]{:S(2)}, u32[]{:S(2)}) collective-permute-start(bf16[98,1024]{1,0:T(8,128)(2,1)} %pad_maximum_fusion.4), channel_id=1, source_target_pairs={{0,8},{8,0},{16,24},{24,16},{1,9},{9,1},{17,25},{25,17},{2,10},{10... | collective-permute-start | bytes 602120 | tf_op jit(solution)/shard_map/ppermute | solution.py:45
  15.9 2.9 %convolution_convert_fusion.6.q_ref = bf16[128,1024]{1,0:T(8,128)(2,1)} fusion(bf16[128,1024]{1,0:T(8,128)(2,1)S(1)} %bitcast.85, bf16[1024,1024]{1,0:T(8,128)(2,1)} %param.12), kind=kOutput, calls=%fused_computation.13 | convolution fusion | flops 268566528 | bytes 2621440 | tf_op jit(solution)/shard_map/dot_general | solution.py:252
  18.8 2.5 %convolution_convert_fusion.3.g_ref = bf16[128,1024]{1,0:T(8,128)(2,1)} fusion(bf16[128,1024]{1,0:T(8,128)(2,1)} %bitcast.96, bf16[1024,1024]{1,0:T(8,128)(2,1)S(1)} %copy-done.5), kind=kOutput, calls=%fused_computation.10 | convolution fusion | flops 268566528 | bytes 2621440 | tf_op jit(solution)/shard_map/dot_general | solution.py:253
  21.6 1.0 copy-done.23
  23.0 0.9 or_convert_fusion.mask_ref
  24.9 3.4 %collective-permute-start.4 = (bf16[4,2048]{1,0:T(4,128)(2,1)S(1)}, bf16[4,2048]{1,0:T(4,128)(2,1)S(1)}, u32[]{:S(2)}, u32[]{:S(2)}) collective-permute-start(bf16[4,2048]{1,0:T(4,128)(2,1)S(1)} %maximum_select_fusion.3), channel_id=1, source_target_pairs={{0,2},{1,3},{2,0},{3,1},{4,6},{5,7},{6,4},{7,5},{8,10},{9,11},{10,... | collective-permute-start | bytes 49160 | tf_op jit(solution)/shard_map/ppermute | solution.py:35
  28.3 0.8 select_dynamic-update-slice_fusion.1
  29.1 0.8 select_dynamic-update-slice_fusion
  30.4 2.1 %collective-permute-done.4 = bf16[4,2048]{1,0:T(4,128)(2,1)S(1)} collective-permute-done((bf16[4,2048]{1,0:T(4,128)(2,1)S(1)}, bf16[4,2048]{1,0:T(4,128)(2,1)S(1)}, u32[]{:S(2)}, u32[]{:S(2)}) %collective-permute-start.4) | collective-permute-done | bytes 16416 | tf_op jit(solution)/shard_map/ppermute | solution.py:35
  32.6 3.8 %collective-permute-start.5 = (bf16[8,2048]{1,0:T(8,128)(2,1)S(1)}, bf16[8,2048]{1,0:T(8,128)(2,1)S(1)}, u32[]{:S(2)}, u32[]{:S(2)}) collective-permute-start(bf16[8,2048]{1,0:T(8,128)(2,1)S(1)} %maximum_select_fusion.2), channel_id=1, source_target_pairs={{0,4},{1,5},{2,6},{3,7},{4,0},{5,1},{6,2},{7,3},{8,12},{9,13},{10,... | collective-permute-start | bytes 98312 | tf_op jit(solution)/shard_map/ppermute | solution.py:35
  36.4 3.4 %convolution_convert_fusion.vh_ref = bf16[480,1024]{1,0:T(8,128)(2,1)} fusion(bf16[480,1024]{1,0:T(8,128)(2,1)} %broadcast_dynamic-update-slice_fusion, bf16[1024,1024]{1,0:T(8,128)(2,1)S(1)} %copy-done), kind=kOutput, calls=%fused_computation.1 | convolution fusion | flops 1007124480 | bytes 4063232 | tf_op jit(solution)/shard_map/dot_general | solution.py:270
  39.8 1.3 %collective-permute-start.6 = (bf16[16,2048]{1,0:T(8,128)(2,1)S(1)}, bf16[16,2048]{1,0:T(8,128)(2,1)S(1)}, u32[]{:S(2)}, u32[]{:S(2)}) collective-permute-start(bf16[16,2048]{1,0:T(8,128)(2,1)S(1)} %maximum_select_fusion.1), channel_id=1, source_target_pairs={{0,16},{8,24},{16,0},{24,8},{1,17},{9,25},{17,1},{25,9},{2,18},{10... | collective-permute-start | bytes 196616 | tf_op jit(solution)/shard_map/ppermute | solution.py:35
  41.1 2.2 %convolution_convert_fusion.1.kh_ref = bf16[480,1024]{1,0:T(8,128)(2,1)} fusion(bf16[480,1024]{1,0:T(8,128)(2,1)S(1)} %copy-done.24, bf16[1024,1024]{1,0:T(8,128)(2,1)S(1)} %copy-done.2), kind=kOutput, calls=%fused_computation.2 | convolution fusion | flops 1007124480 | bytes 4063232 | tf_op jit(solution)/shard_map/dot_general | solution.py:267
  43.3 0.9 collective-permute-done.6
  45.6 17.7 %shard_map.122 = (bf16[128,1024]{1,0:T(8,128)(2,1)}, bf16[128,1024]{1,0:T(8,128)(2,1)}, bf16[2,640,1024]{2,1,0:T(8,128)(2,1)}, f32[2,160,1024]{2,1,0:T(8,128)}) custom-call(bf16[128,1024]{1,0:T(8,128)(2,1)} %convolution_convert_fusion.6.q_ref, bf16[128,1024]{1,0:T(8,128)(2,1)} %copy-done.19, bf16[480,1024]{1,0:T(8,128)(2,1)} %convolution_convert_fusion.1.kh_ref, ...), custom_call_target="tpu_custom_call" | custom-call | flops 2013265920 | bytes 8978432 | tf_op jit(solution)/shard_map/pallas_call | solution.py:152
  63.3 2.6 %fusion.9 = f32[240,1024]{1,0:T(8,128)S(1)} fusion(bf16[1024,1024]{1,0:T(8,128)(2,1)} %param.13, bf16[2,640,1024]{2,1,0:T(8,128)(2,1)} %get-tuple-element.8), kind=kOutput, calls=%fused_computation.22 | convolution fusion | flops 503316480 | bytes 3571712 | tf_op jit(solution)/shard_map/dot_general | solution.py:332
  66.0 3.1 %fusion.4 = f32[320,1024]{1,0:T(8,128)} fusion(bf16[1024,1024]{1,0:T(8,128)(2,1)S(1)} %copy-done.3, bf16[2,640,1024]{2,1,0:T(8,128)(2,1)} %get-tuple-element.8), kind=kOutput, calls=%fused_computation.16 | convolution fusion | flops 671088640 | bytes 4063232 | tf_op jit(solution)/shard_map/dot_general | solution.py:332
  69.1 1.0 slice.144
  70.0 0.8 reshape.188
  70.9 1.3 %fusion.20 = (f32[2,2,2,2,2,1,1024]{6,5,4,3,2,1,0:T(1,128)S(1)}, f32[2,2,2,2,2,1,1024]{6,5,4,3,2,1,0:T(1,128)S(1)}) fusion(f32[2,2,2,2,2,2,1024]{6,5,4,3,2,1,0:T(2,128)} %reshape.188), kind=kLoop, calls=%fused_computation.90 | loop fusion | bytes 524288 | tf_op jit(solution)/shard_map/slice | solution.py:73
  72.4 0.8 copy.17
  73.1 1.0 select_n.354
  74.2 1.9 %fusion = bf16[240,1024]{1,0:T(8,128)(2,1)S(1)} fusion(f32[240,1024]{1,0:T(8,128)S(1)} %fusion.9, bf16[1024,1024]{1,0:T(8,128)(2,1)S(1)} %copy-done, bf16[2,640,1024]{2,1,0:T(8,128)(2,1)} %get-tuple-element.8), kind=kOutput, calls=%fused_computation.5 | convolution fusion | flops 503808000 | bytes 4063232 | tf_op jit(solution)/shard_map/dot_general | solution.py:334
  76.8 1.3 %collective-permute-start.8 = (bf16[120,1024]{1,0:T(8,128)(2,1)}, bf16[120,1024]{1,0:T(8,128)(2,1)}, u32[]{:S(2)}, u32[]{:S(2)}) collective-permute-start(bf16[120,1024]{1,0:T(8,128)(2,1)} %get-tuple-element.28), channel_id=1, source_target_pairs={{1,2},{3,4},{5,6},{2,1},{4,3},{6,5},{9,10},{11,12},{13,14},{10,9},... | collective-permute-start | bytes 737288 | tf_op jit(solution)/shard_map/ppermute | solution.py:47
  78.2 2.6 %collective-permute-start.7 = (bf16[184,1024]{1,0:T(8,128)(2,1)S(1)}, bf16[184,1024]{1,0:T(8,128)(2,1)S(1)}, u32[]{:S(2)}, u32[]{:S(2)}) collective-permute-start(bf16[184,1024]{1,0:T(8,128)(2,1)S(1)} %pad_maximum_fusion.1), channel_id=1, source_target_pairs={{0,1},{1,0},{2,3},{3,2},{4,5},{5,4},{6,7},{7,6},{8,9},{9,8},{10,11... | collective-permute-start | bytes 1130504 | tf_op jit(solution)/shard_map/ppermute | solution.py:45
  80.7 2.0 %convolution_add_fusion = f32[320,1024]{1,0:T(8,128)S(1)} fusion(f32[320,1024]{1,0:T(8,128)S(1)} %copy-done.11, bf16[1024,1024]{1,0:T(8,128)(2,1)S(1)} %copy-done, bf16[2,640,1024]{2,1,0:T(8,128)(2,1)} %get-tuple-element.8), kind=kOutput, calls=%fused_computation.3 | convolution fusion | flops 671416320 | bytes 5373952 | tf_op jit(solution)/shard_map/dot_general | solution.py:334
  82.7 1.0 fusion.19
  83.7 0.8 copy-done.17
  85.2 1.6 %reshape.189 = f32[2,2,2,2,2,1024]{5,4,3,2,1,0:T(2,128)} reshape(f32[32,1024]{1,0:T(8,128)} %convert_add_fusion.1) | data formatting | bytes 262144 | tf_op jit(solution)/shard_map/reshape | solution.py:358
  86.8 1.2 bitcast_add_fusion
  89.5 1.9 %broadcast_select_fusion.3 = (bf16[120,1024]{1,0:T(8,128)(2,1)S(1)}, bf16[120,1024]{1,0:T(8,128)(2,1)}) fusion(bf16[120,1024]{1,0:T(8,128)(2,1)} %collective-permute-done.8, pred[]{:T(512)S(6)} %eq.69, bf16[184,1024]{1,0:T(8,128)(2,1)} %copy-done.17), kind=kLoop, calls=%fused_computation.39 | loop fusion | flops 245760 | bytes 983041 | tf_op jit(solution)/shard_map/jit(_where)/select_n | solution.py:52
  91.4 1.0 reshape.192
  92.5 0.9 broadcast_select_fusion.7
  93.4 0.8 pad_maximum_fusion.3
  94.3 1.3 %collective-permute-start.9 = (bf16[128,1024]{1,0:T(8,128)(2,1)S(1)}, bf16[128,1024]{1,0:T(8,128)(2,1)S(1)}, u32[]{:S(2)}, u32[]{:S(2)}) collective-permute-start(bf16[128,1024]{1,0:T(8,128)(2,1)S(1)} %pad_maximum_fusion.3), channel_id=1, source_target_pairs={{0,8},{8,0},{16,24},{24,16},{1,9},{9,1},{17,25},{25,17},{2,10},{10... | collective-permute-start | bytes 786440 | tf_op jit(solution)/shard_map/ppermute | solution.py:45
  95.6 1.2 convolution_convert_fusion.2
  96.7 5.8 %collective-permute-done.9 = bf16[128,1024]{1,0:T(8,128)(2,1)S(1)} collective-permute-done((bf16[128,1024]{1,0:T(8,128)(2,1)S(1)}, bf16[128,1024]{1,0:T(8,128)(2,1)S(1)}, u32[]{:S(2)}, u32[]{:S(2)}) %collective-permute-start.9) | collective-permute-done | bytes 262176 | tf_op jit(solution)/shard_map/ppermute | solution.py:45
  104.6 2.8 %collective-permute-done.10 = f32[2,2,2,1024]{3,0,1,2:T(2,128)S(1)} collective-permute-done((f32[2,2,2,1024]{3,0,1,2:T(2,128)S(1)}, f32[2,2,2,1024]{3,0,1,2:T(2,128)S(1)}, u32[]{:S(2)}, u32[]{:S(2)}) %collective-permute-start.10) | collective-permute-done | bytes 32800 | tf_op jit(solution)/shard_map/ppermute | solution.py:35
  107.5 1.6 %collective-permute-start.11 = (f32[2,2,1024]{2,0,1:T(2,128)S(1)}, f32[2,2,1024]{2,0,1:T(2,128)S(1)}, u32[]{:S(2)}, u32[]{:S(2)}) collective-permute-start(f32[2,2,1024]{2,0,1:T(2,128)S(1)} %select_bitcast_fusion.1), channel_id=1, source_target_pairs={{0,4},{1,5},{2,6},{3,7},{4,0},{5,1},{6,2},{7,3},{8,12},{9,13},{10,... | collective-permute-start | bytes 49160 | tf_op jit(solution)/shard_map/ppermute | solution.py:35
  109.1 1.0 broadcast_select_fusion.11
  110.1 2.1 %collective-permute-done.11 = f32[2,2,1024]{2,0,1:T(2,128)S(1)} collective-permute-done((f32[2,2,1024]{2,0,1:T(2,128)S(1)}, f32[2,2,1024]{2,0,1:T(2,128)S(1)}, u32[]{:S(2)}, u32[]{:S(2)}) %collective-permute-start.11) | collective-permute-done | bytes 16416 | tf_op jit(solution)/shard_map/ppermute | solution.py:35
  112.2 2.6 %collective-permute-start.12 = (f32[2,1024]{1,0:T(2,128)S(1)}, f32[2,1024]{1,0:T(2,128)S(1)}, u32[]{:S(2)}, u32[]{:S(2)}) collective-permute-start(f32[2,1024]{1,0:T(2,128)S(1)} %select_bitcast_fusion.2), channel_id=1, source_target_pairs={{0,16},{8,24},{16,0},{24,8},{1,17},{9,25},{17,1},{25,9},{2,18},{10... | collective-permute-start | bytes 24584 | tf_op jit(solution)/shard_map/ppermute | solution.py:35
  115.0 1.5 %collective-permute-done.12 = f32[2,1024]{1,0:T(2,128)S(1)} collective-permute-done((f32[2,1024]{1,0:T(2,128)S(1)}, f32[2,1024]{1,0:T(2,128)S(1)}, u32[]{:S(2)}, u32[]{:S(2)}) %collective-permute-start.12) | collective-permute-done | bytes 8224 | tf_op jit(solution)/shard_map/ppermute | solution.py:35
  116.5 0.9 add_convert_fusion
  118.8 3.1 %fusion.2 = bf16[128,1024]{1,0:T(8,128)(2,1)} fusion(f32[128,1024]{1,0:T(8,128)S(1)} %bitcast.86, f32[128,1024]{1,0:T(8,128)S(1)} %dynamic_update_slice.3, bf16[128,1024]{1,0:T(8,128)(2,1)S(1)} %copy-done.20, bf16[1024,1024]{1,0:T(8,128)(2,1)} %param.12), kind=kOutput, calls=%fused_computation.8 | convolution fusion | flops 268828672 | bytes 3670016 | tf_op jit(solution)/shard_map/dot_general | solution.py:399
  (130 shorter events, 12.4 us)
Async XLA Ops:
  0.6 6.5 %copy-start = (bf16[1024,1024]{1,0:T(8,128)(2,1)S(1)}, bf16[1024,1024]{1,0:T(8,128)(2,1)}, u32[]{:S(2)}) copy-start(bf16[1024,1024]{1,0:T(8,128)(2,1)} %param.14) | copy-start | bytes 6291460
  0.6 8.0 %copy-start.7 = (bf16[8,16,1024]{2,1,0:T(8,128)(2,1)S(1)}, bf16[8,16,1024]{2,1,0:T(8,128)(2,1)}, u32[]{:S(2)}) copy-start(bf16[8,16,1024]{2,1,0:T(8,128)(2,1)} %param.11) | copy-start | bytes 786436
  2.5 18.9 %collective-permute-start = (bf16[96,1024]{1,0:T(8,128)(2,1)}, bf16[96,1024]{1,0:T(8,128)(2,1)S(1)}, u32[]{:S(2)}, u32[]{:S(2)}) collective-permute-start(bf16[96,1024]{1,0:T(8,128)(2,1)} %bitcast.1), channel_id=1, source_target_pairs={{8,16},{16,8},{9,17},{17,9},{10,18},{18,10},{11,19},{19,11},{12,20... | collective-permute-start | bytes 589832 | tf_op jit(solution)/shard_map/ppermute | solution.py:47
  7.1 1.7 %copy-start.1 = (bf16[1024,1024]{1,0:T(8,128)(2,1)S(1)}, bf16[1024,1024]{1,0:T(8,128)(2,1)}, u32[]{:S(2)}) copy-start(bf16[1024,1024]{1,0:T(8,128)(2,1)} %param.13) | copy-start | bytes 6291460
  8.8 10.0 %copy-start.18 = (bf16[128,1024]{1,0:T(8,128)(2,1)}, bf16[128,1024]{1,0:T(8,128)(2,1)S(1)}, u32[]{:S(2)}) copy-start(bf16[128,1024]{1,0:T(8,128)(2,1)S(1)} %convolution_convert_fusion.4.vo_ref) | copy-start | bytes 786436
  9.2 12.1 %copy-start.19 = (bf16[128,1024]{1,0:T(8,128)(2,1)}, bf16[128,1024]{1,0:T(8,128)(2,1)S(1)}, u32[]{:S(2)}) copy-start(bf16[128,1024]{1,0:T(8,128)(2,1)S(1)} %convolution_convert_fusion.5.ko_ref) | copy-start | bytes 786436
  10.0 11.3 %collective-permute-start.1 = (bf16[98,1024]{1,0:T(8,128)(2,1)}, bf16[98,1024]{1,0:T(8,128)(2,1)S(1)}, u32[]{:S(2)}, u32[]{:S(2)}) collective-permute-start(bf16[98,1024]{1,0:T(8,128)(2,1)} %pad_maximum_fusion.4), channel_id=1, source_target_pairs={{0,8},{8,0},{16,24},{24,16},{1,9},{9,1},{17,25},{25,17},{2,10},{10... | collective-permute-start | bytes 602120 | tf_op jit(solution)/shard_map/ppermute | solution.py:45
  15.9 2.9 %copy-start.5 = (bf16[1024,1024]{1,0:T(8,128)(2,1)S(1)}, bf16[1024,1024]{1,0:T(8,128)(2,1)}, u32[]{:S(2)}) copy-start(bf16[1024,1024]{1,0:T(8,128)(2,1)} %param.15) | copy-start | bytes 6291460
  15.9 5.4 %copy-start.25 = (s32[640]{0:T(1024)S(1)}, s32[640]{0:T(1024)}, u32[]{:S(2)}) copy-start(s32[640]{0:T(1024)} %constant.137.clone) | copy-start | bytes 7684
  15.9 5.4 %copy-start.26 = (s32[640]{0:T(1024)S(1)}, s32[640]{0:T(1024)}, u32[]{:S(2)}) copy-start(s32[640]{0:T(1024)} %constant.136.clone) | copy-start | bytes 7684
  21.5 1.5 %copy-start.27 = (pred[640]{0:T(1024)(128)(4,1)S(1)}, pred[640]{0:T(1024)(128)(4,1)}, u32[]{:S(2)}) copy-start(pred[640]{0:T(1024)(128)(4,1)} %constant.155) | copy-start | bytes 1924
  21.5 1.4 %copy-start.28 = (pred[640]{0:T(1024)(128)(4,1)S(1)}, pred[640]{0:T(1024)(128)(4,1)}, u32[]{:S(2)}) copy-start(pred[640]{0:T(1024)(128)(4,1)} %constant.154) | copy-start | bytes 1924
  21.6 1.0 copy-start.23
  22.6 2.1 %copy-start.29 = (s32[32]{0:T(128)S(1)}, s32[32]{0:T(128)}, u32[]{:S(2)}) copy-start(s32[32]{0:T(128)} %constant.157) | copy-start | bytes 388
  22.9 1.9 %collective-permute-start.3 = (bf16[124,1024]{1,0:T(8,128)(2,1)S(1)}, bf16[124,1024]{1,0:T(8,128)(2,1)S(1)}, u32[]{:S(2)}, u32[]{:S(2)}) collective-permute-start(bf16[124,1024]{1,0:T(8,128)(2,1)S(1)} %pad_maximum_fusion.2), channel_id=1, source_target_pairs={{0,1},{1,0},{2,3},{3,2},{4,5},{5,4},{6,7},{7,6},{8,9},{9,8},{10,11... | collective-permute-start | bytes 761864 | tf_op jit(solution)/shard_map/ppermute | solution.py:45
  24.0 4.3 %collective-permute-start.2 = (bf16[120,1024]{1,0:T(8,128)(2,1)S(1)}, bf16[120,1024]{1,0:T(8,128)(2,1)S(1)}, u32[]{:S(2)}, u32[]{:S(2)}) collective-permute-start(bf16[120,1024]{1,0:T(8,128)(2,1)S(1)} %select_n.321), channel_id=1, source_target_pairs={{1,2},{3,4},{5,6},{2,1},{4,3},{6,5},{9,10},{11,12},{13,14},{10,9},... | collective-permute-start | bytes 737288 | tf_op jit(solution)/shard_map/ppermute | solution.py:47
  24.9 7.7 %collective-permute-start.4 = (bf16[4,2048]{1,0:T(4,128)(2,1)S(1)}, bf16[4,2048]{1,0:T(4,128)(2,1)S(1)}, u32[]{:S(2)}, u32[]{:S(2)}) collective-permute-start(bf16[4,2048]{1,0:T(4,128)(2,1)S(1)} %maximum_select_fusion.3), channel_id=1, source_target_pairs={{0,2},{1,3},{2,0},{3,1},{4,6},{5,7},{6,4},{7,5},{8,10},{9,11},{10,... | collective-permute-start | bytes 49160 | tf_op jit(solution)/shard_map/ppermute | solution.py:35
  32.6 8.5 %copy-start.2 = (bf16[1024,1024]{1,0:T(8,128)(2,1)S(1)}, bf16[1024,1024]{1,0:T(8,128)(2,1)}, u32[]{:S(2)}) copy-start(bf16[1024,1024]{1,0:T(8,128)(2,1)} %param.13) | copy-start | bytes 6291460
  32.6 8.5 %copy-start.24 = (bf16[480,1024]{1,0:T(8,128)(2,1)S(1)}, bf16[480,1024]{1,0:T(8,128)(2,1)}, u32[]{:S(2)}) copy-start(bf16[480,1024]{1,0:T(8,128)(2,1)} %broadcast_dynamic-update-slice_fusion) | copy-start | bytes 2949124
  32.6 7.2 %collective-permute-start.5 = (bf16[8,2048]{1,0:T(8,128)(2,1)S(1)}, bf16[8,2048]{1,0:T(8,128)(2,1)S(1)}, u32[]{:S(2)}, u32[]{:S(2)}) collective-permute-start(bf16[8,2048]{1,0:T(8,128)(2,1)S(1)} %maximum_select_fusion.2), channel_id=1, source_target_pairs={{0,4},{1,5},{2,6},{3,7},{4,0},{5,1},{6,2},{7,3},{8,12},{9,13},{10,... | collective-permute-start | bytes 98312 | tf_op jit(solution)/shard_map/ppermute | solution.py:35
  39.8 4.4 %collective-permute-start.6 = (bf16[16,2048]{1,0:T(8,128)(2,1)S(1)}, bf16[16,2048]{1,0:T(8,128)(2,1)S(1)}, u32[]{:S(2)}, u32[]{:S(2)}) collective-permute-start(bf16[16,2048]{1,0:T(8,128)(2,1)S(1)} %maximum_select_fusion.1), channel_id=1, source_target_pairs={{0,16},{8,24},{16,0},{24,8},{1,17},{9,25},{17,1},{25,9},{2,18},{10... | collective-permute-start | bytes 196616 | tf_op jit(solution)/shard_map/ppermute | solution.py:35
  63.3 2.6 %copy-start.3 = (bf16[1024,1024]{1,0:T(8,128)(2,1)S(1)}, bf16[1024,1024]{1,0:T(8,128)(2,1)}, u32[]{:S(2)}) copy-start(bf16[1024,1024]{1,0:T(8,128)(2,1)} %param.13) | copy-start | bytes 6291460
  72.2 3.9 %copy-start.14 = (f32[2,2,2,2,2,1,1024]{6,5,4,3,2,1,0:T(1,128)}, f32[2,2,2,2,2,1,1024]{6,5,4,3,2,1,0:T(1,128)S(1)}, u32[]{:S(2)}) copy-start(f32[2,2,2,2,2,1,1024]{6,5,4,3,2,1,0:T(1,128)S(1)} %get-tuple-element.32) | copy-start | bytes 393220
  74.2 6.6 %copy-start.11 = (f32[320,1024]{1,0:T(8,128)S(1)}, f32[320,1024]{1,0:T(8,128)}, u32[]{:S(2)}) copy-start(f32[320,1024]{1,0:T(8,128)} %fusion.4) | copy-start | bytes 3932164
  76.8 12.7 %collective-permute-start.8 = (bf16[120,1024]{1,0:T(8,128)(2,1)}, bf16[120,1024]{1,0:T(8,128)(2,1)}, u32[]{:S(2)}, u32[]{:S(2)}) collective-permute-start(bf16[120,1024]{1,0:T(8,128)(2,1)} %get-tuple-element.28), channel_id=1, source_target_pairs={{1,2},{3,4},{5,6},{2,1},{4,3},{6,5},{9,10},{11,12},{13,14},{10,9},... | collective-permute-start | bytes 737288 | tf_op jit(solution)/shard_map/ppermute | solution.py:47
  78.2 5.6 %collective-permute-start.7 = (bf16[184,1024]{1,0:T(8,128)(2,1)S(1)}, bf16[184,1024]{1,0:T(8,128)(2,1)S(1)}, u32[]{:S(2)}, u32[]{:S(2)}) collective-permute-start(bf16[184,1024]{1,0:T(8,128)(2,1)S(1)} %pad_maximum_fusion.1), channel_id=1, source_target_pairs={{0,1},{1,0},{2,3},{3,2},{4,5},{5,4},{6,7},{7,6},{8,9},{9,8},{10,11... | collective-permute-start | bytes 1130504 | tf_op jit(solution)/shard_map/ppermute | solution.py:45
  82.7 6.7 %copy-start.8 = (f32[320,1024]{1,0:T(8,128)}, f32[320,1024]{1,0:T(8,128)S(1)}, u32[]{:S(2)}) copy-start(f32[320,1024]{1,0:T(8,128)S(1)} %convolution_add_fusion) | copy-start | bytes 3932164
  83.7 0.8 copy-start.17
  88.0 0.7 copy-start.12
  89.5 3.0 %copy-start.9 = (f32[96,1024]{1,0:T(8,128)S(1)}, f32[96,1024]{1,0:T(8,128)}, u32[]{:S(2)}) copy-start(f32[96,1024]{1,0:T(8,128)} %get-tuple-element.21) | copy-start | bytes 1179652
  89.5 3.0 %copy-start.10 = (f32[96,1024]{1,0:T(8,128)S(1)}, f32[96,1024]{1,0:T(8,128)}, u32[]{:S(2)}) copy-start(f32[96,1024]{1,0:T(8,128)} %get-tuple-element.22) | copy-start | bytes 1179652
  92.5 3.1 %copy-start.6 = (bf16[1024,1024]{1,0:T(8,128)(2,1)S(1)}, bf16[1024,1024]{1,0:T(8,128)(2,1)}, u32[]{:S(2)}) copy-start(bf16[1024,1024]{1,0:T(8,128)(2,1)} %param.15) | copy-start | bytes 6291460
  92.5 3.1 %copy-start.21 = (bf16[128,1024]{1,0:T(8,128)(2,1)S(1)}, bf16[128,1024]{1,0:T(8,128)(2,1)}, u32[]{:S(2)}) copy-start(bf16[128,1024]{1,0:T(8,128)(2,1)} %get-tuple-element.6) | copy-start | bytes 786436
  93.4 9.9 %copy-start.13 = (f32[2,2,2,2,2,1024]{5,0,1,3,4,2:T(2,128)S(1)}, f32[2,2,2,2,2,1024]{5,0,1,3,4,2:T(2,128)}, u32[]{:S(2)}) copy-start(f32[2,2,2,2,2,1024]{5,0,1,3,4,2:T(2,128)} %copy-done.12) | copy-start | bytes 393220
  93.4 10.5 %copy-start.15 = (bf16[6,16,1024]{2,1,0:T(8,128)(2,1)S(1)}, bf16[6,16,1024]{2,1,0:T(8,128)(2,1)}, u32[]{:S(2)}) copy-start(bf16[6,16,1024]{2,1,0:T(8,128)(2,1)} %get-tuple-element.11) | copy-start | bytes 589828
  93.4 10.5 %copy-start.16 = (bf16[6,16,1024]{2,1,0:T(8,128)(2,1)S(1)}, bf16[6,16,1024]{2,1,0:T(8,128)(2,1)}, u32[]{:S(2)}) copy-start(bf16[6,16,1024]{2,1,0:T(8,128)(2,1)} %get-tuple-element.12) | copy-start | bytes 589828
  94.3 8.3 %collective-permute-start.9 = (bf16[128,1024]{1,0:T(8,128)(2,1)S(1)}, bf16[128,1024]{1,0:T(8,128)(2,1)S(1)}, u32[]{:S(2)}, u32[]{:S(2)}) collective-permute-start(bf16[128,1024]{1,0:T(8,128)(2,1)S(1)} %pad_maximum_fusion.3), channel_id=1, source_target_pairs={{0,8},{8,0},{16,24},{24,16},{1,9},{9,1},{17,25},{25,17},{2,10},{10... | collective-permute-start | bytes 786440 | tf_op jit(solution)/shard_map/ppermute | solution.py:45
  102.6 0.7 copy-start.22
  103.4 4.0 %collective-permute-start.10 = (f32[2,2,2,1024]{3,0,1,2:T(2,128)S(1)}, f32[2,2,2,1024]{3,0,1,2:T(2,128)S(1)}, u32[]{:S(2)}, u32[]{:S(2)}) collective-permute-start(f32[2,2,2,1024]{3,0,1,2:T(2,128)S(1)} %select_bitcast_fusion), channel_id=1, source_target_pairs={{0,2},{1,3},{2,0},{3,1},{4,6},{5,7},{6,4},{7,5},{8,10},{9,11},{10,... | collective-permute-start | bytes 98312 | tf_op jit(solution)/shard_map/ppermute | solution.py:35
  103.9 5.2 %collective-permute-start.13 = (bf16[96,1024]{1,0:T(8,128)(2,1)S(1)}, bf16[96,1024]{1,0:T(8,128)(2,1)S(1)}, u32[]{:S(2)}, u32[]{:S(2)}) collective-permute-start(bf16[96,1024]{1,0:T(8,128)(2,1)S(1)} %bitcast.98), channel_id=1, source_target_pairs={{8,16},{16,8},{9,17},{17,9},{10,18},{18,10},{11,19},{19,11},{12,20... | collective-permute-start | bytes 589832 | tf_op jit(solution)/shard_map/ppermute | solution.py:47
  107.5 4.7 %collective-permute-start.11 = (f32[2,2,1024]{2,0,1:T(2,128)S(1)}, f32[2,2,1024]{2,0,1:T(2,128)S(1)}, u32[]{:S(2)}, u32[]{:S(2)}) collective-permute-start(f32[2,2,1024]{2,0,1:T(2,128)S(1)} %select_bitcast_fusion.1), channel_id=1, source_target_pairs={{0,4},{1,5},{2,6},{3,7},{4,0},{5,1},{6,2},{7,3},{8,12},{9,13},{10,... | collective-permute-start | bytes 49160 | tf_op jit(solution)/shard_map/ppermute | solution.py:35
  110.1 8.0 %copy-start.4 = (bf16[1024,1024]{1,0:T(8,128)(2,1)S(1)}, bf16[1024,1024]{1,0:T(8,128)(2,1)}, u32[]{:S(2)}) copy-start(bf16[1024,1024]{1,0:T(8,128)(2,1)} %param.13) | copy-start | bytes 6291460
  112.2 4.3 %collective-permute-start.12 = (f32[2,1024]{1,0:T(2,128)S(1)}, f32[2,1024]{1,0:T(2,128)S(1)}, u32[]{:S(2)}, u32[]{:S(2)}) collective-permute-start(f32[2,1024]{1,0:T(2,128)S(1)} %select_bitcast_fusion.2), channel_id=1, source_target_pairs={{0,16},{8,24},{16,0},{24,8},{1,17},{9,25},{17,1},{25,9},{2,18},{10... | collective-permute-start | bytes 24584 | tf_op jit(solution)/shard_map/ppermute | solution.py:35
  117.4 1.3 %slice-start = ((f32[320,1024]{1,0:T(8,128)}), f32[128,1024]{1,0:T(8,128)S(1)}, s32[]{:S(2)}) async-start(f32[320,1024]{1,0:T(8,128)} %copy-done.8), calls=%async_computation | async-start | bytes 1048576 | tf_op jit(solution)/shard_map/slice | solution.py:342
  117.4 1.4 %copy-start.20 = (bf16[128,1024]{1,0:T(8,128)(2,1)S(1)}, bf16[128,1024]{1,0:T(8,128)(2,1)}, u32[]{:S(2)}) copy-start(bf16[128,1024]{1,0:T(8,128)(2,1)} %get-tuple-element.7) | copy-start | bytes 786436

commit v15 on v12

--- a/solution.py
+++ b/solution.py
@@ -97,7 +97,8 @@
         mine = lane_head == head
         q_head = jnp.where(mine, q, jnp.zeros_like(q))
         g_head = jnp.where(mine, g, jnp.zeros_like(g))
-        scores = lax.dot_general(q_head, k, rows, preferred_element_type=jnp.float32)
+        lanes = slice(head * head_size, (head + 1) * head_size)
+        scores = lax.dot_general(q[:, lanes], k[:, lanes], rows, preferred_element_type=jnp.float32)
         scores = jnp.where(keep, scores, -1e30)
         row_max = jnp.max(scores, axis=1, keepdims=True)
         exps = jnp.exp(scores - row_max)
@@ -109,7 +110,7 @@
         delta = jnp.sum(
             jnp.where(mine, g.astype(jnp.float32) * attended, 0.0), axis=1, keepdims=True
         )
-        dots = lax.dot_general(g_head, v, rows, preferred_element_type=jnp.float32)
+        dots = lax.dot_general(g[:, lanes], v[:, lanes], rows, preferred_element_type=jnp.float32)
         slopes = (probs * (dots - delta)).astype(jnp.bfloat16)
         dq = jnp.where(
             mine, jnp.dot(slopes, k, preferred_element_type=jnp.float32) * score_scale, dq

time: 121 us -> 121 us (level)
  no operation moved by 1% of the time
where the time goes in v15:
time: 121 us
  matrix products  28.1 us (23%)
  starting transfers between devices  26.2 us (22%)
  Pallas kernels  16.4 us (14%)
  local copies, waits for them, and re-layouts  15.8 us (13%)
  waiting for transfers between devices  15.3 us (13%)
  other arithmetic  14.8 us (12%)
  between operations  4.04 us (3%)
    pallas_call x1, Pallas kernels, attention(): pl.pallas_call(functools.partial(attention_kernel, tokens, first, last),...  16.4 us
    ppermute x6, starting transfers between devices, partner(): return lax.ppermute(x, axis, [(i, i ^ 1 << bit) for i in range(size)])  13.2 us
    ppermute x4, starting transfers between devices, exchange(): got_first = lax.ppermute(first, axis, [(i, i ^ 1) for i in range(size)])  9.62 us
    ppermute x6, waiting for transfers between devices, partner(): return lax.ppermute(x, axis, [(i, i ^ 1 << bit) for i in range(size)])  9.45 us
    ppermute x4, waiting for transfers between devices, exchange(): got_first = lax.ppermute(first, axis, [(i, i ^ 1) for i in range(size)])  5.83 us
    dot_general x2, matrix products, contribution(): jnp.dot(rounded_grads[0, lo:hi], w_key.T, preferred_element_type=jnp.floa...  5.73 us
    dot_general x2, matrix products, contribution(): jnp.dot(rounded_grads[1, lo:hi], w_value.T, preferred_element_type=jnp.fl...  3.84 us
    select_n x4, other arithmetic, exchange(): first = jnp.where(even, to_higher, to_lower)  3.61 us
  transfers between devices with their start and end apart: 14, of which 6 were waited for; matrix products, arithmetic and copies ran while one was open for 23% of the time, Pallas kernels for 0%

profile of v15, /device:TPU:0, one launch (start us, length us, event | category | flops | bytes accessed | tf_op | source)
XLA Modules:
  0.0 120.7 jit_solution(2496584449025359717)
XLA Ops:
  0.7 1.9 %broadcast_select_fusion.8 = (bf16[6,16,1024]{2,1,0:T(8,128)(2,1)S(1)}, bf16[6,16,1024]{2,1,0:T(8,128)(2,1)}) fusion(pred[]{:T(512)S(6)} %eq.68, bf16[8,16,1024]{2,1,0:T(8,128)(2,1)} %param.11), kind=kLoop, calls=%fused_computation.45 | loop fusion | flops 196608 | bytes 786433 | tf_op jit(solution)/shard_map/jit(_where)/select_n | solution.py:41
  3.2 1.2 %dynamic_slice.13 = s32[1]{0:T(128)} dynamic-slice(s32[32]{0:T(128)} %param.16, s32[]{:T(128)S(6)} %select_n.311), dynamic_slice_sizes={1} | dynamic-slice | bytes 12 | tf_op jit(solution)/shard_map/jit(dynamic_index_in_dim)/dynamic_slice | solution.py:218
  7.1 1.5 %convolution_convert_fusion.4.vo_ref = bf16[128,1024]{1,0:T(8,128)(2,1)S(1)} fusion(bf16[128,1024]{1,0:T(8,128)(2,1)} %bitcast.83, bf16[1024,1024]{1,0:T(8,128)(2,1)S(1)} %copy-done), kind=kOutput, calls=%fused_computation.11 | convolution fusion | flops 268566528 | bytes 2621440 | tf_op jit(solution)/shard_map/dot_general | solution.py:213
  10.0 5.7 %collective-permute-start.1 = (bf16[98,1024]{1,0:T(8,128)(2,1)}, bf16[98,1024]{1,0:T(8,128)(2,1)S(1)}, u32[]{:S(2)}, u32[]{:S(2)}) collective-permute-start(bf16[98,1024]{1,0:T(8,128)(2,1)} %pad_maximum_fusion.4), channel_id=1, source_target_pairs={{0,8},{8,0},{16,24},{24,16},{1,9},{9,1},{17,25},{25,17},{2,10},{10... | collective-permute-start | bytes 602120 | tf_op jit(solution)/shard_map/ppermute | solution.py:45
  15.9 2.9 %convolution_convert_fusion.6.q_ref = bf16[128,1024]{1,0:T(8,128)(2,1)} fusion(bf16[128,1024]{1,0:T(8,128)(2,1)S(1)} %bitcast.85, bf16[1024,1024]{1,0:T(8,128)(2,1)} %param.12), kind=kOutput, calls=%fused_computation.13 | convolution fusion | flops 268566528 | bytes 2621440 | tf_op jit(solution)/shard_map/dot_general | solution.py:252
  18.8 2.5 %convolution_convert_fusion.3.g_ref = bf16[128,1024]{1,0:T(8,128)(2,1)} fusion(bf16[128,1024]{1,0:T(8,128)(2,1)} %bitcast.96, bf16[1024,1024]{1,0:T(8,128)(2,1)S(1)} %copy-done.5), kind=kOutput, calls=%fused_computation.10 | convolution fusion | flops 268566528 | bytes 2621440 | tf_op jit(solution)/shard_map/dot_general | solution.py:253
  21.6 1.0 copy-done.23
  23.0 0.9 or_convert_fusion.mask_ref
  24.9 3.4 %collective-permute-start.4 = (bf16[4,2048]{1,0:T(4,128)(2,1)S(1)}, bf16[4,2048]{1,0:T(4,128)(2,1)S(1)}, u32[]{:S(2)}, u32[]{:S(2)}) collective-permute-start(bf16[4,2048]{1,0:T(4,128)(2,1)S(1)} %maximum_select_fusion.3), channel_id=1, source_target_pairs={{0,2},{1,3},{2,0},{3,1},{4,6},{5,7},{6,4},{7,5},{8,10},{9,11},{10,... | collective-permute-start | bytes 49160 | tf_op jit(solution)/shard_map/ppermute | solution.py:35
  28.3 0.8 select_dynamic-update-slice_fusion.1
  29.1 0.8 select_dynamic-update-slice_fusion
  30.4 2.1 %collective-permute-done.4 = bf16[4,2048]{1,0:T(4,128)(2,1)S(1)} collective-permute-done((bf16[4,2048]{1,0:T(4,128)(2,1)S(1)}, bf16[4,2048]{1,0:T(4,128)(2,1)S(1)}, u32[]{:S(2)}, u32[]{:S(2)}) %collective-permute-start.4) | collective-permute-done | bytes 16416 | tf_op jit(solution)/shard_map/ppermute | solution.py:35
  32.6 3.8 %collective-permute-start.5 = (bf16[8,2048]{1,0:T(8,128)(2,1)S(1)}, bf16[8,2048]{1,0:T(8,128)(2,1)S(1)}, u32[]{:S(2)}, u32[]{:S(2)}) collective-permute-start(bf16[8,2048]{1,0:T(8,128)(2,1)S(1)} %maximum_select_fusion.2), channel_id=1, source_target_pairs={{0,4},{1,5},{2,6},{3,7},{4,0},{5,1},{6,2},{7,3},{8,12},{9,13},{10,... | collective-permute-start | bytes 98312 | tf_op jit(solution)/shard_map/ppermute | solution.py:35
  36.4 3.4 %convolution_convert_fusion.vh_ref = bf16[480,1024]{1,0:T(8,128)(2,1)} fusion(bf16[480,1024]{1,0:T(8,128)(2,1)} %broadcast_dynamic-update-slice_fusion, bf16[1024,1024]{1,0:T(8,128)(2,1)S(1)} %copy-done), kind=kOutput, calls=%fused_computation.1 | convolution fusion | flops 1007124480 | bytes 4063232 | tf_op jit(solution)/shard_map/dot_general | solution.py:270
  39.8 1.3 %collective-permute-start.6 = (bf16[16,2048]{1,0:T(8,128)(2,1)S(1)}, bf16[16,2048]{1,0:T(8,128)(2,1)S(1)}, u32[]{:S(2)}, u32[]{:S(2)}) collective-permute-start(bf16[16,2048]{1,0:T(8,128)(2,1)S(1)} %maximum_select_fusion.1), channel_id=1, source_target_pairs={{0,16},{8,24},{16,0},{24,8},{1,17},{9,25},{17,1},{25,9},{2,18},{10... | collective-permute-start | bytes 196616 | tf_op jit(solution)/shard_map/ppermute | solution.py:35
  41.1 2.2 %convolution_convert_fusion.1.kh_ref = bf16[480,1024]{1,0:T(8,128)(2,1)} fusion(bf16[480,1024]{1,0:T(8,128)(2,1)S(1)} %copy-done.24, bf16[1024,1024]{1,0:T(8,128)(2,1)S(1)} %copy-done.2), kind=kOutput, calls=%fused_computation.2 | convolution fusion | flops 1007124480 | bytes 4063232 | tf_op jit(solution)/shard_map/dot_general | solution.py:267
  43.3 0.9 collective-permute-done.6
  45.6 16.4 %shard_map.122 = (bf16[128,1024]{1,0:T(8,128)(2,1)}, bf16[128,1024]{1,0:T(8,128)(2,1)}, bf16[2,640,1024]{2,1,0:T(8,128)(2,1)}, f32[2,160,1024]{2,1,0:T(8,128)}) custom-call(bf16[128,1024]{1,0:T(8,128)(2,1)} %convolution_convert_fusion.6.q_ref, bf16[128,1024]{1,0:T(8,128)(2,1)} %copy-done.19, bf16[480,1024]{1,0:T(8,128)(2,1)} %convolution_convert_fusion.1.kh_ref, ...), custom_call_target="tpu_custom_call" | custom-call | flops 2013265920 | bytes 8978432 | tf_op jit(solution)/shard_map/pallas_call | solution.py:152
  62.1 2.6 %fusion.9 = f32[240,1024]{1,0:T(8,128)S(1)} fusion(bf16[1024,1024]{1,0:T(8,128)(2,1)} %param.13, bf16[2,640,1024]{2,1,0:T(8,128)(2,1)} %get-tuple-element.8), kind=kOutput, calls=%fused_computation.22 | convolution fusion | flops 503316480 | bytes 3571712 | tf_op jit(solution)/shard_map/dot_general | solution.py:332
  64.7 3.1 %fusion.4 = f32[320,1024]{1,0:T(8,128)} fusion(bf16[1024,1024]{1,0:T(8,128)(2,1)S(1)} %copy-done.3, bf16[2,640,1024]{2,1,0:T(8,128)(2,1)} %get-tuple-element.8), kind=kOutput, calls=%fused_computation.16 | convolution fusion | flops 671088640 | bytes 4063232 | tf_op jit(solution)/shard_map/dot_general | solution.py:332
  67.8 1.0 slice.144
  68.8 0.8 reshape.188
  69.6 1.3 %fusion.20 = (f32[2,2,2,2,2,1,1024]{6,5,4,3,2,1,0:T(1,128)S(1)}, f32[2,2,2,2,2,1,1024]{6,5,4,3,2,1,0:T(1,128)S(1)}) fusion(f32[2,2,2,2,2,2,1024]{6,5,4,3,2,1,0:T(2,128)} %reshape.188), kind=kLoop, calls=%fused_computation.90 | loop fusion | bytes 524288 | tf_op jit(solution)/shard_map/slice | solution.py:73
  71.1 0.8 copy.17
  71.9 1.0 select_n.354
  72.9 1.9 %fusion = bf16[240,1024]{1,0:T(8,128)(2,1)S(1)} fusion(f32[240,1024]{1,0:T(8,128)S(1)} %fusion.9, bf16[1024,1024]{1,0:T(8,128)(2,1)S(1)} %copy-done, bf16[2,640,1024]{2,1,0:T(8,128)(2,1)} %get-tuple-element.8), kind=kOutput, calls=%fused_computation.5 | convolution fusion | flops 503808000 | bytes 4063232 | tf_op jit(solution)/shard_map/dot_general | solution.py:334
  75.5 1.3 %collective-permute-start.8 = (bf16[120,1024]{1,0:T(8,128)(2,1)}, bf16[120,1024]{1,0:T(8,128)(2,1)}, u32[]{:S(2)}, u32[]{:S(2)}) collective-permute-start(bf16[120,1024]{1,0:T(8,128)(2,1)} %get-tuple-element.28), channel_id=1, source_target_pairs={{1,2},{3,4},{5,6},{2,1},{4,3},{6,5},{9,10},{11,12},{13,14},{10,9},... | collective-permute-start | bytes 737288 | tf_op jit(solution)/shard_map/ppermute | solution.py:47
  76.9 2.6 %collective-permute-start.7 = (bf16[184,1024]{1,0:T(8,128)(2,1)S(1)}, bf16[184,1024]{1,0:T(8,128)(2,1)S(1)}, u32[]{:S(2)}, u32[]{:S(2)}) collective-permute-start(bf16[184,1024]{1,0:T(8,128)(2,1)S(1)} %pad_maximum_fusion.1), channel_id=1, source_target_pairs={{0,1},{1,0},{2,3},{3,2},{4,5},{5,4},{6,7},{7,6},{8,9},{9,8},{10,11... | collective-permute-start | bytes 1130504 | tf_op jit(solution)/shard_map/ppermute | solution.py:45
  79.5 2.0 %convolution_add_fusion = f32[320,1024]{1,0:T(8,128)S(1)} fusion(f32[320,1024]{1,0:T(8,128)S(1)} %copy-done.11, bf16[1024,1024]{1,0:T(8,128)(2,1)S(1)} %copy-done, bf16[2,640,1024]{2,1,0:T(8,128)(2,1)} %get-tuple-element.8), kind=kOutput, calls=%fused_computation.3 | convolution fusion | flops 671416320 | bytes 5373952 | tf_op jit(solution)/shard_map/dot_general | solution.py:334
  81.5 1.0 fusion.19
  82.5 0.8 copy-done.17
  83.9 1.6 %reshape.189 = f32[2,2,2,2,2,1024]{5,4,3,2,1,0:T(2,128)} reshape(f32[32,1024]{1,0:T(8,128)} %convert_add_fusion.1) | data formatting | bytes 262144 | tf_op jit(solution)/shard_map/reshape | solution.py:358
  85.5 1.2 %bitcast_add_fusion = f32[2,2,2,2,2,1024]{5,0,1,3,4,2:T(2,128)S(1)} fusion(f32[2,2,2,2,2,1024]{5,4,3,2,1,0:T(2,128)} %reshape.189, pred[]{:T(512)S(6)} %eq.83, f32[2,2,2,2,2,1,1024]{6,5,4,3,2,1,0:T(1,128)} %copy-done.14, f32[2,2,2,2,2,1,1024]{6,5,4,3,2,1,0:T(1,128)S(1)} %get-tuple-element.31), kind=kLoop, calls=%fused_computation.52 | loop fusion | flops 65536 | bytes 524289 | tf_op jit(solution)/shard_map/add | solution.py:358
  88.2 1.9 %broadcast_select_fusion.3 = (bf16[120,1024]{1,0:T(8,128)(2,1)S(1)}, bf16[120,1024]{1,0:T(8,128)(2,1)}) fusion(bf16[120,1024]{1,0:T(8,128)(2,1)} %collective-permute-done.8, pred[]{:T(512)S(6)} %eq.69, bf16[184,1024]{1,0:T(8,128)(2,1)} %copy-done.17), kind=kLoop, calls=%fused_computation.39 | loop fusion | flops 245760 | bytes 983041 | tf_op jit(solution)/shard_map/jit(_where)/select_n | solution.py:52
  90.2 1.0 reshape.192
  91.2 0.9 broadcast_select_fusion.7
  92.2 0.8 pad_maximum_fusion.3
  93.0 1.3 %collective-permute-start.9 = (bf16[128,1024]{1,0:T(8,128)(2,1)S(1)}, bf16[128,1024]{1,0:T(8,128)(2,1)S(1)}, u32[]{:S(2)}, u32[]{:S(2)}) collective-permute-start(bf16[128,1024]{1,0:T(8,128)(2,1)S(1)} %pad_maximum_fusion.3), channel_id=1, source_target_pairs={{0,8},{8,0},{16,24},{24,16},{1,9},{9,1},{17,25},{25,17},{2,10},{10... | collective-permute-start | bytes 786440 | tf_op jit(solution)/shard_map/ppermute | solution.py:45
  94.3 1.2 convolution_convert_fusion.2
  95.5 5.8 %collective-permute-done.9 = bf16[128,1024]{1,0:T(8,128)(2,1)S(1)} collective-permute-done((bf16[128,1024]{1,0:T(8,128)(2,1)S(1)}, bf16[128,1024]{1,0:T(8,128)(2,1)S(1)}, u32[]{:S(2)}, u32[]{:S(2)}) %collective-permute-start.9) | collective-permute-done | bytes 262176 | tf_op jit(solution)/shard_map/ppermute | solution.py:45
  103.4 2.8 %collective-permute-done.10 = f32[2,2,2,1024]{3,0,1,2:T(2,128)S(1)} collective-permute-done((f32[2,2,2,1024]{3,0,1,2:T(2,128)S(1)}, f32[2,2,2,1024]{3,0,1,2:T(2,128)S(1)}, u32[]{:S(2)}, u32[]{:S(2)}) %collective-permute-start.10) | collective-permute-done | bytes 32800 | tf_op jit(solution)/shard_map/ppermute | solution.py:35
  106.2 1.6 %collective-permute-start.11 = (f32[2,2,1024]{2,0,1:T(2,128)S(1)}, f32[2,2,1024]{2,0,1:T(2,128)S(1)}, u32[]{:S(2)}, u32[]{:S(2)}) collective-permute-start(f32[2,2,1024]{2,0,1:T(2,128)S(1)} %select_bitcast_fusion.1), channel_id=1, source_target_pairs={{0,4},{1,5},{2,6},{3,7},{4,0},{5,1},{6,2},{7,3},{8,12},{9,13},{10,... | collective-permute-start | bytes 49160 | tf_op jit(solution)/shard_map/ppermute | solution.py:35
  107.8 1.0 broadcast_select_fusion.11
  108.8 2.1 %collective-permute-done.11 = f32[2,2,1024]{2,0,1:T(2,128)S(1)} collective-permute-done((f32[2,2,1024]{2,0,1:T(2,128)S(1)}, f32[2,2,1024]{2,0,1:T(2,128)S(1)}, u32[]{:S(2)}, u32[]{:S(2)}) %collective-permute-start.11) | collective-permute-done | bytes 16416 | tf_op jit(solution)/shard_map/ppermute | solution.py:35
  111.0 2.6 %collective-permute-start.12 = (f32[2,1024]{1,0:T(2,128)S(1)}, f32[2,1024]{1,0:T(2,128)S(1)}, u32[]{:S(2)}, u32[]{:S(2)}) collective-permute-start(f32[2,1024]{1,0:T(2,128)S(1)} %select_bitcast_fusion.2), channel_id=1, source_target_pairs={{0,16},{8,24},{16,0},{24,8},{1,17},{9,25},{17,1},{25,9},{2,18},{10... | collective-permute-start | bytes 24584 | tf_op jit(solution)/shard_map/ppermute | solution.py:35
  113.7 1.5 %collective-permute-done.12 = f32[2,1024]{1,0:T(2,128)S(1)} collective-permute-done((f32[2,1024]{1,0:T(2,128)S(1)}, f32[2,1024]{1,0:T(2,128)S(1)}, u32[]{:S(2)}, u32[]{:S(2)}) %collective-permute-start.12) | collective-permute-done | bytes 8224 | tf_op jit(solution)/shard_map/ppermute | solution.py:35
  115.2 0.9 add_convert_fusion
  117.6 3.1 %fusion.2 = bf16[128,1024]{1,0:T(8,128)(2,1)} fusion(f32[128,1024]{1,0:T(8,128)S(1)} %bitcast.86, f32[128,1024]{1,0:T(8,128)S(1)} %dynamic_update_slice.3, bf16[128,1024]{1,0:T(8,128)(2,1)S(1)} %copy-done.20, bf16[1024,1024]{1,0:T(8,128)(2,1)} %param.12), kind=kOutput, calls=%fused_computation.8 | convolution fusion | flops 268828672 | bytes 3670016 | tf_op jit(solution)/shard_map/dot_general | solution.py:399
  (130 shorter events, 12.4 us)
Async XLA Ops:
  0.6 6.5 %copy-start = (bf16[1024,1024]{1,0:T(8,128)(2,1)S(1)}, bf16[1024,1024]{1,0:T(8,128)(2,1)}, u32[]{:S(2)}) copy-start(bf16[1024,1024]{1,0:T(8,128)(2,1)} %param.14) | copy-start | bytes 6291460
  0.6 8.0 %copy-start.7 = (bf16[8,16,1024]{2,1,0:T(8,128)(2,1)S(1)}, bf16[8,16,1024]{2,1,0:T(8,128)(2,1)}, u32[]{:S(2)}) copy-start(bf16[8,16,1024]{2,1,0:T(8,128)(2,1)} %param.11) | copy-start | bytes 786436
  2.5 18.9 %collective-permute-start = (bf16[96,1024]{1,0:T(8,128)(2,1)}, bf16[96,1024]{1,0:T(8,128)(2,1)S(1)}, u32[]{:S(2)}, u32[]{:S(2)}) collective-permute-start(bf16[96,1024]{1,0:T(8,128)(2,1)} %bitcast.1), channel_id=1, source_target_pairs={{8,16},{16,8},{9,17},{17,9},{10,18},{18,10},{11,19},{19,11},{12,20... | collective-permute-start | bytes 589832 | tf_op jit(solution)/shard_map/ppermute | solution.py:47
  7.1 1.7 %copy-start.1 = (bf16[1024,1024]{1,0:T(8,128)(2,1)S(1)}, bf16[1024,1024]{1,0:T(8,128)(2,1)}, u32[]{:S(2)}) copy-start(bf16[1024,1024]{1,0:T(8,128)(2,1)} %param.13) | copy-start | bytes 6291460
  8.8 10.0 %copy-start.18 = (bf16[128,1024]{1,0:T(8,128)(2,1)}, bf16[128,1024]{1,0:T(8,128)(2,1)S(1)}, u32[]{:S(2)}) copy-start(bf16[128,1024]{1,0:T(8,128)(2,1)S(1)} %convolution_convert_fusion.4.vo_ref) | copy-start | bytes 786436
  9.2 12.1 %copy-start.19 = (bf16[128,1024]{1,0:T(8,128)(2,1)}, bf16[128,1024]{1,0:T(8,128)(2,1)S(1)}, u32[]{:S(2)}) copy-start(bf16[128,1024]{1,0:T(8,128)(2,1)S(1)} %convolution_convert_fusion.5.ko_ref) | copy-start | bytes 786436
  10.0 11.3 %collective-permute-start.1 = (bf16[98,1024]{1,0:T(8,128)(2,1)}, bf16[98,1024]{1,0:T(8,128)(2,1)S(1)}, u32[]{:S(2)}, u32[]{:S(2)}) collective-permute-start(bf16[98,1024]{1,0:T(8,128)(2,1)} %pad_maximum_fusion.4), channel_id=1, source_target_pairs={{0,8},{8,0},{16,24},{24,16},{1,9},{9,1},{17,25},{25,17},{2,10},{10... | collective-permute-start | bytes 602120 | tf_op jit(solution)/shard_map/ppermute | solution.py:45
  15.9 2.9 %copy-start.5 = (bf16[1024,1024]{1,0:T(8,128)(2,1)S(1)}, bf16[1024,1024]{1,0:T(8,128)(2,1)}, u32[]{:S(2)}) copy-start(bf16[1024,1024]{1,0:T(8,128)(2,1)} %param.15) | copy-start | bytes 6291460
  15.9 5.4 %copy-start.25 = (s32[640]{0:T(1024)S(1)}, s32[640]{0:T(1024)}, u32[]{:S(2)}) copy-start(s32[640]{0:T(1024)} %constant.137.clone) | copy-start | bytes 7684
  15.9 5.4 %copy-start.26 = (s32[640]{0:T(1024)S(1)}, s32[640]{0:T(1024)}, u32[]{:S(2)}) copy-start(s32[640]{0:T(1024)} %constant.136.clone) | copy-start | bytes 7684
  21.5 1.5 %copy-start.27 = (pred[640]{0:T(1024)(128)(4,1)S(1)}, pred[640]{0:T(1024)(128)(4,1)}, u32[]{:S(2)}) copy-start(pred[640]{0:T(1024)(128)(4,1)} %constant.155) | copy-start | bytes 1924
  21.5 1.4 %copy-start.28 = (pred[640]{0:T(1024)(128)(4,1)S(1)}, pred[640]{0:T(1024)(128)(4,1)}, u32[]{:S(2)}) copy-start(pred[640]{0:T(1024)(128)(4,1)} %constant.154) | copy-start | bytes 1924
  21.6 1.0 copy-start.23
  22.6 2.1 %copy-start.29 = (s32[32]{0:T(128)S(1)}, s32[32]{0:T(128)}, u32[]{:S(2)}) copy-start(s32[32]{0:T(128)} %constant.157) | copy-start | bytes 388
  22.9 1.9 %collective-permute-start.3 = (bf16[124,1024]{1,0:T(8,128)(2,1)S(1)}, bf16[124,1024]{1,0:T(8,128)(2,1)S(1)}, u32[]{:S(2)}, u32[]{:S(2)}) collective-permute-start(bf16[124,1024]{1,0:T(8,128)(2,1)S(1)} %pad_maximum_fusion.2), channel_id=1, source_target_pairs={{0,1},{1,0},{2,3},{3,2},{4,5},{5,4},{6,7},{7,6},{8,9},{9,8},{10,11... | collective-permute-start | bytes 761864 | tf_op jit(solution)/shard_map/ppermute | solution.py:45
  24.0 4.3 %collective-permute-start.2 = (bf16[120,1024]{1,0:T(8,128)(2,1)S(1)}, bf16[120,1024]{1,0:T(8,128)(2,1)S(1)}, u32[]{:S(2)}, u32[]{:S(2)}) collective-permute-start(bf16[120,1024]{1,0:T(8,128)(2,1)S(1)} %select_n.321), channel_id=1, source_target_pairs={{1,2},{3,4},{5,6},{2,1},{4,3},{6,5},{9,10},{11,12},{13,14},{10,9},... | collective-permute-start | bytes 737288 | tf_op jit(solution)/shard_map/ppermute | solution.py:47
  24.9 7.7 %collective-permute-start.4 = (bf16[4,2048]{1,0:T(4,128)(2,1)S(1)}, bf16[4,2048]{1,0:T(4,128)(2,1)S(1)}, u32[]{:S(2)}, u32[]{:S(2)}) collective-permute-start(bf16[4,2048]{1,0:T(4,128)(2,1)S(1)} %maximum_select_fusion.3), channel_id=1, source_target_pairs={{0,2},{1,3},{2,0},{3,1},{4,6},{5,7},{6,4},{7,5},{8,10},{9,11},{10,... | collective-permute-start | bytes 49160 | tf_op jit(solution)/shard_map/ppermute | solution.py:35
  32.6 8.5 %copy-start.2 = (bf16[1024,1024]{1,0:T(8,128)(2,1)S(1)}, bf16[1024,1024]{1,0:T(8,128)(2,1)}, u32[]{:S(2)}) copy-start(bf16[1024,1024]{1,0:T(8,128)(2,1)} %param.13) | copy-start | bytes 6291460
  32.6 8.5 %copy-start.24 = (bf16[480,1024]{1,0:T(8,128)(2,1)S(1)}, bf16[480,1024]{1,0:T(8,128)(2,1)}, u32[]{:S(2)}) copy-start(bf16[480,1024]{1,0:T(8,128)(2,1)} %broadcast_dynamic-update-slice_fusion) | copy-start | bytes 2949124
  32.6 7.2 %collective-permute-start.5 = (bf16[8,2048]{1,0:T(8,128)(2,1)S(1)}, bf16[8,2048]{1,0:T(8,128)(2,1)S(1)}, u32[]{:S(2)}, u32[]{:S(2)}) collective-permute-start(bf16[8,2048]{1,0:T(8,128)(2,1)S(1)} %maximum_select_fusion.2), channel_id=1, source_target_pairs={{0,4},{1,5},{2,6},{3,7},{4,0},{5,1},{6,2},{7,3},{8,12},{9,13},{10,... | collective-permute-start | bytes 98312 | tf_op jit(solution)/shard_map/ppermute | solution.py:35
  39.8 4.4 %collective-permute-start.6 = (bf16[16,2048]{1,0:T(8,128)(2,1)S(1)}, bf16[16,2048]{1,0:T(8,128)(2,1)S(1)}, u32[]{:S(2)}, u32[]{:S(2)}) collective-permute-start(bf16[16,2048]{1,0:T(8,128)(2,1)S(1)} %maximum_select_fusion.1), channel_id=1, source_target_pairs={{0,16},{8,24},{16,0},{24,8},{1,17},{9,25},{17,1},{25,9},{2,18},{10... | collective-permute-start | bytes 196616 | tf_op jit(solution)/shard_map/ppermute | solution.py:35
  62.0 2.6 %copy-start.3 = (bf16[1024,1024]{1,0:T(8,128)(2,1)S(1)}, bf16[1024,1024]{1,0:T(8,128)(2,1)}, u32[]{:S(2)}) copy-start(bf16[1024,1024]{1,0:T(8,128)(2,1)} %param.13) | copy-start | bytes 6291460
  70.9 3.9 %copy-start.14 = (f32[2,2,2,2,2,1,1024]{6,5,4,3,2,1,0:T(1,128)}, f32[2,2,2,2,2,1,1024]{6,5,4,3,2,1,0:T(1,128)S(1)}, u32[]{:S(2)}) copy-start(f32[2,2,2,2,2,1,1024]{6,5,4,3,2,1,0:T(1,128)S(1)} %get-tuple-element.32) | copy-start | bytes 393220
  72.9 6.6 %copy-start.11 = (f32[320,1024]{1,0:T(8,128)S(1)}, f32[320,1024]{1,0:T(8,128)}, u32[]{:S(2)}) copy-start(f32[320,1024]{1,0:T(8,128)} %fusion.4) | copy-start | bytes 3932164
  75.5 12.7 %collective-permute-start.8 = (bf16[120,1024]{1,0:T(8,128)(2,1)}, bf16[120,1024]{1,0:T(8,128)(2,1)}, u32[]{:S(2)}, u32[]{:S(2)}) collective-permute-start(bf16[120,1024]{1,0:T(8,128)(2,1)} %get-tuple-element.28), channel_id=1, source_target_pairs={{1,2},{3,4},{5,6},{2,1},{4,3},{6,5},{9,10},{11,12},{13,14},{10,9},... | collective-permute-start | bytes 737288 | tf_op jit(solution)/shard_map/ppermute | solution.py:47
  76.9 5.6 %collective-permute-start.7 = (bf16[184,1024]{1,0:T(8,128)(2,1)S(1)}, bf16[184,1024]{1,0:T(8,128)(2,1)S(1)}, u32[]{:S(2)}, u32[]{:S(2)}) collective-permute-start(bf16[184,1024]{1,0:T(8,128)(2,1)S(1)} %pad_maximum_fusion.1), channel_id=1, source_target_pairs={{0,1},{1,0},{2,3},{3,2},{4,5},{5,4},{6,7},{7,6},{8,9},{9,8},{10,11... | collective-permute-start | bytes 1130504 | tf_op jit(solution)/shard_map/ppermute | solution.py:45
  81.5 6.7 %copy-start.8 = (f32[320,1024]{1,0:T(8,128)}, f32[320,1024]{1,0:T(8,128)S(1)}, u32[]{:S(2)}) copy-start(f32[320,1024]{1,0:T(8,128)S(1)} %convolution_add_fusion) | copy-start | bytes 3932164
  82.5 0.8 copy-start.17
  86.8 0.7 copy-start.12
  88.2 3.0 %copy-start.9 = (f32[96,1024]{1,0:T(8,128)S(1)}, f32[96,1024]{1,0:T(8,128)}, u32[]{:S(2)}) copy-start(f32[96,1024]{1,0:T(8,128)} %get-tuple-element.21) | copy-start | bytes 1179652
  88.2 3.0 %copy-start.10 = (f32[96,1024]{1,0:T(8,128)S(1)}, f32[96,1024]{1,0:T(8,128)}, u32[]{:S(2)}) copy-start(f32[96,1024]{1,0:T(8,128)} %get-tuple-element.22) | copy-start | bytes 1179652
  91.2 3.1 %copy-start.6 = (bf16[1024,1024]{1,0:T(8,128)(2,1)S(1)}, bf16[1024,1024]{1,0:T(8,128)(2,1)}, u32[]{:S(2)}) copy-start(bf16[1024,1024]{1,0:T(8,128)(2,1)} %param.15) | copy-start | bytes 6291460
  91.2 3.1 %copy-start.21 = (bf16[128,1024]{1,0:T(8,128)(2,1)S(1)}, bf16[128,1024]{1,0:T(8,128)(2,1)}, u32[]{:S(2)}) copy-start(bf16[128,1024]{1,0:T(8,128)(2,1)} %get-tuple-element.6) | copy-start | bytes 786436
  92.1 9.9 %copy-start.13 = (f32[2,2,2,2,2,1024]{5,0,1,3,4,2:T(2,128)S(1)}, f32[2,2,2,2,2,1024]{5,0,1,3,4,2:T(2,128)}, u32[]{:S(2)}) copy-start(f32[2,2,2,2,2,1024]{5,0,1,3,4,2:T(2,128)} %copy-done.12) | copy-start | bytes 393220
  92.1 10.5 %copy-start.15 = (bf16[6,16,1024]{2,1,0:T(8,128)(2,1)S(1)}, bf16[6,16,1024]{2,1,0:T(8,128)(2,1)}, u32[]{:S(2)}) copy-start(bf16[6,16,1024]{2,1,0:T(8,128)(2,1)} %get-tuple-element.11) | copy-start | bytes 589828
  92.2 10.5 %copy-start.16 = (bf16[6,16,1024]{2,1,0:T(8,128)(2,1)S(1)}, bf16[6,16,1024]{2,1,0:T(8,128)(2,1)}, u32[]{:S(2)}) copy-start(bf16[6,16,1024]{2,1,0:T(8,128)(2,1)} %get-tuple-element.12) | copy-start | bytes 589828
  93.0 8.3 %collective-permute-start.9 = (bf16[128,1024]{1,0:T(8,128)(2,1)S(1)}, bf16[128,1024]{1,0:T(8,128)(2,1)S(1)}, u32[]{:S(2)}, u32[]{:S(2)}) collective-permute-start(bf16[128,1024]{1,0:T(8,128)(2,1)S(1)} %pad_maximum_fusion.3), channel_id=1, source_target_pairs={{0,8},{8,0},{16,24},{24,16},{1,9},{9,1},{17,25},{25,17},{2,10},{10... | collective-permute-start | bytes 786440 | tf_op jit(solution)/shard_map/ppermute | solution.py:45
  101.3 0.7 copy-start.22
  102.2 4.0 %collective-permute-start.10 = (f32[2,2,2,1024]{3,0,1,2:T(2,128)S(1)}, f32[2,2,2,1024]{3,0,1,2:T(2,128)S(1)}, u32[]{:S(2)}, u32[]{:S(2)}) collective-permute-start(f32[2,2,2,1024]{3,0,1,2:T(2,128)S(1)} %select_bitcast_fusion), channel_id=1, source_target_pairs={{0,2},{1,3},{2,0},{3,1},{4,6},{5,7},{6,4},{7,5},{8,10},{9,11},{10,... | collective-permute-start | bytes 98312 | tf_op jit(solution)/shard_map/ppermute | solution.py:35
  102.7 5.2 %collective-permute-start.13 = (bf16[96,1024]{1,0:T(8,128)(2,1)S(1)}, bf16[96,1024]{1,0:T(8,128)(2,1)S(1)}, u32[]{:S(2)}, u32[]{:S(2)}) collective-permute-start(bf16[96,1024]{1,0:T(8,128)(2,1)S(1)} %bitcast.98), channel_id=1, source_target_pairs={{8,16},{16,8},{9,17},{17,9},{10,18},{18,10},{11,19},{19,11},{12,20... | collective-permute-start | bytes 589832 | tf_op jit(solution)/shard_map/ppermute | solution.py:47
  106.2 4.7 %collective-permute-start.11 = (f32[2,2,1024]{2,0,1:T(2,128)S(1)}, f32[2,2,1024]{2,0,1:T(2,128)S(1)}, u32[]{:S(2)}, u32[]{:S(2)}) collective-permute-start(f32[2,2,1024]{2,0,1:T(2,128)S(1)} %select_bitcast_fusion.1), channel_id=1, source_target_pairs={{0,4},{1,5},{2,6},{3,7},{4,0},{5,1},{6,2},{7,3},{8,12},{9,13},{10,... | collective-permute-start | bytes 49160 | tf_op jit(solution)/shard_map/ppermute | solution.py:35
  108.8 8.0 %copy-start.4 = (bf16[1024,1024]{1,0:T(8,128)(2,1)S(1)}, bf16[1024,1024]{1,0:T(8,128)(2,1)}, u32[]{:S(2)}) copy-start(bf16[1024,1024]{1,0:T(8,128)(2,1)} %param.13) | copy-start | bytes 6291460
  111.0 4.3 %collective-permute-start.12 = (f32[2,1024]{1,0:T(2,128)S(1)}, f32[2,1024]{1,0:T(2,128)S(1)}, u32[]{:S(2)}, u32[]{:S(2)}) collective-permute-start(f32[2,1024]{1,0:T(2,128)S(1)} %select_bitcast_fusion.2), channel_id=1, source_target_pairs={{0,16},{8,24},{16,0},{24,8},{1,17},{9,25},{17,1},{25,9},{2,18},{10... | collective-permute-start | bytes 24584 | tf_op jit(solution)/shard_map/ppermute | solution.py:35
  116.1 1.3 %slice-start = ((f32[320,1024]{1,0:T(8,128)}), f32[128,1024]{1,0:T(8,128)S(1)}, s32[]{:S(2)}) async-start(f32[320,1024]{1,0:T(8,128)} %copy-done.8), calls=%async_computation | async-start | bytes 1048576 | tf_op jit(solution)/shard_map/slice | solution.py:342
  116.1 1.4 %copy-start.20 = (bf16[128,1024]{1,0:T(8,128)(2,1)S(1)}, bf16[128,1024]{1,0:T(8,128)(2,1)}, u32[]{:S(2)}) copy-start(bf16[128,1024]{1,0:T(8,128)(2,1)} %get-tuple-element.7) | copy-start | bytes 786436

commit v16 on v12

--- a/solution.py
+++ b/solution.py
@@ -38,13 +38,20 @@
 def exchange(to_lower, to_higher, axis, rider=None, rider_dim=0):
     size = lax.axis_size(axis)
     even = lax.axis_index(axis) % 2 == 0
-    first = jnp.where(even, to_higher, to_lower)
+    picked = None
+    if isinstance(to_lower, tuple):
+        source, dim, low_at, high_at, count = to_lower
+        take = lambda at: lax.dynamic_slice_in_dim(source, at, count, dim)
+        picked = (take(jnp.where(even, high_at, low_at)), take(jnp.where(even, low_at, high_at)))
+        to_lower = to_higher = None
+    first = picked[0] if picked else jnp.where(even, to_higher, to_lower)
     length = first.shape[rider_dim]
     if rider is not None:
         first = jnp.concatenate([first, rider], axis=rider_dim)
     got_first = lax.ppermute(first, axis, [(i, i ^ 1) for i in range(size)])
     links = [(i, i + 1) for i in range(1, size - 1, 2)] + [(i, i - 1) for i in range(2, size, 2)]
-    got_second = lax.ppermute(jnp.where(even, to_lower, to_higher), axis, links)
+    second = picked[1] if picked else jnp.where(even, to_lower, to_higher)
+    got_second = lax.ppermute(second, axis, links)
     rider_got = None
     if rider is not None:
         rider_got = lax.slice_in_dim(got_first, length, None, axis=rider_dim)
@@ -226,8 +233,8 @@
     order = [col_bits, 0] + list(range(1, col_bits)) + list(range(col_bits + 1, all_bits))
 
     from_above, from_below, got = exchange(
-        features[:RAD].reshape(-1, model_width),
-        features[tile_rows - RAD :].reshape(-1, model_width),
+        (flat_tokens, 0, 0, (tile_rows - RAD) * tile_cols, RAD * tile_cols),
+        None,
         "rows",
         gathered.reshape(-1, model_width),
     )

time: 121 us -> 121 us (level)
  other arithmetic: 14.8 us -> 12.9 us
  local copies, waits for them, and re-layouts: 15.8 us -> 17.7 us
    select_n x5 -> x4, other arithmetic: 3.63 us -> 1.76 us  [the longest x3 1.73 us: exchange(): first = picked[0] if picked else jnp.where(even, to_higher, to_lower)]
    dynamic_slice x0 -> x1, local copies, waits for them, and re-layouts: none -> 1.87 us  [exchange(): take = lambda at: lax.dynamic_slice_in_dim(source, at, count, dim)]
where the time goes in v16:
time: 121 us; the launch traced here: 120 us
  matrix products  28.1 us (23%)
  starting transfers between devices  26.3 us (22%)
  local copies, waits for them, and re-layouts  17.7 us (15%)
  Pallas kernels  15.9 us (13%)
  waiting for transfers between devices  15.3 us (13%)
  other arithmetic  12.9 us (11%)
  between operations  4.04 us (3%)
    pallas_call x1, Pallas kernels, attention(): pl.pallas_call(functools.partial(attention_kernel, tokens, first, last),...  15.9 us
    ppermute x6, starting transfers between devices, partner(): return lax.ppermute(x, axis, [(i, i ^ 1 << bit) for i in range(size)])  13.3 us
    ppermute x4, starting transfers between devices, exchange(): got_first = lax.ppermute(first, axis, [(i, i ^ 1) for i in range(size)])  9.63 us
    ppermute x6, waiting for transfers between devices, partner(): return lax.ppermute(x, axis, [(i, i ^ 1 << bit) for i in range(size)])  9.45 us
    ppermute x4, waiting for transfers between devices, exchange(): got_first = lax.ppermute(first, axis, [(i, i ^ 1) for i in range(size)])  5.82 us
    dot_general x2, matrix products, contribution(): jnp.dot(rounded_grads[0, lo:hi], w_key.T, preferred_element_type=jnp.floa...  5.74 us
    dot_general x2, matrix products, contribution(): jnp.dot(rounded_grads[1, lo:hi], w_value.T, preferred_element_type=jnp.fl...  3.84 us
    dot_general x1, matrix products, shards(): jnp.dot(halo_features, w_value, preferred_element_type=jnp.float32)  3.36 us
  transfers between devices with their start and end apart: 14, of which 6 were waited for; matrix products, arithmetic and copies ran while one was open for 23% of the time, Pallas kernels for 0%

profile of v16, /device:TPU:0, one launch (start us, length us, event | category | flops | bytes accessed | tf_op | source)
XLA Modules:
  0.0 120.2 jit_solution(15439867944810189388)
XLA Ops:
  0.7 1.9 %constant_dynamic-slice_fusion.2 = (bf16[96,1024]{1,0:T(8,128)(2,1)S(1)}, bf16[96,1024]{1,0:T(8,128)(2,1)}) fusion(bf16[128,1024]{1,0:T(8,128)(2,1)} %bitcast.81, s32[]{:T(128)S(6)} %select_n.302, s32[]{:T(128)S(6)} %select_n.301), kind=kLoop, calls=%fused_computation.85 | loop fusion | bytes 786440 | tf_op jit(solution)/shard_map/dynamic_slice | solution.py:44
  3.2 1.2 %dynamic_slice.21 = s32[1]{0:T(128)} dynamic-slice(s32[32]{0:T(128)} %param.16, s32[]{:T(128)S(6)} %select_n.303), dynamic_slice_sizes={1} | dynamic-slice | bytes 12 | tf_op jit(solution)/shard_map/jit(dynamic_index_in_dim)/dynamic_slice | solution.py:224
  7.1 1.5 %convolution_convert_fusion.4.vo_ref = bf16[128,1024]{1,0:T(8,128)(2,1)S(1)} fusion(bf16[128,1024]{1,0:T(8,128)(2,1)} %bitcast.82, bf16[1024,1024]{1,0:T(8,128)(2,1)S(1)} %copy-done), kind=kOutput, calls=%fused_computation.11 | convolution fusion | flops 268566528 | bytes 2621440 | tf_op jit(solution)/shard_map/dot_general | solution.py:219
  10.0 5.7 %collective-permute-start.1 = (bf16[98,1024]{1,0:T(8,128)(2,1)}, bf16[98,1024]{1,0:T(8,128)(2,1)S(1)}, u32[]{:S(2)}, u32[]{:S(2)}) collective-permute-start(bf16[98,1024]{1,0:T(8,128)(2,1)} %pad_maximum_fusion.4), channel_id=1, source_target_pairs={{0,8},{8,0},{16,24},{24,16},{1,9},{9,1},{17,25},{25,17},{2,10},{10... | collective-permute-start | bytes 602120 | tf_op jit(solution)/shard_map/ppermute | solution.py:51
  15.9 2.9 %convolution_convert_fusion.6.q_ref = bf16[128,1024]{1,0:T(8,128)(2,1)} fusion(bf16[128,1024]{1,0:T(8,128)(2,1)S(1)} %bitcast.84, bf16[1024,1024]{1,0:T(8,128)(2,1)} %param.12), kind=kOutput, calls=%fused_computation.13 | convolution fusion | flops 268566528 | bytes 2621440 | tf_op jit(solution)/shard_map/dot_general | solution.py:258
  18.8 2.5 %convolution_convert_fusion.3.g_ref = bf16[128,1024]{1,0:T(8,128)(2,1)} fusion(bf16[128,1024]{1,0:T(8,128)(2,1)} %bitcast.94, bf16[1024,1024]{1,0:T(8,128)(2,1)S(1)} %copy-done.5), kind=kOutput, calls=%fused_computation.10 | convolution fusion | flops 268566528 | bytes 2621440 | tf_op jit(solution)/shard_map/dot_general | solution.py:259
  21.6 1.0 copy-done.23
  23.0 0.9 or_convert_fusion.mask_ref
  24.9 3.4 %collective-permute-start.4 = (bf16[4,2048]{1,0:T(4,128)(2,1)S(1)}, bf16[4,2048]{1,0:T(4,128)(2,1)S(1)}, u32[]{:S(2)}, u32[]{:S(2)}) collective-permute-start(bf16[4,2048]{1,0:T(4,128)(2,1)S(1)} %maximum_select_fusion.3), channel_id=1, source_target_pairs={{0,2},{1,3},{2,0},{3,1},{4,6},{5,7},{6,4},{7,5},{8,10},{9,11},{10,... | collective-permute-start | bytes 49160 | tf_op jit(solution)/shard_map/ppermute | solution.py:35
  28.3 0.8 select_dynamic-update-slice_fusion.1
  29.1 0.8 select_dynamic-update-slice_fusion
  30.5 2.1 %collective-permute-done.4 = bf16[4,2048]{1,0:T(4,128)(2,1)S(1)} collective-permute-done((bf16[4,2048]{1,0:T(4,128)(2,1)S(1)}, bf16[4,2048]{1,0:T(4,128)(2,1)S(1)}, u32[]{:S(2)}, u32[]{:S(2)}) %collective-permute-start.4) | collective-permute-done | bytes 16416 | tf_op jit(solution)/shard_map/ppermute | solution.py:35
  32.6 3.8 %collective-permute-start.5 = (bf16[8,2048]{1,0:T(8,128)(2,1)S(1)}, bf16[8,2048]{1,0:T(8,128)(2,1)S(1)}, u32[]{:S(2)}, u32[]{:S(2)}) collective-permute-start(bf16[8,2048]{1,0:T(8,128)(2,1)S(1)} %maximum_select_fusion.2), channel_id=1, source_target_pairs={{0,4},{1,5},{2,6},{3,7},{4,0},{5,1},{6,2},{7,3},{8,12},{9,13},{10,... | collective-permute-start | bytes 98312 | tf_op jit(solution)/shard_map/ppermute | solution.py:35
  36.4 3.4 %convolution_convert_fusion.vh_ref = bf16[480,1024]{1,0:T(8,128)(2,1)} fusion(bf16[480,1024]{1,0:T(8,128)(2,1)} %broadcast_dynamic-update-slice_fusion, bf16[1024,1024]{1,0:T(8,128)(2,1)S(1)} %copy-done), kind=kOutput, calls=%fused_computation.1 | convolution fusion | flops 1007124480 | bytes 4063232 | tf_op jit(solution)/shard_map/dot_general | solution.py:276
  39.8 1.3 %collective-permute-start.6 = (bf16[16,2048]{1,0:T(8,128)(2,1)S(1)}, bf16[16,2048]{1,0:T(8,128)(2,1)S(1)}, u32[]{:S(2)}, u32[]{:S(2)}) collective-permute-start(bf16[16,2048]{1,0:T(8,128)(2,1)S(1)} %maximum_select_fusion.1), channel_id=1, source_target_pairs={{0,16},{8,24},{16,0},{24,8},{1,17},{9,25},{17,1},{25,9},{2,18},{10... | collective-permute-start | bytes 196616 | tf_op jit(solution)/shard_map/ppermute | solution.py:35
  41.1 2.2 %convolution_convert_fusion.1.kh_ref = bf16[480,1024]{1,0:T(8,128)(2,1)} fusion(bf16[480,1024]{1,0:T(8,128)(2,1)S(1)} %copy-done.24, bf16[1024,1024]{1,0:T(8,128)(2,1)S(1)} %copy-done.2), kind=kOutput, calls=%fused_computation.2 | convolution fusion | flops 1007124480 | bytes 4063232 | tf_op jit(solution)/shard_map/dot_general | solution.py:273
  43.3 0.9 collective-permute-done.6
  45.6 15.9 %shard_map.122 = (bf16[128,1024]{1,0:T(8,128)(2,1)}, bf16[128,1024]{1,0:T(8,128)(2,1)}, bf16[2,640,1024]{2,1,0:T(8,128)(2,1)}, f32[2,160,1024]{2,1,0:T(8,128)}) custom-call(bf16[128,1024]{1,0:T(8,128)(2,1)} %convolution_convert_fusion.6.q_ref, bf16[128,1024]{1,0:T(8,128)(2,1)} %copy-done.19, bf16[480,1024]{1,0:T(8,128)(2,1)} %convolution_convert_fusion.1.kh_ref, ...), custom_call_target="tpu_custom_call" | custom-call | flops 2013265920 | bytes 8978432 | tf_op jit(solution)/shard_map/pallas_call | solution.py:158
  61.5 2.6 %fusion.9 = f32[240,1024]{1,0:T(8,128)S(1)} fusion(bf16[1024,1024]{1,0:T(8,128)(2,1)} %param.13, bf16[2,640,1024]{2,1,0:T(8,128)(2,1)} %get-tuple-element.8), kind=kOutput, calls=%fused_computation.22 | convolution fusion | flops 503316480 | bytes 3571712 | tf_op jit(solution)/shard_map/dot_general | solution.py:338
  64.2 3.1 %fusion.4 = f32[320,1024]{1,0:T(8,128)} fusion(bf16[1024,1024]{1,0:T(8,128)(2,1)S(1)} %copy-done.3, bf16[2,640,1024]{2,1,0:T(8,128)(2,1)} %get-tuple-element.8), kind=kOutput, calls=%fused_computation.16 | convolution fusion | flops 671088640 | bytes 4063232 | tf_op jit(solution)/shard_map/dot_general | solution.py:338
  67.3 1.0 slice.136
  68.3 0.8 reshape.182
  69.1 1.3 %fusion.20 = (f32[2,2,2,2,2,1,1024]{6,5,4,3,2,1,0:T(1,128)S(1)}, f32[2,2,2,2,2,1,1024]{6,5,4,3,2,1,0:T(1,128)S(1)}) fusion(f32[2,2,2,2,2,2,1024]{6,5,4,3,2,1,0:T(2,128)} %reshape.182), kind=kLoop, calls=%fused_computation.90 | loop fusion | bytes 524288 | tf_op jit(solution)/shard_map/slice | solution.py:80
  70.6 0.8 copy.17
  71.3 1.0 select_n.346
  72.4 1.9 %fusion = bf16[240,1024]{1,0:T(8,128)(2,1)S(1)} fusion(f32[240,1024]{1,0:T(8,128)S(1)} %fusion.9, bf16[1024,1024]{1,0:T(8,128)(2,1)S(1)} %copy-done, bf16[2,640,1024]{2,1,0:T(8,128)(2,1)} %get-tuple-element.8), kind=kOutput, calls=%fused_computation.5 | convolution fusion | flops 503808000 | bytes 4063232 | tf_op jit(solution)/shard_map/dot_general | solution.py:340
  75.0 1.3 %collective-permute-start.8 = (bf16[120,1024]{1,0:T(8,128)(2,1)}, bf16[120,1024]{1,0:T(8,128)(2,1)}, u32[]{:S(2)}, u32[]{:S(2)}) collective-permute-start(bf16[120,1024]{1,0:T(8,128)(2,1)} %get-tuple-element.28), channel_id=1, source_target_pairs={{1,2},{3,4},{5,6},{2,1},{4,3},{6,5},{9,10},{11,12},{13,14},{10,9},... | collective-permute-start | bytes 737288 | tf_op jit(solution)/shard_map/ppermute | solution.py:54
  76.4 2.6 %collective-permute-start.7 = (bf16[184,1024]{1,0:T(8,128)(2,1)S(1)}, bf16[184,1024]{1,0:T(8,128)(2,1)S(1)}, u32[]{:S(2)}, u32[]{:S(2)}) collective-permute-start(bf16[184,1024]{1,0:T(8,128)(2,1)S(1)} %pad_maximum_fusion.1), channel_id=1, source_target_pairs={{0,1},{1,0},{2,3},{3,2},{4,5},{5,4},{6,7},{7,6},{8,9},{9,8},{10,11... | collective-permute-start | bytes 1130504 | tf_op jit(solution)/shard_map/ppermute | solution.py:51
  78.9 2.0 %convolution_add_fusion = f32[320,1024]{1,0:T(8,128)S(1)} fusion(f32[320,1024]{1,0:T(8,128)S(1)} %copy-done.11, bf16[1024,1024]{1,0:T(8,128)(2,1)S(1)} %copy-done, bf16[2,640,1024]{2,1,0:T(8,128)(2,1)} %get-tuple-element.8), kind=kOutput, calls=%fused_computation.3 | convolution fusion | flops 671416320 | bytes 5373952 | tf_op jit(solution)/shard_map/dot_general | solution.py:340
  80.9 1.0 fusion.19
  82.0 0.8 copy-done.17
  83.4 1.6 %reshape.183 = f32[2,2,2,2,2,1024]{5,4,3,2,1,0:T(2,128)} reshape(f32[32,1024]{1,0:T(8,128)} %convert_add_fusion.1) | data formatting | bytes 262144 | tf_op jit(solution)/shard_map/reshape | solution.py:364
  85.0 1.2 %bitcast_add_fusion = f32[2,2,2,2,2,1024]{5,0,1,3,4,2:T(2,128)S(1)} fusion(f32[2,2,2,2,2,1024]{5,4,3,2,1,0:T(2,128)} %reshape.183, pred[]{:T(512)S(6)} %eq.83, f32[2,2,2,2,2,1,1024]{6,5,4,3,2,1,0:T(1,128)} %copy-done.14, f32[2,2,2,2,2,1,1024]{6,5,4,3,2,1,0:T(1,128)S(1)} %get-tuple-element.31), kind=kLoop, calls=%fused_computation.50 | loop fusion | flops 65536 | bytes 524289 | tf_op jit(solution)/shard_map/add | solution.py:364
  87.7 1.9 %broadcast_select_fusion.3 = (bf16[120,1024]{1,0:T(8,128)(2,1)S(1)}, bf16[120,1024]{1,0:T(8,128)(2,1)}) fusion(bf16[120,1024]{1,0:T(8,128)(2,1)} %collective-permute-done.8, pred[]{:T(512)S(6)} %eq.69, bf16[184,1024]{1,0:T(8,128)(2,1)} %copy-done.17), kind=kLoop, calls=%fused_computation.39 | loop fusion | flops 245760 | bytes 983041 | tf_op jit(solution)/shard_map/jit(_where)/select_n | solution.py:59
  89.6 1.0 reshape.186
  90.7 0.9 broadcast_select_fusion.7
  91.6 0.8 pad_maximum_fusion.3
  92.5 1.3 %collective-permute-start.9 = (bf16[128,1024]{1,0:T(8,128)(2,1)S(1)}, bf16[128,1024]{1,0:T(8,128)(2,1)S(1)}, u32[]{:S(2)}, u32[]{:S(2)}) collective-permute-start(bf16[128,1024]{1,0:T(8,128)(2,1)S(1)} %pad_maximum_fusion.3), channel_id=1, source_target_pairs={{0,8},{8,0},{16,24},{24,16},{1,9},{9,1},{17,25},{25,17},{2,10},{10... | collective-permute-start | bytes 786440 | tf_op jit(solution)/shard_map/ppermute | solution.py:51
  93.8 1.2 convolution_convert_fusion.2
  95.0 5.8 %collective-permute-done.9 = bf16[128,1024]{1,0:T(8,128)(2,1)S(1)} collective-permute-done((bf16[128,1024]{1,0:T(8,128)(2,1)S(1)}, bf16[128,1024]{1,0:T(8,128)(2,1)S(1)}, u32[]{:S(2)}, u32[]{:S(2)}) %collective-permute-start.9) | collective-permute-done | bytes 262176 | tf_op jit(solution)/shard_map/ppermute | solution.py:51
  102.8 2.8 %collective-permute-done.10 = f32[2,2,2,1024]{3,0,1,2:T(2,128)S(1)} collective-permute-done((f32[2,2,2,1024]{3,0,1,2:T(2,128)S(1)}, f32[2,2,2,1024]{3,0,1,2:T(2,128)S(1)}, u32[]{:S(2)}, u32[]{:S(2)}) %collective-permute-start.10) | collective-permute-done | bytes 32800 | tf_op jit(solution)/shard_map/ppermute | solution.py:35
  105.7 1.6 %collective-permute-start.11 = (f32[2,2,1024]{2,0,1:T(2,128)S(1)}, f32[2,2,1024]{2,0,1:T(2,128)S(1)}, u32[]{:S(2)}, u32[]{:S(2)}) collective-permute-start(f32[2,2,1024]{2,0,1:T(2,128)S(1)} %select_bitcast_fusion.1), channel_id=1, source_target_pairs={{0,4},{1,5},{2,6},{3,7},{4,0},{5,1},{6,2},{7,3},{8,12},{9,13},{10,... | collective-permute-start | bytes 49160 | tf_op jit(solution)/shard_map/ppermute | solution.py:35
  107.3 1.0 broadcast_select_fusion.9
  108.3 2.1 %collective-permute-done.11 = f32[2,2,1024]{2,0,1:T(2,128)S(1)} collective-permute-done((f32[2,2,1024]{2,0,1:T(2,128)S(1)}, f32[2,2,1024]{2,0,1:T(2,128)S(1)}, u32[]{:S(2)}, u32[]{:S(2)}) %collective-permute-start.11) | collective-permute-done | bytes 16416 | tf_op jit(solution)/shard_map/ppermute | solution.py:35
  110.4 2.7 %collective-permute-start.12 = (f32[2,1024]{1,0:T(2,128)S(1)}, f32[2,1024]{1,0:T(2,128)S(1)}, u32[]{:S(2)}, u32[]{:S(2)}) collective-permute-start(f32[2,1024]{1,0:T(2,128)S(1)} %select_bitcast_fusion.2), channel_id=1, source_target_pairs={{0,16},{8,24},{16,0},{24,8},{1,17},{9,25},{17,1},{25,9},{2,18},{10... | collective-permute-start | bytes 24584 | tf_op jit(solution)/shard_map/ppermute | solution.py:35
  113.2 1.5 %collective-permute-done.12 = f32[2,1024]{1,0:T(2,128)S(1)} collective-permute-done((f32[2,1024]{1,0:T(2,128)S(1)}, f32[2,1024]{1,0:T(2,128)S(1)}, u32[]{:S(2)}, u32[]{:S(2)}) %collective-permute-start.12) | collective-permute-done | bytes 8224 | tf_op jit(solution)/shard_map/ppermute | solution.py:35
  114.7 0.9 add_convert_fusion
  117.0 3.1 %fusion.2 = bf16[128,1024]{1,0:T(8,128)(2,1)} fusion(f32[128,1024]{1,0:T(8,128)S(1)} %bitcast.85, f32[128,1024]{1,0:T(8,128)S(1)} %dynamic_update_slice.3, bf16[128,1024]{1,0:T(8,128)(2,1)S(1)} %copy-done.20, bf16[1024,1024]{1,0:T(8,128)(2,1)} %param.12), kind=kOutput, calls=%fused_computation.8 | convolution fusion | flops 268828672 | bytes 3670016 | tf_op jit(solution)/shard_map/dot_general | solution.py:405
  (130 shorter events, 12.4 us)
Async XLA Ops:
  0.6 6.5 %copy-start = (bf16[1024,1024]{1,0:T(8,128)(2,1)S(1)}, bf16[1024,1024]{1,0:T(8,128)(2,1)}, u32[]{:S(2)}) copy-start(bf16[1024,1024]{1,0:T(8,128)(2,1)} %param.14) | copy-start | bytes 6291460
  0.6 8.0 %copy-start.7 = (bf16[8,16,1024]{2,1,0:T(8,128)(2,1)S(1)}, bf16[8,16,1024]{2,1,0:T(8,128)(2,1)}, u32[]{:S(2)}) copy-start(bf16[8,16,1024]{2,1,0:T(8,128)(2,1)} %param.11) | copy-start | bytes 786436
  2.6 18.9 %collective-permute-start = (bf16[96,1024]{1,0:T(8,128)(2,1)}, bf16[96,1024]{1,0:T(8,128)(2,1)S(1)}, u32[]{:S(2)}, u32[]{:S(2)}) collective-permute-start(bf16[96,1024]{1,0:T(8,128)(2,1)} %get-tuple-element.34), channel_id=1, source_target_pairs={{8,16},{16,8},{9,17},{17,9},{10,18},{18,10},{11,19},{19,11},{12,20... | collective-permute-start | bytes 589832 | tf_op jit(solution)/shard_map/ppermute | solution.py:54
  7.1 1.7 %copy-start.1 = (bf16[1024,1024]{1,0:T(8,128)(2,1)S(1)}, bf16[1024,1024]{1,0:T(8,128)(2,1)}, u32[]{:S(2)}) copy-start(bf16[1024,1024]{1,0:T(8,128)(2,1)} %param.13) | copy-start | bytes 6291460
  8.8 10.0 %copy-start.18 = (bf16[128,1024]{1,0:T(8,128)(2,1)}, bf16[128,1024]{1,0:T(8,128)(2,1)S(1)}, u32[]{:S(2)}) copy-start(bf16[128,1024]{1,0:T(8,128)(2,1)S(1)} %convolution_convert_fusion.4.vo_ref) | copy-start | bytes 786436
  9.2 12.1 %copy-start.19 = (bf16[128,1024]{1,0:T(8,128)(2,1)}, bf16[128,1024]{1,0:T(8,128)(2,1)S(1)}, u32[]{:S(2)}) copy-start(bf16[128,1024]{1,0:T(8,128)(2,1)S(1)} %convolution_convert_fusion.5.ko_ref) | copy-start | bytes 786436
  10.0 11.3 %collective-permute-start.1 = (bf16[98,1024]{1,0:T(8,128)(2,1)}, bf16[98,1024]{1,0:T(8,128)(2,1)S(1)}, u32[]{:S(2)}, u32[]{:S(2)}) collective-permute-start(bf16[98,1024]{1,0:T(8,128)(2,1)} %pad_maximum_fusion.4), channel_id=1, source_target_pairs={{0,8},{8,0},{16,24},{24,16},{1,9},{9,1},{17,25},{25,17},{2,10},{10... | collective-permute-start | bytes 602120 | tf_op jit(solution)/shard_map/ppermute | solution.py:51
  15.9 2.9 %copy-start.5 = (bf16[1024,1024]{1,0:T(8,128)(2,1)S(1)}, bf16[1024,1024]{1,0:T(8,128)(2,1)}, u32[]{:S(2)}) copy-start(bf16[1024,1024]{1,0:T(8,128)(2,1)} %param.15) | copy-start | bytes 6291460
  15.9 5.4 %copy-start.25 = (s32[640]{0:T(1024)S(1)}, s32[640]{0:T(1024)}, u32[]{:S(2)}) copy-start(s32[640]{0:T(1024)} %constant.140.clone) | copy-start | bytes 7684
  15.9 5.4 %copy-start.26 = (s32[640]{0:T(1024)S(1)}, s32[640]{0:T(1024)}, u32[]{:S(2)}) copy-start(s32[640]{0:T(1024)} %constant.139.clone) | copy-start | bytes 7684
  21.5 1.5 %copy-start.27 = (pred[640]{0:T(1024)(128)(4,1)S(1)}, pred[640]{0:T(1024)(128)(4,1)}, u32[]{:S(2)}) copy-start(pred[640]{0:T(1024)(128)(4,1)} %constant.158) | copy-start | bytes 1924
  21.5 1.4 %copy-start.28 = (pred[640]{0:T(1024)(128)(4,1)S(1)}, pred[640]{0:T(1024)(128)(4,1)}, u32[]{:S(2)}) copy-start(pred[640]{0:T(1024)(128)(4,1)} %constant.157) | copy-start | bytes 1924
  21.6 1.0 copy-start.23
  22.6 2.1 %copy-start.29 = (s32[32]{0:T(128)S(1)}, s32[32]{0:T(128)}, u32[]{:S(2)}) copy-start(s32[32]{0:T(128)} %constant.160) | copy-start | bytes 388
  22.9 1.9 %collective-permute-start.3 = (bf16[124,1024]{1,0:T(8,128)(2,1)S(1)}, bf16[124,1024]{1,0:T(8,128)(2,1)S(1)}, u32[]{:S(2)}, u32[]{:S(2)}) collective-permute-start(bf16[124,1024]{1,0:T(8,128)(2,1)S(1)} %pad_maximum_fusion.2), channel_id=1, source_target_pairs={{0,1},{1,0},{2,3},{3,2},{4,5},{5,4},{6,7},{7,6},{8,9},{9,8},{10,11... | collective-permute-start | bytes 761864 | tf_op jit(solution)/shard_map/ppermute | solution.py:51
  24.0 4.3 %collective-permute-start.2 = (bf16[120,1024]{1,0:T(8,128)(2,1)S(1)}, bf16[120,1024]{1,0:T(8,128)(2,1)S(1)}, u32[]{:S(2)}, u32[]{:S(2)}) collective-permute-start(bf16[120,1024]{1,0:T(8,128)(2,1)S(1)} %select_n.313), channel_id=1, source_target_pairs={{1,2},{3,4},{5,6},{2,1},{4,3},{6,5},{9,10},{11,12},{13,14},{10,9},... | collective-permute-start | bytes 737288 | tf_op jit(solution)/shard_map/ppermute | solution.py:54
  24.9 7.7 %collective-permute-start.4 = (bf16[4,2048]{1,0:T(4,128)(2,1)S(1)}, bf16[4,2048]{1,0:T(4,128)(2,1)S(1)}, u32[]{:S(2)}, u32[]{:S(2)}) collective-permute-start(bf16[4,2048]{1,0:T(4,128)(2,1)S(1)} %maximum_select_fusion.3), channel_id=1, source_target_pairs={{0,2},{1,3},{2,0},{3,1},{4,6},{5,7},{6,4},{7,5},{8,10},{9,11},{10,... | collective-permute-start | bytes 49160 | tf_op jit(solution)/shard_map/ppermute | solution.py:35
  32.6 8.5 %copy-start.2 = (bf16[1024,1024]{1,0:T(8,128)(2,1)S(1)}, bf16[1024,1024]{1,0:T(8,128)(2,1)}, u32[]{:S(2)}) copy-start(bf16[1024,1024]{1,0:T(8,128)(2,1)} %param.13) | copy-start | bytes 6291460
  32.6 8.5 %copy-start.24 = (bf16[480,1024]{1,0:T(8,128)(2,1)S(1)}, bf16[480,1024]{1,0:T(8,128)(2,1)}, u32[]{:S(2)}) copy-start(bf16[480,1024]{1,0:T(8,128)(2,1)} %broadcast_dynamic-update-slice_fusion) | copy-start | bytes 2949124
  32.6 7.2 %collective-permute-start.5 = (bf16[8,2048]{1,0:T(8,128)(2,1)S(1)}, bf16[8,2048]{1,0:T(8,128)(2,1)S(1)}, u32[]{:S(2)}, u32[]{:S(2)}) collective-permute-start(bf16[8,2048]{1,0:T(8,128)(2,1)S(1)} %maximum_select_fusion.2), channel_id=1, source_target_pairs={{0,4},{1,5},{2,6},{3,7},{4,0},{5,1},{6,2},{7,3},{8,12},{9,13},{10,... | collective-permute-start | bytes 98312 | tf_op jit(solution)/shard_map/ppermute | solution.py:35
  39.8 4.4 %collective-permute-start.6 = (bf16[16,2048]{1,0:T(8,128)(2,1)S(1)}, bf16[16,2048]{1,0:T(8,128)(2,1)S(1)}, u32[]{:S(2)}, u32[]{:S(2)}) collective-permute-start(bf16[16,2048]{1,0:T(8,128)(2,1)S(1)} %maximum_select_fusion.1), channel_id=1, source_target_pairs={{0,16},{8,24},{16,0},{24,8},{1,17},{9,25},{17,1},{25,9},{2,18},{10... | collective-permute-start | bytes 196616 | tf_op jit(solution)/shard_map/ppermute | solution.py:35
  61.5 2.6 %copy-start.3 = (bf16[1024,1024]{1,0:T(8,128)(2,1)S(1)}, bf16[1024,1024]{1,0:T(8,128)(2,1)}, u32[]{:S(2)}) copy-start(bf16[1024,1024]{1,0:T(8,128)(2,1)} %param.13) | copy-start | bytes 6291460
  70.4 3.9 %copy-start.14 = (f32[2,2,2,2,2,1,1024]{6,5,4,3,2,1,0:T(1,128)}, f32[2,2,2,2,2,1,1024]{6,5,4,3,2,1,0:T(1,128)S(1)}, u32[]{:S(2)}) copy-start(f32[2,2,2,2,2,1,1024]{6,5,4,3,2,1,0:T(1,128)S(1)} %get-tuple-element.32) | copy-start | bytes 393220
  72.4 6.6 %copy-start.11 = (f32[320,1024]{1,0:T(8,128)S(1)}, f32[320,1024]{1,0:T(8,128)}, u32[]{:S(2)}) copy-start(f32[320,1024]{1,0:T(8,128)} %fusion.4) | copy-start | bytes 3932164
  75.0 12.7 %collective-permute-start.8 = (bf16[120,1024]{1,0:T(8,128)(2,1)}, bf16[120,1024]{1,0:T(8,128)(2,1)}, u32[]{:S(2)}, u32[]{:S(2)}) collective-permute-start(bf16[120,1024]{1,0:T(8,128)(2,1)} %get-tuple-element.28), channel_id=1, source_target_pairs={{1,2},{3,4},{5,6},{2,1},{4,3},{6,5},{9,10},{11,12},{13,14},{10,9},... | collective-permute-start | bytes 737288 | tf_op jit(solution)/shard_map/ppermute | solution.py:54
  76.4 5.6 %collective-permute-start.7 = (bf16[184,1024]{1,0:T(8,128)(2,1)S(1)}, bf16[184,1024]{1,0:T(8,128)(2,1)S(1)}, u32[]{:S(2)}, u32[]{:S(2)}) collective-permute-start(bf16[184,1024]{1,0:T(8,128)(2,1)S(1)} %pad_maximum_fusion.1), channel_id=1, source_target_pairs={{0,1},{1,0},{2,3},{3,2},{4,5},{5,4},{6,7},{7,6},{8,9},{9,8},{10,11... | collective-permute-start | bytes 1130504 | tf_op jit(solution)/shard_map/ppermute | solution.py:51
  80.9 6.7 %copy-start.8 = (f32[320,1024]{1,0:T(8,128)}, f32[320,1024]{1,0:T(8,128)S(1)}, u32[]{:S(2)}) copy-start(f32[320,1024]{1,0:T(8,128)S(1)} %convolution_add_fusion) | copy-start | bytes 3932164
  82.0 0.8 copy-start.17
  86.2 0.7 copy-start.12
  87.7 3.0 %copy-start.9 = (f32[96,1024]{1,0:T(8,128)S(1)}, f32[96,1024]{1,0:T(8,128)}, u32[]{:S(2)}) copy-start(f32[96,1024]{1,0:T(8,128)} %get-tuple-element.21) | copy-start | bytes 1179652
  87.7 3.0 %copy-start.10 = (f32[96,1024]{1,0:T(8,128)S(1)}, f32[96,1024]{1,0:T(8,128)}, u32[]{:S(2)}) copy-start(f32[96,1024]{1,0:T(8,128)} %get-tuple-element.22) | copy-start | bytes 1179652
  90.7 3.1 %copy-start.6 = (bf16[1024,1024]{1,0:T(8,128)(2,1)S(1)}, bf16[1024,1024]{1,0:T(8,128)(2,1)}, u32[]{:S(2)}) copy-start(bf16[1024,1024]{1,0:T(8,128)(2,1)} %param.15) | copy-start | bytes 6291460
  90.7 3.1 %copy-start.21 = (bf16[128,1024]{1,0:T(8,128)(2,1)S(1)}, bf16[128,1024]{1,0:T(8,128)(2,1)}, u32[]{:S(2)}) copy-start(bf16[128,1024]{1,0:T(8,128)(2,1)} %get-tuple-element.6) | copy-start | bytes 786436
  91.6 9.9 %copy-start.13 = (f32[2,2,2,2,2,1024]{5,0,1,3,4,2:T(2,128)S(1)}, f32[2,2,2,2,2,1024]{5,0,1,3,4,2:T(2,128)}, u32[]{:S(2)}) copy-start(f32[2,2,2,2,2,1024]{5,0,1,3,4,2:T(2,128)} %copy-done.12) | copy-start | bytes 393220
  91.6 10.5 %copy-start.15 = (bf16[6,16,1024]{2,1,0:T(8,128)(2,1)S(1)}, bf16[6,16,1024]{2,1,0:T(8,128)(2,1)}, u32[]{:S(2)}) copy-start(bf16[6,16,1024]{2,1,0:T(8,128)(2,1)} %get-tuple-element.11) | copy-start | bytes 589828
  91.6 10.5 %copy-start.16 = (bf16[6,16,1024]{2,1,0:T(8,128)(2,1)S(1)}, bf16[6,16,1024]{2,1,0:T(8,128)(2,1)}, u32[]{:S(2)}) copy-start(bf16[6,16,1024]{2,1,0:T(8,128)(2,1)} %get-tuple-element.12) | copy-start | bytes 589828
  92.5 8.3 %collective-permute-start.9 = (bf16[128,1024]{1,0:T(8,128)(2,1)S(1)}, bf16[128,1024]{1,0:T(8,128)(2,1)S(1)}, u32[]{:S(2)}, u32[]{:S(2)}) collective-permute-start(bf16[128,1024]{1,0:T(8,128)(2,1)S(1)} %pad_maximum_fusion.3), channel_id=1, source_target_pairs={{0,8},{8,0},{16,24},{24,16},{1,9},{9,1},{17,25},{25,17},{2,10},{10... | collective-permute-start | bytes 786440 | tf_op jit(solution)/shard_map/ppermute | solution.py:51
  100.8 0.7 copy-start.22
  101.7 4.0 %collective-permute-start.10 = (f32[2,2,2,1024]{3,0,1,2:T(2,128)S(1)}, f32[2,2,2,1024]{3,0,1,2:T(2,128)S(1)}, u32[]{:S(2)}, u32[]{:S(2)}) collective-permute-start(f32[2,2,2,1024]{3,0,1,2:T(2,128)S(1)} %select_bitcast_fusion), channel_id=1, source_target_pairs={{0,2},{1,3},{2,0},{3,1},{4,6},{5,7},{6,4},{7,5},{8,10},{9,11},{10,... | collective-permute-start | bytes 98312 | tf_op jit(solution)/shard_map/ppermute | solution.py:35
  102.1 5.2 %collective-permute-start.13 = (bf16[96,1024]{1,0:T(8,128)(2,1)S(1)}, bf16[96,1024]{1,0:T(8,128)(2,1)S(1)}, u32[]{:S(2)}, u32[]{:S(2)}) collective-permute-start(bf16[96,1024]{1,0:T(8,128)(2,1)S(1)} %bitcast.96), channel_id=1, source_target_pairs={{8,16},{16,8},{9,17},{17,9},{10,18},{18,10},{11,19},{19,11},{12,20... | collective-permute-start | bytes 589832 | tf_op jit(solution)/shard_map/ppermute | solution.py:54
  105.7 4.7 %collective-permute-start.11 = (f32[2,2,1024]{2,0,1:T(2,128)S(1)}, f32[2,2,1024]{2,0,1:T(2,128)S(1)}, u32[]{:S(2)}, u32[]{:S(2)}) collective-permute-start(f32[2,2,1024]{2,0,1:T(2,128)S(1)} %select_bitcast_fusion.1), channel_id=1, source_target_pairs={{0,4},{1,5},{2,6},{3,7},{4,0},{5,1},{6,2},{7,3},{8,12},{9,13},{10,... | collective-permute-start | bytes 49160 | tf_op jit(solution)/shard_map/ppermute | solution.py:35
  108.3 8.0 %copy-start.4 = (bf16[1024,1024]{1,0:T(8,128)(2,1)S(1)}, bf16[1024,1024]{1,0:T(8,128)(2,1)}, u32[]{:S(2)}) copy-start(bf16[1024,1024]{1,0:T(8,128)(2,1)} %param.13) | copy-start | bytes 6291460
  110.4 4.3 %collective-permute-start.12 = (f32[2,1024]{1,0:T(2,128)S(1)}, f32[2,1024]{1,0:T(2,128)S(1)}, u32[]{:S(2)}, u32[]{:S(2)}) collective-permute-start(f32[2,1024]{1,0:T(2,128)S(1)} %select_bitcast_fusion.2), channel_id=1, source_target_pairs={{0,16},{8,24},{16,0},{24,8},{1,17},{9,25},{17,1},{25,9},{2,18},{10... | collective-permute-start | bytes 24584 | tf_op jit(solution)/shard_map/ppermute | solution.py:35
  115.6 1.3 %slice-start = ((f32[320,1024]{1,0:T(8,128)}), f32[128,1024]{1,0:T(8,128)S(1)}, s32[]{:S(2)}) async-start(f32[320,1024]{1,0:T(8,128)} %copy-done.8), calls=%async_computation | async-start | bytes 1048576 | tf_op jit(solution)/shard_map/slice | solution.py:348
  115.6 1.4 %copy-start.20 = (bf16[128,1024]{1,0:T(8,128)(2,1)S(1)}, bf16[128,1024]{1,0:T(8,128)(2,1)}, u32[]{:S(2)}) copy-start(bf16[128,1024]{1,0:T(8,128)(2,1)} %get-tuple-element.7) | copy-start | bytes 786436

commit v17 on v12

--- a/solution.py
+++ b/solution.py
@@ -385,20 +385,18 @@
         scatter = keep_part + partner(send_part, position)
     own_grads = scatter.reshape(2, 1, model_width)
 
-    own_given = given(0, tokens)
+    query_part = jnp.dot(query_grads, w_query.T, preferred_element_type=jnp.float32)
+    base = query_part + given(0, tokens)
     own_row = (lax.dynamic_slice_in_dim(wide_grads, own_local, 1, 1) + own_grads).astype(
         jnp.bfloat16
     )
-    own_row_given = jnp.dot(own_row[0], w_key.T, preferred_element_type=jnp.float32) + jnp.dot(
-        own_row[1], w_value.T, preferred_element_type=jnp.float32
-    )
-    own_given = lax.dynamic_update_slice_in_dim(own_given, own_row_given, own_local, 0)
-
-    grad_in = (
-        jnp.dot(query_grads, w_query.T, preferred_element_type=jnp.float32)
-        + own_given
-        + received.reshape(tokens, model_width)
-    )
+    own_row_given = (
+        lax.dynamic_slice_in_dim(query_part, own_local, 1, 0)
+        + jnp.dot(own_row[0], w_key.T, preferred_element_type=jnp.float32)
+        + jnp.dot(own_row[1], w_value.T, preferred_element_type=jnp.float32)
+    )
+    base = lax.dynamic_update_slice_in_dim(base, own_row_given, own_local, 0)
+    grad_in = base + received.reshape(tokens, model_width)
     grad_in = grad_in.astype(jnp.bfloat16).reshape(features.shape)
     return (layer_out, grad_in)
 

time: 121 us -> 125 us (1.033)
  matrix products: 28.1 us -> 30.4 us
  waiting for transfers between devices: 15.3 us -> 13.5 us
  local copies, waits for them, and re-layouts: 15.8 us -> 17.5 us
  starting transfers between devices: 26.2 us -> 27.7 us
    select_n x1 -> x2, other arithmetic: 0.02 us -> 2.99 us  [exchange(): got_second = lax.ppermute(jnp.where(even, to_lower, to_higher), axis, links)]
    dot_general x1, matrix products: 1.15 us -> 2.84 us  [shards(): jnp.dot(attended, w_out, preferred_element_type=jnp.float32)]
    reshape x1, local copies, waits for them, and re-layouts: 0.08 us -> 1.76 us  [shards(): from_left.astype(jnp.float32).reshape(strip_shape)]
    select_n x4 -> x3, other arithmetic: 3.61 us -> 2 us  [exchange(): first = jnp.where(even, to_higher, to_lower)]
    ppermute x6, starting transfers between devices: 13.2 us -> 14.8 us  [partner(): return lax.ppermute(x, axis, [(i, i ^ 1 << bit) for i in range(size)])]
    dot_general x1, matrix products: 3.13 us -> 1.82 us  [shards(): jnp.dot(query_grads, w_query.T, preferred_element_type=jnp.float32)]
    unnamed x62 -> x58, local copies, waits for them, and re-layouts: 3.3 us -> 3.19 us
  transfers between devices with their start and end apart: 14 -> 14, of which waited for: 6 -> 5; matrix products, arithmetic and copies ran while one was open for 23% -> 27% of each run, Pallas kernels for 0% -> 0%
where the time goes in v17:
time: 125 us
  matrix products  30.4 us (24%)
  starting transfers between devices  27.7 us (22%)
  local copies, waits for them, and re-layouts  17.5 us (14%)
  Pallas kernels  15.9 us (13%)
  other arithmetic  15.5 us (12%)
  waiting for transfers between devices  13.5 us (11%)
  between operations  4 us (3%)
    pallas_call x1, Pallas kernels, attention(): pl.pallas_call(functools.partial(attention_kernel, tokens, first, last),...  15.9 us
    ppermute x6, starting transfers between devices, partner(): return lax.ppermute(x, axis, [(i, i ^ 1 << bit) for i in range(size)])  14.8 us
    ppermute x4, starting transfers between devices, exchange(): got_first = lax.ppermute(first, axis, [(i, i ^ 1) for i in range(size)])  9.61 us
    ppermute x6, waiting for transfers between devices, partner(): return lax.ppermute(x, axis, [(i, i ^ 1 << bit) for i in range(size)])  8.32 us
    ppermute x4, waiting for transfers between devices, exchange(): got_first = lax.ppermute(first, axis, [(i, i ^ 1) for i in range(size)])  5.16 us
    dot_general x2, matrix products, contribution(): jnp.dot(rounded_grads[0, lo:hi], w_key.T, preferred_element_type=jnp.floa...  4.82 us
    dot_general x2, matrix products, contribution(): jnp.dot(rounded_grads[1, lo:hi], w_value.T, preferred_element_type=jnp.fl...  4.6 us
    dot_general x1, matrix products, shards(): jnp.dot(halo_features, w_value, preferred_element_type=jnp.float32)  4.08 us
  transfers between devices with their start and end apart: 14, of which 5 were waited for; matrix products, arithmetic and copies ran while one was open for 27% of the time, Pallas kernels for 0%

profile of v17, /device:TPU:0, one launch (start us, length us, event | category | flops | bytes accessed | tf_op | source)
XLA Modules:
  0.0 124.6 jit_solution(10923504953828264261)
XLA Ops:
  0.7 1.9 %broadcast_select_fusion.8 = (bf16[6,16,1024]{2,1,0:T(8,128)(2,1)S(1)}, bf16[6,16,1024]{2,1,0:T(8,128)(2,1)}) fusion(pred[]{:T(512)S(6)} %eq.68, bf16[8,16,1024]{2,1,0:T(8,128)(2,1)} %param.11), kind=kLoop, calls=%fused_computation.47 | loop fusion | flops 196608 | bytes 786433 | tf_op jit(solution)/shard_map/jit(_where)/select_n | solution.py:41
  3.2 1.2 dynamic_slice.16
  7.1 2.1 %convolution_convert_fusion.4.vo_ref = bf16[128,1024]{1,0:T(8,128)(2,1)S(1)} fusion(bf16[128,1024]{1,0:T(8,128)(2,1)} %bitcast.85, bf16[1024,1024]{1,0:T(8,128)(2,1)} %param.14), kind=kOutput, calls=%fused_computation.8 | convolution fusion | flops 268566528 | bytes 2621440 | tf_op jit(solution)/shard_map/dot_general | solution.py:212
  10.5 5.7 %collective-permute-start.1 = (bf16[98,1024]{1,0:T(8,128)(2,1)}, bf16[98,1024]{1,0:T(8,128)(2,1)S(1)}, u32[]{:S(2)}, u32[]{:S(2)}) collective-permute-start(bf16[98,1024]{1,0:T(8,128)(2,1)} %pad_maximum_fusion.4), channel_id=1, source_target_pairs={{0,8},{8,0},{16,24},{24,16},{1,9},{9,1},{17,25},{25,17},{2,10},{10... | collective-permute-start | bytes 602120 | tf_op jit(solution)/shard_map/ppermute | solution.py:45
  16.4 2.9 %convolution_convert_fusion.6.q_ref = bf16[128,1024]{1,0:T(8,128)(2,1)} fusion(bf16[128,1024]{1,0:T(8,128)(2,1)S(1)} %bitcast.87, bf16[1024,1024]{1,0:T(8,128)(2,1)} %param.12), kind=kOutput, calls=%fused_computation.10 | convolution fusion | flops 268566528 | bytes 2621440 | tf_op jit(solution)/shard_map/dot_general | solution.py:251
  19.3 2.5 %convolution_convert_fusion.3.g_ref = bf16[128,1024]{1,0:T(8,128)(2,1)} fusion(bf16[128,1024]{1,0:T(8,128)(2,1)} %bitcast.96, bf16[1024,1024]{1,0:T(8,128)(2,1)S(1)} %copy-done.3), kind=kOutput, calls=%fused_computation.7 | convolution fusion | flops 268566528 | bytes 2621440 | tf_op jit(solution)/shard_map/dot_general | solution.py:252
  22.1 1.0 copy-done.21
  23.5 0.9 or_convert_fusion.mask_ref
  25.4 3.4 %collective-permute-start.4 = (bf16[4,2048]{1,0:T(4,128)(2,1)S(1)}, bf16[4,2048]{1,0:T(4,128)(2,1)S(1)}, u32[]{:S(2)}, u32[]{:S(2)}) collective-permute-start(bf16[4,2048]{1,0:T(4,128)(2,1)S(1)} %maximum_select_fusion.3), channel_id=1, source_target_pairs={{0,2},{1,3},{2,0},{3,1},{4,6},{5,7},{6,4},{7,5},{8,10},{9,11},{10,... | collective-permute-start | bytes 49160 | tf_op jit(solution)/shard_map/ppermute | solution.py:35
  28.8 0.8 select_dynamic-update-slice_fusion.1
  29.6 0.8 select_dynamic-update-slice_fusion
  30.9 2.1 %collective-permute-done.4 = bf16[4,2048]{1,0:T(4,128)(2,1)S(1)} collective-permute-done((bf16[4,2048]{1,0:T(4,128)(2,1)S(1)}, bf16[4,2048]{1,0:T(4,128)(2,1)S(1)}, u32[]{:S(2)}, u32[]{:S(2)}) %collective-permute-start.4) | collective-permute-done | bytes 16416 | tf_op jit(solution)/shard_map/ppermute | solution.py:35
  33.1 3.8 %collective-permute-start.5 = (bf16[8,2048]{1,0:T(8,128)(2,1)S(1)}, bf16[8,2048]{1,0:T(8,128)(2,1)S(1)}, u32[]{:S(2)}, u32[]{:S(2)}) collective-permute-start(bf16[8,2048]{1,0:T(8,128)(2,1)S(1)} %maximum_select_fusion.2), channel_id=1, source_target_pairs={{0,4},{1,5},{2,6},{3,7},{4,0},{5,1},{6,2},{7,3},{8,12},{9,13},{10,... | collective-permute-start | bytes 98312 | tf_op jit(solution)/shard_map/ppermute | solution.py:35
  36.9 4.1 %convolution_convert_fusion.vh_ref = bf16[480,1024]{1,0:T(8,128)(2,1)} fusion(bf16[480,1024]{1,0:T(8,128)(2,1)} %broadcast_dynamic-update-slice_fusion, bf16[1024,1024]{1,0:T(8,128)(2,1)} %param.14), kind=kOutput, calls=%fused_computation.1 | convolution fusion | flops 1007124480 | bytes 4063232 | tf_op jit(solution)/shard_map/dot_general | solution.py:269
  41.0 1.3 %collective-permute-start.6 = (bf16[16,2048]{1,0:T(8,128)(2,1)S(1)}, bf16[16,2048]{1,0:T(8,128)(2,1)S(1)}, u32[]{:S(2)}, u32[]{:S(2)}) collective-permute-start(bf16[16,2048]{1,0:T(8,128)(2,1)S(1)} %maximum_select_fusion.1), channel_id=1, source_target_pairs={{0,16},{8,24},{16,0},{24,8},{1,17},{9,25},{17,1},{25,9},{2,18},{10... | collective-permute-start | bytes 196616 | tf_op jit(solution)/shard_map/ppermute | solution.py:35
  42.3 2.2 %convolution_convert_fusion.1.kh_ref = bf16[480,1024]{1,0:T(8,128)(2,1)} fusion(bf16[480,1024]{1,0:T(8,128)(2,1)S(1)} %copy-done.22, bf16[1024,1024]{1,0:T(8,128)(2,1)S(1)} %copy-done), kind=kOutput, calls=%fused_computation.2 | convolution fusion | flops 1007124480 | bytes 4063232 | tf_op jit(solution)/shard_map/dot_general | solution.py:266
  44.5 1.0 collective-permute-done.6
  46.8 15.9 %shard_map.122 = (bf16[128,1024]{1,0:T(8,128)(2,1)}, bf16[128,1024]{1,0:T(8,128)(2,1)}, bf16[2,640,1024]{2,1,0:T(8,128)(2,1)}, f32[2,160,1024]{2,1,0:T(8,128)}) custom-call(bf16[128,1024]{1,0:T(8,128)(2,1)} %convolution_convert_fusion.6.q_ref, bf16[128,1024]{1,0:T(8,128)(2,1)} %copy-done.14, bf16[480,1024]{1,0:T(8,128)(2,1)} %convolution_convert_fusion.1.kh_ref, ...), custom_call_target="tpu_custom_call" | custom-call | flops 2013265920 | bytes 8978432 | tf_op jit(solution)/shard_map/pallas_call | solution.py:151
  62.7 1.8 %fusion.8 = f32[240,1024]{1,0:T(8,128)S(1)} fusion(bf16[1024,1024]{1,0:T(8,128)(2,1)S(1)} %copy-done, bf16[2,640,1024]{2,1,0:T(8,128)(2,1)} %get-tuple-element.8), kind=kOutput, calls=%fused_computation.24 | convolution fusion | flops 503316480 | bytes 3571712 | tf_op jit(solution)/shard_map/dot_general | solution.py:331
  64.5 3.1 %fusion.2 = f32[320,1024]{1,0:T(8,128)} fusion(bf16[1024,1024]{1,0:T(8,128)(2,1)S(1)} %copy-done, bf16[2,640,1024]{2,1,0:T(8,128)(2,1)} %get-tuple-element.8), kind=kOutput, calls=%fused_computation.15 | convolution fusion | flops 671088640 | bytes 4063232 | tf_op jit(solution)/shard_map/dot_general | solution.py:331
  67.5 1.7 %slice.144 = f32[2,32,1024]{2,1,0:T(8,128)} slice(f32[2,160,1024]{2,1,0:T(8,128)} %get-tuple-element.9), slice={[0:2], [128:160], [0:1024]} | slice | bytes 524288 | tf_op jit(solution)/shard_map/slice | solution.py:343
  69.2 1.1 reshape.187
  71.6 2.6 %fusion = bf16[240,1024]{1,0:T(8,128)(2,1)S(1)} fusion(f32[240,1024]{1,0:T(8,128)S(1)} %fusion.8, bf16[1024,1024]{1,0:T(8,128)(2,1)} %param.14, bf16[2,640,1024]{2,1,0:T(8,128)(2,1)} %get-tuple-element.8), kind=kOutput, calls=%fused_computation.5 | convolution fusion | flops 503808000 | bytes 4063232 | tf_op jit(solution)/shard_map/dot_general | solution.py:333
  74.3 0.7 broadcast_select_fusion.4
  75.0 1.3 %collective-permute-start.8 = (bf16[120,1024]{1,0:T(8,128)(2,1)}, bf16[120,1024]{1,0:T(8,128)(2,1)}, u32[]{:S(2)}, u32[]{:S(2)}) collective-permute-start(bf16[120,1024]{1,0:T(8,128)(2,1)} %get-tuple-element.27), channel_id=1, source_target_pairs={{1,2},{3,4},{5,6},{2,1},{4,3},{6,5},{9,10},{11,12},{13,14},{10,9},... | collective-permute-start | bytes 737288 | tf_op jit(solution)/shard_map/ppermute | solution.py:47
  76.4 2.6 %collective-permute-start.7 = (bf16[184,1024]{1,0:T(8,128)(2,1)S(1)}, bf16[184,1024]{1,0:T(8,128)(2,1)S(1)}, u32[]{:S(2)}, u32[]{:S(2)}) collective-permute-start(bf16[184,1024]{1,0:T(8,128)(2,1)S(1)} %pad_maximum_fusion.1), channel_id=1, source_target_pairs={{0,1},{1,0},{2,3},{3,2},{4,5},{5,4},{6,7},{7,6},{8,9},{9,8},{10,11... | collective-permute-start | bytes 1130504 | tf_op jit(solution)/shard_map/ppermute | solution.py:45
  78.9 2.0 %convolution_add_fusion = f32[320,1024]{1,0:T(8,128)S(1)} fusion(f32[320,1024]{1,0:T(8,128)S(1)} %copy-done.9, bf16[1024,1024]{1,0:T(8,128)(2,1)S(1)} %copy-done.1, bf16[2,640,1024]{2,1,0:T(8,128)(2,1)} %get-tuple-element.8), kind=kOutput, calls=%fused_computation.3 | convolution fusion | flops 671416320 | bytes 5373952 | tf_op jit(solution)/shard_map/dot_general | solution.py:333
  80.9 1.0 fusion.16
  81.9 0.7 copy-done.12
  82.7 0.7 reshape.188
  83.4 1.3 %bitcast_add_fusion.1 = f32[2,2,2,2,2,1024]{5,0,1,3,4,2:T(2,128)S(1)} fusion(f32[2,2,2,2,2,1024]{5,4,3,2,1,0:T(2,128)} %reshape.188, pred[]{:T(512)S(6)} %eq.83, f32[2,2,2,2,2,1,1024]{6,5,4,3,2,1,0:T(1,128)} %copy-done.11, f32[2,2,2,2,2,1,1024]{6,5,4,3,2,1,0:T(1,128)} %copy-done.10), kind=kLoop, calls=%fused_computation.54 | loop fusion | flops 65536 | bytes 524289 | tf_op jit(solution)/shard_map/add | solution.py:357
  85.4 1.5 %select_n.364 = f32[16,1024]{1,0:T(8,128)} reshape(f32[2,2,1,2,2,1024]{5,4,3,1,0,2:T(2,128)} %copy.19) | data formatting | bytes 131072 | tf_op jit(solution)/shard_map/jit(_where)/select_n | solution.py:75
  86.9 1.5 %subtract_convert_fusion.1 = (bf16[16,1024]{1,0:T(8,128)(2,1)}, bf16[16,1024]{1,0:T(8,128)(2,1)}) fusion(f32[16,1024]{1,0:T(8,128)} %select_n.364), kind=kLoop, calls=%fused_computation.61 | loop fusion | flops 65536 | bytes 131072 | tf_op jit(solution)/shard_map/convert_element_type | solution.py:180
  88.4 1.9 %broadcast_select_fusion.3 = (bf16[120,1024]{1,0:T(8,128)(2,1)}, bf16[120,1024]{1,0:T(8,128)(2,1)}) fusion(bf16[120,1024]{1,0:T(8,128)(2,1)} %collective-permute-done.8, pred[]{:T(512)S(6)} %eq.69, bf16[184,1024]{1,0:T(8,128)(2,1)} %copy-done.12), kind=kLoop, calls=%fused_computation.41 | loop fusion | flops 245760 | bytes 983041 | tf_op jit(solution)/shard_map/jit(_where)/select_n | solution.py:52
  90.3 1.8 %reshape.190 = bf16[20,6,1024]{2,1,0:T(8,128)(2,1)} reshape(bf16[120,1024]{1,0:T(8,128)(2,1)} %get-tuple-element.25) | data formatting | bytes 491520 | tf_op jit(solution)/shard_map/reshape | solution.py:359
  92.1 1.8 %reshape.191 = bf16[20,6,1024]{2,1,0:T(8,128)(2,1)} reshape(bf16[120,1024]{1,0:T(8,128)(2,1)} %get-tuple-element.26) | data formatting | bytes 491520 | tf_op jit(solution)/shard_map/reshape | solution.py:361
  93.9 2.3 %broadcast_select_fusion.6 = (bf16[6,16,1024]{2,1,0:T(8,128)(2,1)}, bf16[6,16,1024]{2,1,0:T(8,128)(2,1)S(1)}, bf16[6,16,1024]{2,1,0:T(8,128)(2,1)S(1)}) fusion(pred[]{:T(512)S(6)} %eq.68, f32[6,16,1024]{2,1,0:T(8,128)} %bitcast.89, bf16[20,6,1024]{2,1,0:T(8,128)(2,1)} %reshape.191, bf16[20,6,1024]{2,1,0:T(8,128)(2,1)} %reshape.190, f32[6,16,1024]{2,1,0:T(8,128)} %bitcast.88), kind=kLoop, calls=%fused_computation.45 | loop fusion | flops 1081344 | bytes 1867777 | tf_op jit(solution)/shard_map/jit(_where)/select_n | solution.py:47
  96.2 1.3 %collective-permute-start.9 = (bf16[128,1024]{1,0:T(8,128)(2,1)S(1)}, bf16[128,1024]{1,0:T(8,128)(2,1)S(1)}, u32[]{:S(2)}, u32[]{:S(2)}) collective-permute-start(bf16[128,1024]{1,0:T(8,128)(2,1)S(1)} %pad_maximum_fusion.3), channel_id=1, source_target_pairs={{0,8},{8,0},{16,24},{24,16},{1,9},{9,1},{17,25},{25,17},{2,10},{10... | collective-permute-start | bytes 786440 | tf_op jit(solution)/shard_map/ppermute | solution.py:45
  97.5 1.8 %slice_add_fusion = (f32[128,1024]{1,0:T(8,128)}, f32[128,1024]{1,0:T(8,128)}) fusion(f32[320,1024]{1,0:T(8,128)S(1)} %convolution_add_fusion, bf16[128,1024]{1,0:T(8,128)(2,1)S(1)} %copy-done.17, bf16[1024,1024]{1,0:T(8,128)(2,1)S(1)} %copy-done.4), kind=kOutput, calls=%fused_computation.19 | convolution fusion | flops 268566528 | bytes 3932160 | tf_op jit(solution)/shard_map/dot_general | solution.py:388
  99.3 5.2 %collective-permute-done.9 = bf16[128,1024]{1,0:T(8,128)(2,1)S(1)} collective-permute-done((bf16[128,1024]{1,0:T(8,128)(2,1)S(1)}, bf16[128,1024]{1,0:T(8,128)(2,1)S(1)}, u32[]{:S(2)}, u32[]{:S(2)}) %collective-permute-start.9) | collective-permute-done | bytes 262176 | tf_op jit(solution)/shard_map/ppermute | solution.py:45
  105.8 2.8 %convolution_convert_fusion.2 = bf16[128,1024]{1,0:T(8,128)(2,1)} fusion(bf16[128,1024]{1,0:T(8,128)(2,1)} %get-tuple-element.6, bf16[1024,1024]{1,0:T(8,128)(2,1)} %param.15), kind=kOutput, calls=%fused_computation.6 | convolution fusion | flops 268566528 | bytes 2621440 | tf_op jit(solution)/shard_map/dot_general | solution.py:323
  109.4 0.9 collective-permute-start.11
  110.4 3.7 %collective-permute-done.11 = f32[2,2,1024]{2,0,1:T(2,128)S(1)} collective-permute-done((f32[2,2,1024]{2,0,1:T(2,128)S(1)}, f32[2,2,1024]{2,0,1:T(2,128)S(1)}, u32[]{:S(2)}, u32[]{:S(2)}) %collective-permute-start.11) | collective-permute-done | bytes 16416 | tf_op jit(solution)/shard_map/ppermute | solution.py:35
  114.2 4.9 %collective-permute-start.12 = (f32[2,1024]{1,0:T(2,128)S(1)}, f32[2,1024]{1,0:T(2,128)S(1)}, u32[]{:S(2)}, u32[]{:S(2)}) collective-permute-start(f32[2,1024]{1,0:T(2,128)S(1)} %select_bitcast_fusion.2), channel_id=1, source_target_pairs={{0,16},{8,24},{16,0},{24,8},{1,17},{9,25},{17,1},{25,9},{2,18},{10... | collective-permute-start | bytes 24584 | tf_op jit(solution)/shard_map/ppermute | solution.py:35
  119.2 1.5 %collective-permute-done.12 = f32[2,1024]{1,0:T(2,128)S(1)} collective-permute-done((f32[2,1024]{1,0:T(2,128)S(1)}, f32[2,1024]{1,0:T(2,128)S(1)}, u32[]{:S(2)}, u32[]{:S(2)}) %collective-permute-start.12) | collective-permute-done | bytes 8224 | tf_op jit(solution)/shard_map/ppermute | solution.py:35
  120.7 0.9 add_convert_fusion
  121.6 1.5 %convolution_add_fusion.3 = f32[1,1024]{1,0:T(1,128)S(1)} fusion(bf16[1024,1024]{1,0:T(8,128)(2,1)S(1)} %copy-done, bf16[2,1,1024]{2,1,0:T(2,128)(2,1)S(1)} %add_convert_fusion, f32[128,1024]{1,0:T(8,128)} %get-tuple-element.38, s32[]{:T(128)S(6)} %select_n.315), kind=kOutput, calls=%fused_computation.12 | convolution fusion | flops 2098176 | bytes 2109444 | tf_op jit(solution)/shard_map/dot_general | solution.py:395
  123.8 0.8 fusion.6
  (124 shorter events, 10.6 us)
Async XLA Ops:
  0.6 8.6 %copy-start = (bf16[1024,1024]{1,0:T(8,128)(2,1)S(1)}, bf16[1024,1024]{1,0:T(8,128)(2,1)}, u32[]{:S(2)}) copy-start(bf16[1024,1024]{1,0:T(8,128)(2,1)} %param.13) | copy-start | bytes 6291460
  0.6 8.6 %copy-start.5 = (bf16[8,16,1024]{2,1,0:T(8,128)(2,1)S(1)}, bf16[8,16,1024]{2,1,0:T(8,128)(2,1)}, u32[]{:S(2)}) copy-start(bf16[8,16,1024]{2,1,0:T(8,128)(2,1)} %param.11) | copy-start | bytes 786436
  2.5 19.4 %collective-permute-start = (bf16[96,1024]{1,0:T(8,128)(2,1)}, bf16[96,1024]{1,0:T(8,128)(2,1)S(1)}, u32[]{:S(2)}, u32[]{:S(2)}) collective-permute-start(bf16[96,1024]{1,0:T(8,128)(2,1)} %bitcast.1), channel_id=1, source_target_pairs={{8,16},{16,8},{9,17},{17,9},{10,18},{18,10},{11,19},{19,11},{12,20... | collective-permute-start | bytes 589832 | tf_op jit(solution)/shard_map/ppermute | solution.py:47
  9.3 10.0 %copy-start.13 = (bf16[128,1024]{1,0:T(8,128)(2,1)}, bf16[128,1024]{1,0:T(8,128)(2,1)S(1)}, u32[]{:S(2)}) copy-start(bf16[128,1024]{1,0:T(8,128)(2,1)S(1)} %convolution_convert_fusion.4.vo_ref) | copy-start | bytes 786436
  9.7 12.1 %copy-start.14 = (bf16[128,1024]{1,0:T(8,128)(2,1)}, bf16[128,1024]{1,0:T(8,128)(2,1)S(1)}, u32[]{:S(2)}) copy-start(bf16[128,1024]{1,0:T(8,128)(2,1)S(1)} %convolution_convert_fusion.5.ko_ref) | copy-start | bytes 786436
  10.5 11.3 %collective-permute-start.1 = (bf16[98,1024]{1,0:T(8,128)(2,1)}, bf16[98,1024]{1,0:T(8,128)(2,1)S(1)}, u32[]{:S(2)}, u32[]{:S(2)}) collective-permute-start(bf16[98,1024]{1,0:T(8,128)(2,1)} %pad_maximum_fusion.4), channel_id=1, source_target_pairs={{0,8},{8,0},{16,24},{24,16},{1,9},{9,1},{17,25},{25,17},{2,10},{10... | collective-permute-start | bytes 602120 | tf_op jit(solution)/shard_map/ppermute | solution.py:45
  16.4 2.9 %copy-start.3 = (bf16[1024,1024]{1,0:T(8,128)(2,1)S(1)}, bf16[1024,1024]{1,0:T(8,128)(2,1)}, u32[]{:S(2)}) copy-start(bf16[1024,1024]{1,0:T(8,128)(2,1)} %param.15) | copy-start | bytes 6291460
  16.4 5.4 %copy-start.23 = (s32[640]{0:T(1024)S(1)}, s32[640]{0:T(1024)}, u32[]{:S(2)}) copy-start(s32[640]{0:T(1024)} %constant.137.clone) | copy-start | bytes 7684
  16.4 5.4 %copy-start.24 = (s32[640]{0:T(1024)S(1)}, s32[640]{0:T(1024)}, u32[]{:S(2)}) copy-start(s32[640]{0:T(1024)} %constant.136.clone) | copy-start | bytes 7684
  22.0 1.5 %copy-start.25 = (pred[640]{0:T(1024)(128)(4,1)S(1)}, pred[640]{0:T(1024)(128)(4,1)}, u32[]{:S(2)}) copy-start(pred[640]{0:T(1024)(128)(4,1)} %constant.155) | copy-start | bytes 1924
  22.0 1.4 %copy-start.26 = (pred[640]{0:T(1024)(128)(4,1)S(1)}, pred[640]{0:T(1024)(128)(4,1)}, u32[]{:S(2)}) copy-start(pred[640]{0:T(1024)(128)(4,1)} %constant.154) | copy-start | bytes 1924
  22.1 1.0 copy-start.21
  23.1 2.1 %copy-start.27 = (s32[32]{0:T(128)S(1)}, s32[32]{0:T(128)}, u32[]{:S(2)}) copy-start(s32[32]{0:T(128)} %constant.157) | copy-start | bytes 388
  23.4 1.9 %collective-permute-start.3 = (bf16[124,1024]{1,0:T(8,128)(2,1)S(1)}, bf16[124,1024]{1,0:T(8,128)(2,1)S(1)}, u32[]{:S(2)}, u32[]{:S(2)}) collective-permute-start(bf16[124,1024]{1,0:T(8,128)(2,1)S(1)} %pad_maximum_fusion.2), channel_id=1, source_target_pairs={{0,1},{1,0},{2,3},{3,2},{4,5},{5,4},{6,7},{7,6},{8,9},{9,8},{10,11... | collective-permute-start | bytes 761864 | tf_op jit(solution)/shard_map/ppermute | solution.py:45
  24.5 4.3 %collective-permute-start.2 = (bf16[120,1024]{1,0:T(8,128)(2,1)S(1)}, bf16[120,1024]{1,0:T(8,128)(2,1)S(1)}, u32[]{:S(2)}, u32[]{:S(2)}) collective-permute-start(bf16[120,1024]{1,0:T(8,128)(2,1)S(1)} %select_n.322), channel_id=1, source_target_pairs={{1,2},{3,4},{5,6},{2,1},{4,3},{6,5},{9,10},{11,12},{13,14},{10,9},... | collective-permute-start | bytes 737288 | tf_op jit(solution)/shard_map/ppermute | solution.py:47
  25.4 7.7 %collective-permute-start.4 = (bf16[4,2048]{1,0:T(4,128)(2,1)S(1)}, bf16[4,2048]{1,0:T(4,128)(2,1)S(1)}, u32[]{:S(2)}, u32[]{:S(2)}) collective-permute-start(bf16[4,2048]{1,0:T(4,128)(2,1)S(1)} %maximum_select_fusion.3), channel_id=1, source_target_pairs={{0,2},{1,3},{2,0},{3,1},{4,6},{5,7},{6,4},{7,5},{8,10},{9,11},{10,... | collective-permute-start | bytes 49160 | tf_op jit(solution)/shard_map/ppermute | solution.py:35
  33.1 9.2 %copy-start.22 = (bf16[480,1024]{1,0:T(8,128)(2,1)S(1)}, bf16[480,1024]{1,0:T(8,128)(2,1)}, u32[]{:S(2)}) copy-start(bf16[480,1024]{1,0:T(8,128)(2,1)} %broadcast_dynamic-update-slice_fusion) | copy-start | bytes 2949124
  33.1 7.9 %collective-permute-start.5 = (bf16[8,2048]{1,0:T(8,128)(2,1)S(1)}, bf16[8,2048]{1,0:T(8,128)(2,1)S(1)}, u32[]{:S(2)}, u32[]{:S(2)}) collective-permute-start(bf16[8,2048]{1,0:T(8,128)(2,1)S(1)} %maximum_select_fusion.2), channel_id=1, source_target_pairs={{0,4},{1,5},{2,6},{3,7},{4,0},{5,1},{6,2},{7,3},{8,12},{9,13},{10,... | collective-permute-start | bytes 98312 | tf_op jit(solution)/shard_map/ppermute | solution.py:35
  41.0 4.4 %collective-permute-start.6 = (bf16[16,2048]{1,0:T(8,128)(2,1)S(1)}, bf16[16,2048]{1,0:T(8,128)(2,1)S(1)}, u32[]{:S(2)}, u32[]{:S(2)}) collective-permute-start(bf16[16,2048]{1,0:T(8,128)(2,1)S(1)} %maximum_select_fusion.1), channel_id=1, source_target_pairs={{0,16},{8,24},{16,0},{24,8},{1,17},{9,25},{17,1},{25,9},{2,18},{10... | collective-permute-start | bytes 196616 | tf_op jit(solution)/shard_map/ppermute | solution.py:35
  70.5 0.7 copy-start.10
  70.6 0.8 copy-start.11
  71.6 7.3 %copy-start.1 = (bf16[1024,1024]{1,0:T(8,128)(2,1)S(1)}, bf16[1024,1024]{1,0:T(8,128)(2,1)}, u32[]{:S(2)}) copy-start(bf16[1024,1024]{1,0:T(8,128)(2,1)} %param.14) | copy-start | bytes 6291460
  71.6 7.3 %copy-start.9 = (f32[320,1024]{1,0:T(8,128)S(1)}, f32[320,1024]{1,0:T(8,128)}, u32[]{:S(2)}) copy-start(f32[320,1024]{1,0:T(8,128)} %fusion.2) | copy-start | bytes 3932164
  75.0 13.4 %collective-permute-start.8 = (bf16[120,1024]{1,0:T(8,128)(2,1)}, bf16[120,1024]{1,0:T(8,128)(2,1)}, u32[]{:S(2)}, u32[]{:S(2)}) collective-permute-start(bf16[120,1024]{1,0:T(8,128)(2,1)} %get-tuple-element.27), channel_id=1, source_target_pairs={{1,2},{3,4},{5,6},{2,1},{4,3},{6,5},{9,10},{11,12},{13,14},{10,9},... | collective-permute-start | bytes 737288 | tf_op jit(solution)/shard_map/ppermute | solution.py:47
  76.4 5.5 %collective-permute-start.7 = (bf16[184,1024]{1,0:T(8,128)(2,1)S(1)}, bf16[184,1024]{1,0:T(8,128)(2,1)S(1)}, u32[]{:S(2)}, u32[]{:S(2)}) collective-permute-start(bf16[184,1024]{1,0:T(8,128)(2,1)S(1)} %pad_maximum_fusion.1), channel_id=1, source_target_pairs={{0,1},{1,0},{2,3},{3,2},{4,5},{5,4},{6,7},{7,6},{8,9},{9,8},{10,11... | collective-permute-start | bytes 1130504 | tf_op jit(solution)/shard_map/ppermute | solution.py:45
  81.9 0.7 copy-start.12
  93.8 2.3 %copy-start.19 = (bf16[16,1024]{1,0:T(8,128)(2,1)S(1)}, bf16[16,1024]{1,0:T(8,128)(2,1)}, u32[]{:S(2)}) copy-start(bf16[16,1024]{1,0:T(8,128)(2,1)} %get-tuple-element.13) | copy-start | bytes 98308
  93.8 2.3 %copy-start.20 = (bf16[16,1024]{1,0:T(8,128)(2,1)S(1)}, bf16[16,1024]{1,0:T(8,128)(2,1)}, u32[]{:S(2)}) copy-start(bf16[16,1024]{1,0:T(8,128)(2,1)} %get-tuple-element.14) | copy-start | bytes 98308
  93.9 3.7 %copy-start.4 = (bf16[1024,1024]{1,0:T(8,128)(2,1)S(1)}, bf16[1024,1024]{1,0:T(8,128)(2,1)}, u32[]{:S(2)}) copy-start(bf16[1024,1024]{1,0:T(8,128)(2,1)} %param.12) | copy-start | bytes 6291460
  93.9 3.7 %copy-start.17 = (bf16[128,1024]{1,0:T(8,128)(2,1)S(1)}, bf16[128,1024]{1,0:T(8,128)(2,1)}, u32[]{:S(2)}) copy-start(bf16[128,1024]{1,0:T(8,128)(2,1)} %get-tuple-element.7) | copy-start | bytes 786436
  96.2 8.3 %collective-permute-start.9 = (bf16[128,1024]{1,0:T(8,128)(2,1)S(1)}, bf16[128,1024]{1,0:T(8,128)(2,1)S(1)}, u32[]{:S(2)}, u32[]{:S(2)}) collective-permute-start(bf16[128,1024]{1,0:T(8,128)(2,1)S(1)} %pad_maximum_fusion.3), channel_id=1, source_target_pairs={{0,8},{8,0},{16,24},{24,16},{1,9},{9,1},{17,25},{25,17},{2,10},{10... | collective-permute-start | bytes 786440 | tf_op jit(solution)/shard_map/ppermute | solution.py:45
  99.3 9.4 %copy-start.18 = (bf16[6,16,1024]{2,1,0:T(8,128)(2,1)S(1)}, bf16[6,16,1024]{2,1,0:T(8,128)(2,1)}, u32[]{:S(2)}) copy-start(bf16[6,16,1024]{2,1,0:T(8,128)(2,1)} %get-tuple-element.10) | copy-start | bytes 589828
  104.5 0.7 copy-start.15
  105.2 5.1 %copy-start.16 = (bf16[128,1024]{1,0:T(8,128)(2,1)S(1)}, bf16[128,1024]{1,0:T(8,128)(2,1)}, u32[]{:S(2)}) copy-start(bf16[128,1024]{1,0:T(8,128)(2,1)} %copy-done.15) | copy-start | bytes 786436
  105.2 13.9 %copy-start.6 = (bf16[20,6,1024]{2,1,0:T(8,128)(2,1)S(1)}, bf16[20,6,1024]{2,1,0:T(8,128)(2,1)}, u32[]{:S(2)}) copy-start(bf16[20,6,1024]{2,1,0:T(8,128)(2,1)} %reshape.190) | copy-start | bytes 737284
  105.2 13.9 %copy-start.7 = (bf16[20,6,1024]{2,1,0:T(8,128)(2,1)S(1)}, bf16[20,6,1024]{2,1,0:T(8,128)(2,1)}, u32[]{:S(2)}) copy-start(bf16[20,6,1024]{2,1,0:T(8,128)(2,1)} %reshape.191) | copy-start | bytes 737284
  105.4 4.0 %collective-permute-start.10 = (f32[2,2,2,1024]{3,0,1,2:T(2,128)S(1)}, f32[2,2,2,1024]{3,0,1,2:T(2,128)S(1)}, u32[]{:S(2)}, u32[]{:S(2)}) collective-permute-start(f32[2,2,2,1024]{3,0,1,2:T(2,128)S(1)} %select_bitcast_fusion), channel_id=1, source_target_pairs={{0,2},{1,3},{2,0},{3,1},{4,6},{5,7},{6,4},{7,5},{8,10},{9,11},{10,... | collective-permute-start | bytes 98312 | tf_op jit(solution)/shard_map/ppermute | solution.py:35
  108.7 1.6 %collective-permute-start.13 = (bf16[96,1024]{1,0:T(8,128)(2,1)S(1)}, bf16[96,1024]{1,0:T(8,128)(2,1)S(1)}, u32[]{:S(2)}, u32[]{:S(2)}) collective-permute-start(bf16[96,1024]{1,0:T(8,128)(2,1)S(1)} %bitcast.99), channel_id=1, source_target_pairs={{8,16},{16,8},{9,17},{17,9},{10,18},{18,10},{11,19},{19,11},{12,20... | collective-permute-start | bytes 589832 | tf_op jit(solution)/shard_map/ppermute | solution.py:47
  109.4 4.7 %collective-permute-start.11 = (f32[2,2,1024]{2,0,1:T(2,128)S(1)}, f32[2,2,1024]{2,0,1:T(2,128)S(1)}, u32[]{:S(2)}, u32[]{:S(2)}) collective-permute-start(f32[2,2,1024]{2,0,1:T(2,128)S(1)} %select_bitcast_fusion.1), channel_id=1, source_target_pairs={{0,4},{1,5},{2,6},{3,7},{4,0},{5,1},{6,2},{7,3},{8,12},{9,13},{10,... | collective-permute-start | bytes 49160 | tf_op jit(solution)/shard_map/ppermute | solution.py:35
  110.4 12.7 %copy-start.2 = (bf16[1024,1024]{1,0:T(8,128)(2,1)S(1)}, bf16[1024,1024]{1,0:T(8,128)(2,1)}, u32[]{:S(2)}) copy-start(bf16[1024,1024]{1,0:T(8,128)(2,1)} %param.14) | copy-start | bytes 6291460
  114.2 6.6 %collective-permute-start.12 = (f32[2,1024]{1,0:T(2,128)S(1)}, f32[2,1024]{1,0:T(2,128)S(1)}, u32[]{:S(2)}, u32[]{:S(2)}) collective-permute-start(f32[2,1024]{1,0:T(2,128)S(1)} %select_bitcast_fusion.2), channel_id=1, source_target_pairs={{0,16},{8,24},{16,0},{24,8},{1,17},{9,25},{17,1},{25,9},{2,18},{10... | collective-permute-start | bytes 24584 | tf_op jit(solution)/shard_map/ppermute | solution.py:35
  121.6 2.1 %copy-start.8 = (f32[128,1024]{1,0:T(8,128)S(1)}, f32[128,1024]{1,0:T(8,128)}, u32[]{:S(2)}) copy-start(f32[128,1024]{1,0:T(8,128)} %get-tuple-element.37) | copy-start | bytes 1572868

commit v18 on v12

--- a/solution.py
+++ b/solution.py
@@ -308,7 +308,7 @@
         & (cell_cols < start_cols + KW)
     )
     key_kind = jnp.asarray(kind)[None, :]
-    keep = ((inside & (key_kind == 0)) | (key_kind == 1)).astype(jnp.float32)
+    keep = ((inside & (key_kind == 0)) | (key_kind == 1)).astype(jnp.bfloat16)
 
     attended, query_grads, rounded_grads, wide_grads = attention(
         queries,

time: 121 us -> 121 us (level)
  no operation moved by 1% of the time
where the time goes in v18:
time: 121 us; the launch traced here: 120 us
  matrix products  28.1 us (23%)
  starting transfers between devices  26.2 us (22%)
  Pallas kernels  16.1 us (13%)
  local copies, waits for them, and re-layouts  15.8 us (13%)
  waiting for transfers between devices  15.3 us (13%)
  other arithmetic  14.8 us (12%)
  between operations  4.04 us (3%)
    pallas_call x1, Pallas kernels, attention(): pl.pallas_call(functools.partial(attention_kernel, tokens, first, last),...  16.1 us
    ppermute x6, starting transfers between devices, partner(): return lax.ppermute(x, axis, [(i, i ^ 1 << bit) for i in range(size)])  13.2 us
    ppermute x4, starting transfers between devices, exchange(): got_first = lax.ppermute(first, axis, [(i, i ^ 1) for i in range(size)])  9.62 us
    ppermute x6, waiting for transfers between devices, partner(): return lax.ppermute(x, axis, [(i, i ^ 1 << bit) for i in range(size)])  9.45 us
    ppermute x4, waiting for transfers between devices, exchange(): got_first = lax.ppermute(first, axis, [(i, i ^ 1) for i in range(size)])  5.83 us
    dot_general x2, matrix products, contribution(): jnp.dot(rounded_grads[0, lo:hi], w_key.T, preferred_element_type=jnp.floa...  5.74 us
    dot_general x2, matrix products, contribution(): jnp.dot(rounded_grads[1, lo:hi], w_value.T, preferred_element_type=jnp.fl...  3.84 us
    select_n x4, other arithmetic, exchange(): first = jnp.where(even, to_higher, to_lower)  3.61 us
  transfers between devices with their start and end apart: 14, of which 6 were waited for; matrix products, arithmetic and copies ran while one was open for 23% of the time, Pallas kernels for 0%

profile of v18, /device:TPU:0, one launch (start us, length us, event | category | flops | bytes accessed | tf_op | source)
XLA Modules:
  0.0 120.3 jit_solution(5318338816854733905)
XLA Ops:
  0.7 1.9 %broadcast_select_fusion.8 = (bf16[6,16,1024]{2,1,0:T(8,128)(2,1)S(1)}, bf16[6,16,1024]{2,1,0:T(8,128)(2,1)}) fusion(pred[]{:T(512)S(6)} %eq.68, bf16[8,16,1024]{2,1,0:T(8,128)(2,1)} %param.11), kind=kLoop, calls=%fused_computation.45 | loop fusion | flops 196608 | bytes 786433 | tf_op jit(solution)/shard_map/jit(_where)/select_n | solution.py:41
  3.2 1.2 %dynamic_slice.13 = s32[1]{0:T(128)} dynamic-slice(s32[32]{0:T(128)} %param.16, s32[]{:T(128)S(6)} %select_n.311), dynamic_slice_sizes={1} | dynamic-slice | bytes 12 | tf_op jit(solution)/shard_map/jit(dynamic_index_in_dim)/dynamic_slice | solution.py:217
  7.1 1.5 %convolution_convert_fusion.4.vo_ref = bf16[128,1024]{1,0:T(8,128)(2,1)S(1)} fusion(bf16[128,1024]{1,0:T(8,128)(2,1)} %bitcast.83, bf16[1024,1024]{1,0:T(8,128)(2,1)S(1)} %copy-done), kind=kOutput, calls=%fused_computation.11 | convolution fusion | flops 268566528 | bytes 2621440 | tf_op jit(solution)/shard_map/dot_general | solution.py:212
  10.0 5.7 %collective-permute-start.1 = (bf16[98,1024]{1,0:T(8,128)(2,1)}, bf16[98,1024]{1,0:T(8,128)(2,1)S(1)}, u32[]{:S(2)}, u32[]{:S(2)}) collective-permute-start(bf16[98,1024]{1,0:T(8,128)(2,1)} %pad_maximum_fusion.4), channel_id=1, source_target_pairs={{0,8},{8,0},{16,24},{24,16},{1,9},{9,1},{17,25},{25,17},{2,10},{10... | collective-permute-start | bytes 602120 | tf_op jit(solution)/shard_map/ppermute | solution.py:45
  15.9 2.9 %convolution_convert_fusion.6.q_ref = bf16[128,1024]{1,0:T(8,128)(2,1)} fusion(bf16[128,1024]{1,0:T(8,128)(2,1)S(1)} %bitcast.85, bf16[1024,1024]{1,0:T(8,128)(2,1)} %param.12), kind=kOutput, calls=%fused_computation.13 | convolution fusion | flops 268566528 | bytes 2621440 | tf_op jit(solution)/shard_map/dot_general | solution.py:251
  18.8 2.5 %convolution_convert_fusion.3.g_ref = bf16[128,1024]{1,0:T(8,128)(2,1)} fusion(bf16[128,1024]{1,0:T(8,128)(2,1)} %bitcast.96, bf16[1024,1024]{1,0:T(8,128)(2,1)S(1)} %copy-done.5), kind=kOutput, calls=%fused_computation.10 | convolution fusion | flops 268566528 | bytes 2621440 | tf_op jit(solution)/shard_map/dot_general | solution.py:252
  21.6 1.0 copy-done.23
  23.0 0.9 or_convert_fusion.mask_ref
  24.8 3.4 %collective-permute-start.4 = (bf16[4,2048]{1,0:T(4,128)(2,1)S(1)}, bf16[4,2048]{1,0:T(4,128)(2,1)S(1)}, u32[]{:S(2)}, u32[]{:S(2)}) collective-permute-start(bf16[4,2048]{1,0:T(4,128)(2,1)S(1)} %maximum_select_fusion.3), channel_id=1, source_target_pairs={{0,2},{1,3},{2,0},{3,1},{4,6},{5,7},{6,4},{7,5},{8,10},{9,11},{10,... | collective-permute-start | bytes 49160 | tf_op jit(solution)/shard_map/ppermute | solution.py:35
  28.2 0.8 select_dynamic-update-slice_fusion.1
  29.0 0.8 select_dynamic-update-slice_fusion
  30.4 2.1 %collective-permute-done.4 = bf16[4,2048]{1,0:T(4,128)(2,1)S(1)} collective-permute-done((bf16[4,2048]{1,0:T(4,128)(2,1)S(1)}, bf16[4,2048]{1,0:T(4,128)(2,1)S(1)}, u32[]{:S(2)}, u32[]{:S(2)}) %collective-permute-start.4) | collective-permute-done | bytes 16416 | tf_op jit(solution)/shard_map/ppermute | solution.py:35
  32.5 3.8 %collective-permute-start.5 = (bf16[8,2048]{1,0:T(8,128)(2,1)S(1)}, bf16[8,2048]{1,0:T(8,128)(2,1)S(1)}, u32[]{:S(2)}, u32[]{:S(2)}) collective-permute-start(bf16[8,2048]{1,0:T(8,128)(2,1)S(1)} %maximum_select_fusion.2), channel_id=1, source_target_pairs={{0,4},{1,5},{2,6},{3,7},{4,0},{5,1},{6,2},{7,3},{8,12},{9,13},{10,... | collective-permute-start | bytes 98312 | tf_op jit(solution)/shard_map/ppermute | solution.py:35
  36.4 3.4 %convolution_convert_fusion.vh_ref = bf16[480,1024]{1,0:T(8,128)(2,1)} fusion(bf16[480,1024]{1,0:T(8,128)(2,1)} %broadcast_dynamic-update-slice_fusion, bf16[1024,1024]{1,0:T(8,128)(2,1)S(1)} %copy-done), kind=kOutput, calls=%fused_computation.1 | convolution fusion | flops 1007124480 | bytes 4063232 | tf_op jit(solution)/shard_map/dot_general | solution.py:269
  39.7 1.3 %collective-permute-start.6 = (bf16[16,2048]{1,0:T(8,128)(2,1)S(1)}, bf16[16,2048]{1,0:T(8,128)(2,1)S(1)}, u32[]{:S(2)}, u32[]{:S(2)}) collective-permute-start(bf16[16,2048]{1,0:T(8,128)(2,1)S(1)} %maximum_select_fusion.1), channel_id=1, source_target_pairs={{0,16},{8,24},{16,0},{24,8},{1,17},{9,25},{17,1},{25,9},{2,18},{10... | collective-permute-start | bytes 196616 | tf_op jit(solution)/shard_map/ppermute | solution.py:35
  41.0 2.2 %convolution_convert_fusion.1.kh_ref = bf16[480,1024]{1,0:T(8,128)(2,1)} fusion(bf16[480,1024]{1,0:T(8,128)(2,1)S(1)} %copy-done.24, bf16[1024,1024]{1,0:T(8,128)(2,1)S(1)} %copy-done.2), kind=kOutput, calls=%fused_computation.2 | convolution fusion | flops 1007124480 | bytes 4063232 | tf_op jit(solution)/shard_map/dot_general | solution.py:266
  43.2 0.9 collective-permute-done.6
  45.5 16.1 %shard_map.122 = (bf16[128,1024]{1,0:T(8,128)(2,1)}, bf16[128,1024]{1,0:T(8,128)(2,1)}, bf16[2,640,1024]{2,1,0:T(8,128)(2,1)}, f32[2,160,1024]{2,1,0:T(8,128)}) custom-call(bf16[128,1024]{1,0:T(8,128)(2,1)} %convolution_convert_fusion.6.q_ref, bf16[128,1024]{1,0:T(8,128)(2,1)} %copy-done.19, bf16[480,1024]{1,0:T(8,128)(2,1)} %convolution_convert_fusion.1.kh_ref, ...), custom_call_target="tpu_custom_call" | custom-call | flops 2013265920 | bytes 8978432 | tf_op jit(solution)/shard_map/pallas_call | solution.py:151
  61.6 2.6 %fusion.9 = f32[240,1024]{1,0:T(8,128)S(1)} fusion(bf16[1024,1024]{1,0:T(8,128)(2,1)} %param.13, bf16[2,640,1024]{2,1,0:T(8,128)(2,1)} %get-tuple-element.8), kind=kOutput, calls=%fused_computation.22 | convolution fusion | flops 503316480 | bytes 3571712 | tf_op jit(solution)/shard_map/dot_general | solution.py:331
  64.3 3.1 %fusion.4 = f32[320,1024]{1,0:T(8,128)} fusion(bf16[1024,1024]{1,0:T(8,128)(2,1)S(1)} %copy-done.3, bf16[2,640,1024]{2,1,0:T(8,128)(2,1)} %get-tuple-element.8), kind=kOutput, calls=%fused_computation.16 | convolution fusion | flops 671088640 | bytes 4063232 | tf_op jit(solution)/shard_map/dot_general | solution.py:331
  67.4 1.0 slice.144
  68.4 0.8 reshape.188
  69.2 1.3 %fusion.20 = (f32[2,2,2,2,2,1,1024]{6,5,4,3,2,1,0:T(1,128)S(1)}, f32[2,2,2,2,2,1,1024]{6,5,4,3,2,1,0:T(1,128)S(1)}) fusion(f32[2,2,2,2,2,2,1024]{6,5,4,3,2,1,0:T(2,128)} %reshape.188), kind=kLoop, calls=%fused_computation.90 | loop fusion | bytes 524288 | tf_op jit(solution)/shard_map/slice | solution.py:73
  70.7 0.8 copy.17
  71.5 1.0 select_n.354
  72.5 1.9 %fusion = bf16[240,1024]{1,0:T(8,128)(2,1)S(1)} fusion(f32[240,1024]{1,0:T(8,128)S(1)} %fusion.9, bf16[1024,1024]{1,0:T(8,128)(2,1)S(1)} %copy-done, bf16[2,640,1024]{2,1,0:T(8,128)(2,1)} %get-tuple-element.8), kind=kOutput, calls=%fused_computation.5 | convolution fusion | flops 503808000 | bytes 4063232 | tf_op jit(solution)/shard_map/dot_general | solution.py:333
  75.1 1.3 %collective-permute-start.8 = (bf16[120,1024]{1,0:T(8,128)(2,1)}, bf16[120,1024]{1,0:T(8,128)(2,1)}, u32[]{:S(2)}, u32[]{:S(2)}) collective-permute-start(bf16[120,1024]{1,0:T(8,128)(2,1)} %get-tuple-element.28), channel_id=1, source_target_pairs={{1,2},{3,4},{5,6},{2,1},{4,3},{6,5},{9,10},{11,12},{13,14},{10,9},... | collective-permute-start | bytes 737288 | tf_op jit(solution)/shard_map/ppermute | solution.py:47
  76.5 2.6 %collective-permute-start.7 = (bf16[184,1024]{1,0:T(8,128)(2,1)S(1)}, bf16[184,1024]{1,0:T(8,128)(2,1)S(1)}, u32[]{:S(2)}, u32[]{:S(2)}) collective-permute-start(bf16[184,1024]{1,0:T(8,128)(2,1)S(1)} %pad_maximum_fusion.1), channel_id=1, source_target_pairs={{0,1},{1,0},{2,3},{3,2},{4,5},{5,4},{6,7},{7,6},{8,9},{9,8},{10,11... | collective-permute-start | bytes 1130504 | tf_op jit(solution)/shard_map/ppermute | solution.py:45
  79.0 2.0 %convolution_add_fusion = f32[320,1024]{1,0:T(8,128)S(1)} fusion(f32[320,1024]{1,0:T(8,128)S(1)} %copy-done.11, bf16[1024,1024]{1,0:T(8,128)(2,1)S(1)} %copy-done, bf16[2,640,1024]{2,1,0:T(8,128)(2,1)} %get-tuple-element.8), kind=kOutput, calls=%fused_computation.3 | convolution fusion | flops 671416320 | bytes 5373952 | tf_op jit(solution)/shard_map/dot_general | solution.py:333
  81.0 1.0 fusion.19
  82.1 0.8 copy-done.17
  83.5 1.6 %reshape.189 = f32[2,2,2,2,2,1024]{5,4,3,2,1,0:T(2,128)} reshape(f32[32,1024]{1,0:T(8,128)} %convert_add_fusion.1) | data formatting | bytes 262144 | tf_op jit(solution)/shard_map/reshape | solution.py:357
  85.1 1.2 %bitcast_add_fusion = f32[2,2,2,2,2,1024]{5,0,1,3,4,2:T(2,128)S(1)} fusion(f32[2,2,2,2,2,1024]{5,4,3,2,1,0:T(2,128)} %reshape.189, pred[]{:T(512)S(6)} %eq.83, f32[2,2,2,2,2,1,1024]{6,5,4,3,2,1,0:T(1,128)} %copy-done.14, f32[2,2,2,2,2,1,1024]{6,5,4,3,2,1,0:T(1,128)S(1)} %get-tuple-element.31), kind=kLoop, calls=%fused_computation.52 | loop fusion | flops 65536 | bytes 524289 | tf_op jit(solution)/shard_map/add | solution.py:357
  87.8 1.9 %broadcast_select_fusion.3 = (bf16[120,1024]{1,0:T(8,128)(2,1)S(1)}, bf16[120,1024]{1,0:T(8,128)(2,1)}) fusion(bf16[120,1024]{1,0:T(8,128)(2,1)} %collective-permute-done.8, pred[]{:T(512)S(6)} %eq.69, bf16[184,1024]{1,0:T(8,128)(2,1)} %copy-done.17), kind=kLoop, calls=%fused_computation.39 | loop fusion | flops 245760 | bytes 983041 | tf_op jit(solution)/shard_map/jit(_where)/select_n | solution.py:52
  89.7 1.0 reshape.192
  90.8 0.9 broadcast_select_fusion.7
  91.7 0.8 pad_maximum_fusion.3
  92.6 1.3 %collective-permute-start.9 = (bf16[128,1024]{1,0:T(8,128)(2,1)S(1)}, bf16[128,1024]{1,0:T(8,128)(2,1)S(1)}, u32[]{:S(2)}, u32[]{:S(2)}) collective-permute-start(bf16[128,1024]{1,0:T(8,128)(2,1)S(1)} %pad_maximum_fusion.3), channel_id=1, source_target_pairs={{0,8},{8,0},{16,24},{24,16},{1,9},{9,1},{17,25},{25,17},{2,10},{10... | collective-permute-start | bytes 786440 | tf_op jit(solution)/shard_map/ppermute | solution.py:45
  93.9 1.2 convolution_convert_fusion.2
  95.1 5.8 %collective-permute-done.9 = bf16[128,1024]{1,0:T(8,128)(2,1)S(1)} collective-permute-done((bf16[128,1024]{1,0:T(8,128)(2,1)S(1)}, bf16[128,1024]{1,0:T(8,128)(2,1)S(1)}, u32[]{:S(2)}, u32[]{:S(2)}) %collective-permute-start.9) | collective-permute-done | bytes 262176 | tf_op jit(solution)/shard_map/ppermute | solution.py:45
  102.9 2.8 %collective-permute-done.10 = f32[2,2,2,1024]{3,0,1,2:T(2,128)S(1)} collective-permute-done((f32[2,2,2,1024]{3,0,1,2:T(2,128)S(1)}, f32[2,2,2,1024]{3,0,1,2:T(2,128)S(1)}, u32[]{:S(2)}, u32[]{:S(2)}) %collective-permute-start.10) | collective-permute-done | bytes 32800 | tf_op jit(solution)/shard_map/ppermute | solution.py:35
  105.8 1.6 %collective-permute-start.11 = (f32[2,2,1024]{2,0,1:T(2,128)S(1)}, f32[2,2,1024]{2,0,1:T(2,128)S(1)}, u32[]{:S(2)}, u32[]{:S(2)}) collective-permute-start(f32[2,2,1024]{2,0,1:T(2,128)S(1)} %select_bitcast_fusion.1), channel_id=1, source_target_pairs={{0,4},{1,5},{2,6},{3,7},{4,0},{5,1},{6,2},{7,3},{8,12},{9,13},{10,... | collective-permute-start | bytes 49160 | tf_op jit(solution)/shard_map/ppermute | solution.py:35
  107.4 1.0 broadcast_select_fusion.11
  108.4 2.1 %collective-permute-done.11 = f32[2,2,1024]{2,0,1:T(2,128)S(1)} collective-permute-done((f32[2,2,1024]{2,0,1:T(2,128)S(1)}, f32[2,2,1024]{2,0,1:T(2,128)S(1)}, u32[]{:S(2)}, u32[]{:S(2)}) %collective-permute-start.11) | collective-permute-done | bytes 16416 | tf_op jit(solution)/shard_map/ppermute | solution.py:35
  110.5 2.6 %collective-permute-start.12 = (f32[2,1024]{1,0:T(2,128)S(1)}, f32[2,1024]{1,0:T(2,128)S(1)}, u32[]{:S(2)}, u32[]{:S(2)}) collective-permute-start(f32[2,1024]{1,0:T(2,128)S(1)} %select_bitcast_fusion.2), channel_id=1, source_target_pairs={{0,16},{8,24},{16,0},{24,8},{1,17},{9,25},{17,1},{25,9},{2,18},{10... | collective-permute-start | bytes 24584 | tf_op jit(solution)/shard_map/ppermute | solution.py:35
  113.3 1.5 %collective-permute-done.12 = f32[2,1024]{1,0:T(2,128)S(1)} collective-permute-done((f32[2,1024]{1,0:T(2,128)S(1)}, f32[2,1024]{1,0:T(2,128)S(1)}, u32[]{:S(2)}, u32[]{:S(2)}) %collective-permute-start.12) | collective-permute-done | bytes 8224 | tf_op jit(solution)/shard_map/ppermute | solution.py:35
  114.8 0.9 add_convert_fusion
  117.1 3.1 %fusion.2 = bf16[128,1024]{1,0:T(8,128)(2,1)} fusion(f32[128,1024]{1,0:T(8,128)S(1)} %bitcast.86, f32[128,1024]{1,0:T(8,128)S(1)} %dynamic_update_slice.3, bf16[128,1024]{1,0:T(8,128)(2,1)S(1)} %copy-done.20, bf16[1024,1024]{1,0:T(8,128)(2,1)} %param.12), kind=kOutput, calls=%fused_computation.8 | convolution fusion | flops 268828672 | bytes 3670016 | tf_op jit(solution)/shard_map/dot_general | solution.py:398
  (130 shorter events, 12.4 us)
Async XLA Ops:
  0.6 6.5 %copy-start = (bf16[1024,1024]{1,0:T(8,128)(2,1)S(1)}, bf16[1024,1024]{1,0:T(8,128)(2,1)}, u32[]{:S(2)}) copy-start(bf16[1024,1024]{1,0:T(8,128)(2,1)} %param.14) | copy-start | bytes 6291460
  0.6 8.0 %copy-start.7 = (bf16[8,16,1024]{2,1,0:T(8,128)(2,1)S(1)}, bf16[8,16,1024]{2,1,0:T(8,128)(2,1)}, u32[]{:S(2)}) copy-start(bf16[8,16,1024]{2,1,0:T(8,128)(2,1)} %param.11) | copy-start | bytes 786436
  2.5 18.9 %collective-permute-start = (bf16[96,1024]{1,0:T(8,128)(2,1)}, bf16[96,1024]{1,0:T(8,128)(2,1)S(1)}, u32[]{:S(2)}, u32[]{:S(2)}) collective-permute-start(bf16[96,1024]{1,0:T(8,128)(2,1)} %bitcast.1), channel_id=1, source_target_pairs={{8,16},{16,8},{9,17},{17,9},{10,18},{18,10},{11,19},{19,11},{12,20... | collective-permute-start | bytes 589832 | tf_op jit(solution)/shard_map/ppermute | solution.py:47
  7.1 1.7 %copy-start.1 = (bf16[1024,1024]{1,0:T(8,128)(2,1)S(1)}, bf16[1024,1024]{1,0:T(8,128)(2,1)}, u32[]{:S(2)}) copy-start(bf16[1024,1024]{1,0:T(8,128)(2,1)} %param.13) | copy-start | bytes 6291460
  8.8 10.0 %copy-start.18 = (bf16[128,1024]{1,0:T(8,128)(2,1)}, bf16[128,1024]{1,0:T(8,128)(2,1)S(1)}, u32[]{:S(2)}) copy-start(bf16[128,1024]{1,0:T(8,128)(2,1)S(1)} %convolution_convert_fusion.4.vo_ref) | copy-start | bytes 786436
  9.2 12.1 %copy-start.19 = (bf16[128,1024]{1,0:T(8,128)(2,1)}, bf16[128,1024]{1,0:T(8,128)(2,1)S(1)}, u32[]{:S(2)}) copy-start(bf16[128,1024]{1,0:T(8,128)(2,1)S(1)} %convolution_convert_fusion.5.ko_ref) | copy-start | bytes 786436
  10.0 11.3 %collective-permute-start.1 = (bf16[98,1024]{1,0:T(8,128)(2,1)}, bf16[98,1024]{1,0:T(8,128)(2,1)S(1)}, u32[]{:S(2)}, u32[]{:S(2)}) collective-permute-start(bf16[98,1024]{1,0:T(8,128)(2,1)} %pad_maximum_fusion.4), channel_id=1, source_target_pairs={{0,8},{8,0},{16,24},{24,16},{1,9},{9,1},{17,25},{25,17},{2,10},{10... | collective-permute-start | bytes 602120 | tf_op jit(solution)/shard_map/ppermute | solution.py:45
  15.9 2.9 %copy-start.5 = (bf16[1024,1024]{1,0:T(8,128)(2,1)S(1)}, bf16[1024,1024]{1,0:T(8,128)(2,1)}, u32[]{:S(2)}) copy-start(bf16[1024,1024]{1,0:T(8,128)(2,1)} %param.15) | copy-start | bytes 6291460
  15.9 5.4 %copy-start.25 = (s32[640]{0:T(1024)S(1)}, s32[640]{0:T(1024)}, u32[]{:S(2)}) copy-start(s32[640]{0:T(1024)} %constant.137.clone) | copy-start | bytes 7684
  15.9 5.4 %copy-start.26 = (s32[640]{0:T(1024)S(1)}, s32[640]{0:T(1024)}, u32[]{:S(2)}) copy-start(s32[640]{0:T(1024)} %constant.136.clone) | copy-start | bytes 7684
  21.5 1.5 %copy-start.27 = (pred[640]{0:T(1024)(128)(4,1)S(1)}, pred[640]{0:T(1024)(128)(4,1)}, u32[]{:S(2)}) copy-start(pred[640]{0:T(1024)(128)(4,1)} %constant.155) | copy-start | bytes 1924
  21.5 1.4 %copy-start.28 = (pred[640]{0:T(1024)(128)(4,1)S(1)}, pred[640]{0:T(1024)(128)(4,1)}, u32[]{:S(2)}) copy-start(pred[640]{0:T(1024)(128)(4,1)} %constant.154) | copy-start | bytes 1924
  21.6 1.0 copy-start.23
  22.6 2.1 %copy-start.29 = (s32[32]{0:T(128)S(1)}, s32[32]{0:T(128)}, u32[]{:S(2)}) copy-start(s32[32]{0:T(128)} %constant.157) | copy-start | bytes 388
  22.9 1.8 %collective-permute-start.3 = (bf16[124,1024]{1,0:T(8,128)(2,1)S(1)}, bf16[124,1024]{1,0:T(8,128)(2,1)S(1)}, u32[]{:S(2)}, u32[]{:S(2)}) collective-permute-start(bf16[124,1024]{1,0:T(8,128)(2,1)S(1)} %pad_maximum_fusion.2), channel_id=1, source_target_pairs={{0,1},{1,0},{2,3},{3,2},{4,5},{5,4},{6,7},{7,6},{8,9},{9,8},{10,11... | collective-permute-start | bytes 761864 | tf_op jit(solution)/shard_map/ppermute | solution.py:45
  23.9 4.3 %collective-permute-start.2 = (bf16[120,1024]{1,0:T(8,128)(2,1)S(1)}, bf16[120,1024]{1,0:T(8,128)(2,1)S(1)}, u32[]{:S(2)}, u32[]{:S(2)}) collective-permute-start(bf16[120,1024]{1,0:T(8,128)(2,1)S(1)} %select_n.321), channel_id=1, source_target_pairs={{1,2},{3,4},{5,6},{2,1},{4,3},{6,5},{9,10},{11,12},{13,14},{10,9},... | collective-permute-start | bytes 737288 | tf_op jit(solution)/shard_map/ppermute | solution.py:47
  24.8 7.7 %collective-permute-start.4 = (bf16[4,2048]{1,0:T(4,128)(2,1)S(1)}, bf16[4,2048]{1,0:T(4,128)(2,1)S(1)}, u32[]{:S(2)}, u32[]{:S(2)}) collective-permute-start(bf16[4,2048]{1,0:T(4,128)(2,1)S(1)} %maximum_select_fusion.3), channel_id=1, source_target_pairs={{0,2},{1,3},{2,0},{3,1},{4,6},{5,7},{6,4},{7,5},{8,10},{9,11},{10,... | collective-permute-start | bytes 49160 | tf_op jit(solution)/shard_map/ppermute | solution.py:35
  32.5 8.5 %copy-start.2 = (bf16[1024,1024]{1,0:T(8,128)(2,1)S(1)}, bf16[1024,1024]{1,0:T(8,128)(2,1)}, u32[]{:S(2)}) copy-start(bf16[1024,1024]{1,0:T(8,128)(2,1)} %param.13) | copy-start | bytes 6291460
  32.5 8.5 %copy-start.24 = (bf16[480,1024]{1,0:T(8,128)(2,1)S(1)}, bf16[480,1024]{1,0:T(8,128)(2,1)}, u32[]{:S(2)}) copy-start(bf16[480,1024]{1,0:T(8,128)(2,1)} %broadcast_dynamic-update-slice_fusion) | copy-start | bytes 2949124
  32.5 7.2 %collective-permute-start.5 = (bf16[8,2048]{1,0:T(8,128)(2,1)S(1)}, bf16[8,2048]{1,0:T(8,128)(2,1)S(1)}, u32[]{:S(2)}, u32[]{:S(2)}) collective-permute-start(bf16[8,2048]{1,0:T(8,128)(2,1)S(1)} %maximum_select_fusion.2), channel_id=1, source_target_pairs={{0,4},{1,5},{2,6},{3,7},{4,0},{5,1},{6,2},{7,3},{8,12},{9,13},{10,... | collective-permute-start | bytes 98312 | tf_op jit(solution)/shard_map/ppermute | solution.py:35
  39.7 4.4 %collective-permute-start.6 = (bf16[16,2048]{1,0:T(8,128)(2,1)S(1)}, bf16[16,2048]{1,0:T(8,128)(2,1)S(1)}, u32[]{:S(2)}, u32[]{:S(2)}) collective-permute-start(bf16[16,2048]{1,0:T(8,128)(2,1)S(1)} %maximum_select_fusion.1), channel_id=1, source_target_pairs={{0,16},{8,24},{16,0},{24,8},{1,17},{9,25},{17,1},{25,9},{2,18},{10... | collective-permute-start | bytes 196616 | tf_op jit(solution)/shard_map/ppermute | solution.py:35
  61.6 2.6 %copy-start.3 = (bf16[1024,1024]{1,0:T(8,128)(2,1)S(1)}, bf16[1024,1024]{1,0:T(8,128)(2,1)}, u32[]{:S(2)}) copy-start(bf16[1024,1024]{1,0:T(8,128)(2,1)} %param.13) | copy-start | bytes 6291460
  70.5 3.9 %copy-start.14 = (f32[2,2,2,2,2,1,1024]{6,5,4,3,2,1,0:T(1,128)}, f32[2,2,2,2,2,1,1024]{6,5,4,3,2,1,0:T(1,128)S(1)}, u32[]{:S(2)}) copy-start(f32[2,2,2,2,2,1,1024]{6,5,4,3,2,1,0:T(1,128)S(1)} %get-tuple-element.32) | copy-start | bytes 393220
  72.5 6.6 %copy-start.11 = (f32[320,1024]{1,0:T(8,128)S(1)}, f32[320,1024]{1,0:T(8,128)}, u32[]{:S(2)}) copy-start(f32[320,1024]{1,0:T(8,128)} %fusion.4) | copy-start | bytes 3932164
  75.1 12.7 %collective-permute-start.8 = (bf16[120,1024]{1,0:T(8,128)(2,1)}, bf16[120,1024]{1,0:T(8,128)(2,1)}, u32[]{:S(2)}, u32[]{:S(2)}) collective-permute-start(bf16[120,1024]{1,0:T(8,128)(2,1)} %get-tuple-element.28), channel_id=1, source_target_pairs={{1,2},{3,4},{5,6},{2,1},{4,3},{6,5},{9,10},{11,12},{13,14},{10,9},... | collective-permute-start | bytes 737288 | tf_op jit(solution)/shard_map/ppermute | solution.py:47
  76.5 5.6 %collective-permute-start.7 = (bf16[184,1024]{1,0:T(8,128)(2,1)S(1)}, bf16[184,1024]{1,0:T(8,128)(2,1)S(1)}, u32[]{:S(2)}, u32[]{:S(2)}) collective-permute-start(bf16[184,1024]{1,0:T(8,128)(2,1)S(1)} %pad_maximum_fusion.1), channel_id=1, source_target_pairs={{0,1},{1,0},{2,3},{3,2},{4,5},{5,4},{6,7},{7,6},{8,9},{9,8},{10,11... | collective-permute-start | bytes 1130504 | tf_op jit(solution)/shard_map/ppermute | solution.py:45
  81.0 6.7 %copy-start.8 = (f32[320,1024]{1,0:T(8,128)}, f32[320,1024]{1,0:T(8,128)S(1)}, u32[]{:S(2)}) copy-start(f32[320,1024]{1,0:T(8,128)S(1)} %convolution_add_fusion) | copy-start | bytes 3932164
  82.1 0.8 copy-start.17
  86.3 0.7 copy-start.12
  87.8 3.0 %copy-start.9 = (f32[96,1024]{1,0:T(8,128)S(1)}, f32[96,1024]{1,0:T(8,128)}, u32[]{:S(2)}) copy-start(f32[96,1024]{1,0:T(8,128)} %get-tuple-element.21) | copy-start | bytes 1179652
  87.8 3.0 %copy-start.10 = (f32[96,1024]{1,0:T(8,128)S(1)}, f32[96,1024]{1,0:T(8,128)}, u32[]{:S(2)}) copy-start(f32[96,1024]{1,0:T(8,128)} %get-tuple-element.22) | copy-start | bytes 1179652
  90.8 3.1 %copy-start.6 = (bf16[1024,1024]{1,0:T(8,128)(2,1)S(1)}, bf16[1024,1024]{1,0:T(8,128)(2,1)}, u32[]{:S(2)}) copy-start(bf16[1024,1024]{1,0:T(8,128)(2,1)} %param.15) | copy-start | bytes 6291460
  90.8 3.1 %copy-start.21 = (bf16[128,1024]{1,0:T(8,128)(2,1)S(1)}, bf16[128,1024]{1,0:T(8,128)(2,1)}, u32[]{:S(2)}) copy-start(bf16[128,1024]{1,0:T(8,128)(2,1)} %get-tuple-element.6) | copy-start | bytes 786436
  91.7 9.9 %copy-start.13 = (f32[2,2,2,2,2,1024]{5,0,1,3,4,2:T(2,128)S(1)}, f32[2,2,2,2,2,1024]{5,0,1,3,4,2:T(2,128)}, u32[]{:S(2)}) copy-start(f32[2,2,2,2,2,1024]{5,0,1,3,4,2:T(2,128)} %copy-done.12) | copy-start | bytes 393220
  91.7 10.5 %copy-start.15 = (bf16[6,16,1024]{2,1,0:T(8,128)(2,1)S(1)}, bf16[6,16,1024]{2,1,0:T(8,128)(2,1)}, u32[]{:S(2)}) copy-start(bf16[6,16,1024]{2,1,0:T(8,128)(2,1)} %get-tuple-element.11) | copy-start | bytes 589828
  91.7 10.5 %copy-start.16 = (bf16[6,16,1024]{2,1,0:T(8,128)(2,1)S(1)}, bf16[6,16,1024]{2,1,0:T(8,128)(2,1)}, u32[]{:S(2)}) copy-start(bf16[6,16,1024]{2,1,0:T(8,128)(2,1)} %get-tuple-element.12) | copy-start | bytes 589828
  92.6 8.3 %collective-permute-start.9 = (bf16[128,1024]{1,0:T(8,128)(2,1)S(1)}, bf16[128,1024]{1,0:T(8,128)(2,1)S(1)}, u32[]{:S(2)}, u32[]{:S(2)}) collective-permute-start(bf16[128,1024]{1,0:T(8,128)(2,1)S(1)} %pad_maximum_fusion.3), channel_id=1, source_target_pairs={{0,8},{8,0},{16,24},{24,16},{1,9},{9,1},{17,25},{25,17},{2,10},{10... | collective-permute-start | bytes 786440 | tf_op jit(solution)/shard_map/ppermute | solution.py:45
  100.9 0.7 copy-start.22
  101.8 4.0 %collective-permute-start.10 = (f32[2,2,2,1024]{3,0,1,2:T(2,128)S(1)}, f32[2,2,2,1024]{3,0,1,2:T(2,128)S(1)}, u32[]{:S(2)}, u32[]{:S(2)}) collective-permute-start(f32[2,2,2,1024]{3,0,1,2:T(2,128)S(1)} %select_bitcast_fusion), channel_id=1, source_target_pairs={{0,2},{1,3},{2,0},{3,1},{4,6},{5,7},{6,4},{7,5},{8,10},{9,11},{10,... | collective-permute-start | bytes 98312 | tf_op jit(solution)/shard_map/ppermute | solution.py:35
  102.2 5.2 %collective-permute-start.13 = (bf16[96,1024]{1,0:T(8,128)(2,1)S(1)}, bf16[96,1024]{1,0:T(8,128)(2,1)S(1)}, u32[]{:S(2)}, u32[]{:S(2)}) collective-permute-start(bf16[96,1024]{1,0:T(8,128)(2,1)S(1)} %bitcast.98), channel_id=1, source_target_pairs={{8,16},{16,8},{9,17},{17,9},{10,18},{18,10},{11,19},{19,11},{12,20... | collective-permute-start | bytes 589832 | tf_op jit(solution)/shard_map/ppermute | solution.py:47
  105.8 4.7 %collective-permute-start.11 = (f32[2,2,1024]{2,0,1:T(2,128)S(1)}, f32[2,2,1024]{2,0,1:T(2,128)S(1)}, u32[]{:S(2)}, u32[]{:S(2)}) collective-permute-start(f32[2,2,1024]{2,0,1:T(2,128)S(1)} %select_bitcast_fusion.1), channel_id=1, source_target_pairs={{0,4},{1,5},{2,6},{3,7},{4,0},{5,1},{6,2},{7,3},{8,12},{9,13},{10,... | collective-permute-start | bytes 49160 | tf_op jit(solution)/shard_map/ppermute | solution.py:35
  108.4 8.0 %copy-start.4 = (bf16[1024,1024]{1,0:T(8,128)(2,1)S(1)}, bf16[1024,1024]{1,0:T(8,128)(2,1)}, u32[]{:S(2)}) copy-start(bf16[1024,1024]{1,0:T(8,128)(2,1)} %param.13) | copy-start | bytes 6291460
  110.5 4.3 %collective-permute-start.12 = (f32[2,1024]{1,0:T(2,128)S(1)}, f32[2,1024]{1,0:T(2,128)S(1)}, u32[]{:S(2)}, u32[]{:S(2)}) collective-permute-start(f32[2,1024]{1,0:T(2,128)S(1)} %select_bitcast_fusion.2), channel_id=1, source_target_pairs={{0,16},{8,24},{16,0},{24,8},{1,17},{9,25},{17,1},{25,9},{2,18},{10... | collective-permute-start | bytes 24584 | tf_op jit(solution)/shard_map/ppermute | solution.py:35
  115.7 1.3 %slice-start = ((f32[320,1024]{1,0:T(8,128)}), f32[128,1024]{1,0:T(8,128)S(1)}, s32[]{:S(2)}) async-start(f32[320,1024]{1,0:T(8,128)} %copy-done.8), calls=%async_computation | async-start | bytes 1048576 | tf_op jit(solution)/shard_map/slice | solution.py:341
  115.7 1.4 %copy-start.20 = (bf16[128,1024]{1,0:T(8,128)(2,1)S(1)}, bf16[128,1024]{1,0:T(8,128)(2,1)}, u32[]{:S(2)}) copy-start(bf16[128,1024]{1,0:T(8,128)(2,1)} %get-tuple-element.7) | copy-start | bytes 786436
